TPU v7x, 32 devices: a whole 2x2x4 slice. The times are simulated.
32 devices in a mesh: groups: 2 (over y), dp: 4 (over x, core), head: 4 (over z).
Axes of the slice: x: 2, y: 2, z: 4, core: 2. Of those that a mesh axis runs over, the one named last changes fastest.
Arguments:
- activations: bfloat16 [64, 4, 2048], P(('groups', 'head'), None, 'dp'), parts along dimension 0, may hold values from -6 to 6
- w_qk: bfloat16 [2048, 4096], P('dp', 'head'), may hold values from -0.125 to 0.125
- w_vz: bfloat16 [2048, 8192], P('dp', 'head'), may hold values from -0.125 to 0.125
- w_ba: bfloat16 [2048, 64], P('dp', 'head'), may hold values from -0.125 to 0.125
- conv_qk: bfloat16 [4, 4096], P(None, 'head'), may hold values from -3 to 3
- conv_v: bfloat16 [4, 4096], P(None, 'head'), may hold values from -3 to 3
- a_log: float32 [32], P('head'), may hold values from -1.5 to 1.5
- dt_bias: float32 [32], P('head'), may hold values from -2 to 1
- norm_gain: float32 [128], replicated, may hold values from 0.1 to 1.9
- w_out: bfloat16 [4096, 2048], P('head', 'dp'), may hold values from -0.09375 to 0.09375
- conv_state_qk: bfloat16 [64, 3, 4096], P(('groups', 'dp'), None, 'head'), parts along dimension 0, may hold values from -6 to 6
- conv_state_v: bfloat16 [64, 3, 4096], P(('groups', 'dp'), None, 'head'), parts along dimension 0, may hold values from -6 to 6
- memory_state: float32 [64, 32, 128, 128], P(('groups', 'dp'), 'head'), parts along dimension 0, may hold values from -4 to 4
Outputs:
- layer_out: bfloat16 [64, 4, 2048], P(('groups', 'head'), None, 'dp'), parts along dimension 0
- new_state: float32 [64, 32, 128, 128], P(('groups', 'dp'), 'head'), parts along dimension 0
There are 2 independent parts, one for each index of `groups`. A program takes and returns all parts, laid end to end along the dimension named above; an argument that names none is the same for every part. Nothing has to cross between parts.
All inputs are finite; a program needn't handle non-finite values.
Results may differ from a plain program's by a relative error of at most 0.0069.
Values may be sent and summed in bfloat16 or wider, within the bound.
No kernel may reach another device: no remote copies, remote signals or barrier semaphores. Data moves between devices by JAX's collectives and lax.ppermute only.
A program may use at most 64 MiB of HBM per device.

v0:
```python
import jax
import jax.numpy as jnp
from jax import lax
from jax.sharding import PartitionSpec as P

HK = 16
HV = 32
DK = 128
DV = 128


def conv_apply(window, taps):
    mixed = jnp.sum(window.astype(jnp.float32) * taps.astype(jnp.float32)[None], axis=1)
    return jax.nn.silu(mixed)


def normalize(vectors):
    return vectors * lax.rsqrt(jnp.sum(vectors * vectors, axis=-1, keepdims=True) + 1e-06)


def prepare(
    qk_proj,
    vz_proj,
    ba_proj,
    conv_qk,
    conv_v,
    a_log,
    dt_bias,
    conv_state_qk,
    conv_state_v,
    head_ratio,
):
    row_count = qk_proj.shape[0]
    window_qk = jnp.concatenate([conv_state_qk, qk_proj[:, None, :]], axis=1)
    split_vz = vz_proj.reshape(row_count, -1, 2, DV)
    values_now = split_vz[:, :, 0, :].reshape(row_count, -1)
    gate_z = split_vz[:, :, 1, :].astype(jnp.float32)
    window_v = jnp.concatenate([conv_state_v, values_now[:, None, :]], axis=1)
    qk_conv = conv_apply(window_qk, conv_qk).reshape(row_count, -1, 2, DK)
    v_conv = conv_apply(window_v, conv_v).reshape(row_count, -1, DV)
    queries = normalize(qk_conv[:, :, 0, :]) * DK ** (-0.5)
    key_vec = normalize(qk_conv[:, :, 1, :])
    queries = jnp.repeat(queries, head_ratio, axis=1)
    key_vec = jnp.repeat(key_vec, head_ratio, axis=1)
    split_ba = ba_proj.reshape(row_count, -1, 2).astype(jnp.float32)
    beta_gate = jax.nn.sigmoid(split_ba[:, :, 0])
    log_decay = -jnp.exp(a_log)[None, :] * jax.nn.softplus(split_ba[:, :, 1] + dt_bias[None, :])
    return (
        queries,
        key_vec,
        v_conv,
        gate_z,
        beta_gate,
        log_decay,
        window_qk[:, 1:],
        window_v[:, 1:],
    )


def recurrent(queries, key_vec, values, beta_gate, log_decay, memory_state):
    memory_state = memory_state * jnp.exp(log_decay)[:, :, None, None]
    recalled = jnp.sum(key_vec[:, :, :, None] * memory_state, axis=2)
    correction = (values - recalled) * beta_gate[:, :, None]
    memory_state = memory_state + key_vec[:, :, :, None] * correction[:, :, None, :]
    readout = jnp.sum(queries[:, :, :, None] * memory_state, axis=2)
    return (memory_state, readout)


def finish(readout, gate_z, norm_gain):
    scale = lax.rsqrt(jnp.mean(readout * readout, axis=-1, keepdims=True) + 1e-06)
    normed = readout * scale * norm_gain[None, None, :] * jax.nn.silu(gate_z)
    return normed.reshape(readout.shape[0], -1).astype(jnp.bfloat16)


def shards(
    activations,
    w_qk,
    w_vz,
    w_ba,
    conv_qk,
    conv_v,
    a_log,
    dt_bias,
    norm_gain,
    w_out,
    conv_state_qk,
    conv_state_v,
    memory_state,
):
    head_ratio = HV // HK
    step_count = activations.shape[1]
    width_qk = w_qk.shape[1]
    width_vz = w_vz.shape[1]
    joined = jnp.concatenate([w_qk, w_vz, w_ba], axis=1)
    outputs = []
    for step_index in range(step_count):
        step_rows = lax.all_gather(activations[:, step_index, :], "head", axis=0, tiled=True)
        summed = lax.psum_scatter(
            jnp.dot(step_rows, joined, preferred_element_type=jnp.float32),
            "dp",
            scatter_dimension=0,
            tiled=True,
        )
        qk_proj = summed[..., :width_qk].astype(jnp.bfloat16)
        vz_proj = summed[..., width_qk : width_qk + width_vz].astype(jnp.bfloat16)
        ba_proj = summed[..., width_qk + width_vz :].astype(jnp.bfloat16)
        queries, key_vec, values, gate_z, beta_gate, log_decay, conv_state_qk, conv_state_v = (
            prepare(
                qk_proj,
                vz_proj,
                ba_proj,
                conv_qk,
                conv_v,
                a_log,
                dt_bias,
                conv_state_qk,
                conv_state_v,
                head_ratio,
            )
        )
        memory_state, readout = recurrent(
            queries, key_vec, values, beta_gate, log_decay, memory_state
        )
        normed = finish(readout, gate_z, norm_gain)
        partials = jnp.dot(
            lax.all_gather(normed, "dp", axis=0, tiled=True),
            w_out,
            preferred_element_type=jnp.float32,
        )
        outputs.append(
            lax.psum_scatter(partials, "head", scatter_dimension=0, tiled=True).astype(jnp.bfloat16)
        )
    layer_out = jnp.stack(outputs, axis=1)
    return (layer_out, memory_state)


def solution(mesh):
    in_specs = (
        P(("groups", "head"), None, "dp"),
        P("dp", "head"),
        P("dp", "head"),
        P("dp", "head"),
        P(None, "head"),
        P(None, "head"),
        P("head"),
        P("head"),
        P(),
        P("head", "dp"),
        P(("groups", "dp"), None, "head"),
        P(("groups", "dp"), None, "head"),
        P(("groups", "dp"), "head", None, None),
    )
    out_specs = (P(("groups", "head"), None, "dp"), P(("groups", "dp"), "head", None, None))
    return jax.shard_map(shards, mesh=mesh, in_specs=in_specs, out_specs=out_specs, check_vma=False)
```

profile of v0, /device:TPU:0, one launch (start us, length us, event | category | flops | bytes accessed | tf_op | source)
XLA Modules:
  0.0 257.1 jit_solution(13594392952404040665)
XLA Ops:
  7.2 1.0 fusion.68
  8.3 14.8 %all-gather.3 = bf16[32,1,512]{2,0,1:T(8,128)(2,1)S(1)} all-gather(bf16[8,1,512]{2,0,1:T(8,128)(2,1)S(1)} %copy.396), channel_id=5, replica_groups=mesh['groups'=2,'dp'=4,'head'=4] {'head'}, dimensions={0}, use_global_device_ids=true | all-gather | bytes 40960 | tf_op jit(solution)/shard_map/all_gather | solution.py:97
  23.1 13.1 %all-gather = bf16[32,1,512]{2,0,1:T(8,128)(2,1)S(1)} all-gather(bf16[8,1,512]{2,0,1:T(8,128)(2,1)S(1)} %copy.384), channel_id=2, replica_groups=mesh['groups'=2,'dp'=4,'head'=4] {'head'}, dimensions={0}, use_global_device_ids=true | all-gather | bytes 40960 | tf_op jit(solution)/shard_map/all_gather | solution.py:97
  36.2 13.1 %all-gather.1 = bf16[32,1,512]{2,0,1:T(8,128)(2,1)S(1)} all-gather(bf16[8,1,512]{2,0,1:T(8,128)(2,1)S(1)} %copy.388), channel_id=3, replica_groups=mesh['groups'=2,'dp'=4,'head'=4] {'head'}, dimensions={0}, use_global_device_ids=true | all-gather | bytes 40960 | tf_op jit(solution)/shard_map/all_gather | solution.py:97
  49.3 13.1 %all-gather.2 = bf16[32,1,512]{2,0,1:T(8,128)(2,1)S(1)} all-gather(bf16[8,1,512]{2,0,1:T(8,128)(2,1)S(1)} %copy.392), channel_id=4, replica_groups=mesh['groups'=2,'dp'=4,'head'=4] {'head'}, dimensions={0}, use_global_device_ids=true | all-gather | bytes 40960 | tf_op jit(solution)/shard_map/all_gather | solution.py:97
  62.4 0.8 copy.321
  63.3 2.5 convolution_bitcast_fusion.1
  65.8 2.7 %convolution_bitcast_fusion.2 = f32[32,3088]{1,0:T(8,128)S(1)} fusion(bf16[32,1,512]{2,0,1:T(8,128)(2,1)S(1)} %all-gather.1, bf16[512,16]{1,0:T(8,128)(2,1)S(1)} %copy.321, bf16[512,2048]{1,0:T(8,128)(2,1)} %param.15, bf16[512,1024]{1,0:T(8,128)(2,1)} %param.14), kind=kOutput, calls=%fused_computation.2 | convolution fusion | flops 110673920 | bytes 3590144 | tf_op jit(solution)/shard_map/dot_general | solution.py:99
  68.6 0.7 convolution_bitcast_fusion.3
  69.3 0.7 convolution_bitcast_fusion
  71.3 33.3 %all-reduce.6 = (bf16[32,3088]{1,0:T(8,128)(2,1)S(1)}, bf16[32,3088]{1,0:T(8,128)(2,1)S(1)}, bf16[32,3088]{1,0:T(8,128)(2,1)S(1)}, bf16[32,3088]{1,0:T(8,128)(2,1)S(1)}) all-reduce(f32[32,3088]{1,0:T(8,128)S(1)} %convolution_bitcast_fusion, ...), channel_id=12, replica_groups=mesh['groups'=2,'dp'=4,'head'=4] {'dp'}, use_global_device_ids=true, to_apply=%region_27.28.clone | all-reduce | flops 395264 | bytes 2371584
  105.0 0.7 slice_bitcast_fusion
  105.7 0.8 slice.239
  106.9 0.7 slice_bitcast_fusion.2
  108.7 0.7 slice_bitcast_fusion.1
  110.4 0.7 slice_bitcast_fusion.3
  113.5 0.8 constant_dynamic-update-slice_fusion.1
  115.7 1.7 copy.363
  117.4 1.8 fusion.67
  119.2 1.7 copy.407
  122.9 1.0 copy.337
  123.9 0.8 fusion.65
  124.7 1.1 copy.391
  125.9 0.8 fusion.70
  128.4 0.8 fusion.72
  129.9 0.9 multiply_reduce_fusion.15
  131.8 0.7 fusion.63
  132.6 3.1 %multiply_reduce_fusion.7 = f32[8,8,128]{2,1,0:T(8,128)S(1)} fusion(f32[8,8,128,128]{3,2,1,0:T(8,128)} %param.25, f32[8,8,128]{2,1,0:T(8,128)S(1)} %bitcast.331, f32[8,8]{1,0:T(8,128)S(1)} %get-tuple-element.80), kind=kLoop, calls=%fused_computation.15 | loop fusion | flops 3137536 | bytes 4260096 | tf_op jit(solution)/shard_map/reduce_sum | solution.py:62
  135.8 3.0 %multiply_reduce_fusion.5 = f32[8,8,128]{2,1,0:T(8,128)S(1)} fusion(f32[8,8,128,128]{3,2,1,0:T(8,128)S(1)} %copy-done.1, f32[8,8,128]{2,1,0:T(8,128)S(1)} %bitcast.340, f32[8,8]{1,0:T(8,128)S(1)} %get-tuple-element.78, f32[8,8,128]{2,1,0:T(8,128)S(1)} %fusion.40, f32[8,8,128]{2,1,0:T(8,128)S(1)} %bitcast.332, f32[8,8]{1,0:T(8,128)S(1)} %get-tuple-element.80), kind=kLoop, calls=%fused_computation.12 | loop fusion | flops 6283264 | bytes 4325888 | tf_op jit(solution)/shard_map/reduce_sum | solution.py:62
  139.0 5.3 %multiply_reduce_fusion.4 = (f32[8,8,128]{2,1,0:T(8,128)S(1)}, f32[8,8,128]{2,1,0:T(8,128)S(1)}) fusion(f32[8,8,128]{2,1,0:T(8,128)S(1)} %bitcast.353, f32[8,8,128]{2,1,0:T(8,128)S(1)} %fusion.31, f32[8,8,128]{2,1,0:T(8,128)S(1)} %bitcast.341, f32[8,8]{1,0:T(8,128)S(1)} %get-tuple-element.78, f32[8,8,128]{2,1,0:T(8,128)S(1)} %fusion.40, ...), kind=kLoop, calls=%fused_computation.10 | loop fusion | flops 11517952 | bytes 4457216 | tf_op jit(solution)/shard_map/reduce_sum | solution.py:65
  144.8 9.5 %multiply_reduce_fusion.2 = (f32[8,8,128]{2,1,0:T(8,128)S(1)}, f32[8,8,128]{2,1,0:T(8,128)S(1)}, f32[8,8,128]{2,1,0:T(8,128)S(1)}) fusion(f32[8,8,128]{2,1,0:T(8,128)S(1)} %fusion.22, f32[8,8,128]{2,1,0:T(8,128)S(1)} %bitcast.345, f32[8,8]{1,0:T(8,128)S(1)} %get-tuple-element.79, f32[8,8,128]{2,1,0:T(8,128)S(1)} %bitcast.352, f32[8,8,128]{2,1,0:T(8,128)S(1)} %fusion.31, ...), kind=kLoop, calls=%fused_computation.7 | loop fusion | flops 16752640 | bytes 4588544 | tf_op jit(solution)/shard_map/reduce_sum | solution.py:65
  155.1 9.4 %multiply_reduce_fusion = (f32[8,8,128]{2,1,0:T(8,128)S(1)}, f32[8,8,128,128]{3,2,1,0:T(8,128)}) fusion(f32[8,8,128]{2,1,0:T(8,128)S(1)} %bitcast.350, f32[8,8,128]{2,1,0:T(8,128)S(1)} %fusion.13, f32[8,8,128]{2,1,0:T(8,128)S(1)} %bitcast.348, f32[8,8]{1,0:T(8,128)S(1)} %get-tuple-element.77, f32[8,8,128]{2,1,0:T(8,128)S(1)} %fusion.22, ...), kind=kLoop, calls=%fused_computation.4 | loop fusion | flops 14671872 | bytes 8717312 | tf_op jit(solution)/shard_map/reduce_sum | solution.py:65
  164.9 5.2 %all_gather.25 = bf16[32,1024]{1,0:T(8,128)(2,1)S(1)} all-gather(bf16[8,1024]{1,0:T(8,128)(2,1)S(1)} %get-tuple-element.65), channel_id=1, replica_groups=mesh['groups'=2,'dp'=4,'head'=4] {'dp'}, dimensions={0}, use_global_device_ids=true | all-gather | bytes 81920 | tf_op jit(solution)/shard_map/all_gather | solution.py:126
  170.1 0.9 fusion.73
  171.1 5.2 %all_gather.27 = bf16[32,1024]{1,0:T(8,128)(2,1)S(1)} all-gather(bf16[8,1024]{1,0:T(8,128)(2,1)S(1)} %get-tuple-element.66), channel_id=1, replica_groups=mesh['groups'=2,'dp'=4,'head'=4] {'dp'}, dimensions={0}, use_global_device_ids=true | all-gather | bytes 81920 | tf_op jit(solution)/shard_map/all_gather | solution.py:126
  176.3 0.9 fusion.74
  177.3 5.2 %all_gather.29 = bf16[32,1024]{1,0:T(8,128)(2,1)S(1)} all-gather(bf16[8,1024]{1,0:T(8,128)(2,1)S(1)} %get-tuple-element.67), channel_id=1, replica_groups=mesh['groups'=2,'dp'=4,'head'=4] {'dp'}, dimensions={0}, use_global_device_ids=true | all-gather | bytes 81920 | tf_op jit(solution)/shard_map/all_gather | solution.py:126
  182.6 0.9 fusion.75
  183.5 5.2 %all_gather.31 = bf16[32,1024]{1,0:T(8,128)(2,1)S(1)} all-gather(bf16[8,1024]{1,0:T(8,128)(2,1)S(1)} %get-tuple-element.68), channel_id=1, replica_groups=mesh['groups'=2,'dp'=4,'head'=4] {'dp'}, dimensions={0}, use_global_device_ids=true | all-gather | bytes 81920 | tf_op jit(solution)/shard_map/all_gather | solution.py:126
  188.8 0.9 fusion.76
  189.7 1.0 reduce-scatter.5.cloned.1.call-done
  190.7 0.7 convert_bitcast_fusion.7
  191.4 18.9 %reduce-scatter.7.cloned.1.call-done = f32[8,512]{1,0:T(8,128)} async-done(((f32[32,512]{1,0:T(8,128)}), f32[8,512]{1,0:T(8,128)}) %reduce-scatter.7.cloned.1.call-update) | async-done | bytes 16400 | tf_op jit(solution)/shard_map/reduce_scatter | solution.py:131
  210.3 0.7 convert_bitcast_fusion.6
  211.1 18.8 %reduce-scatter.9.cloned.1.call-done = f32[8,512]{1,0:T(8,128)} async-done(((f32[32,512]{1,0:T(8,128)}), f32[8,512]{1,0:T(8,128)}) %reduce-scatter.9.cloned.1.call-update) | async-done | bytes 16400 | tf_op jit(solution)/shard_map/reduce_scatter | solution.py:131
  229.8 0.7 convert_bitcast_fusion.5
  230.5 18.6 %reduce-scatter.11.cloned.1.call-done = f32[8,512]{1,0:T(8,128)} async-done(((f32[32,512]{1,0:T(8,128)}), f32[8,512]{1,0:T(8,128)}) %reduce-scatter.11.cloned.1.call-update) | async-done | bytes 16400 | tf_op jit(solution)/shard_map/reduce_scatter | solution.py:131
  249.2 0.7 convert_bitcast_fusion.4
  (173 shorter events, 15.4 us)
Async XLA Ops:
  7.2 162.9 %copy-start = (bf16[1024,512]{1,0:T(8,128)(2,1)S(1)}, bf16[1024,512]{1,0:T(8,128)(2,1)}, u32[]{:S(2)}) copy-start(bf16[1024,512]{1,0:T(8,128)(2,1)} %param.22) | copy-start | bytes 3145732
  7.2 183.5 %reduce-scatter.5.cloned.1.call-start = ((), (), s32[]{:S(2)}) async-start(), calls=%async_computation.4 | async-start | bytes 81920 | tf_op jit(solution)/shard_map/reduce_scatter | solution.py:131
  65.8 2.7 %copy-start.18 = (bf16[512,2048]{1,0:T(8,128)(2,1)S(1)}, bf16[512,2048]{1,0:T(8,128)(2,1)}, u32[]{:S(2)}) copy-start(bf16[512,2048]{1,0:T(8,128)(2,1)} %param.15) | copy-start | bytes 6291460
  65.8 2.8 %copy-start.19 = (bf16[512,1024]{1,0:T(8,128)(2,1)S(1)}, bf16[512,1024]{1,0:T(8,128)(2,1)}, u32[]{:S(2)}) copy-start(bf16[512,1024]{1,0:T(8,128)(2,1)} %param.14) | copy-start | bytes 3145732
  69.3 0.7 copy-start.21
  105.7 5.5 %copy-start.20 = (f32[8]{0:T(128)S(1)}, f32[8]{0:T(128)}, u32[]{:S(2)}) copy-start(f32[8]{0:T(128)} %param.19) | copy-start | bytes 100
  105.7 6.0 %copy-start.17 = (f32[128]{0:T(128)S(1)}, f32[128]{0:T(128)}, u32[]{:S(2)}) copy-start(f32[128]{0:T(128)} %param.21) | copy-start | bytes 1540
  105.7 6.6 %copy-start.15 = (bf16[4,1024]{1,0:T(4,128)(2,1)S(1)}, bf16[4,1024]{1,0:T(4,128)(2,1)}, u32[]{:S(2)}) copy-start(bf16[4,1024]{1,0:T(4,128)(2,1)} %param.17) | copy-start | bytes 24580
  105.7 7.2 %copy-start.16 = (bf16[4,1024]{1,0:T(4,128)(2,1)S(1)}, bf16[4,1024]{1,0:T(4,128)(2,1)}, u32[]{:S(2)}) copy-start(bf16[4,1024]{1,0:T(4,128)(2,1)} %param.18) | copy-start | bytes 24580
  111.2 16.8 %copy-start.3 = (bf16[8,1,1024]{0,2,1:T(8,128)(2,1)S(1)}, bf16[8,1,1024]{0,2,1:T(8,128)(2,1)}, u32[]{:S(2)}) copy-start(bf16[8,1,1024]{0,2,1:T(8,128)(2,1)} %slice_bitcast_fusion.1) | copy-start | bytes 49156
  111.2 18.2 %copy-start.2 = (bf16[8,1,1024]{0,2,1:T(8,128)(2,1)S(1)}, bf16[8,1,1024]{0,2,1:T(8,128)(2,1)}, u32[]{:S(2)}) copy-start(bf16[8,1,1024]{0,2,1:T(8,128)(2,1)} %slice_bitcast_fusion.3) | copy-start | bytes 49156
  111.2 18.6 %copy-start.4 = (bf16[8,3,1024]{2,0,1:T(8,128)(2,1)S(1)}, bf16[8,3,1024]{2,0,1:T(8,128)(2,1)}, u32[]{:S(2)}) copy-start(bf16[8,3,1024]{2,0,1:T(8,128)(2,1)} %param.23) | copy-start | bytes 147460
  125.9 4.0 %copy-start.7 = (bf16[8,1,1024]{2,0,1:T(8,128)(2,1)S(1)}, bf16[8,1,1024]{2,0,1:T(8,128)(2,1)}, u32[]{:S(2)}) copy-start(bf16[8,1,1024]{2,0,1:T(8,128)(2,1)} %copy.363) | copy-start | bytes 49156
  128.1 3.7 %copy-start.12 = (f32[8,8,1]{1,0,2:T(8,128)S(1)}, f32[8,8,1]{1,0,2:T(8,128)}, u32[]{:S(2)}) copy-start(f32[8,8,1]{1,0,2:T(8,128)} %copy.341) | copy-start | bytes 772
  128.1 3.7 %copy-start.13 = (f32[8,8,1]{1,0,2:T(8,128)S(1)}, f32[8,8,1]{1,0,2:T(8,128)}, u32[]{:S(2)}) copy-start(f32[8,8,1]{1,0,2:T(8,128)} %copy.354) | copy-start | bytes 772
  129.3 6.3 %copy-start.6 = (bf16[8,1,1024]{2,0,1:T(8,128)(2,1)S(1)}, bf16[8,1,1024]{2,0,1:T(8,128)(2,1)}, u32[]{:S(2)}) copy-start(bf16[8,1,1024]{2,0,1:T(8,128)(2,1)} %copy.407) | copy-start | bytes 49156
  129.3 6.3 %copy-start.8 = (f32[4,1024]{1,0:T(4,128)S(1)}, f32[4,1024]{1,0:T(4,128)}, u32[]{:S(2)}) copy-start(f32[4,1024]{1,0:T(4,128)} %convert_element_type.129) | copy-start | bytes 49156
  129.8 6.1 %copy-start.1 = (f32[8,8,128,128]{3,2,1,0:T(8,128)S(1)}, f32[8,8,128,128]{3,2,1,0:T(8,128)}, u32[]{:S(2)}) copy-start(f32[8,8,128,128]{3,2,1,0:T(8,128)} %param.25) | copy-start | bytes 12582916
  132.6 6.2 %copy-start.10 = (f32[8,8]{1,0:T(8,128)S(1)}, f32[8,8]{1,0:T(8,128)}, u32[]{:S(2)}) copy-start(f32[8,8]{1,0:T(8,128)} %divide_bitcast_fusion.2) | copy-start | bytes 772
  135.8 8.8 %copy-start.11 = (f32[8,8]{1,0:T(8,128)S(1)}, f32[8,8]{1,0:T(8,128)}, u32[]{:S(2)}) copy-start(f32[8,8]{1,0:T(8,128)} %divide_bitcast_fusion.1) | copy-start | bytes 772
  138.9 16.0 %copy-start.9 = (f32[8,8]{1,0:T(8,128)S(1)}, f32[8,8]{1,0:T(8,128)}, u32[]{:S(2)}) copy-start(f32[8,8]{1,0:T(8,128)} %divide_bitcast_fusion) | copy-start | bytes 772
  155.1 9.7 %copy-start.5 = (f32[1,8,8,128]{3,2,1,0:T(8,128)S(1)}, f32[1,8,8,128]{3,2,1,0:T(8,128)}, u32[]{:S(2)}) copy-start(f32[1,8,8,128]{3,2,1,0:T(8,128)} %convert_bitcast_fusion) | copy-start | bytes 98308
  155.1 9.7 %copy-start.14 = (f32[1024]{0:T(1024)S(1)}, f32[1024]{0:T(1024)}, u32[]{:S(2)}) copy-start(f32[1024]{0:T(1024)} %broadcast_bitcast_fusion) | copy-start | bytes 12292
  171.0 39.3 %reduce-scatter.7.cloned.1.call-start = ((), (), s32[]{:S(2)}) async-start(), calls=%async_computation.5 | async-start | bytes 81920 | tf_op jit(solution)/shard_map/reduce_scatter | solution.py:131
  177.3 52.5 %reduce-scatter.9.cloned.1.call-start = ((), (), s32[]{:S(2)}) async-start(), calls=%async_computation.6 | async-start | bytes 81920 | tf_op jit(solution)/shard_map/reduce_scatter | solution.py:131
  183.5 65.7 %reduce-scatter.11.cloned.1.call-start = ((), (), s32[]{:S(2)}) async-start(), calls=%async_computation.7 | async-start | bytes 81920 | tf_op jit(solution)/shard_map/reduce_scatter | solution.py:131
Sparse Core Ops, SparseCore 0:
  171.2 19.5 reduce-scatter.4
  193.0 17.2 reduce-scatter.6
  212.6 17.1 reduce-scatter.8
  232.0 17.1 reduce-scatter.10
where the time goes:
time: 258 us; the launch traced here: 257 us
  blocking collectives  108 us (42%)
  waiting for transfers between devices  57.4 us (22%)
  other arithmetic  41 us (16%)
  local copies, waits for them, and re-layouts  24.8 us (10%)
  between operations  15.1 us (6%)
  matrix products  10.2 us (4%)
    reduce_scatter x4, waiting for transfers between devices, shards(): lax.psum_scatter(partials, 'head', scatter_dimension=0, tiled=True)  57.3 us
    all_gather x4, blocking collectives, shards(): lax.all_gather(activations[:, step_index, :], 'head', axis=0, tiled=True)  54.2 us
    unnamed x1, blocking collectives  33.3 us
    reduce_sum x3, other arithmetic, recurrent(): readout = jnp.sum(queries[:, :, :, None] * memory_state, axis=2)  24.2 us
    all_gather x4, blocking collectives, shards(): lax.all_gather(normed, 'dp', axis=0, tiled=True)  21 us
    dot_general x4, matrix products, shards(): jnp.dot(step_rows, joined, preferred_element_type=jnp.float32)  6.59 us
    reduce_sum x2, other arithmetic, recurrent(): recalled = jnp.sum(key_vec[:, :, :, None] * memory_state, axis=2)  6.01 us
    broadcast_in_dim x8, local copies, waits for them, and re-layouts, prepare(): window_qk = jnp.concatenate([conv_state_qk, qk_proj[:, None, :]], axis=1)  5.8 us
  transfers between devices with their start and end apart: 4, of which 4 were waited for; matrix products, arithmetic and copies ran while one was open for 2% of the time, Pallas kernels for 0%

commit v1 on v0

v1 whole, which is shorter than its diff:
```python
import functools

import jax
import jax.numpy as jnp
from jax import lax
from jax.experimental import pallas as pl
from jax.experimental.pallas import tpu as pltpu
from jax.sharding import PartitionSpec as P

HK = 16
HV = 32
DK = 128
DV = 128


def normalize(vectors):
    return vectors * lax.rsqrt(jnp.sum(vectors * vectors, axis=-1, keepdims=True) + 1e-06)


def conv_steps(state, proj, taps):
    seq = jnp.concatenate([state, proj], axis=1).astype(jnp.float32)
    taps = taps.astype(jnp.float32)
    kernel = taps.shape[0]
    steps = proj.shape[1]
    mixed = sum(seq[:, k : k + steps, :] * taps[k][None, None, :] for k in range(kernel))
    return jax.nn.silu(mixed)


def recurrence_kernel(decay_ref, beta_ref, qt_ref, kt_ref, v_ref, s_ref, s_out, o_ref, *, heads, steps):
    r = pl.program_id(0)
    for h in range(heads):
        state = s_ref[0, h]
        for t in range(steps):
            c = t * heads + h
            key_col = kt_ref[0, :, c : c + 1]
            query_col = qt_ref[0, :, c : c + 1]
            state = state * decay_ref[r, c]
            recalled = jnp.sum(key_col * state, axis=0, keepdims=True)
            correction = (v_ref[0, c : c + 1, :] - recalled) * beta_ref[r, c]
            state = state + key_col * correction
            o_ref[0, c : c + 1, :] = jnp.sum(query_col * state, axis=0, keepdims=True)
        s_out[0, h] = state


def recurrence(decay, beta, qt, kt, values, memory_state):
    rows, heads = memory_state.shape[0], memory_state.shape[1]
    cols = decay.shape[1]
    steps = cols // heads
    kern = functools.partial(recurrence_kernel, heads=heads, steps=steps)
    return pl.pallas_call(
        kern,
        grid=(rows,),
        in_specs=[
            pl.BlockSpec(memory_space=pltpu.SMEM),
            pl.BlockSpec(memory_space=pltpu.SMEM),
            pl.BlockSpec((1, DK, cols), lambda r: (r, 0, 0)),
            pl.BlockSpec((1, DK, cols), lambda r: (r, 0, 0)),
            pl.BlockSpec((1, cols, DV), lambda r: (r, 0, 0)),
            pl.BlockSpec((1, heads, DK, DV), lambda r: (r, 0, 0, 0)),
        ],
        out_specs=[
            pl.BlockSpec((1, heads, DK, DV), lambda r: (r, 0, 0, 0)),
            pl.BlockSpec((1, cols, DV), lambda r: (r, 0, 0)),
        ],
        out_shape=[
            jax.ShapeDtypeStruct(memory_state.shape, jnp.float32),
            jax.ShapeDtypeStruct((rows, cols, DV), jnp.float32),
        ],
        cost_estimate=pl.CostEstimate(
            flops=8 * rows * cols * DK * DV,
            bytes_accessed=2 * memory_state.size * 4,
            transcendentals=0,
        ),
    )(decay, beta, qt, kt, values, memory_state)


def shards(
    activations,
    w_qk,
    w_vz,
    w_ba,
    conv_qk,
    conv_v,
    a_log,
    dt_bias,
    norm_gain,
    w_out,
    conv_state_qk,
    conv_state_v,
    memory_state,
):
    head_ratio = HV // HK
    step_count = activations.shape[1]
    rows_mem = memory_state.shape[0]
    heads = memory_state.shape[1]
    width_qk = w_qk.shape[1]
    width_vz = w_vz.shape[1]

    step_rows = lax.all_gather(activations, "head", axis=0, tiled=True)
    flat_rows = step_rows.reshape(-1, step_rows.shape[-1])
    partial_qk = jnp.dot(flat_rows, w_qk, preferred_element_type=jnp.float32)
    partial_vz = jnp.dot(flat_rows, w_vz, preferred_element_type=jnp.float32)
    partial_ba = jnp.dot(flat_rows, w_ba, preferred_element_type=jnp.float32)
    summed = lax.psum_scatter(
        jnp.concatenate([partial_qk, partial_vz, partial_ba], axis=1),
        "dp",
        scatter_dimension=0,
        tiled=True,
    )
    summed_qk = summed[:, :width_qk]
    summed_vz = summed[:, width_qk : width_qk + width_vz]
    summed_ba = summed[:, width_qk + width_vz :]
    qk_proj = summed_qk.astype(jnp.bfloat16).reshape(rows_mem, step_count, width_qk)
    vz_proj = summed_vz.astype(jnp.bfloat16).reshape(rows_mem, step_count, width_vz)
    ba_proj = summed_ba.astype(jnp.bfloat16).reshape(rows_mem, step_count, -1)

    split_vz = vz_proj.reshape(rows_mem, step_count, heads, 2, DV)
    values_now = split_vz[:, :, :, 0, :].reshape(rows_mem, step_count, heads * DV)
    gate_z = split_vz[:, :, :, 1, :].astype(jnp.float32)

    qk_conv = conv_steps(conv_state_qk, qk_proj, conv_qk).reshape(rows_mem, step_count, -1, 2, DK)
    v_conv = conv_steps(conv_state_v, values_now, conv_v).reshape(rows_mem, step_count * heads, DV)
    queries = normalize(qk_conv[:, :, :, 0, :]) * DK ** (-0.5)
    key_vec = normalize(qk_conv[:, :, :, 1, :])
    queries = jnp.repeat(queries, head_ratio, axis=2)
    key_vec = jnp.repeat(key_vec, head_ratio, axis=2)
    qt = queries.transpose(0, 3, 1, 2).reshape(rows_mem, DK, step_count * heads)
    kt = key_vec.transpose(0, 3, 1, 2).reshape(rows_mem, DK, step_count * heads)

    split_ba = ba_proj.reshape(rows_mem, step_count, heads, 2).astype(jnp.float32)
    beta_gate = jax.nn.sigmoid(split_ba[..., 0])
    log_decay = -jnp.exp(a_log)[None, None, :] * jax.nn.softplus(split_ba[..., 1] + dt_bias[None, None, :])
    decay = jnp.exp(log_decay).reshape(rows_mem, step_count * heads)
    beta_gate = beta_gate.reshape(rows_mem, step_count * heads)

    new_state, readout = recurrence(decay, beta_gate, qt, kt, v_conv, memory_state)
    readout = readout.reshape(rows_mem, step_count, heads, DV)

    scale = lax.rsqrt(jnp.mean(readout * readout, axis=-1, keepdims=True) + 1e-06)
    normed = readout * scale * norm_gain[None, None, None, :] * jax.nn.silu(gate_z)
    normed = normed.reshape(rows_mem, step_count, heads * DV).astype(jnp.bfloat16)

    all_normed = lax.all_gather(normed, "dp", axis=0, tiled=True)
    partials = jnp.dot(
        all_normed.reshape(-1, all_normed.shape[-1]), w_out, preferred_element_type=jnp.float32
    )
    layer_out = lax.psum_scatter(partials, "head", scatter_dimension=0, tiled=True)
    layer_out = layer_out.astype(jnp.bfloat16).reshape(-1, step_count, w_out.shape[1])
    return (layer_out, new_state)


def solution(mesh):
    in_specs = (
        P(("groups", "head"), None, "dp"),
        P("dp", "head"),
        P("dp", "head"),
        P("dp", "head"),
        P(None, "head"),
        P(None, "head"),
        P("head"),
        P("head"),
        P(),
        P("head", "dp"),
        P(("groups", "dp"), None, "head"),
        P(("groups", "dp"), None, "head"),
        P(("groups", "dp"), "head", None, None),
    )
    out_specs = (P(("groups", "head"), None, "dp"), P(("groups", "dp"), "head", None, None))
    return jax.shard_map(shards, mesh=mesh, in_specs=in_specs, out_specs=out_specs, check_vma=False)
```

time: 258 us -> 120 us (0.47)
  blocking collectives: 108 us -> 21.2 us
  other arithmetic: 41 us -> 5.56 us
  Pallas kernels: 0 us -> 12 us
  waiting for transfers between devices: 57.4 us -> 47.3 us
  local copies, waits for them, and re-layouts: 24.8 us -> 15 us
  matrix products: 10.2 us -> 3.6 us
    all_gather x8 -> x2, blocking collectives: 75.2 us -> 21.2 us  [the longest x1 15.4 us: shards(): step_rows = lax.all_gather(activations, 'head', axis=0, tiled=True)]
    reduce_scatter x4 -> x1, waiting for transfers between devices: 57.3 us -> 19.8 us  [shards(): lax.psum_scatter(partials, 'head', scatter_dimension=0, tiled=True)]
    unnamed x1 -> x0, blocking collectives: 33.3 us -> none
    reduce_sum x11 -> x1, other arithmetic: 31.6 us -> 1.01 us  [shards(): jnp.mean(readout * readout, axis=-1, keepdims=True) + 1e-06]
    unnamed x4 -> x3, waiting for transfers between devices: 0.07 us -> 27.4 us
    pallas_call x0 -> x1, Pallas kernels: none -> 12 us  [recurrence(): pl.pallas_call(kern, grid=(rows,), in_specs=[pl.BlockSpec(memory_space=pl...]
    dot_general x8 -> x4, matrix products: 10.2 us -> 3.6 us  [the longest x1 1.97 us: shards(): jnp.dot(all_normed.reshape(-1, all_normed.shape[-1]), w_out, preferred_el...]
    broadcast_in_dim x16 -> x2, local copies, waits for them, and re-layouts: 5.9 us -> 0.02 us  [the longest x1 0.01 us: shards(): queries = jnp.repeat(queries, head_ratio, axis=2)]
  transfers between devices with their start and end apart: 4 -> 2, of which waited for: 4 -> 2; matrix products, arithmetic and copies ran while one was open for 2% -> 2% of each run, Pallas kernels for 0% -> 0%
where the time goes in v1:
time: 120 us; the launch traced here: 119 us
  waiting for transfers between devices  47.3 us (39%)
  blocking collectives  21.2 us (18%)
  local copies, waits for them, and re-layouts  15 us (12%)
  between operations  14.5 us (12%)
  Pallas kernels  12 us (10%)
  other arithmetic  5.56 us (5%)
  matrix products  3.6 us (3%)
    unnamed x3, waiting for transfers between devices  27.4 us
    reduce_scatter x1, waiting for transfers between devices, shards(): lax.psum_scatter(partials, 'head', scatter_dimension=0, tiled=True)  19.8 us
    all_gather x1, blocking collectives, shards(): step_rows = lax.all_gather(activations, 'head', axis=0, tiled=True)  15.4 us
    pallas_call x1, Pallas kernels, recurrence(): pl.pallas_call(kern, grid=(rows,), in_specs=[pl.BlockSpec(memory_space=pl...  12 us
    all_gather x1, blocking collectives, shards(): all_normed = lax.all_gather(normed, 'dp', axis=0, tiled=True)  5.79 us
  transfers between devices with their start and end apart: 2, of which 2 were waited for; matrix products, arithmetic and copies ran while one was open for 2% of the time, Pallas kernels for 0%

profile of v1, /device:TPU:0, one launch (start us, length us, event | category | flops | bytes accessed | tf_op | source)
XLA Modules:
  0.0 119.2 jit_solution(1020629083298980101)
XLA Ops:
  7.2 15.4 %all_gather.6 = bf16[32,4,512]{2,1,0:T(4,128)(2,1)S(1)} all-gather(bf16[8,4,512]{2,1,0:T(4,128)(2,1)} %param.13), channel_id=1, replica_groups=mesh['groups'=2,'dp'=4,'head'=4] {'head'}, dimensions={0}, use_global_device_ids=true | all-gather | bytes 163840 | tf_op jit(solution)/shard_map/all_gather | solution.py:99
  22.7 0.9 fusion.16
  23.6 0.4 fusion.15
  24.0 0.3 fusion.14
  24.4 1.3 %pad_maximum_fusion = f32[128,3088]{1,0:T(8,128)} fusion(f32[128,16]{1,0:T(8,128)S(1)} %fusion.16, f32[128,2048]{1,0:T(8,128)S(1)} %fusion.15, f32[128,1024]{1,0:T(8,128)S(1)} %fusion.14), kind=kLoop, calls=%fused_computation | loop fusion | flops 790528 | bytes 3162112 | tf_op jit(solution)/shard_map/concatenate | solution.py:105
  25.8 0.6 add.86
  26.4 0.6 mul.166
  27.2 0.6 fusion.13
  27.8 0.6 fusion.12
  28.4 27.4 %reduce-scatter.7.cloned.1.call-done = f32[32,3088]{1,0:T(8,128)} async-done(((f32[128,3088]{1,0:T(8,128)}), f32[32,3088]{1,0:T(8,128)}) %reduce-scatter.7.cloned.1.call-update) | async-done | bytes 395280
  55.8 1.4 %copy.133 = bf16[32,3088]{0,1:T(8,128)(2,1)S(1)} copy(f32[32,3088]{1,0:T(8,128)} %reduce-scatter.7.cloned.1.call-done) | data formatting | bytes 592896
  57.2 0.7 slice.106
  58.0 0.2 copy.119
  58.2 0.1 reshape_reshape.4
  58.2 0.4 slice_reduce_fusion
  58.7 0.1 reshape.110
  58.8 0.1 copy.110
  58.9 0.1 squeeze.11
  59.0 0.1 copy.134
  59.2 0.7 div.26.beta_ref
  59.8 1.1 copy.113
  60.9 0.1 maximum_convert_fusion
  61.1 0.9 divide_multiply_fusion.2
  62.0 0.1 reshape.101
  62.1 0.1 fusion.10
  62.2 0.1 multiply_reduce_fusion.2
  62.4 0.1 multiply_multiply_fusion
  62.5 1.0 copy.123.qt_ref
  63.5 0.1 multiply_reduce_fusion.1
  63.7 0.1 broadcast_multiply_fusion
  63.8 1.0 copy.124.kt_ref
  64.9 0.1 maximum_convert_fusion.1
  65.0 0.2 divide_multiply_fusion.1
  65.1 0.7 reshape.106.v_ref
  65.9 0.6 fusion.9.decay_ref
  66.5 12.0 %shard_map.140 = (f32[8,8,128,128]{3,2,1,0:T(8,128)}, f32[8,32,128]{2,1,0:T(8,128)}) custom-call(f32[8,32]{1,0:T(8,128)} %fusion.9.decay_ref, f32[8,32]{1,0:T(8,128)} %div.26.beta_ref, f32[8,128,32]{2,1,0:T(8,128)} %copy.123.qt_ref, f32[8,128,32]{2,1,0:T(8,128)} %copy.124.kt_ref, f32[8,32,128]{2,1,0:T(8,128)} %reshape.106.v_ref, f32[8,8,128,128]{3,2,1,0:T(8,128)} %s_ref.1), custom_call_target="tpu_custom_call" | custom-call | flops 33554432 | bytes 8388608 | tf_op jit(solution)/shard_map/pallas_call | solution.py:50
  78.4 1.0 reshape.107
  79.5 1.0 multiply_reduce_fusion
  80.6 0.1 rsqrt.30
  80.7 0.7 mul.204
  81.4 0.9 mul.205
  82.4 0.1 fusion.7
  82.5 5.8 %all_gather.7 = bf16[32,4,1024]{2,1,0:T(4,128)(2,1)S(1)} all-gather(bf16[8,4,1024]{2,1,0:T(4,128)(2,1)S(1)} %fusion.7), channel_id=1, replica_groups=mesh['groups'=2,'dp'=4,'head'=4] {'dp'}, dimensions={0}, use_global_device_ids=true | all-gather | bytes 327680 | tf_op jit(solution)/shard_map/all_gather | solution.py:143
  88.3 0.8 reshape.108
  89.0 2.0 %fusion.17 = f32[128,512]{1,0:T(8,128)} fusion(bf16[128,1024]{1,0:T(8,128)(2,1)} %reshape.108, bf16[1024,512]{1,0:T(8,128)(2,1)S(1)} %copy-done.1), kind=kOutput, calls=%fused_computation.46 | convolution fusion | flops 134217728 | bytes 1572864 | tf_op jit(solution)/shard_map/dot_general | solution.py:144
  91.0 19.8 %reduce-scatter.5.cloned.1.call-done = f32[32,512]{1,0:T(8,128)} async-done(((f32[128,512]{1,0:T(8,128)}), f32[32,512]{1,0:T(8,128)}) %reduce-scatter.5.cloned.1.call-update) | async-done | bytes 65552 | tf_op jit(solution)/shard_map/reduce_scatter | solution.py:147
  110.9 0.8 convert_element_type.43
  111.7 0.6 reshape.109
  (59 shorter events, 0.6 us)
Async XLA Ops:
  7.2 16.4 %copy-start = (bf16[512,2048]{1,0:T(8,128)(2,1)S(1)}, bf16[512,2048]{1,0:T(8,128)(2,1)}, u32[]{:S(2)}) copy-start(bf16[512,2048]{1,0:T(8,128)(2,1)} %param.15) | copy-start | bytes 6291460
  7.2 16.8 %copy-start.2 = (bf16[512,1024]{1,0:T(8,128)(2,1)S(1)}, bf16[512,1024]{1,0:T(8,128)(2,1)}, u32[]{:S(2)}) copy-start(bf16[512,1024]{1,0:T(8,128)(2,1)} %param.14) | copy-start | bytes 3145732
  7.2 48.6 %reduce-scatter.7.cloned.1.call-start = ((), (), s32[]{:S(2)}) async-start(), calls=%async_computation.3 | async-start | bytes 2048000
  24.3 1.4 %copy-start.13 = (f32[8]{0:T(128)S(1)}, f32[8]{0:T(128)}, u32[]{:S(2)}) copy-start(f32[8]{0:T(128)} %param.20) | copy-start | bytes 100
  24.4 2.0 %copy-start.15 = (f32[8]{0:T(128)S(1)}, f32[8]{0:T(128)}, u32[]{:S(2)}) copy-start(f32[8]{0:T(128)} %param.19) | copy-start | bytes 100
  24.4 2.7 %copy-start.3 = (bf16[8,3,1024]{2,0,1:T(8,128)(2,1)S(1)}, bf16[8,3,1024]{2,0,1:T(8,128)(2,1)}, u32[]{:S(2)}) copy-start(bf16[8,3,1024]{2,0,1:T(8,128)(2,1)} %param.23) | copy-start | bytes 147460
  24.4 2.7 %copy-start.4 = (bf16[8,3,1024]{2,0,1:T(8,128)(2,1)S(1)}, bf16[8,3,1024]{2,0,1:T(8,128)(2,1)}, u32[]{:S(2)}) copy-start(bf16[8,3,1024]{2,0,1:T(8,128)(2,1)} %param.24) | copy-start | bytes 147460
  24.4 2.8 %copy-start.14 = (f32[128]{0:T(128)S(1)}, f32[128]{0:T(128)}, u32[]{:S(2)}) copy-start(f32[128]{0:T(128)} %param.21) | copy-start | bytes 1540
  24.4 2.8 %copy-start.5 = (bf16[4,1024]{1,0:T(4,128)(2,1)S(1)}, bf16[4,1024]{1,0:T(4,128)(2,1)}, u32[]{:S(2)}) copy-start(bf16[4,1024]{1,0:T(4,128)(2,1)} %param.17) | copy-start | bytes 24580
  24.4 3.4 %copy-start.6 = (bf16[4,1024]{1,0:T(4,128)(2,1)S(1)}, bf16[4,1024]{1,0:T(4,128)(2,1)}, u32[]{:S(2)}) copy-start(bf16[4,1024]{1,0:T(4,128)(2,1)} %param.18) | copy-start | bytes 24580
  25.7 85.1 %reduce-scatter.5.cloned.1.call-start = ((), (), s32[]{:S(2)}) async-start(), calls=%async_computation.2 | async-start | bytes 327680 | tf_op jit(solution)/shard_map/reduce_scatter | solution.py:147
  61.0 3.9 %copy-start.7 = (f32[1,1024]{1,0:T(1,128)S(1)}, f32[1,1024]{1,0:T(1,128)}, u32[]{:S(2)}) copy-start(f32[1,1024]{1,0:T(1,128)} %get-tuple-element.12) | copy-start | bytes 12292
  61.0 3.9 %copy-start.8 = (f32[1,1024]{1,0:T(1,128)S(1)}, f32[1,1024]{1,0:T(1,128)}, u32[]{:S(2)}) copy-start(f32[1,1024]{1,0:T(1,128)} %get-tuple-element.13) | copy-start | bytes 12292
  61.0 3.9 %copy-start.9 = (f32[1,1024]{1,0:T(1,128)S(1)}, f32[1,1024]{1,0:T(1,128)}, u32[]{:S(2)}) copy-start(f32[1,1024]{1,0:T(1,128)} %get-tuple-element.14) | copy-start | bytes 12292
  61.1 3.9 %copy-start.10 = (f32[1,1024]{1,0:T(1,128)S(1)}, f32[1,1024]{1,0:T(1,128)}, u32[]{:S(2)}) copy-start(f32[1,1024]{1,0:T(1,128)} %get-tuple-element.15) | copy-start | bytes 12292
  62.1 3.8 %copy-start.11 = (f32[32]{0:T(128)S(1)}, f32[32]{0:T(128)}, u32[]{:S(2)}) copy-start(f32[32]{0:T(128)} %add.86) | copy-start | bytes 388
  62.1 3.8 %copy-start.12 = (f32[32]{0:T(128)S(1)}, f32[32]{0:T(128)}, u32[]{:S(2)}) copy-start(f32[32]{0:T(128)} %mul.166) | copy-start | bytes 388
  78.4 10.6 %copy-start.1 = (bf16[1024,512]{1,0:T(8,128)(2,1)S(1)}, bf16[1024,512]{1,0:T(8,128)(2,1)}, u32[]{:S(2)}) copy-start(bf16[1024,512]{1,0:T(8,128)(2,1)} %param.22) | copy-start | bytes 3145732
Sparse Core Ops, SparseCore 0:
  25.9 29.9 reduce-scatter.6
  91.1 19.6 reduce-scatter.4

commit v2 on v1

--- a/solution.py
+++ b/solution.py
@@ -24,6 +24,47 @@
     steps = proj.shape[1]
     mixed = sum(seq[:, k : k + steps, :] * taps[k][None, None, :] for k in range(kernel))
     return jax.nn.silu(mixed)
+
+
+def gather_rows(x, axis):
+    n = lax.axis_size(axis)
+    me = lax.axis_index(axis)
+    pieces = [x]
+    for s in range(1, n):
+        pieces.append(lax.ppermute(x, axis, [(i, (i + s) % n) for i in range(n)]))
+    stacked = jnp.stack(pieces)
+    source = (me - jnp.arange(n)) % n
+    order = jnp.argsort(source)
+    return jnp.take(stacked, order, axis=0).reshape(n * x.shape[0], *x.shape[1:])
+
+
+def scatter_sum_rows(x, axis):
+    n = lax.axis_size(axis)
+    me = lax.axis_index(axis)
+    chunks = x.reshape(n, x.shape[0] // n, *x.shape[1:])
+    acc = jnp.take(chunks, me, axis=0)
+    for s in range(1, n):
+        send = jnp.take(chunks, (me + s) % n, axis=0)
+        acc = acc + lax.ppermute(send, axis, [(i, (i + s) % n) for i in range(n)])
+    return acc
+
+
+def scatter_sum_rows_paired(x, axis):
+    n = lax.axis_size(axis)
+    m = n // 2
+    me = lax.axis_index(axis)
+    core = me % 2
+    chip = me // 2
+    chunks = x.reshape(m, 2, x.shape[0] // n, *x.shape[1:])
+    keep = jnp.take(chunks, core, axis=1)
+    send = jnp.take(chunks, 1 - core, axis=1)
+    part = keep + lax.ppermute(send, axis, [(i, i ^ 1) for i in range(n)])
+    acc = jnp.take(part, chip, axis=0)
+    for s in range(1, m):
+        send = jnp.take(part, (chip + s) % m, axis=0)
+        perm = [(i, ((i // 2 + s) % m) * 2 + i % 2) for i in range(n)]
+        acc = acc + lax.ppermute(send, axis, perm)
+    return acc
 
 
 def recurrence_kernel(decay_ref, beta_ref, qt_ref, kt_ref, v_ref, s_ref, s_out, o_ref, *, heads, steps):
@@ -96,16 +137,13 @@
     width_qk = w_qk.shape[1]
     width_vz = w_vz.shape[1]
 
-    step_rows = lax.all_gather(activations, "head", axis=0, tiled=True)
+    step_rows = gather_rows(activations, "head")
     flat_rows = step_rows.reshape(-1, step_rows.shape[-1])
     partial_qk = jnp.dot(flat_rows, w_qk, preferred_element_type=jnp.float32)
     partial_vz = jnp.dot(flat_rows, w_vz, preferred_element_type=jnp.float32)
     partial_ba = jnp.dot(flat_rows, w_ba, preferred_element_type=jnp.float32)
-    summed = lax.psum_scatter(
-        jnp.concatenate([partial_qk, partial_vz, partial_ba], axis=1),
-        "dp",
-        scatter_dimension=0,
-        tiled=True,
+    summed = scatter_sum_rows_paired(
+        jnp.concatenate([partial_qk, partial_vz, partial_ba], axis=1), "dp"
     )
     summed_qk = summed[:, :width_qk]
     summed_vz = summed[:, width_qk : width_qk + width_vz]
@@ -140,11 +178,11 @@
     normed = readout * scale * norm_gain[None, None, None, :] * jax.nn.silu(gate_z)
     normed = normed.reshape(rows_mem, step_count, heads * DV).astype(jnp.bfloat16)
 
-    all_normed = lax.all_gather(normed, "dp", axis=0, tiled=True)
+    all_normed = gather_rows(normed, "dp")
     partials = jnp.dot(
         all_normed.reshape(-1, all_normed.shape[-1]), w_out, preferred_element_type=jnp.float32
     )
-    layer_out = lax.psum_scatter(partials, "head", scatter_dimension=0, tiled=True)
+    layer_out = scatter_sum_rows(partials, "head")
     layer_out = layer_out.astype(jnp.bfloat16).reshape(-1, step_count, w_out.shape[1])
     return (layer_out, new_state)
 

time: 120 us -> 87.9 us (0.73)
  waiting for transfers between devices: 47.3 us -> 20.7 us
  blocking collectives: 21.2 us -> 0 us
  starting transfers between devices: 0.08 us -> 15.4 us
  between operations: 14.5 us -> 1.23 us
  other arithmetic: 5.56 us -> 14 us
  local copies, waits for them, and re-layouts: 15 us -> 21.5 us
    unnamed x3 -> x0, waiting for transfers between devices: 27.4 us -> none
    all_gather x2 -> x0, blocking collectives: 21.2 us -> none  [the longest x1 15.4 us: shards(): step_rows = lax.all_gather(activations, 'head', axis=0, tiled=True)]
    ppermute x0 -> x11, waiting for transfers between devices: none -> 20.7 us  [the longest x1 10.3 us: scatter_sum_rows_paired(): acc = acc + lax.ppermute(send, axis, perm)]
    reduce_scatter x1 -> x0, waiting for transfers between devices: 19.8 us -> none  [shards(): lax.psum_scatter(partials, 'head', scatter_dimension=0, tiled=True)]
    ppermute x0 -> x11, starting transfers between devices: none -> 15.4 us  [the longest x6 10 us: gather_rows(): pieces.append(lax.ppermute(x, axis, [(i, (i + s) % n) for i in range(n)]))]
    ppermute x0 -> x2, local copies, waits for them, and re-layouts: none -> 4.79 us  [the longest x1 3.15 us: scatter_sum_rows_paired(): part = keep + lax.ppermute(send, axis, [(i, i ^ 1) for i in range(n)])]
    another operation x0 -> x4, other arithmetic: none -> 4.18 us
    unnamed x36 -> x28, local copies, waits for them, and re-layouts: 1.68 us -> 5.52 us
  transfers between devices with their start and end apart: 2 -> 11, of which waited for: 2 -> 9; matrix products, arithmetic and copies ran while one was open for 2% -> 5% of each run, Pallas kernels for 0% -> 0%
where the time goes in v2:
time: 87.9 us; the launch traced here: 87.3 us
  local copies, waits for them, and re-layouts  21.5 us (24%)
  waiting for transfers between devices  20.7 us (24%)
  starting transfers between devices  15.4 us (18%)
  other arithmetic  14 us (16%)
  Pallas kernels  12 us (14%)
  matrix products  2.62 us (3%)
  between operations  1.23 us (1%)
    pallas_call x1, Pallas kernels, recurrence(): pl.pallas_call(kern, grid=(rows,), in_specs=[pl.BlockSpec(memory_space=pl...  12 us
    ppermute x1, waiting for transfers between devices, scatter_sum_rows_paired(): acc = acc + lax.ppermute(send, axis, perm)  10.3 us
    ppermute x6, starting transfers between devices, gather_rows(): pieces.append(lax.ppermute(x, axis, [(i, (i + s) % n) for i in range(n)]))  10 us
    ppermute x3, waiting for transfers between devices, scatter_sum_rows(): acc = acc + lax.ppermute(send, axis, [(i, (i + s) % n) for i in range(n)])  7.55 us
    unnamed x28, local copies, waits for them, and re-layouts  5.52 us
    ppermute x3, starting transfers between devices, scatter_sum_rows(): acc = acc + lax.ppermute(send, axis, [(i, (i + s) % n) for i in range(n)])  3.83 us
    add x1, other arithmetic, scatter_sum_rows_paired(): part = keep + lax.ppermute(send, axis, [(i, i ^ 1) for i in range(n)])  3.17 us
    ppermute x1, local copies, waits for them, and re-layouts, scatter_sum_rows_paired(): part = keep + lax.ppermute(send, axis, [(i, i ^ 1) for i in range(n)])  3.15 us
  transfers between devices with their start and end apart: 11, of which 9 were waited for; matrix products, arithmetic and copies ran while one was open for 5% of the time, Pallas kernels for 0%

profile of v2, /device:TPU:0, one launch (start us, length us, event | category | flops | bytes accessed | tf_op | source)
XLA Modules:
  0.0 87.3 jit_solution(11196291861762144888)
XLA Ops:
  0.6 3.1 %collective-permute-start = (bf16[8,4,512]{2,1,0:T(4,128)(2,1)}, bf16[8,4,512]{2,1,0:T(4,128)(2,1)S(1)}, u32[]{:S(2)}, u32[]{:S(2)}) collective-permute-start(bf16[8,4,512]{2,1,0:T(4,128)(2,1)} %param.19), channel_id=1, source_target_pairs={{0,1},{1,2},{2,3},{3,0},{4,5},{5,6},{6,7},{7,4},{8,9},{9,10},{10,1... | collective-permute-start | bytes 98312 | tf_op jit(solution)/shard_map/ppermute | solution.py:34
  3.7 2.6 %collective-permute-start.1 = (bf16[8,4,512]{2,1,0:T(4,128)(2,1)}, bf16[8,4,512]{2,1,0:T(4,128)(2,1)S(1)}, u32[]{:S(2)}, u32[]{:S(2)}) collective-permute-start(bf16[8,4,512]{2,1,0:T(4,128)(2,1)} %param.19), channel_id=1, source_target_pairs={{0,2},{1,3},{2,0},{3,1},{4,6},{5,7},{6,4},{7,5},{8,10},{9,11},{10,... | collective-permute-start | bytes 98312 | tf_op jit(solution)/shard_map/ppermute | solution.py:34
  6.3 1.3 %collective-permute-start.2 = (bf16[8,4,512]{2,1,0:T(4,128)(2,1)}, bf16[8,4,512]{2,1,0:T(4,128)(2,1)S(1)}, u32[]{:S(2)}, u32[]{:S(2)}) collective-permute-start(bf16[8,4,512]{2,1,0:T(4,128)(2,1)} %param.19), channel_id=1, source_target_pairs={{0,3},{1,0},{2,1},{3,2},{4,7},{5,4},{6,5},{7,6},{8,11},{9,8},{10,9... | collective-permute-start | bytes 98312 | tf_op jit(solution)/shard_map/ppermute | solution.py:34
  7.7 0.7 sort.32
  8.4 0.7 sort.31
  9.5 1.0 %collective-permute-done.2 = bf16[8,4,512]{2,1,0:T(4,128)(2,1)S(1)} collective-permute-done((bf16[8,4,512]{2,1,0:T(4,128)(2,1)}, bf16[8,4,512]{2,1,0:T(4,128)(2,1)S(1)}, u32[]{:S(2)}, u32[]{:S(2)}) %collective-permute-start.2) | collective-permute-done | bytes 32800 | tf_op jit(solution)/shard_map/ppermute | solution.py:34
  10.4 0.9 pad_maximum_fusion.2
  11.3 0.7 gather_fusion
  12.0 0.5 fusion.25
  12.5 0.7 copy-done.3
  13.3 0.3 fusion.26
  13.6 0.4 copy-done.10
  14.4 1.0 %constant_dynamic-slice_fusion = (f32[2,1,32,3088]{3,2,1,0:T(8,128)S(1)}, f32[2,32,3088]{2,1,0:T(8,128)}) fusion(f32[2,2,32,3088]{3,2,1,0:T(8,128)S(1)} %bitcast.77, s32[]{:T(128)S(6)} %select_n.113, s32[]{:T(128)S(6)} %select_n.115, pred[]{:T(512)S(6)} %and.80), kind=kLoop, calls=%fused_computation.71 | loop fusion | flops 197632 | bytes 3162121 | tf_op jit(solution)/shard_map/jit(_take) | solution.py:59
  15.8 2.2 %copy.130 = f32[2,1,32,3088]{2,3,0,1:T(8,128)} copy(f32[2,1,32,3088]{3,2,1,0:T(8,128)S(1)} %get-tuple-element.46) | data formatting | bytes 1581056
  18.1 3.1 %copy.106 = f32[2,32,3088]{1,2,0:T(8,128)} copy(f32[2,32,3088]{2,1,0:T(8,128)} %collective-permute-done.3) | data formatting | bytes 1581056 | tf_op jit(solution)/shard_map/ppermute | solution.py:61
  21.2 3.2 %bitcast_add_fusion = f32[2,32,3088]{1,2,0:T(8,128)S(1)} fusion(f32[2,32,3088]{1,2,0:T(8,128)} %copy.106, f32[2,1,32,3088]{2,3,0,1:T(8,128)} %copy.130, pred[]{:T(512)S(6)} %and.79), kind=kLoop, calls=%fused_computation.2 | loop fusion | flops 395264 | bytes 2371585 | tf_op jit(solution)/shard_map/add | solution.py:61
  24.4 1.7 %copy-done.1 = f32[2,32,3088]{1,2,0:T(8,128)} copy-done((f32[2,32,3088]{1,2,0:T(8,128)}, f32[2,32,3088]{1,2,0:T(8,128)S(1)}, u32[]{:S(2)}) %copy-start.1) | copy-done | bytes 790552
  26.1 1.3 %select_bitcast_fusion = f32[32,3088]{0,1:T(8,128)} fusion(f32[2,32,3088]{1,2,0:T(8,128)S(1)} %bitcast_add_fusion, s32[]{:T(128)S(6)} %select_n.119, pred[]{:T(512)S(6)} %and.82), kind=kLoop, calls=%fused_computation.6 | loop fusion | flops 98816 | bytes 790533 | tf_op jit(solution)/shard_map/jit(_take)/select_n | solution.py:64
  27.3 1.9 %copy.107 = f32[32,3088]{1,0:T(8,128)S(1)} copy(f32[32,3088]{0,1:T(8,128)} %select_bitcast_fusion) | data formatting | bytes 790528 | tf_op jit(solution)/shard_map/jit(_take)/select_n | solution.py:64
  29.2 1.5 %collective-permute-start.4 = (f32[32,3088]{1,0:T(8,128)S(1)}, f32[32,3088]{1,0:T(8,128)S(1)}, u32[]{:S(2)}, u32[]{:S(2)}) collective-permute-start(f32[32,3088]{1,0:T(8,128)S(1)} %copy.107), channel_id=1, source_target_pairs={{0,8},{4,12},{8,0},{12,4},{1,9},{5,13},{9,1},{13,5},{2,10},{6,14},... | collective-permute-start | bytes 1185800 | tf_op jit(solution)/shard_map/ppermute | solution.py:66
  30.8 10.3 %collective-permute-done.4 = f32[32,3088]{1,0:T(8,128)S(1)} collective-permute-done((f32[32,3088]{1,0:T(8,128)S(1)}, f32[32,3088]{1,0:T(8,128)S(1)}, u32[]{:S(2)}, u32[]{:S(2)}) %collective-permute-start.4) | collective-permute-done | bytes 395296 | tf_op jit(solution)/shard_map/ppermute | solution.py:66
  41.1 1.6 %copy.108 = f32[32,3088]{0,1:T(8,128)} copy(f32[32,3088]{1,0:T(8,128)S(1)} %collective-permute-done.4) | data formatting | bytes 790528 | tf_op jit(solution)/shard_map/ppermute | solution.py:66
  42.8 2.1 %fusion = bf16[32,3088]{0,1:T(8,128)(2,1)S(1)} fusion(f32[32,3088]{0,1:T(8,128)} %copy.108, f32[2,32,3088]{1,2,0:T(8,128)} %copy-done.1, s32[]{:T(128)S(6)} %select_n.117, pred[]{:T(512)S(6)} %and.81), kind=kLoop, calls=%fused_computation.5 | loop fusion | flops 296448 | bytes 988165 | tf_op jit(solution)/shard_map/convert.5
  45.4 0.3 copy-done.2
  46.1 1.0 %copy.123.kt_ref = f32[8,128,32]{2,1,0:T(8,128)} copy(f32[8,128,32]{1,0,2:T(8,128)S(1)} %bitcast.83) | data formatting | bytes 262144 | tf_op jit(solution)/shard_map/reshape | solution.py:166
  47.4 1.0 %copy.122.qt_ref = f32[8,128,32]{2,1,0:T(8,128)} copy(f32[8,128,32]{1,0,2:T(8,128)S(1)} %bitcast.84) | data formatting | bytes 262144 | tf_op jit(solution)/shard_map/reshape | solution.py:165
  48.7 0.4 slice_reduce_fusion
  49.4 0.7 reshape.183.v_ref
  50.4 0.7 div.46.beta_ref
  51.3 0.6 fusion.20.decay_ref
  51.9 12.0 %shard_map.140 = (f32[8,8,128,128]{3,2,1,0:T(8,128)}, f32[8,32,128]{2,1,0:T(8,128)}) custom-call(f32[8,32]{1,0:T(8,128)} %fusion.20.decay_ref, f32[8,32]{1,0:T(8,128)} %div.46.beta_ref, f32[8,128,32]{2,1,0:T(8,128)} %copy.122.qt_ref, f32[8,128,32]{2,1,0:T(8,128)} %copy.123.kt_ref, f32[8,32,128]{2,1,0:T(8,128)} %reshape.183.v_ref, f32[8,8,128,128]{3,2,1,0:T(8,128)} %s_ref.1), custom_call_target="tpu_custom_call" | custom-call | flops 33554432 | bytes 8388608 | tf_op jit(solution)/shard_map/pallas_call | solution.py:91
  63.8 1.0 %multiply_reduce_fusion = f32[8,32]{1,0:T(8,128)S(1)} fusion(f32[8,32,128]{2,1,0:T(8,128)} %get-tuple-element.11), kind=kLoop, calls=%fused_computation.39 | loop fusion | flops 65280 | bytes 132096 | tf_op jit(solution)/shard_map/reduce_sum | solution.py:177
  64.9 0.9 %reshape.184 = f32[1,8,4,1024]{3,2,1,0:T(4,128)S(1)} reshape(f32[8,32,128]{2,1,0:T(8,128)} %get-tuple-element.11) | data formatting | bytes 262144 | tf_op jit(solution)/shard_map/reshape | solution.py:175
  65.8 0.4 fusion.27
  66.5 0.9 %reshape.185 = f32[8,4,1024]{2,1,0:T(4,128)S(1)} reshape(f32[8,32,128]{2,1,0:T(8,128)} %get-tuple-element.11) | data formatting | bytes 262144 | tf_op jit(solution)/shard_map/reshape | solution.py:175
  67.7 1.6 %collective-permute-start.6 = (bf16[8,4,1024]{2,1,0:T(4,128)(2,1)S(1)}, bf16[8,4,1024]{2,1,0:T(4,128)(2,1)S(1)}, u32[]{:S(2)}, u32[]{:S(2)}) collective-permute-start(bf16[8,4,1024]{2,1,0:T(4,128)(2,1)S(1)} %fusion.14), channel_id=1, source_target_pairs={{0,8},{4,12},{8,0},{12,4},{1,9},{5,13},{9,1},{13,5},{2,10},{6,14},... | collective-permute-start | bytes 196616 | tf_op jit(solution)/shard_map/ppermute | solution.py:34
  69.2 1.4 %collective-permute-start.7 = (bf16[8,4,1024]{2,1,0:T(4,128)(2,1)S(1)}, bf16[8,4,1024]{2,1,0:T(4,128)(2,1)S(1)}, u32[]{:S(2)}, u32[]{:S(2)}) collective-permute-start(bf16[8,4,1024]{2,1,0:T(4,128)(2,1)S(1)} %fusion.14), channel_id=1, source_target_pairs={{0,12},{4,0},{8,4},{12,8},{1,13},{5,1},{9,5},{13,9},{2,14},{6,2},{... | collective-permute-start | bytes 196616 | tf_op jit(solution)/shard_map/ppermute | solution.py:34
  70.8 0.7 collective-permute-done.5
  71.5 0.9 collective-permute-done.6
  72.5 0.2 pad_maximum_fusion.1
  72.8 0.8 gather_fusion.1
  73.6 1.6 %fusion.1 = f32[4,32,512]{2,1,0:T(8,128)S(1)} fusion(bf16[1024,512]{1,0:T(8,128)(2,1)} %param.28, bf16[4,32,1024]{2,1,0:T(8,128)(2,1)S(1)} %gather.24, pred[4]{0:T(512)(128)(4,1)S(1)} %get-tuple-element.66), kind=kOutput, calls=%fused_computation.7 | convolution fusion | flops 134348800 | bytes 1572868 | tf_op jit(solution)/shard_map/dot_general | solution.py:182
  75.2 3.2 %collective-permute-start.10 = (f32[32,512]{1,0:T(8,128)S(1)}, f32[32,512]{1,0:T(8,128)S(1)}, u32[]{:S(2)}, u32[]{:S(2)}) collective-permute-start(f32[32,512]{1,0:T(8,128)S(1)} %get-tuple-element.49), channel_id=1, source_target_pairs={{0,3},{1,0},{2,1},{3,2},{4,7},{5,4},{6,5},{7,6},{8,11},{9,8},{10,9... | collective-permute-start | bytes 196616 | tf_op jit(solution)/shard_map/ppermute | solution.py:48
  78.4 0.6 collective-permute-start.9
  79.1 1.9 %collective-permute-done.10 = f32[32,512]{1,0:T(8,128)S(1)} collective-permute-done((f32[32,512]{1,0:T(8,128)S(1)}, f32[32,512]{1,0:T(8,128)S(1)}, u32[]{:S(2)}, u32[]{:S(2)}) %collective-permute-start.10) | collective-permute-done | bytes 65568 | tf_op jit(solution)/shard_map/ppermute | solution.py:48
  80.9 4.3 %collective-permute-done.8 = f32[32,512]{1,0:T(8,128)S(1)} collective-permute-done((f32[32,512]{1,0:T(8,128)S(1)}, f32[32,512]{1,0:T(8,128)S(1)}, u32[]{:S(2)}, u32[]{:S(2)}) %collective-permute-start.8) | collective-permute-done | bytes 65568 | tf_op jit(solution)/shard_map/ppermute | solution.py:48
  85.2 1.4 %collective-permute-done.9 = f32[32,512]{1,0:T(8,128)S(1)} collective-permute-done((f32[32,512]{1,0:T(8,128)S(1)}, f32[32,512]{1,0:T(8,128)S(1)}, u32[]{:S(2)}, u32[]{:S(2)}) %collective-permute-start.9) | collective-permute-done | bytes 65568 | tf_op jit(solution)/shard_map/ppermute | solution.py:48
  86.6 0.6 reshape.186
  (95 shorter events, 4.2 us)
Async XLA Ops:
  0.6 11.4 %copy-start = (bf16[512,2048]{1,0:T(8,128)(2,1)S(1)}, bf16[512,2048]{1,0:T(8,128)(2,1)}, u32[]{:S(2)}) copy-start(bf16[512,2048]{1,0:T(8,128)(2,1)} %param.21) | copy-start | bytes 6291460
  0.6 8.8 %collective-permute-start = (bf16[8,4,512]{2,1,0:T(4,128)(2,1)}, bf16[8,4,512]{2,1,0:T(4,128)(2,1)S(1)}, u32[]{:S(2)}, u32[]{:S(2)}) collective-permute-start(bf16[8,4,512]{2,1,0:T(4,128)(2,1)} %param.19), channel_id=1, source_target_pairs={{0,1},{1,2},{2,3},{3,0},{4,5},{5,6},{6,7},{7,4},{8,9},{9,10},{10,1... | collective-permute-start | bytes 98312 | tf_op jit(solution)/shard_map/ppermute | solution.py:34
  3.7 5.7 %collective-permute-start.1 = (bf16[8,4,512]{2,1,0:T(4,128)(2,1)}, bf16[8,4,512]{2,1,0:T(4,128)(2,1)S(1)}, u32[]{:S(2)}, u32[]{:S(2)}) collective-permute-start(bf16[8,4,512]{2,1,0:T(4,128)(2,1)} %param.19), channel_id=1, source_target_pairs={{0,2},{1,3},{2,0},{3,1},{4,6},{5,7},{6,4},{7,5},{8,10},{9,11},{10,... | collective-permute-start | bytes 98312 | tf_op jit(solution)/shard_map/ppermute | solution.py:34
  6.3 4.1 %collective-permute-start.2 = (bf16[8,4,512]{2,1,0:T(4,128)(2,1)}, bf16[8,4,512]{2,1,0:T(4,128)(2,1)S(1)}, u32[]{:S(2)}, u32[]{:S(2)}) collective-permute-start(bf16[8,4,512]{2,1,0:T(4,128)(2,1)} %param.19), channel_id=1, source_target_pairs={{0,3},{1,0},{2,1},{3,2},{4,7},{5,4},{6,5},{7,6},{8,11},{9,8},{10,9... | collective-permute-start | bytes 98312 | tf_op jit(solution)/shard_map/ppermute | solution.py:34
  12.0 1.2 %copy-start.3 = (bf16[512,1024]{1,0:T(8,128)(2,1)S(1)}, bf16[512,1024]{1,0:T(8,128)(2,1)}, u32[]{:S(2)}) copy-start(bf16[512,1024]{1,0:T(8,128)(2,1)} %param.20) | copy-start | bytes 3145732
  13.3 0.7 copy-start.10
  14.3 1.1 %copy-start.4 = (bf16[8,3,1024]{2,0,1:T(8,128)(2,1)S(1)}, bf16[8,3,1024]{2,0,1:T(8,128)(2,1)}, u32[]{:S(2)}) copy-start(bf16[8,3,1024]{2,0,1:T(8,128)(2,1)} %param.29) | copy-start | bytes 147460
  14.3 1.1 %copy-start.5 = (bf16[8,3,1024]{2,0,1:T(8,128)(2,1)S(1)}, bf16[8,3,1024]{2,0,1:T(8,128)(2,1)}, u32[]{:S(2)}) copy-start(bf16[8,3,1024]{2,0,1:T(8,128)(2,1)} %param.30) | copy-start | bytes 147460
  14.4 1.2 %copy-start.11 = (f32[8]{0:T(128)S(1)}, f32[8]{0:T(128)}, u32[]{:S(2)}) copy-start(f32[8]{0:T(128)} %param.25) | copy-start | bytes 100
  14.4 1.3 %copy-start.8 = (f32[8]{0:T(128)S(1)}, f32[8]{0:T(128)}, u32[]{:S(2)}) copy-start(f32[8]{0:T(128)} %param.26) | copy-start | bytes 100
  14.4 1.4 %copy-start.6 = (bf16[4,1024]{1,0:T(4,128)(2,1)S(1)}, bf16[4,1024]{1,0:T(4,128)(2,1)}, u32[]{:S(2)}) copy-start(bf16[4,1024]{1,0:T(4,128)(2,1)} %param.23) | copy-start | bytes 24580
  15.4 2.7 %collective-permute-start.3 = (f32[2,32,3088]{2,1,0:T(8,128)}, f32[2,32,3088]{2,1,0:T(8,128)}, u32[]{:S(2)}, u32[]{:S(2)}) collective-permute-start(f32[2,32,3088]{2,1,0:T(8,128)} %get-tuple-element.47), channel_id=1, source_target_pairs={{0,4},{4,0},{8,12},{12,8},{1,5},{5,1},{9,13},{13,9},{2,6},{6,2},{1... | collective-permute-start | bytes 2371592 | tf_op jit(solution)/shard_map/ppermute | solution.py:61
  24.4 1.7 %copy-start.1 = (f32[2,32,3088]{1,2,0:T(8,128)}, f32[2,32,3088]{1,2,0:T(8,128)S(1)}, u32[]{:S(2)}) copy-start(f32[2,32,3088]{1,2,0:T(8,128)S(1)} %bitcast_add_fusion) | copy-start | bytes 2371588
  27.3 3.5 %copy-start.9 = (f32[128]{0:T(128)S(1)}, f32[128]{0:T(128)}, u32[]{:S(2)}) copy-start(f32[128]{0:T(128)} %param.27) | copy-start | bytes 1540
  27.3 3.5 %copy-start.7 = (bf16[4,1024]{1,0:T(4,128)(2,1)S(1)}, bf16[4,1024]{1,0:T(4,128)(2,1)}, u32[]{:S(2)}) copy-start(bf16[4,1024]{1,0:T(4,128)(2,1)} %param.24) | copy-start | bytes 24580
  29.2 11.9 %collective-permute-start.4 = (f32[32,3088]{1,0:T(8,128)S(1)}, f32[32,3088]{1,0:T(8,128)S(1)}, u32[]{:S(2)}, u32[]{:S(2)}) collective-permute-start(f32[32,3088]{1,0:T(8,128)S(1)} %copy.107), channel_id=1, source_target_pairs={{0,8},{4,12},{8,0},{12,4},{1,9},{5,13},{9,1},{13,5},{2,10},{6,14},... | collective-permute-start | bytes 1185800 | tf_op jit(solution)/shard_map/ppermute | solution.py:66
  44.8 0.9 %copy-start.2 = (bf16[32,3088]{0,1:T(8,128)(2,1)}, bf16[32,3088]{0,1:T(8,128)(2,1)S(1)}, u32[]{:S(2)}) copy-start(bf16[32,3088]{0,1:T(8,128)(2,1)S(1)} %fusion) | copy-start | bytes 592900
  45.8 2.6 %slice-start = ((bf16[32,3088]{0,1:T(8,128)(2,1)}), bf16[32,2048]{0,1:T(8,128)(2,1)S(1)}, s32[]{:S(2)}) async-start(bf16[32,3088]{0,1:T(8,128)(2,1)} %copy-done.2), calls=%async_computation | async-start | bytes 1048576 | tf_op jit(solution)/shard_map/slice | solution.py:149
  67.6 3.8 %collective-permute-start.5 = (bf16[8,4,1024]{2,1,0:T(4,128)(2,1)S(1)}, bf16[8,4,1024]{2,1,0:T(4,128)(2,1)S(1)}, u32[]{:S(2)}, u32[]{:S(2)}) collective-permute-start(bf16[8,4,1024]{2,1,0:T(4,128)(2,1)S(1)} %fusion.14), channel_id=1, source_target_pairs={{0,4},{4,8},{8,12},{12,0},{1,5},{5,9},{9,13},{13,1},{2,6},{6,10},{... | collective-permute-start | bytes 196616 | tf_op jit(solution)/shard_map/ppermute | solution.py:34
  67.7 4.6 %collective-permute-start.6 = (bf16[8,4,1024]{2,1,0:T(4,128)(2,1)S(1)}, bf16[8,4,1024]{2,1,0:T(4,128)(2,1)S(1)}, u32[]{:S(2)}, u32[]{:S(2)}) collective-permute-start(bf16[8,4,1024]{2,1,0:T(4,128)(2,1)S(1)} %fusion.14), channel_id=1, source_target_pairs={{0,8},{4,12},{8,0},{12,4},{1,9},{5,13},{9,1},{13,5},{2,10},{6,14},... | collective-permute-start | bytes 196616 | tf_op jit(solution)/shard_map/ppermute | solution.py:34
  69.2 3.3 %collective-permute-start.7 = (bf16[8,4,1024]{2,1,0:T(4,128)(2,1)S(1)}, bf16[8,4,1024]{2,1,0:T(4,128)(2,1)S(1)}, u32[]{:S(2)}, u32[]{:S(2)}) collective-permute-start(bf16[8,4,1024]{2,1,0:T(4,128)(2,1)S(1)} %fusion.14), channel_id=1, source_target_pairs={{0,12},{4,0},{8,4},{12,8},{1,13},{5,1},{9,5},{13,9},{2,14},{6,2},{... | collective-permute-start | bytes 196616 | tf_op jit(solution)/shard_map/ppermute | solution.py:34
  75.2 5.7 %collective-permute-start.10 = (f32[32,512]{1,0:T(8,128)S(1)}, f32[32,512]{1,0:T(8,128)S(1)}, u32[]{:S(2)}, u32[]{:S(2)}) collective-permute-start(f32[32,512]{1,0:T(8,128)S(1)} %get-tuple-element.49), channel_id=1, source_target_pairs={{0,3},{1,0},{2,1},{3,2},{4,7},{5,4},{6,5},{7,6},{8,11},{9,8},{10,9... | collective-permute-start | bytes 196616 | tf_op jit(solution)/shard_map/ppermute | solution.py:48
  78.4 6.8 %collective-permute-start.8 = (f32[32,512]{1,0:T(8,128)S(1)}, f32[32,512]{1,0:T(8,128)S(1)}, u32[]{:S(2)}, u32[]{:S(2)}) collective-permute-start(f32[32,512]{1,0:T(8,128)S(1)} %get-tuple-element.48), channel_id=1, source_target_pairs={{0,1},{1,2},{2,3},{3,0},{4,5},{5,6},{6,7},{7,4},{8,9},{9,10},{10,1... | collective-permute-start | bytes 196616 | tf_op jit(solution)/shard_map/ppermute | solution.py:48
  78.4 8.2 %collective-permute-start.9 = (f32[32,512]{1,0:T(8,128)S(1)}, f32[32,512]{1,0:T(8,128)S(1)}, u32[]{:S(2)}, u32[]{:S(2)}) collective-permute-start(f32[32,512]{1,0:T(8,128)S(1)} %get-tuple-element.50), channel_id=1, source_target_pairs={{0,2},{1,3},{2,0},{3,1},{4,6},{5,7},{6,4},{7,5},{8,10},{9,11},{10,... | collective-permute-start | bytes 196616 | tf_op jit(solution)/shard_map/ppermute | solution.py:48

commit v3 on v2

--- a/solution.py
+++ b/solution.py
@@ -33,8 +33,7 @@
     for s in range(1, n):
         pieces.append(lax.ppermute(x, axis, [(i, (i + s) % n) for i in range(n)]))
     stacked = jnp.stack(pieces)
-    source = (me - jnp.arange(n)) % n
-    order = jnp.argsort(source)
+    order = (me - jnp.arange(n)) % n
     return jnp.take(stacked, order, axis=0).reshape(n * x.shape[0], *x.shape[1:])
 
 
@@ -65,6 +64,40 @@
         perm = [(i, ((i // 2 + s) % m) * 2 + i % 2) for i in range(n)]
         acc = acc + lax.ppermute(send, axis, perm)
     return acc
+
+
+def gather_pieces(x, axis):
+    n = lax.axis_size(axis)
+    pieces = [x]
+    for s in range(1, n):
+        pieces.append(lax.ppermute(x, axis, [(i, (i + s) % n) for i in range(n)]))
+    return jnp.stack(pieces)
+
+
+def projection_kernel(x_ref, wqk_ref, wvz_ref, wba_ref, *outs):
+    x = x_ref[...]
+    section = outs[0].shape[0]
+    offset = 0
+    for w_ref in (wqk_ref, wvz_ref, wba_ref):
+        width = w_ref.shape[1]
+        y = jnp.dot(x, w_ref[...], preferred_element_type=jnp.float32)
+        for i, o_ref in enumerate(outs):
+            o_ref[:, offset : offset + width] = y[i * section : (i + 1) * section]
+        offset += width
+
+
+def projection(x, w_qk, w_vz, w_ba, sections):
+    rows = x.shape[0] // sections
+    cols = w_qk.shape[1] + w_vz.shape[1] + w_ba.shape[1]
+    return pl.pallas_call(
+        projection_kernel,
+        out_shape=[jax.ShapeDtypeStruct((rows, cols), jnp.float32)] * sections,
+        cost_estimate=pl.CostEstimate(
+            flops=2 * x.shape[0] * x.shape[1] * cols,
+            bytes_accessed=2 * x.shape[1] * cols + 2 * x.size + 4 * x.shape[0] * cols,
+            transcendentals=0,
+        ),
+    )(x, w_qk, w_vz, w_ba)
 
 
 def recurrence_kernel(decay_ref, beta_ref, qt_ref, kt_ref, v_ref, s_ref, s_out, o_ref, *, heads, steps):
@@ -137,14 +170,32 @@
     width_qk = w_qk.shape[1]
     width_vz = w_vz.shape[1]
 
-    step_rows = gather_rows(activations, "head")
-    flat_rows = step_rows.reshape(-1, step_rows.shape[-1])
-    partial_qk = jnp.dot(flat_rows, w_qk, preferred_element_type=jnp.float32)
-    partial_vz = jnp.dot(flat_rows, w_vz, preferred_element_type=jnp.float32)
-    partial_ba = jnp.dot(flat_rows, w_ba, preferred_element_type=jnp.float32)
-    summed = scatter_sum_rows_paired(
-        jnp.concatenate([partial_qk, partial_vz, partial_ba], axis=1), "dp"
-    )
+    pieces = gather_pieces(activations, "head")
+    n_head, rows_head = pieces.shape[0], pieces.shape[1]
+    flat_pieces = pieces.reshape(-1, pieces.shape[-1])
+    me_head = lax.axis_index("head")
+    n_dp = lax.axis_size("dp")
+    chips = n_dp // 2
+    me_dp = lax.axis_index("dp")
+    core, chip = me_dp % 2, me_dp // 2
+    local_rows = jnp.arange(rows_mem)
+    steps = jnp.arange(step_count)
+    index_blocks = []
+    for which in (1 - core, core):
+        for s in range(chips):
+            block = ((chip + s) % chips) * 2 + which
+            rows = block * rows_mem + local_rows
+            source = (me_head - rows // rows_head) % n_head
+            flat = (source * rows_head + rows % rows_head)[:, None] * step_count + steps[None, :]
+            index_blocks.append(flat.reshape(-1))
+    flat_rows = jnp.take(flat_pieces, jnp.concatenate(index_blocks), axis=0)
+    outs = projection(flat_rows, w_qk, w_vz, w_ba, 2 * chips)
+    pair = [(i, i ^ 1) for i in range(n_dp)]
+    part = [keep + lax.ppermute(send, "dp", pair) for send, keep in zip(outs[:chips], outs[chips:])]
+    summed = part[0]
+    for s in range(1, chips):
+        perm = [(i, ((i // 2 + s) % chips) * 2 + i % 2) for i in range(n_dp)]
+        summed = summed + lax.ppermute(part[s], "dp", perm)
     summed_qk = summed[:, :width_qk]
     summed_vz = summed[:, width_qk : width_qk + width_vz]
     summed_ba = summed[:, width_qk + width_vz :]

time: 87.9 us -> 71.8 us (0.82)
  local copies, waits for them, and re-layouts: 21.5 us -> 12 us
  other arithmetic: 14 us -> 7.69 us
  Pallas kernels: 12 us -> 15.7 us
  matrix products: 2.62 us -> 0.31 us
  waiting for transfers between devices: 20.7 us -> 19.2 us
    ppermute x2 -> x6, starting transfers between devices: 1.55 us -> 9.14 us  [the longest x3 7.01 us: gather_pieces(): pieces.append(lax.ppermute(x, axis, [(i, (i + s) % n) for i in range(n)]))]
    ppermute x6 -> x3, starting transfers between devices: 10 us -> 3 us  [gather_rows(): pieces.append(lax.ppermute(x, axis, [(i, (i + s) % n) for i in range(n)]))]
    ppermute x2 -> x0, local copies, waits for them, and re-layouts: 4.79 us -> none  [the longest x1 3.15 us: scatter_sum_rows_paired(): part = keep + lax.ppermute(send, axis, [(i, i ^ 1) for i in range(n)])]
    unnamed x28 -> x14, local copies, waits for them, and re-layouts: 5.52 us -> 1.64 us
    pallas_call x0 -> x1, Pallas kernels: none -> 3.74 us  [projection(): pl.pallas_call(projection_kernel, out_shape=[jax.ShapeDtypeStruct((rows,...]
    select_n x1 -> x0, local copies, waits for them, and re-layouts: 1.9 us -> none  [scatter_sum_rows_paired(): send = jnp.take(part, (chip + s) % m, axis=0)]
    add x1 -> x5, other arithmetic: 3.17 us -> 1.34 us  [the longest x1 1.06 us: shards(): keep + lax.ppermute(send, 'dp', pair)]
    sort x2 -> x0, other arithmetic: 1.49 us -> none  [gather_rows(): order = jnp.argsort(source)]
  transfers between devices with their start and end apart: 11 -> 12, of which waited for: 9 -> 7; matrix products, arithmetic and copies ran while one was open for 5% -> 8% of each run, Pallas kernels for 0% -> 0%
where the time goes in v3:
time: 71.8 us; the launch traced here: 71.2 us
  waiting for transfers between devices  19.2 us (27%)
  Pallas kernels  15.7 us (22%)
  starting transfers between devices  15.2 us (21%)
  local copies, waits for them, and re-layouts  12 us (17%)
  other arithmetic  7.69 us (11%)
  between operations  1.03 us (1%)
    pallas_call x1, Pallas kernels, recurrence(): pl.pallas_call(kern, grid=(rows,), in_specs=[pl.BlockSpec(memory_space=pl...  12 us
    ppermute x1, waiting for transfers between devices, shards(): summed = summed + lax.ppermute(part[s], 'dp', perm)  9.98 us
    ppermute x3, starting transfers between devices, gather_pieces(): pieces.append(lax.ppermute(x, axis, [(i, (i + s) % n) for i in range(n)]))  7.01 us
    ppermute x3, waiting for transfers between devices, scatter_sum_rows(): acc = acc + lax.ppermute(send, axis, [(i, (i + s) % n) for i in range(n)])  6.12 us
    pallas_call x1, Pallas kernels, projection(): pl.pallas_call(projection_kernel, out_shape=[jax.ShapeDtypeStruct((rows,...  3.74 us
    ppermute x3, starting transfers between devices, scatter_sum_rows(): acc = acc + lax.ppermute(send, axis, [(i, (i + s) % n) for i in range(n)])  3.11 us
    ppermute x3, starting transfers between devices, gather_rows(): pieces.append(lax.ppermute(x, axis, [(i, (i + s) % n) for i in range(n)]))  3 us
    reshape x2, local copies, waits for them, and re-layouts, shards(): readout = readout.reshape(rows_mem, step_count, heads, DV)  1.89 us
  transfers between devices with their start and end apart: 12, of which 7 were waited for; matrix products, arithmetic and copies ran while one was open for 8% of the time, Pallas kernels for 0%

profile of v3, /device:TPU:0, one launch (start us, length us, event | category | flops | bytes accessed | tf_op | source)
XLA Modules:
  0.0 71.2 jit_solution(5934825535060886098)
XLA Ops:
  0.7 3.1 %collective-permute-start = (bf16[8,4,512]{2,1,0:T(4,128)(2,1)}, bf16[8,4,512]{2,1,0:T(4,128)(2,1)S(1)}, u32[]{:S(2)}, u32[]{:S(2)}) collective-permute-start(bf16[8,4,512]{2,1,0:T(4,128)(2,1)} %param.15), channel_id=1, source_target_pairs={{0,1},{1,2},{2,3},{3,0},{4,5},{5,6},{6,7},{7,4},{8,9},{9,10},{10,1... | collective-permute-start | bytes 98312 | tf_op jit(solution)/shard_map/ppermute | solution.py:73
  3.8 2.6 %collective-permute-start.1 = (bf16[8,4,512]{2,1,0:T(4,128)(2,1)}, bf16[8,4,512]{2,1,0:T(4,128)(2,1)S(1)}, u32[]{:S(2)}, u32[]{:S(2)}) collective-permute-start(bf16[8,4,512]{2,1,0:T(4,128)(2,1)} %param.15), channel_id=1, source_target_pairs={{0,2},{1,3},{2,0},{3,1},{4,6},{5,7},{6,4},{7,5},{8,10},{9,11},{10,... | collective-permute-start | bytes 98312 | tf_op jit(solution)/shard_map/ppermute | solution.py:73
  6.3 1.3 %collective-permute-start.2 = (bf16[8,4,512]{2,1,0:T(4,128)(2,1)}, bf16[8,4,512]{2,1,0:T(4,128)(2,1)S(1)}, u32[]{:S(2)}, u32[]{:S(2)}) collective-permute-start(bf16[8,4,512]{2,1,0:T(4,128)(2,1)} %param.15), channel_id=1, source_target_pairs={{0,3},{1,0},{2,1},{3,2},{4,7},{5,4},{6,5},{7,6},{8,11},{9,8},{10,9... | collective-permute-start | bytes 98312 | tf_op jit(solution)/shard_map/ppermute | solution.py:73
  8.8 0.7 exponential_negate_fusion
  9.5 1.5 %copy.78.wba_ref = bf16[512,16]{1,0:T(8,128)(2,1)} copy(bf16[512,16]{0,1:T(8,128)(2,1)} %param.18) | data formatting | bytes 32768 | tf_op args[3]
  11.0 0.1 mul.286
  11.1 0.7 add.534
  11.9 0.9 %pad_maximum_fusion.1 = bf16[4,8,4,512]{3,2,1,0:T(4,128)(2,1)S(1)} fusion(bf16[1,8,4,512]{3,2,1,0:T(4,128)(2,1)S(1)} %bitcast.112, bf16[1,8,4,512]{3,2,1,0:T(4,128)(2,1)S(1)} %bitcast.111, bf16[1,8,4,512]{3,2,1,0:T(4,128)(2,1)S(1)} %bitcast.110, bf16[1,8,4,512]{3,2,1,0:T(4,128)(2,1)} %bitcast.109), kind=kLoop, calls=%fused_computation.23 | loop fusion | flops 196608 | bytes 262144 | tf_op jit(solution)/shard_map/stack | solution.py:74
  12.8 0.8 %gather_fusion = bf16[128,512]{1,0:T(8,128)(2,1)S(1)} fusion(bf16[128,512]{1,0:T(8,128)(2,1)S(1)} %reshape.617, s32[1024]{0:T(1024)S(1)} %pad_clamp_fusion.1), kind=kCustom, calls=%fused_computation | custom fusion | bytes 262656 | tf_op jit(solution)/shard_map/jit(_take)/gather | solution.py:191
  13.7 0.7 %broadcast_select_fusion.x_ref = bf16[128,512]{1,0:T(8,128)(2,1)} fusion(bf16[128,512]{1,0:T(8,128)(2,1)S(1)} %gather_fusion, pred[128]{0:T(512)(128)(4,1)S(1)} %compare_and_fusion), kind=kLoop, calls=%fused_computation.35 | loop fusion | flops 65536 | bytes 262272 | tf_op jit(solution)/shard_map/jit(_take)/select_n | solution.py:191
  14.4 3.7 %shard_map.140 = (f32[32,3088]{1,0:T(8,128)}, f32[32,3088]{1,0:T(8,128)}, f32[32,3088]{1,0:T(8,128)}, f32[32,3088]{1,0:T(8,128)}) custom-call(bf16[128,512]{1,0:T(8,128)(2,1)} %broadcast_select_fusion.x_ref, bf16[512,1024]{1,0:T(8,128)(2,1)} %wqk_ref.1, bf16[512,2048]{1,0:T(8,128)(2,1)} %wvz_ref.1, bf16[512,16]{1,0:T(8,128)(2,1)} %copy.78.wba_ref), custom_call_target="tpu_custom_call" | custom-call | flops 404750336 | bytes 4874240 | tf_op jit(solution)/shard_map/pallas_call | solution.py:92
  18.2 0.6 collective-permute-start.3
  18.8 1.3 %collective-permute-done.4 = f32[32,3088]{1,0:T(8,128)S(1)} collective-permute-done((f32[32,3088]{1,0:T(8,128)}, f32[32,3088]{1,0:T(8,128)S(1)}, u32[]{:S(2)}, u32[]{:S(2)}) %collective-permute-start.4) | collective-permute-done | bytes 395296 | tf_op jit(solution)/shard_map/ppermute | solution.py:194
  20.1 1.1 %add.532 = f32[32,3088]{1,0:T(8,128)S(1)} add(f32[32,3088]{1,0:T(8,128)} %get-tuple-element.11, f32[32,3088]{1,0:T(8,128)S(1)} %collective-permute-done.4) | non-fusion elementwise | flops 98816 | bytes 1185792 | tf_op jit(solution)/shard_map/add | solution.py:194
  21.1 1.6 %collective-permute-start.5 = (f32[32,3088]{1,0:T(8,128)S(1)}, f32[32,3088]{1,0:T(8,128)S(1)}, u32[]{:S(2)}, u32[]{:S(2)}) collective-permute-start(f32[32,3088]{1,0:T(8,128)S(1)} %add.532), channel_id=1, source_target_pairs={{0,8},{4,12},{8,0},{12,4},{1,9},{5,13},{9,1},{13,5},{2,10},{6,14},... | collective-permute-start | bytes 1185800 | tf_op jit(solution)/shard_map/ppermute | solution.py:198
  22.7 10.0 %collective-permute-done.5 = f32[32,3088]{1,0:T(8,128)S(1)} collective-permute-done((f32[32,3088]{1,0:T(8,128)S(1)}, f32[32,3088]{1,0:T(8,128)S(1)}, u32[]{:S(2)}, u32[]{:S(2)}) %collective-permute-start.5) | collective-permute-done | bytes 395296 | tf_op jit(solution)/shard_map/ppermute | solution.py:198
  32.7 1.1 %add_convert_fusion = bf16[32,3088]{1,0:T(8,128)(2,1)S(1)} fusion(f32[32,3088]{1,0:T(8,128)S(1)} %collective-permute-done.5, f32[32,3088]{1,0:T(8,128)} %get-tuple-element.9, f32[32,3088]{1,0:T(8,128)S(1)} %collective-permute-done.3), kind=kLoop, calls=%fused_computation.4 | loop fusion | flops 296448 | bytes 1383424 | tf_op jit(solution)/shard_map/convert.5
  34.0 0.1 multiply_reduce_fusion.1
  34.2 0.1 fusion.18
  34.3 1.0 %copy.90.qt_ref = f32[8,128,32]{2,1,0:T(8,128)} copy(f32[8,128,32]{1,0,2:T(8,128)S(1)} %bitcast.102) | data formatting | bytes 262144 | tf_op jit(solution)/shard_map/reshape | solution.py:216
  35.3 1.0 %copy.91.kt_ref = f32[8,128,32]{2,1,0:T(8,128)} copy(f32[8,128,32]{1,0,2:T(8,128)S(1)} %bitcast.103) | data formatting | bytes 262144 | tf_op jit(solution)/shard_map/reshape | solution.py:217
  36.4 0.4 fusion.41
  37.0 0.1 copy.89
  37.1 0.7 reshape.624.v_ref
  38.0 0.1 copy.107
  38.2 0.7 div.95.beta_ref
  38.9 0.1 copy.80
  39.1 0.6 fusion.20.decay_ref
  39.7 12.0 %shard_map.141 = (f32[8,8,128,128]{3,2,1,0:T(8,128)}, f32[8,32,128]{2,1,0:T(8,128)}) custom-call(f32[8,32]{1,0:T(8,128)} %fusion.20.decay_ref, f32[8,32]{1,0:T(8,128)} %div.95.beta_ref, f32[8,128,32]{2,1,0:T(8,128)} %copy.90.qt_ref, f32[8,128,32]{2,1,0:T(8,128)} %copy.91.kt_ref, f32[8,32,128]{2,1,0:T(8,128)} %reshape.624.v_ref, f32[8,8,128,128]{3,2,1,0:T(8,128)} %s_ref.1), custom_call_target="tpu_custom_call" | custom-call | flops 33554432 | bytes 8388608 | tf_op jit(solution)/shard_map/pallas_call | solution.py:124
  51.6 0.9 %reshape.625 = f32[1,8,4,1024]{3,2,1,0:T(4,128)S(1)} reshape(f32[8,32,128]{2,1,0:T(8,128)} %get-tuple-element.13) | data formatting | bytes 262144 | tf_op jit(solution)/shard_map/reshape | solution.py:226
  52.6 1.0 %multiply_reduce_fusion = f32[8,32]{1,0:T(8,128)S(1)} fusion(f32[8,32,128]{2,1,0:T(8,128)} %get-tuple-element.13), kind=kLoop, calls=%fused_computation.32 | loop fusion | flops 65280 | bytes 132096 | tf_op jit(solution)/shard_map/reduce_sum | solution.py:228
  53.6 0.9 %reshape.626 = f32[8,4,1024]{2,1,0:T(4,128)S(1)} reshape(f32[8,32,128]{2,1,0:T(8,128)} %get-tuple-element.13) | data formatting | bytes 262144 | tf_op jit(solution)/shard_map/reshape | solution.py:226
  54.8 0.2 fusion.11
  55.0 1.6 %collective-permute-start.7 = (bf16[8,4,1024]{2,0,1:T(8,128)(2,1)S(1)}, bf16[8,4,1024]{2,0,1:T(8,128)(2,1)S(1)}, u32[]{:S(2)}, u32[]{:S(2)}) collective-permute-start(bf16[8,4,1024]{2,0,1:T(8,128)(2,1)S(1)} %fusion.11), channel_id=1, source_target_pairs={{0,8},{4,12},{8,0},{12,4},{1,9},{5,13},{9,1},{13,5},{2,10},{6,14},... | collective-permute-start | bytes 196616 | tf_op jit(solution)/shard_map/ppermute | solution.py:34
  56.6 1.4 %collective-permute-start.8 = (bf16[8,4,1024]{2,0,1:T(8,128)(2,1)S(1)}, bf16[8,4,1024]{2,0,1:T(8,128)(2,1)S(1)}, u32[]{:S(2)}, u32[]{:S(2)}) collective-permute-start(bf16[8,4,1024]{2,0,1:T(8,128)(2,1)S(1)} %fusion.11), channel_id=1, source_target_pairs={{0,12},{4,0},{8,4},{12,8},{1,13},{5,1},{9,5},{13,9},{2,14},{6,2},{... | collective-permute-start | bytes 196616 | tf_op jit(solution)/shard_map/ppermute | solution.py:34
  58.0 0.2 fusion.14
  58.2 0.6 collective-permute-done.6
  58.8 0.9 %collective-permute-done.7 = bf16[8,4,1024]{2,0,1:T(8,128)(2,1)S(1)} collective-permute-done((bf16[8,4,1024]{2,0,1:T(8,128)(2,1)S(1)}, bf16[8,4,1024]{2,0,1:T(8,128)(2,1)S(1)}, u32[]{:S(2)}, u32[]{:S(2)}) %collective-permute-start.7) | collective-permute-done | bytes 65568 | tf_op jit(solution)/shard_map/ppermute | solution.py:34
  59.7 0.2 collective-permute-done.8
  59.9 0.6 gather_fusion.1
  60.5 0.2 copy.100
  60.7 0.2 bitcast_select_fusion
  60.9 0.3 fusion
  61.3 0.4 collective-permute-start.10
  61.7 2.7 %collective-permute-start.11 = (f32[32,512]{1,0:T(8,128)S(1)}, f32[32,512]{1,0:T(8,128)S(1)}, u32[]{:S(2)}, u32[]{:S(2)}) collective-permute-start(f32[32,512]{1,0:T(8,128)S(1)} %get-tuple-element.29), channel_id=1, source_target_pairs={{0,3},{1,0},{2,1},{3,2},{4,7},{5,4},{6,5},{7,6},{8,11},{9,8},{10,9... | collective-permute-start | bytes 196616 | tf_op jit(solution)/shard_map/ppermute | solution.py:47
  64.4 4.2 %collective-permute-done.10 = f32[32,512]{1,0:T(8,128)S(1)} collective-permute-done((f32[32,512]{1,0:T(8,128)S(1)}, f32[32,512]{1,0:T(8,128)S(1)}, u32[]{:S(2)}, u32[]{:S(2)}) %collective-permute-start.10) | collective-permute-done | bytes 65568 | tf_op jit(solution)/shard_map/ppermute | solution.py:47
  68.6 1.9 %collective-permute-done.9 = f32[32,512]{1,0:T(8,128)S(1)} collective-permute-done((f32[32,512]{1,0:T(8,128)S(1)}, f32[32,512]{1,0:T(8,128)S(1)}, u32[]{:S(2)}, u32[]{:S(2)}) %collective-permute-start.9) | collective-permute-done | bytes 65568 | tf_op jit(solution)/shard_map/ppermute | solution.py:47
  70.5 0.6 reshape.627
  (76 shorter events, 2.4 us)
Async XLA Ops:
  0.6 60.3 %copy-start = (bf16[1024,512]{1,0:T(8,128)(2,1)S(1)}, bf16[1024,512]{1,0:T(8,128)(2,1)}, u32[]{:S(2)}) copy-start(bf16[1024,512]{1,0:T(8,128)(2,1)} %param.24) | copy-start | bytes 3145732
  0.6 17.5 %copy-start.3 = (bf16[4,1024]{1,0:T(4,128)(2,1)S(1)}, bf16[4,1024]{1,0:T(4,128)(2,1)}, u32[]{:S(2)}) copy-start(bf16[4,1024]{1,0:T(4,128)(2,1)} %param.19) | copy-start | bytes 24580
  0.7 22.0 %copy-start.5 = (f32[128]{0:T(128)S(1)}, f32[128]{0:T(128)}, u32[]{:S(2)}) copy-start(f32[128]{0:T(128)} %param.23) | copy-start | bytes 1540
  0.7 22.0 %copy-start.4 = (bf16[4,1024]{1,0:T(4,128)(2,1)S(1)}, bf16[4,1024]{1,0:T(4,128)(2,1)}, u32[]{:S(2)}) copy-start(bf16[4,1024]{1,0:T(4,128)(2,1)} %param.20) | copy-start | bytes 24580
  0.7 11.2 %collective-permute-start = (bf16[8,4,512]{2,1,0:T(4,128)(2,1)}, bf16[8,4,512]{2,1,0:T(4,128)(2,1)S(1)}, u32[]{:S(2)}, u32[]{:S(2)}) collective-permute-start(bf16[8,4,512]{2,1,0:T(4,128)(2,1)} %param.15), channel_id=1, source_target_pairs={{0,1},{1,2},{2,3},{3,0},{4,5},{5,6},{6,7},{7,4},{8,9},{9,10},{10,1... | collective-permute-start | bytes 98312 | tf_op jit(solution)/shard_map/ppermute | solution.py:73
  3.8 8.1 %collective-permute-start.1 = (bf16[8,4,512]{2,1,0:T(4,128)(2,1)}, bf16[8,4,512]{2,1,0:T(4,128)(2,1)S(1)}, u32[]{:S(2)}, u32[]{:S(2)}) collective-permute-start(bf16[8,4,512]{2,1,0:T(4,128)(2,1)} %param.15), channel_id=1, source_target_pairs={{0,2},{1,3},{2,0},{3,1},{4,6},{5,7},{6,4},{7,5},{8,10},{9,11},{10,... | collective-permute-start | bytes 98312 | tf_op jit(solution)/shard_map/ppermute | solution.py:73
  6.3 5.5 %collective-permute-start.2 = (bf16[8,4,512]{2,1,0:T(4,128)(2,1)}, bf16[8,4,512]{2,1,0:T(4,128)(2,1)S(1)}, u32[]{:S(2)}, u32[]{:S(2)}) collective-permute-start(bf16[8,4,512]{2,1,0:T(4,128)(2,1)} %param.15), channel_id=1, source_target_pairs={{0,3},{1,0},{2,1},{3,2},{4,7},{5,4},{6,5},{7,6},{8,11},{9,8},{10,9... | collective-permute-start | bytes 98312 | tf_op jit(solution)/shard_map/ppermute | solution.py:73
  12.8 21.1 %copy-start.1 = (bf16[8,3,1024]{2,0,1:T(8,128)(2,1)S(1)}, bf16[8,3,1024]{2,0,1:T(8,128)(2,1)}, u32[]{:S(2)}) copy-start(bf16[8,3,1024]{2,0,1:T(8,128)(2,1)} %param.25) | copy-start | bytes 147460
  18.1 18.8 %copy-start.2 = (bf16[8,3,1024]{2,0,1:T(8,128)(2,1)S(1)}, bf16[8,3,1024]{2,0,1:T(8,128)(2,1)}, u32[]{:S(2)}) copy-start(bf16[8,3,1024]{2,0,1:T(8,128)(2,1)} %param.26) | copy-start | bytes 147460
  18.1 2.0 %collective-permute-start.4 = (f32[32,3088]{1,0:T(8,128)}, f32[32,3088]{1,0:T(8,128)S(1)}, u32[]{:S(2)}, u32[]{:S(2)}) collective-permute-start(f32[32,3088]{1,0:T(8,128)} %get-tuple-element.12), channel_id=1, source_target_pairs={{0,4},{4,0},{8,12},{12,8},{1,5},{5,1},{9,13},{13,9},{2,6},{6,2},{1... | collective-permute-start | bytes 1185800 | tf_op jit(solution)/shard_map/ppermute | solution.py:194
  18.2 4.5 %collective-permute-start.3 = (f32[32,3088]{1,0:T(8,128)}, f32[32,3088]{1,0:T(8,128)S(1)}, u32[]{:S(2)}, u32[]{:S(2)}) collective-permute-start(f32[32,3088]{1,0:T(8,128)} %get-tuple-element.10), channel_id=1, source_target_pairs={{0,4},{4,0},{8,12},{12,8},{1,5},{5,1},{9,13},{13,9},{2,6},{6,2},{1... | collective-permute-start | bytes 1185800 | tf_op jit(solution)/shard_map/ppermute | solution.py:194
  21.1 11.6 %collective-permute-start.5 = (f32[32,3088]{1,0:T(8,128)S(1)}, f32[32,3088]{1,0:T(8,128)S(1)}, u32[]{:S(2)}, u32[]{:S(2)}) collective-permute-start(f32[32,3088]{1,0:T(8,128)S(1)} %add.532), channel_id=1, source_target_pairs={{0,8},{4,12},{8,0},{12,4},{1,9},{5,13},{9,1},{13,5},{2,10},{6,14},... | collective-permute-start | bytes 1185800 | tf_op jit(solution)/shard_map/ppermute | solution.py:198
  55.0 3.8 %collective-permute-start.6 = (bf16[8,4,1024]{2,0,1:T(8,128)(2,1)S(1)}, bf16[8,4,1024]{2,0,1:T(8,128)(2,1)S(1)}, u32[]{:S(2)}, u32[]{:S(2)}) collective-permute-start(bf16[8,4,1024]{2,0,1:T(8,128)(2,1)S(1)} %fusion.11), channel_id=1, source_target_pairs={{0,4},{4,8},{8,12},{12,0},{1,5},{5,9},{9,13},{13,1},{2,6},{6,10},{... | collective-permute-start | bytes 196616 | tf_op jit(solution)/shard_map/ppermute | solution.py:34
  55.0 4.6 %collective-permute-start.7 = (bf16[8,4,1024]{2,0,1:T(8,128)(2,1)S(1)}, bf16[8,4,1024]{2,0,1:T(8,128)(2,1)S(1)}, u32[]{:S(2)}, u32[]{:S(2)}) collective-permute-start(bf16[8,4,1024]{2,0,1:T(8,128)(2,1)S(1)} %fusion.11), channel_id=1, source_target_pairs={{0,8},{4,12},{8,0},{12,4},{1,9},{5,13},{9,1},{13,5},{2,10},{6,14},... | collective-permute-start | bytes 196616 | tf_op jit(solution)/shard_map/ppermute | solution.py:34
  56.6 3.3 %collective-permute-start.8 = (bf16[8,4,1024]{2,0,1:T(8,128)(2,1)S(1)}, bf16[8,4,1024]{2,0,1:T(8,128)(2,1)S(1)}, u32[]{:S(2)}, u32[]{:S(2)}) collective-permute-start(bf16[8,4,1024]{2,0,1:T(8,128)(2,1)S(1)} %fusion.11), channel_id=1, source_target_pairs={{0,12},{4,0},{8,4},{12,8},{1,13},{5,1},{9,5},{13,9},{2,14},{6,2},{... | collective-permute-start | bytes 196616 | tf_op jit(solution)/shard_map/ppermute | solution.py:34
  61.3 7.3 %collective-permute-start.10 = (f32[32,512]{1,0:T(8,128)S(1)}, f32[32,512]{1,0:T(8,128)S(1)}, u32[]{:S(2)}, u32[]{:S(2)}) collective-permute-start(f32[32,512]{1,0:T(8,128)S(1)} %get-tuple-element.30), channel_id=1, source_target_pairs={{0,2},{1,3},{2,0},{3,1},{4,6},{5,7},{6,4},{7,5},{8,10},{9,11},{10,... | collective-permute-start | bytes 196616 | tf_op jit(solution)/shard_map/ppermute | solution.py:47
  61.7 6.9 %collective-permute-start.11 = (f32[32,512]{1,0:T(8,128)S(1)}, f32[32,512]{1,0:T(8,128)S(1)}, u32[]{:S(2)}, u32[]{:S(2)}) collective-permute-start(f32[32,512]{1,0:T(8,128)S(1)} %get-tuple-element.29), channel_id=1, source_target_pairs={{0,3},{1,0},{2,1},{3,2},{4,7},{5,4},{6,5},{7,6},{8,11},{9,8},{10,9... | collective-permute-start | bytes 196616 | tf_op jit(solution)/shard_map/ppermute | solution.py:47
  64.4 6.1 %collective-permute-start.9 = (f32[32,512]{1,0:T(8,128)S(1)}, f32[32,512]{1,0:T(8,128)S(1)}, u32[]{:S(2)}, u32[]{:S(2)}) collective-permute-start(f32[32,512]{1,0:T(8,128)S(1)} %get-tuple-element.28), channel_id=1, source_target_pairs={{0,1},{1,2},{2,3},{3,0},{4,5},{5,6},{6,7},{7,4},{8,9},{9,10},{10,1... | collective-permute-start | bytes 196616 | tf_op jit(solution)/shard_map/ppermute | solution.py:47

commit v4 on v3

--- a/solution.py
+++ b/solution.py
@@ -195,7 +195,8 @@
     summed = part[0]
     for s in range(1, chips):
         perm = [(i, ((i // 2 + s) % chips) * 2 + i % 2) for i in range(n_dp)]
-        summed = summed + lax.ppermute(part[s], "dp", perm)
+        sent = lax.ppermute(part[s].astype(jnp.bfloat16), "dp", perm)
+        summed = summed + sent.astype(jnp.float32)
     summed_qk = summed[:, :width_qk]
     summed_vz = summed[:, width_qk : width_qk + width_vz]
     summed_ba = summed[:, width_qk + width_vz :]

time: 71.8 us -> 67.4 us (0.939)
  waiting for transfers between devices: 19.2 us -> 14.8 us
    ppermute x1, waiting for transfers between devices: 9.98 us -> 5.62 us  [shards(): sent = lax.ppermute(part[s].astype(jnp.bfloat16), 'dp', perm)]
    add x1 -> x0, other arithmetic: 1.06 us -> none  [shards(): keep + lax.ppermute(send, 'dp', pair)]
    convert_element_type x0 -> x1, other arithmetic: none -> 1.06 us  [shards(): sent = lax.ppermute(part[s].astype(jnp.bfloat16), 'dp', perm)]
where the time goes in v4:
time: 67.4 us; the launch traced here: 66.8 us
  Pallas kernels  15.7 us (23%)
  starting transfers between devices  15.2 us (23%)
  waiting for transfers between devices  14.8 us (22%)
  local copies, waits for them, and re-layouts  12 us (18%)
  other arithmetic  7.7 us (11%)
  between operations  1.03 us (2%)
    pallas_call x1, Pallas kernels, recurrence(): pl.pallas_call(kern, grid=(rows,), in_specs=[pl.BlockSpec(memory_space=pl...  12 us
    ppermute x3, starting transfers between devices, gather_pieces(): pieces.append(lax.ppermute(x, axis, [(i, (i + s) % n) for i in range(n)]))  7.01 us
    ppermute x3, waiting for transfers between devices, scatter_sum_rows(): acc = acc + lax.ppermute(send, axis, [(i, (i + s) % n) for i in range(n)])  6.12 us
    ppermute x1, waiting for transfers between devices, shards(): sent = lax.ppermute(part[s].astype(jnp.bfloat16), 'dp', perm)  5.62 us
    pallas_call x1, Pallas kernels, projection(): pl.pallas_call(projection_kernel, out_shape=[jax.ShapeDtypeStruct((rows,...  3.74 us
    ppermute x3, starting transfers between devices, scatter_sum_rows(): acc = acc + lax.ppermute(send, axis, [(i, (i + s) % n) for i in range(n)])  3.11 us
    ppermute x3, starting transfers between devices, gather_rows(): pieces.append(lax.ppermute(x, axis, [(i, (i + s) % n) for i in range(n)]))  3 us
    reshape x2, local copies, waits for them, and re-layouts, shards(): readout = readout.reshape(rows_mem, step_count, heads, DV)  1.89 us
  transfers between devices with their start and end apart: 12, of which 7 were waited for; matrix products, arithmetic and copies ran while one was open for 8% of the time, Pallas kernels for 0%

profile of v4, /device:TPU:0, one launch (start us, length us, event | category | flops | bytes accessed | tf_op | source)
XLA Modules:
  0.0 66.8 jit_solution(7848957584357223730)
XLA Ops:
  0.7 3.1 %collective-permute-start = (bf16[8,4,512]{2,1,0:T(4,128)(2,1)}, bf16[8,4,512]{2,1,0:T(4,128)(2,1)S(1)}, u32[]{:S(2)}, u32[]{:S(2)}) collective-permute-start(bf16[8,4,512]{2,1,0:T(4,128)(2,1)} %param.15), channel_id=1, source_target_pairs={{0,1},{1,2},{2,3},{3,0},{4,5},{5,6},{6,7},{7,4},{8,9},{9,10},{10,1... | collective-permute-start | bytes 98312 | tf_op jit(solution)/shard_map/ppermute | solution.py:73
  3.8 2.6 %collective-permute-start.1 = (bf16[8,4,512]{2,1,0:T(4,128)(2,1)}, bf16[8,4,512]{2,1,0:T(4,128)(2,1)S(1)}, u32[]{:S(2)}, u32[]{:S(2)}) collective-permute-start(bf16[8,4,512]{2,1,0:T(4,128)(2,1)} %param.15), channel_id=1, source_target_pairs={{0,2},{1,3},{2,0},{3,1},{4,6},{5,7},{6,4},{7,5},{8,10},{9,11},{10,... | collective-permute-start | bytes 98312 | tf_op jit(solution)/shard_map/ppermute | solution.py:73
  6.3 1.3 %collective-permute-start.2 = (bf16[8,4,512]{2,1,0:T(4,128)(2,1)}, bf16[8,4,512]{2,1,0:T(4,128)(2,1)S(1)}, u32[]{:S(2)}, u32[]{:S(2)}) collective-permute-start(bf16[8,4,512]{2,1,0:T(4,128)(2,1)} %param.15), channel_id=1, source_target_pairs={{0,3},{1,0},{2,1},{3,2},{4,7},{5,4},{6,5},{7,6},{8,11},{9,8},{10,9... | collective-permute-start | bytes 98312 | tf_op jit(solution)/shard_map/ppermute | solution.py:73
  8.8 0.7 exponential_negate_fusion
  9.6 1.5 %copy.78.wba_ref = bf16[512,16]{1,0:T(8,128)(2,1)} copy(bf16[512,16]{0,1:T(8,128)(2,1)} %param.18) | data formatting | bytes 32768 | tf_op args[3]
  11.1 0.1 mul.286
  11.1 0.7 add.534
  11.9 0.9 %pad_maximum_fusion.1 = bf16[4,8,4,512]{3,2,1,0:T(4,128)(2,1)S(1)} fusion(bf16[1,8,4,512]{3,2,1,0:T(4,128)(2,1)S(1)} %bitcast.112, bf16[1,8,4,512]{3,2,1,0:T(4,128)(2,1)S(1)} %bitcast.111, bf16[1,8,4,512]{3,2,1,0:T(4,128)(2,1)S(1)} %bitcast.110, bf16[1,8,4,512]{3,2,1,0:T(4,128)(2,1)} %bitcast.109), kind=kLoop, calls=%fused_computation.24 | loop fusion | flops 196608 | bytes 262144 | tf_op jit(solution)/shard_map/stack | solution.py:74
  12.8 0.8 %gather_fusion = bf16[128,512]{1,0:T(8,128)(2,1)S(1)} fusion(bf16[128,512]{1,0:T(8,128)(2,1)S(1)} %reshape.617, s32[1024]{0:T(1024)S(1)} %pad_clamp_fusion.1), kind=kCustom, calls=%fused_computation | custom fusion | bytes 262656 | tf_op jit(solution)/shard_map/jit(_take)/gather | solution.py:191
  13.7 0.7 %broadcast_select_fusion.x_ref = bf16[128,512]{1,0:T(8,128)(2,1)} fusion(bf16[128,512]{1,0:T(8,128)(2,1)S(1)} %gather_fusion, pred[128]{0:T(512)(128)(4,1)S(1)} %compare_and_fusion), kind=kLoop, calls=%fused_computation.36 | loop fusion | flops 65536 | bytes 262272 | tf_op jit(solution)/shard_map/jit(_take)/select_n | solution.py:191
  14.4 3.7 %shard_map.140 = (f32[32,3088]{1,0:T(8,128)}, f32[32,3088]{1,0:T(8,128)}, f32[32,3088]{1,0:T(8,128)}, f32[32,3088]{1,0:T(8,128)}) custom-call(bf16[128,512]{1,0:T(8,128)(2,1)} %broadcast_select_fusion.x_ref, bf16[512,1024]{1,0:T(8,128)(2,1)} %wqk_ref.1, bf16[512,2048]{1,0:T(8,128)(2,1)} %wvz_ref.1, bf16[512,16]{1,0:T(8,128)(2,1)} %copy.78.wba_ref), custom_call_target="tpu_custom_call" | custom-call | flops 404750336 | bytes 4874240 | tf_op jit(solution)/shard_map/pallas_call | solution.py:92
  18.2 0.6 collective-permute-start.3
  18.8 1.3 %collective-permute-done.4 = f32[32,3088]{1,0:T(8,128)S(1)} collective-permute-done((f32[32,3088]{1,0:T(8,128)}, f32[32,3088]{1,0:T(8,128)S(1)}, u32[]{:S(2)}, u32[]{:S(2)}) %collective-permute-start.4) | collective-permute-done | bytes 395296 | tf_op jit(solution)/shard_map/ppermute | solution.py:194
  20.1 1.1 %add_convert_fusion.1 = bf16[32,3088]{1,0:T(8,128)(2,1)S(1)} fusion(f32[32,3088]{1,0:T(8,128)} %get-tuple-element.11, f32[32,3088]{1,0:T(8,128)S(1)} %collective-permute-done.4), kind=kLoop, calls=%fused_computation.5 | loop fusion | flops 197632 | bytes 988160 | tf_op jit(solution)/shard_map/convert_element_type | solution.py:198
  21.2 1.6 %collective-permute-start.5 = (bf16[32,3088]{1,0:T(8,128)(2,1)S(1)}, bf16[32,3088]{1,0:T(8,128)(2,1)S(1)}, u32[]{:S(2)}, u32[]{:S(2)}) collective-permute-start(bf16[32,3088]{1,0:T(8,128)(2,1)S(1)} %add_convert_fusion.1), channel_id=1, source_target_pairs={{0,8},{4,12},{8,0},{12,4},{1,9},{5,13},{9,1},{13,5},{2,10},{6,14},... | collective-permute-start | bytes 592904 | tf_op jit(solution)/shard_map/ppermute | solution.py:198
  22.7 5.6 %collective-permute-done.5 = bf16[32,3088]{1,0:T(8,128)(2,1)S(1)} collective-permute-done((bf16[32,3088]{1,0:T(8,128)(2,1)S(1)}, bf16[32,3088]{1,0:T(8,128)(2,1)S(1)}, u32[]{:S(2)}, u32[]{:S(2)}) %collective-permute-start.5) | collective-permute-done | bytes 197664 | tf_op jit(solution)/shard_map/ppermute | solution.py:198
  28.4 1.1 %add_convert_fusion = bf16[32,3088]{1,0:T(8,128)(2,1)S(1)} fusion(bf16[32,3088]{1,0:T(8,128)(2,1)S(1)} %collective-permute-done.5, f32[32,3088]{1,0:T(8,128)} %get-tuple-element.9, f32[32,3088]{1,0:T(8,128)S(1)} %collective-permute-done.3), kind=kLoop, calls=%fused_computation.4 | loop fusion | flops 395264 | bytes 1185792 | tf_op jit(solution)/shard_map/convert.5
  29.7 0.1 multiply_reduce_fusion.1
  29.8 0.1 fusion.18
  29.9 1.0 %copy.90.qt_ref = f32[8,128,32]{2,1,0:T(8,128)} copy(f32[8,128,32]{1,0,2:T(8,128)S(1)} %bitcast.102) | data formatting | bytes 262144 | tf_op jit(solution)/shard_map/reshape | solution.py:217
  31.0 1.0 %copy.91.kt_ref = f32[8,128,32]{2,1,0:T(8,128)} copy(f32[8,128,32]{1,0,2:T(8,128)S(1)} %bitcast.103) | data formatting | bytes 262144 | tf_op jit(solution)/shard_map/reshape | solution.py:218
  32.1 0.4 fusion.41
  32.7 0.1 copy.89
  32.8 0.7 %reshape.624.v_ref = f32[8,32,128]{2,1,0:T(8,128)} reshape(f32[8,4,1024]{2,1,0:T(4,128)S(1)} %copy.89) | data formatting | bytes 262144 | tf_op jit(solution)/shard_map/reshape | solution.py:212
  33.7 0.1 copy.107
  33.8 0.7 %div.95.beta_ref = f32[8,32]{1,0:T(8,128)} reshape(f32[8,4,8,1]{2,1,0,3:T(4,128)S(1)} %copy.82) | data formatting | bytes 2048 | tf_op jit(solution)/shard_map/div | solution.py:221
  34.5 0.1 copy.80
  34.7 0.6 fusion.20.decay_ref
  35.3 12.0 %shard_map.141 = (f32[8,8,128,128]{3,2,1,0:T(8,128)}, f32[8,32,128]{2,1,0:T(8,128)}) custom-call(f32[8,32]{1,0:T(8,128)} %fusion.20.decay_ref, f32[8,32]{1,0:T(8,128)} %div.95.beta_ref, f32[8,128,32]{2,1,0:T(8,128)} %copy.90.qt_ref, f32[8,128,32]{2,1,0:T(8,128)} %copy.91.kt_ref, f32[8,32,128]{2,1,0:T(8,128)} %reshape.624.v_ref, f32[8,8,128,128]{3,2,1,0:T(8,128)} %s_ref.1), custom_call_target="tpu_custom_call" | custom-call | flops 33554432 | bytes 8388608 | tf_op jit(solution)/shard_map/pallas_call | solution.py:124
  47.3 0.9 %reshape.625 = f32[1,8,4,1024]{3,2,1,0:T(4,128)S(1)} reshape(f32[8,32,128]{2,1,0:T(8,128)} %get-tuple-element.13) | data formatting | bytes 262144 | tf_op jit(solution)/shard_map/reshape | solution.py:227
  48.2 1.0 %multiply_reduce_fusion = f32[8,32]{1,0:T(8,128)S(1)} fusion(f32[8,32,128]{2,1,0:T(8,128)} %get-tuple-element.13), kind=kLoop, calls=%fused_computation.33 | loop fusion | flops 65280 | bytes 132096 | tf_op jit(solution)/shard_map/reduce_sum | solution.py:229
  49.3 0.9 %reshape.626 = f32[8,4,1024]{2,1,0:T(4,128)S(1)} reshape(f32[8,32,128]{2,1,0:T(8,128)} %get-tuple-element.13) | data formatting | bytes 262144 | tf_op jit(solution)/shard_map/reshape | solution.py:227
  50.4 0.2 fusion.11
  50.7 1.6 %collective-permute-start.7 = (bf16[8,4,1024]{2,0,1:T(8,128)(2,1)S(1)}, bf16[8,4,1024]{2,0,1:T(8,128)(2,1)S(1)}, u32[]{:S(2)}, u32[]{:S(2)}) collective-permute-start(bf16[8,4,1024]{2,0,1:T(8,128)(2,1)S(1)} %fusion.11), channel_id=1, source_target_pairs={{0,8},{4,12},{8,0},{12,4},{1,9},{5,13},{9,1},{13,5},{2,10},{6,14},... | collective-permute-start | bytes 196616 | tf_op jit(solution)/shard_map/ppermute | solution.py:34
  52.2 1.4 %collective-permute-start.8 = (bf16[8,4,1024]{2,0,1:T(8,128)(2,1)S(1)}, bf16[8,4,1024]{2,0,1:T(8,128)(2,1)S(1)}, u32[]{:S(2)}, u32[]{:S(2)}) collective-permute-start(bf16[8,4,1024]{2,0,1:T(8,128)(2,1)S(1)} %fusion.11), channel_id=1, source_target_pairs={{0,12},{4,0},{8,4},{12,8},{1,13},{5,1},{9,5},{13,9},{2,14},{6,2},{... | collective-permute-start | bytes 196616 | tf_op jit(solution)/shard_map/ppermute | solution.py:34
  53.6 0.2 fusion.14
  53.8 0.6 collective-permute-done.6
  54.4 0.9 %collective-permute-done.7 = bf16[8,4,1024]{2,0,1:T(8,128)(2,1)S(1)} collective-permute-done((bf16[8,4,1024]{2,0,1:T(8,128)(2,1)S(1)}, bf16[8,4,1024]{2,0,1:T(8,128)(2,1)S(1)}, u32[]{:S(2)}, u32[]{:S(2)}) %collective-permute-start.7) | collective-permute-done | bytes 65568 | tf_op jit(solution)/shard_map/ppermute | solution.py:34
  55.3 0.2 collective-permute-done.8
  55.6 0.6 gather_fusion.1
  56.1 0.2 copy.100
  56.3 0.2 bitcast_select_fusion
  56.6 0.3 fusion
  56.9 0.4 collective-permute-start.10
  57.3 2.7 %collective-permute-start.11 = (f32[32,512]{1,0:T(8,128)S(1)}, f32[32,512]{1,0:T(8,128)S(1)}, u32[]{:S(2)}, u32[]{:S(2)}) collective-permute-start(f32[32,512]{1,0:T(8,128)S(1)} %get-tuple-element.29), channel_id=1, source_target_pairs={{0,3},{1,0},{2,1},{3,2},{4,7},{5,4},{6,5},{7,6},{8,11},{9,8},{10,9... | collective-permute-start | bytes 196616 | tf_op jit(solution)/shard_map/ppermute | solution.py:47
  60.0 4.2 %collective-permute-done.10 = f32[32,512]{1,0:T(8,128)S(1)} collective-permute-done((f32[32,512]{1,0:T(8,128)S(1)}, f32[32,512]{1,0:T(8,128)S(1)}, u32[]{:S(2)}, u32[]{:S(2)}) %collective-permute-start.10) | collective-permute-done | bytes 65568 | tf_op jit(solution)/shard_map/ppermute | solution.py:47
  64.2 1.9 %collective-permute-done.9 = f32[32,512]{1,0:T(8,128)S(1)} collective-permute-done((f32[32,512]{1,0:T(8,128)S(1)}, f32[32,512]{1,0:T(8,128)S(1)}, u32[]{:S(2)}, u32[]{:S(2)}) %collective-permute-start.9) | collective-permute-done | bytes 65568 | tf_op jit(solution)/shard_map/ppermute | solution.py:47
  66.2 0.6 reshape.627
  (76 shorter events, 2.4 us)
Async XLA Ops:
  0.6 55.9 %copy-start = (bf16[1024,512]{1,0:T(8,128)(2,1)S(1)}, bf16[1024,512]{1,0:T(8,128)(2,1)}, u32[]{:S(2)}) copy-start(bf16[1024,512]{1,0:T(8,128)(2,1)} %param.24) | copy-start | bytes 3145732
  0.6 17.5 %copy-start.3 = (bf16[4,1024]{1,0:T(4,128)(2,1)S(1)}, bf16[4,1024]{1,0:T(4,128)(2,1)}, u32[]{:S(2)}) copy-start(bf16[4,1024]{1,0:T(4,128)(2,1)} %param.19) | copy-start | bytes 24580
  0.7 17.5 %copy-start.4 = (bf16[4,1024]{1,0:T(4,128)(2,1)S(1)}, bf16[4,1024]{1,0:T(4,128)(2,1)}, u32[]{:S(2)}) copy-start(bf16[4,1024]{1,0:T(4,128)(2,1)} %param.20) | copy-start | bytes 24580
  0.7 22.1 %copy-start.5 = (f32[128]{0:T(128)S(1)}, f32[128]{0:T(128)}, u32[]{:S(2)}) copy-start(f32[128]{0:T(128)} %param.23) | copy-start | bytes 1540
  0.7 11.2 %collective-permute-start = (bf16[8,4,512]{2,1,0:T(4,128)(2,1)}, bf16[8,4,512]{2,1,0:T(4,128)(2,1)S(1)}, u32[]{:S(2)}, u32[]{:S(2)}) collective-permute-start(bf16[8,4,512]{2,1,0:T(4,128)(2,1)} %param.15), channel_id=1, source_target_pairs={{0,1},{1,2},{2,3},{3,0},{4,5},{5,6},{6,7},{7,4},{8,9},{9,10},{10,1... | collective-permute-start | bytes 98312 | tf_op jit(solution)/shard_map/ppermute | solution.py:73
  3.8 8.1 %collective-permute-start.1 = (bf16[8,4,512]{2,1,0:T(4,128)(2,1)}, bf16[8,4,512]{2,1,0:T(4,128)(2,1)S(1)}, u32[]{:S(2)}, u32[]{:S(2)}) collective-permute-start(bf16[8,4,512]{2,1,0:T(4,128)(2,1)} %param.15), channel_id=1, source_target_pairs={{0,2},{1,3},{2,0},{3,1},{4,6},{5,7},{6,4},{7,5},{8,10},{9,11},{10,... | collective-permute-start | bytes 98312 | tf_op jit(solution)/shard_map/ppermute | solution.py:73
  6.3 5.5 %collective-permute-start.2 = (bf16[8,4,512]{2,1,0:T(4,128)(2,1)}, bf16[8,4,512]{2,1,0:T(4,128)(2,1)S(1)}, u32[]{:S(2)}, u32[]{:S(2)}) collective-permute-start(bf16[8,4,512]{2,1,0:T(4,128)(2,1)} %param.15), channel_id=1, source_target_pairs={{0,3},{1,0},{2,1},{3,2},{4,7},{5,4},{6,5},{7,6},{8,11},{9,8},{10,9... | collective-permute-start | bytes 98312 | tf_op jit(solution)/shard_map/ppermute | solution.py:73
  11.9 17.7 %copy-start.1 = (bf16[8,3,1024]{2,0,1:T(8,128)(2,1)S(1)}, bf16[8,3,1024]{2,0,1:T(8,128)(2,1)}, u32[]{:S(2)}) copy-start(bf16[8,3,1024]{2,0,1:T(8,128)(2,1)} %param.25) | copy-start | bytes 147460
  18.2 14.4 %copy-start.2 = (bf16[8,3,1024]{2,0,1:T(8,128)(2,1)S(1)}, bf16[8,3,1024]{2,0,1:T(8,128)(2,1)}, u32[]{:S(2)}) copy-start(bf16[8,3,1024]{2,0,1:T(8,128)(2,1)} %param.26) | copy-start | bytes 147460
  18.2 2.0 %collective-permute-start.4 = (f32[32,3088]{1,0:T(8,128)}, f32[32,3088]{1,0:T(8,128)S(1)}, u32[]{:S(2)}, u32[]{:S(2)}) collective-permute-start(f32[32,3088]{1,0:T(8,128)} %get-tuple-element.12), channel_id=1, source_target_pairs={{0,4},{4,0},{8,12},{12,8},{1,5},{5,1},{9,13},{13,9},{2,6},{6,2},{1... | collective-permute-start | bytes 1185800 | tf_op jit(solution)/shard_map/ppermute | solution.py:194
  18.2 4.5 %collective-permute-start.3 = (f32[32,3088]{1,0:T(8,128)}, f32[32,3088]{1,0:T(8,128)S(1)}, u32[]{:S(2)}, u32[]{:S(2)}) collective-permute-start(f32[32,3088]{1,0:T(8,128)} %get-tuple-element.10), channel_id=1, source_target_pairs={{0,4},{4,0},{8,12},{12,8},{1,5},{5,1},{9,13},{13,9},{2,6},{6,2},{1... | collective-permute-start | bytes 1185800 | tf_op jit(solution)/shard_map/ppermute | solution.py:194
  21.2 7.2 %collective-permute-start.5 = (bf16[32,3088]{1,0:T(8,128)(2,1)S(1)}, bf16[32,3088]{1,0:T(8,128)(2,1)S(1)}, u32[]{:S(2)}, u32[]{:S(2)}) collective-permute-start(bf16[32,3088]{1,0:T(8,128)(2,1)S(1)} %add_convert_fusion.1), channel_id=1, source_target_pairs={{0,8},{4,12},{8,0},{12,4},{1,9},{5,13},{9,1},{13,5},{2,10},{6,14},... | collective-permute-start | bytes 592904 | tf_op jit(solution)/shard_map/ppermute | solution.py:198
  50.6 3.8 %collective-permute-start.6 = (bf16[8,4,1024]{2,0,1:T(8,128)(2,1)S(1)}, bf16[8,4,1024]{2,0,1:T(8,128)(2,1)S(1)}, u32[]{:S(2)}, u32[]{:S(2)}) collective-permute-start(bf16[8,4,1024]{2,0,1:T(8,128)(2,1)S(1)} %fusion.11), channel_id=1, source_target_pairs={{0,4},{4,8},{8,12},{12,0},{1,5},{5,9},{9,13},{13,1},{2,6},{6,10},{... | collective-permute-start | bytes 196616 | tf_op jit(solution)/shard_map/ppermute | solution.py:34
  50.7 4.6 %collective-permute-start.7 = (bf16[8,4,1024]{2,0,1:T(8,128)(2,1)S(1)}, bf16[8,4,1024]{2,0,1:T(8,128)(2,1)S(1)}, u32[]{:S(2)}, u32[]{:S(2)}) collective-permute-start(bf16[8,4,1024]{2,0,1:T(8,128)(2,1)S(1)} %fusion.11), channel_id=1, source_target_pairs={{0,8},{4,12},{8,0},{12,4},{1,9},{5,13},{9,1},{13,5},{2,10},{6,14},... | collective-permute-start | bytes 196616 | tf_op jit(solution)/shard_map/ppermute | solution.py:34
  52.2 3.3 %collective-permute-start.8 = (bf16[8,4,1024]{2,0,1:T(8,128)(2,1)S(1)}, bf16[8,4,1024]{2,0,1:T(8,128)(2,1)S(1)}, u32[]{:S(2)}, u32[]{:S(2)}) collective-permute-start(bf16[8,4,1024]{2,0,1:T(8,128)(2,1)S(1)} %fusion.11), channel_id=1, source_target_pairs={{0,12},{4,0},{8,4},{12,8},{1,13},{5,1},{9,5},{13,9},{2,14},{6,2},{... | collective-permute-start | bytes 196616 | tf_op jit(solution)/shard_map/ppermute | solution.py:34
  56.9 7.3 %collective-permute-start.10 = (f32[32,512]{1,0:T(8,128)S(1)}, f32[32,512]{1,0:T(8,128)S(1)}, u32[]{:S(2)}, u32[]{:S(2)}) collective-permute-start(f32[32,512]{1,0:T(8,128)S(1)} %get-tuple-element.30), channel_id=1, source_target_pairs={{0,2},{1,3},{2,0},{3,1},{4,6},{5,7},{6,4},{7,5},{8,10},{9,11},{10,... | collective-permute-start | bytes 196616 | tf_op jit(solution)/shard_map/ppermute | solution.py:47
  57.3 6.9 %collective-permute-start.11 = (f32[32,512]{1,0:T(8,128)S(1)}, f32[32,512]{1,0:T(8,128)S(1)}, u32[]{:S(2)}, u32[]{:S(2)}) collective-permute-start(f32[32,512]{1,0:T(8,128)S(1)} %get-tuple-element.29), channel_id=1, source_target_pairs={{0,3},{1,0},{2,1},{3,2},{4,7},{5,4},{6,5},{7,6},{8,11},{9,8},{10,9... | collective-permute-start | bytes 196616 | tf_op jit(solution)/shard_map/ppermute | solution.py:47
  60.0 6.1 %collective-permute-start.9 = (f32[32,512]{1,0:T(8,128)S(1)}, f32[32,512]{1,0:T(8,128)S(1)}, u32[]{:S(2)}, u32[]{:S(2)}) collective-permute-start(f32[32,512]{1,0:T(8,128)S(1)} %get-tuple-element.28), channel_id=1, source_target_pairs={{0,1},{1,2},{2,3},{3,0},{4,5},{5,6},{6,7},{7,4},{8,9},{9,10},{10,1... | collective-permute-start | bytes 196616 | tf_op jit(solution)/shard_map/ppermute | solution.py:47

commit v5 on v3

--- a/solution.py
+++ b/solution.py
@@ -100,26 +100,49 @@
     )(x, w_qk, w_vz, w_ba)
 
 
-def recurrence_kernel(decay_ref, beta_ref, qt_ref, kt_ref, v_ref, s_ref, s_out, o_ref, *, heads, steps):
+def recurrence_kernel(decay_ref, beta_ref, qt_ref, kt_ref, sel_ref, v_ref, s_ref, s_out, o_ref, *, heads, steps):
     r = pl.program_id(0)
+    select = sel_ref[...]
+    key_all = jnp.dot(kt_ref[0], select, preferred_element_type=jnp.float32)
+    query_all = jnp.dot(qt_ref[0], select, preferred_element_type=jnp.float32)
     for h in range(heads):
         state = s_ref[0, h]
         for t in range(steps):
             c = t * heads + h
-            key_col = kt_ref[0, :, c : c + 1]
-            query_col = qt_ref[0, :, c : c + 1]
+            key_b = key_all[:, c * DV : (c + 1) * DV]
+            query_b = query_all[:, c * DV : (c + 1) * DV]
             state = state * decay_ref[r, c]
-            recalled = jnp.sum(key_col * state, axis=0, keepdims=True)
+            recalled = jnp.sum(key_b * state, axis=0, keepdims=True)
             correction = (v_ref[0, c : c + 1, :] - recalled) * beta_ref[r, c]
-            state = state + key_col * correction
-            o_ref[0, c : c + 1, :] = jnp.sum(query_col * state, axis=0, keepdims=True)
+            state = state + key_b * correction
+            o_ref[0, c : c + 1, :] = jnp.sum(query_b * state, axis=0, keepdims=True)
         s_out[0, h] = state
+
+
+def split_three(x, width):
+    hi = lax.reduce_precision(x, exponent_bits=8, mantissa_bits=7)
+    rest = x - hi
+    mid = lax.reduce_precision(rest, exponent_bits=8, mantissa_bits=7)
+    lo = rest - mid
+    parts = jnp.concatenate([hi, mid, lo], axis=-1)
+    parts = jnp.pad(parts, ((0, 0), (0, 0), (0, width - parts.shape[-1])))
+    return parts.astype(jnp.bfloat16)
+
+
+def selector(cols, width):
+    rows = jnp.arange(width)[:, None]
+    lanes = jnp.arange(cols * DV)[None, :]
+    return ((rows % cols == lanes // DV) & (rows < 3 * cols)).astype(jnp.bfloat16)
 
 
 def recurrence(decay, beta, qt, kt, values, memory_state):
     rows, heads = memory_state.shape[0], memory_state.shape[1]
     cols = decay.shape[1]
     steps = cols // heads
+    width = -(-3 * cols // 128) * 128
+    qt3 = split_three(qt, width)
+    kt3 = split_three(kt, width)
+    select = selector(cols, width)
     kern = functools.partial(recurrence_kernel, heads=heads, steps=steps)
     return pl.pallas_call(
         kern,
@@ -127,8 +150,9 @@
         in_specs=[
             pl.BlockSpec(memory_space=pltpu.SMEM),
             pl.BlockSpec(memory_space=pltpu.SMEM),
-            pl.BlockSpec((1, DK, cols), lambda r: (r, 0, 0)),
-            pl.BlockSpec((1, DK, cols), lambda r: (r, 0, 0)),
+            pl.BlockSpec((1, DK, width), lambda r: (r, 0, 0)),
+            pl.BlockSpec((1, DK, width), lambda r: (r, 0, 0)),
+            pl.BlockSpec((width, cols * DV), lambda r: (0, 0)),
             pl.BlockSpec((1, cols, DV), lambda r: (r, 0, 0)),
             pl.BlockSpec((1, heads, DK, DV), lambda r: (r, 0, 0, 0)),
         ],
@@ -141,11 +165,11 @@
             jax.ShapeDtypeStruct((rows, cols, DV), jnp.float32),
         ],
         cost_estimate=pl.CostEstimate(
-            flops=8 * rows * cols * DK * DV,
+            flops=8 * rows * cols * DK * DV + 4 * rows * width * cols * DV * DK,
             bytes_accessed=2 * memory_state.size * 4,
             transcendentals=0,
         ),
-    )(decay, beta, qt, kt, values, memory_state)
+    )(decay, beta, qt3, kt3, select, values, memory_state)
 
 
 def shards(

time: 71.8 us -> 75.5 us (1.052)
  other arithmetic: 7.69 us -> 13.3 us
  waiting for transfers between devices: 19.2 us -> 17.4 us
  Pallas kernels: 15.7 us -> 14.7 us
    concatenate x0 -> x2, other arithmetic: none -> 1.97 us  [split_three(): parts = jnp.concatenate([hi, mid, lo], axis=-1)]
    convert_element_type x0 -> x1, other arithmetic: none -> 1.38 us  [selector(): ((rows % cols == lanes // DV) & (rows < 3 * cols)).astype(jnp.bfloat16)]
    ppermute x2, waiting for transfers between devices: 1.32 us -> 0.18 us  [shards(): lax.ppermute(send, 'dp', pair)]
    pallas_call x1, Pallas kernels: 12 us -> 11 us  [recurrence(): pl.pallas_call(kern, grid=(rows,), in_specs=[pl.BlockSpec(memory_space=pl...]
    reshape x1, local copies, waits for them, and re-layouts: 1.03 us -> 0.21 us  [shards(): kt = key_vec.transpose(0, 3, 1, 2).reshape(rows_mem, DK, step_count * heads)]
    reshape x1, local copies, waits for them, and re-layouts: 1.01 us -> 0.21 us  [shards(): qt = queries.transpose(0, 3, 1, 2).reshape(rows_mem, DK, step_count * heads)]
    unnamed x14 -> x20, local copies, waits for them, and re-layouts: 1.64 us -> 1.64 us
  transfers between devices with their start and end apart: 12 -> 12, of which waited for: 7 -> 7; matrix products, arithmetic and copies ran while one was open for 8% -> 13% of each run, Pallas kernels for 0% -> 0%
where the time goes in v5:
time: 75.5 us; the launch traced here: 74.8 us
  waiting for transfers between devices  17.4 us (23%)
  starting transfers between devices  15.3 us (20%)
  Pallas kernels  14.7 us (19%)
  other arithmetic  13.3 us (18%)
  local copies, waits for them, and re-layouts  12.6 us (17%)
  between operations  1.1 us (1%)
    pallas_call x1, Pallas kernels, recurrence(): pl.pallas_call(kern, grid=(rows,), in_specs=[pl.BlockSpec(memory_space=pl...  11 us
    ppermute x1, waiting for transfers between devices, shards(): summed = summed + lax.ppermute(part[s], 'dp', perm)  9.4 us
    ppermute x3, starting transfers between devices, gather_pieces(): pieces.append(lax.ppermute(x, axis, [(i, (i + s) % n) for i in range(n)]))  7.01 us
    ppermute x3, waiting for transfers between devices, scatter_sum_rows(): acc = acc + lax.ppermute(send, axis, [(i, (i + s) % n) for i in range(n)])  6.12 us
    pallas_call x1, Pallas kernels, projection(): pl.pallas_call(projection_kernel, out_shape=[jax.ShapeDtypeStruct((rows,...  3.74 us
    ppermute x3, starting transfers between devices, scatter_sum_rows(): acc = acc + lax.ppermute(send, axis, [(i, (i + s) % n) for i in range(n)])  3.11 us
    ppermute x3, starting transfers between devices, gather_rows(): pieces.append(lax.ppermute(x, axis, [(i, (i + s) % n) for i in range(n)]))  3 us
    concatenate x2, other arithmetic, split_three(): parts = jnp.concatenate([hi, mid, lo], axis=-1)  1.97 us
  transfers between devices with their start and end apart: 12, of which 7 were waited for; matrix products, arithmetic and copies ran while one was open for 13% of the time, Pallas kernels for 0%

profile of v5, /device:TPU:0, one launch (start us, length us, event | category | flops | bytes accessed | tf_op | source)
XLA Modules:
  0.0 74.8 jit_solution(1951133181197253228)
XLA Ops:
  0.6 3.1 %collective-permute-start = (bf16[8,4,512]{2,1,0:T(4,128)(2,1)}, bf16[8,4,512]{2,1,0:T(4,128)(2,1)S(1)}, u32[]{:S(2)}, u32[]{:S(2)}) collective-permute-start(bf16[8,4,512]{2,1,0:T(4,128)(2,1)} %param.15), channel_id=1, source_target_pairs={{0,1},{1,2},{2,3},{3,0},{4,5},{5,6},{6,7},{7,4},{8,9},{9,10},{10,1... | collective-permute-start | bytes 98312 | tf_op jit(solution)/shard_map/ppermute | solution.py:73
  3.7 2.6 %collective-permute-start.1 = (bf16[8,4,512]{2,1,0:T(4,128)(2,1)}, bf16[8,4,512]{2,1,0:T(4,128)(2,1)S(1)}, u32[]{:S(2)}, u32[]{:S(2)}) collective-permute-start(bf16[8,4,512]{2,1,0:T(4,128)(2,1)} %param.15), channel_id=1, source_target_pairs={{0,2},{1,3},{2,0},{3,1},{4,6},{5,7},{6,4},{7,5},{8,10},{9,11},{10,... | collective-permute-start | bytes 98312 | tf_op jit(solution)/shard_map/ppermute | solution.py:73
  6.3 1.3 %collective-permute-start.2 = (bf16[8,4,512]{2,1,0:T(4,128)(2,1)}, bf16[8,4,512]{2,1,0:T(4,128)(2,1)S(1)}, u32[]{:S(2)}, u32[]{:S(2)}) collective-permute-start(bf16[8,4,512]{2,1,0:T(4,128)(2,1)} %param.15), channel_id=1, source_target_pairs={{0,3},{1,0},{2,1},{3,2},{4,7},{5,4},{6,5},{7,6},{8,11},{9,8},{10,9... | collective-permute-start | bytes 98312 | tf_op jit(solution)/shard_map/ppermute | solution.py:73
  8.8 0.7 exponential_negate_fusion
  9.5 1.4 %and_convert_fusion.sel_ref = bf16[128,4096]{1,0:T(8,128)(2,1)} fusion(s32[4096]{0:T(1024)S(1)} %add_select_fusion, s32[128]{0:T(128)S(1)} %and_select_fusion.1, pred[128]{0:T(512)(128)(4,1)S(1)} %iota_compare_fusion.1), kind=kLoop, calls=%fused_computation.2 | loop fusion | flops 1572864 | bytes 1065600 | tf_op jit(solution)/shard_map/convert_element_type | solution.py:135
  10.9 1.5 %copy.84.wba_ref = bf16[512,16]{1,0:T(8,128)(2,1)} copy(bf16[512,16]{0,1:T(8,128)(2,1)} %param.18) | data formatting | bytes 32768 | tf_op args[3]
  12.4 0.6 mul.286
  13.0 0.7 add.555
  13.7 0.7 add.556
  14.3 0.9 %pad_maximum_fusion.1 = bf16[4,8,4,512]{3,2,1,0:T(4,128)(2,1)S(1)} fusion(bf16[1,8,4,512]{3,2,1,0:T(4,128)(2,1)S(1)} %bitcast.118, bf16[1,8,4,512]{3,2,1,0:T(4,128)(2,1)S(1)} %bitcast.117, bf16[1,8,4,512]{3,2,1,0:T(4,128)(2,1)S(1)} %bitcast.116, bf16[1,8,4,512]{3,2,1,0:T(4,128)(2,1)} %bitcast.115), kind=kLoop, calls=%fused_computation.41 | loop fusion | flops 196608 | bytes 262144 | tf_op jit(solution)/shard_map/stack | solution.py:74
  15.2 0.8 %gather_fusion = bf16[128,512]{1,0:T(8,128)(2,1)S(1)} fusion(bf16[128,512]{1,0:T(8,128)(2,1)S(1)} %reshape.674, s32[1024]{0:T(1024)S(1)} %pad_clamp_fusion.1), kind=kCustom, calls=%fused_computation | custom fusion | bytes 262656 | tf_op jit(solution)/shard_map/jit(_take)/gather | solution.py:215
  16.1 0.7 %broadcast_select_fusion.x_ref = bf16[128,512]{1,0:T(8,128)(2,1)} fusion(bf16[128,512]{1,0:T(8,128)(2,1)S(1)} %gather_fusion, pred[128]{0:T(512)(128)(4,1)S(1)} %compare_and_fusion), kind=kLoop, calls=%fused_computation.55 | loop fusion | flops 65536 | bytes 262272 | tf_op jit(solution)/shard_map/jit(_take)/select_n | solution.py:215
  16.9 3.7 %shard_map.140 = (f32[32,3088]{1,0:T(8,128)}, f32[32,3088]{1,0:T(8,128)}, f32[32,3088]{1,0:T(8,128)}, f32[32,3088]{1,0:T(8,128)}) custom-call(bf16[128,512]{1,0:T(8,128)(2,1)} %broadcast_select_fusion.x_ref, bf16[512,1024]{1,0:T(8,128)(2,1)} %wqk_ref.1, bf16[512,2048]{1,0:T(8,128)(2,1)} %wvz_ref.1, bf16[512,16]{1,0:T(8,128)(2,1)} %copy.84.wba_ref), custom_call_target="tpu_custom_call" | custom-call | flops 404750336 | bytes 4874240 | tf_op jit(solution)/shard_map/pallas_call | solution.py:92
  20.6 0.6 compare_and_fusion.1
  21.2 0.6 pad_clamp_fusion
  21.8 0.6 collective-permute-start.3
  22.6 1.1 %add.553 = f32[32,3088]{1,0:T(8,128)S(1)} add(f32[32,3088]{1,0:T(8,128)} %get-tuple-element.11, f32[32,3088]{1,0:T(8,128)S(1)} %collective-permute-done.4) | non-fusion elementwise | flops 98816 | bytes 1185792 | tf_op jit(solution)/shard_map/add | solution.py:218
  23.6 1.6 %collective-permute-start.5 = (f32[32,3088]{1,0:T(8,128)S(1)}, f32[32,3088]{1,0:T(8,128)S(1)}, u32[]{:S(2)}, u32[]{:S(2)}) collective-permute-start(f32[32,3088]{1,0:T(8,128)S(1)} %add.553), channel_id=1, source_target_pairs={{0,8},{4,12},{8,0},{12,4},{1,9},{5,13},{9,1},{13,5},{2,10},{6,14},... | collective-permute-start | bytes 1185800 | tf_op jit(solution)/shard_map/ppermute | solution.py:222
  25.2 0.6 fusion.58
  25.8 9.4 %collective-permute-done.5 = f32[32,3088]{1,0:T(8,128)S(1)} collective-permute-done((f32[32,3088]{1,0:T(8,128)S(1)}, f32[32,3088]{1,0:T(8,128)S(1)}, u32[]{:S(2)}, u32[]{:S(2)}) %collective-permute-start.5) | collective-permute-done | bytes 395296 | tf_op jit(solution)/shard_map/ppermute | solution.py:222
  35.2 1.1 %add_convert_fusion = bf16[32,3088]{1,0:T(8,128)(2,1)S(1)} fusion(f32[32,3088]{1,0:T(8,128)S(1)} %collective-permute-done.5, f32[32,3088]{1,0:T(8,128)} %get-tuple-element.9, f32[32,3088]{1,0:T(8,128)S(1)} %collective-permute-done.3), kind=kLoop, calls=%fused_computation.18 | loop fusion | flops 296448 | bytes 1383424 | tf_op jit(solution)/shard_map/convert.15
  37.0 0.2 copy.98
  37.3 0.2 copy.92
  37.5 0.2 copy.93
  37.8 0.4 fusion.56
  38.3 0.8 %divide_multiply_fusion = f32[8,4,1024]{2,0,1:T(8,128)S(1)} fusion(f32[8,7,1024]{2,0,1:T(8,128)S(1)} %maximum_convert_fusion.1, f32[1024]{0:T(1024)} %bitcast.122, f32[1024]{0:T(1024)S(1)} %bitcast.121, f32[1024]{0:T(1024)S(1)} %bitcast.120, f32[1024]{0:T(1024)S(1)} %bitcast.119), kind=kLoop, calls=%fused_computation.53 | loop fusion | flops 360448 | bytes 671744 | tf_op jit(solution)/shard_map/jit(silu)/mul | solution.py:26
  39.2 0.7 reshape.681.v_ref
  40.3 0.7 div.103.beta_ref
  41.5 1.0 %fusion.13.kt_ref = bf16[8,128,128]{2,1,0:T(8,128)(2,1)} fusion(bf16[8,128,32]{2,1,0:T(8,128)(2,1)S(1)} %get-tuple-element.29, bf16[8,128,32]{2,1,0:T(8,128)(2,1)S(1)} %get-tuple-element.28, bf16[8,128,32]{2,1,0:T(8,128)(2,1)S(1)} %get-tuple-element.32), kind=kLoop, calls=%fused_computation.22 | loop fusion | flops 1310720 | bytes 458752 | tf_op jit(solution)/shard_map/concatenate | solution.py:127
  42.5 1.0 %fusion.11.qt_ref = bf16[8,128,128]{2,1,0:T(8,128)(2,1)} fusion(bf16[8,128,32]{2,1,0:T(8,128)(2,1)S(1)} %get-tuple-element.31, bf16[8,128,32]{2,1,0:T(8,128)(2,1)S(1)} %get-tuple-element.30, bf16[8,128,32]{2,1,0:T(8,128)(2,1)S(1)} %get-tuple-element.33), kind=kLoop, calls=%fused_computation.20 | loop fusion | flops 1310720 | bytes 458752 | tf_op jit(solution)/shard_map/concatenate | solution.py:127
  43.5 0.6 fusion.35.decay_ref
  44.1 11.0 %shard_map.141 = (f32[8,8,128,128]{3,2,1,0:T(8,128)}, f32[8,32,128]{2,1,0:T(8,128)}) custom-call(f32[8,32]{1,0:T(8,128)} %fusion.35.decay_ref, f32[8,32]{1,0:T(8,128)} %div.103.beta_ref, bf16[8,128,128]{2,1,0:T(8,128)(2,1)} %fusion.11.qt_ref, bf16[8,128,128]{2,1,0:T(8,128)(2,1)} %fusion.13.kt_ref, bf16[128,4096]{1,0:T(8,128)(2,1)} %and_convert_fusion.sel_ref, ...), custom_call_target="tpu_custom_call" | custom-call | flops 2181038080 | bytes 8388608 | tf_op jit(solution)/shard_map/pallas_call | solution.py:147
  55.1 0.9 %reshape.682 = f32[1,8,4,1024]{3,2,1,0:T(4,128)S(1)} reshape(f32[8,32,128]{2,1,0:T(8,128)} %get-tuple-element.13) | data formatting | bytes 262144 | tf_op jit(solution)/shard_map/reshape | solution.py:250
  56.1 1.0 %multiply_reduce_fusion = f32[8,32]{1,0:T(8,128)S(1)} fusion(f32[8,32,128]{2,1,0:T(8,128)} %get-tuple-element.13), kind=kLoop, calls=%fused_computation.52 | loop fusion | flops 65280 | bytes 132096 | tf_op jit(solution)/shard_map/reduce_sum | solution.py:252
  57.1 0.9 %reshape.683 = f32[8,4,1024]{2,1,0:T(4,128)S(1)} reshape(f32[8,32,128]{2,1,0:T(8,128)} %get-tuple-element.13) | data formatting | bytes 262144 | tf_op jit(solution)/shard_map/reshape | solution.py:250
  58.5 1.6 %collective-permute-start.7 = (bf16[8,4,1024]{2,0,1:T(8,128)(2,1)S(1)}, bf16[8,4,1024]{2,0,1:T(8,128)(2,1)S(1)}, u32[]{:S(2)}, u32[]{:S(2)}) collective-permute-start(bf16[8,4,1024]{2,0,1:T(8,128)(2,1)S(1)} %fusion.23), channel_id=1, source_target_pairs={{0,8},{4,12},{8,0},{12,4},{1,9},{5,13},{9,1},{13,5},{2,10},{6,14},... | collective-permute-start | bytes 196616 | tf_op jit(solution)/shard_map/ppermute | solution.py:34
  60.1 1.4 %collective-permute-start.8 = (bf16[8,4,1024]{2,0,1:T(8,128)(2,1)S(1)}, bf16[8,4,1024]{2,0,1:T(8,128)(2,1)S(1)}, u32[]{:S(2)}, u32[]{:S(2)}) collective-permute-start(bf16[8,4,1024]{2,0,1:T(8,128)(2,1)S(1)} %fusion.23), channel_id=1, source_target_pairs={{0,12},{4,0},{8,4},{12,8},{1,13},{5,1},{9,5},{13,9},{2,14},{6,2},{... | collective-permute-start | bytes 196616 | tf_op jit(solution)/shard_map/ppermute | solution.py:34
  61.7 0.6 collective-permute-done.6
  62.3 0.9 %collective-permute-done.7 = bf16[8,4,1024]{2,0,1:T(8,128)(2,1)S(1)} collective-permute-done((bf16[8,4,1024]{2,0,1:T(8,128)(2,1)S(1)}, bf16[8,4,1024]{2,0,1:T(8,128)(2,1)S(1)}, u32[]{:S(2)}, u32[]{:S(2)}) %collective-permute-start.7) | collective-permute-done | bytes 65568 | tf_op jit(solution)/shard_map/ppermute | solution.py:34
  63.2 0.2 collective-permute-done.8
  63.4 0.7 gather_fusion.1
  64.1 0.2 copy.110
  64.6 0.3 fusion
  64.9 0.4 collective-permute-start.10
  65.3 2.7 %collective-permute-start.11 = (f32[32,512]{1,0:T(8,128)S(1)}, f32[32,512]{1,0:T(8,128)S(1)}, u32[]{:S(2)}, u32[]{:S(2)}) collective-permute-start(f32[32,512]{1,0:T(8,128)S(1)} %get-tuple-element.35), channel_id=1, source_target_pairs={{0,3},{1,0},{2,1},{3,2},{4,7},{5,4},{6,5},{7,6},{8,11},{9,8},{10,9... | collective-permute-start | bytes 196616 | tf_op jit(solution)/shard_map/ppermute | solution.py:47
  68.0 4.2 %collective-permute-done.10 = f32[32,512]{1,0:T(8,128)S(1)} collective-permute-done((f32[32,512]{1,0:T(8,128)S(1)}, f32[32,512]{1,0:T(8,128)S(1)}, u32[]{:S(2)}, u32[]{:S(2)}) %collective-permute-start.10) | collective-permute-done | bytes 65568 | tf_op jit(solution)/shard_map/ppermute | solution.py:47
  72.2 1.9 %collective-permute-done.9 = f32[32,512]{1,0:T(8,128)S(1)} collective-permute-done((f32[32,512]{1,0:T(8,128)S(1)}, f32[32,512]{1,0:T(8,128)S(1)}, u32[]{:S(2)}, u32[]{:S(2)}) %collective-permute-start.9) | collective-permute-done | bytes 65568 | tf_op jit(solution)/shard_map/ppermute | solution.py:47
  74.2 0.6 reshape.684
  (94 shorter events, 4.2 us)
Async XLA Ops:
  0.6 63.9 %copy-start = (bf16[1024,512]{1,0:T(8,128)(2,1)S(1)}, bf16[1024,512]{1,0:T(8,128)(2,1)}, u32[]{:S(2)}) copy-start(bf16[1024,512]{1,0:T(8,128)(2,1)} %param.24) | copy-start | bytes 3145732
  0.6 13.7 %collective-permute-start = (bf16[8,4,512]{2,1,0:T(4,128)(2,1)}, bf16[8,4,512]{2,1,0:T(4,128)(2,1)S(1)}, u32[]{:S(2)}, u32[]{:S(2)}) collective-permute-start(bf16[8,4,512]{2,1,0:T(4,128)(2,1)} %param.15), channel_id=1, source_target_pairs={{0,1},{1,2},{2,3},{3,0},{4,5},{5,6},{6,7},{7,4},{8,9},{9,10},{10,1... | collective-permute-start | bytes 98312 | tf_op jit(solution)/shard_map/ppermute | solution.py:73
  3.7 10.6 %collective-permute-start.1 = (bf16[8,4,512]{2,1,0:T(4,128)(2,1)}, bf16[8,4,512]{2,1,0:T(4,128)(2,1)S(1)}, u32[]{:S(2)}, u32[]{:S(2)}) collective-permute-start(bf16[8,4,512]{2,1,0:T(4,128)(2,1)} %param.15), channel_id=1, source_target_pairs={{0,2},{1,3},{2,0},{3,1},{4,6},{5,7},{6,4},{7,5},{8,10},{9,11},{10,... | collective-permute-start | bytes 98312 | tf_op jit(solution)/shard_map/ppermute | solution.py:73
  6.3 8.0 %collective-permute-start.2 = (bf16[8,4,512]{2,1,0:T(4,128)(2,1)}, bf16[8,4,512]{2,1,0:T(4,128)(2,1)S(1)}, u32[]{:S(2)}, u32[]{:S(2)}) collective-permute-start(bf16[8,4,512]{2,1,0:T(4,128)(2,1)} %param.15), channel_id=1, source_target_pairs={{0,3},{1,0},{2,1},{3,2},{4,7},{5,4},{6,5},{7,6},{8,11},{9,8},{10,9... | collective-permute-start | bytes 98312 | tf_op jit(solution)/shard_map/ppermute | solution.py:73
  16.1 5.7 %copy-start.3 = (bf16[4,1024]{1,0:T(4,128)(2,1)S(1)}, bf16[4,1024]{1,0:T(4,128)(2,1)}, u32[]{:S(2)}) copy-start(bf16[4,1024]{1,0:T(4,128)(2,1)} %param.19) | copy-start | bytes 24580
  16.9 8.3 %copy-start.8 = (f32[128]{0:T(128)S(1)}, f32[128]{0:T(128)}, u32[]{:S(2)}) copy-start(f32[128]{0:T(128)} %param.23) | copy-start | bytes 1540
  16.9 8.3 %copy-start.4 = (bf16[4,1024]{1,0:T(4,128)(2,1)S(1)}, bf16[4,1024]{1,0:T(4,128)(2,1)}, u32[]{:S(2)}) copy-start(bf16[4,1024]{1,0:T(4,128)(2,1)} %param.20) | copy-start | bytes 24580
  20.6 15.8 %copy-start.1 = (bf16[8,3,1024]{2,0,1:T(8,128)(2,1)S(1)}, bf16[8,3,1024]{2,0,1:T(8,128)(2,1)}, u32[]{:S(2)}) copy-start(bf16[8,3,1024]{2,0,1:T(8,128)(2,1)} %param.25) | copy-start | bytes 147460
  20.6 2.0 %collective-permute-start.4 = (f32[32,3088]{1,0:T(8,128)}, f32[32,3088]{1,0:T(8,128)S(1)}, u32[]{:S(2)}, u32[]{:S(2)}) collective-permute-start(f32[32,3088]{1,0:T(8,128)} %get-tuple-element.12), channel_id=1, source_target_pairs={{0,4},{4,0},{8,12},{12,8},{1,5},{5,1},{9,13},{13,9},{2,6},{6,2},{1... | collective-permute-start | bytes 1185800 | tf_op jit(solution)/shard_map/ppermute | solution.py:218
  21.8 4.0 %collective-permute-start.3 = (f32[32,3088]{1,0:T(8,128)}, f32[32,3088]{1,0:T(8,128)S(1)}, u32[]{:S(2)}, u32[]{:S(2)}) collective-permute-start(f32[32,3088]{1,0:T(8,128)} %get-tuple-element.10), channel_id=1, source_target_pairs={{0,4},{4,0},{8,12},{12,8},{1,5},{5,1},{9,13},{13,9},{2,6},{6,2},{1... | collective-permute-start | bytes 1185800 | tf_op jit(solution)/shard_map/ppermute | solution.py:218
  23.6 11.6 %collective-permute-start.5 = (f32[32,3088]{1,0:T(8,128)S(1)}, f32[32,3088]{1,0:T(8,128)S(1)}, u32[]{:S(2)}, u32[]{:S(2)}) collective-permute-start(f32[32,3088]{1,0:T(8,128)S(1)} %add.553), channel_id=1, source_target_pairs={{0,8},{4,12},{8,0},{12,4},{1,9},{5,13},{9,1},{13,5},{2,10},{6,14},... | collective-permute-start | bytes 1185800 | tf_op jit(solution)/shard_map/ppermute | solution.py:222
  36.8 1.5 %copy-start.2 = (bf16[8,3,1024]{2,0,1:T(8,128)(2,1)S(1)}, bf16[8,3,1024]{2,0,1:T(8,128)(2,1)}, u32[]{:S(2)}) copy-start(bf16[8,3,1024]{2,0,1:T(8,128)(2,1)} %param.26) | copy-start | bytes 147460
  41.3 2.2 %copy-start.5 = (f32[32]{0:T(128)S(1)}, f32[32]{0:T(128)}, u32[]{:S(2)}) copy-start(f32[32]{0:T(128)} %mul.286) | copy-start | bytes 388
  41.3 2.2 %copy-start.6 = (f32[32]{0:T(128)S(1)}, f32[32]{0:T(128)}, u32[]{:S(2)}) copy-start(f32[32]{0:T(128)} %add.556) | copy-start | bytes 388
  55.1 9.2 %copy-start.7 = (pred[4]{0:T(512)(128)(4,1)S(1)}, pred[4]{0:T(512)(128)(4,1)}, u32[]{:S(2)}) copy-start(pred[4]{0:T(512)(128)(4,1)} %compare_and_fusion.1) | copy-start | bytes 16
  58.5 3.8 %collective-permute-start.6 = (bf16[8,4,1024]{2,0,1:T(8,128)(2,1)S(1)}, bf16[8,4,1024]{2,0,1:T(8,128)(2,1)S(1)}, u32[]{:S(2)}, u32[]{:S(2)}) collective-permute-start(bf16[8,4,1024]{2,0,1:T(8,128)(2,1)S(1)} %fusion.23), channel_id=1, source_target_pairs={{0,4},{4,8},{8,12},{12,0},{1,5},{5,9},{9,13},{13,1},{2,6},{6,10},{... | collective-permute-start | bytes 196616 | tf_op jit(solution)/shard_map/ppermute | solution.py:34
  58.5 4.6 %collective-permute-start.7 = (bf16[8,4,1024]{2,0,1:T(8,128)(2,1)S(1)}, bf16[8,4,1024]{2,0,1:T(8,128)(2,1)S(1)}, u32[]{:S(2)}, u32[]{:S(2)}) collective-permute-start(bf16[8,4,1024]{2,0,1:T(8,128)(2,1)S(1)} %fusion.23), channel_id=1, source_target_pairs={{0,8},{4,12},{8,0},{12,4},{1,9},{5,13},{9,1},{13,5},{2,10},{6,14},... | collective-permute-start | bytes 196616 | tf_op jit(solution)/shard_map/ppermute | solution.py:34
  60.1 3.3 %collective-permute-start.8 = (bf16[8,4,1024]{2,0,1:T(8,128)(2,1)S(1)}, bf16[8,4,1024]{2,0,1:T(8,128)(2,1)S(1)}, u32[]{:S(2)}, u32[]{:S(2)}) collective-permute-start(bf16[8,4,1024]{2,0,1:T(8,128)(2,1)S(1)} %fusion.23), channel_id=1, source_target_pairs={{0,12},{4,0},{8,4},{12,8},{1,13},{5,1},{9,5},{13,9},{2,14},{6,2},{... | collective-permute-start | bytes 196616 | tf_op jit(solution)/shard_map/ppermute | solution.py:34
  64.9 7.3 %collective-permute-start.10 = (f32[32,512]{1,0:T(8,128)S(1)}, f32[32,512]{1,0:T(8,128)S(1)}, u32[]{:S(2)}, u32[]{:S(2)}) collective-permute-start(f32[32,512]{1,0:T(8,128)S(1)} %get-tuple-element.36), channel_id=1, source_target_pairs={{0,2},{1,3},{2,0},{3,1},{4,6},{5,7},{6,4},{7,5},{8,10},{9,11},{10,... | collective-permute-start | bytes 196616 | tf_op jit(solution)/shard_map/ppermute | solution.py:47
  65.3 6.9 %collective-permute-start.11 = (f32[32,512]{1,0:T(8,128)S(1)}, f32[32,512]{1,0:T(8,128)S(1)}, u32[]{:S(2)}, u32[]{:S(2)}) collective-permute-start(f32[32,512]{1,0:T(8,128)S(1)} %get-tuple-element.35), channel_id=1, source_target_pairs={{0,3},{1,0},{2,1},{3,2},{4,7},{5,4},{6,5},{7,6},{8,11},{9,8},{10,9... | collective-permute-start | bytes 196616 | tf_op jit(solution)/shard_map/ppermute | solution.py:47
  68.0 6.1 %collective-permute-start.9 = (f32[32,512]{1,0:T(8,128)S(1)}, f32[32,512]{1,0:T(8,128)S(1)}, u32[]{:S(2)}, u32[]{:S(2)}) collective-permute-start(f32[32,512]{1,0:T(8,128)S(1)} %get-tuple-element.34), channel_id=1, source_target_pairs={{0,1},{1,2},{2,3},{3,0},{4,5},{5,6},{6,7},{7,4},{8,9},{9,10},{10,1... | collective-permute-start | bytes 196616 | tf_op jit(solution)/shard_map/ppermute | solution.py:47

commit v6 on v3

--- a/solution.py
+++ b/solution.py
@@ -100,35 +100,42 @@
     )(x, w_qk, w_vz, w_ba)
 
 
-def recurrence_kernel(decay_ref, beta_ref, qt_ref, kt_ref, v_ref, s_ref, s_out, o_ref, *, heads, steps):
+def recurrence_kernel(decay_ref, beta_ref, qt_ref, kt_ref, v_ref, s_ref, s_out, o_ref, *, heads, steps, ratio):
     r = pl.program_id(0)
-    for h in range(heads):
-        state = s_ref[0, h]
+    key_heads = heads // ratio
+    for kh in range(key_heads):
+        group = [kh * ratio + j for j in range(ratio)]
+        states = [s_ref[0, h] for h in group]
         for t in range(steps):
-            c = t * heads + h
-            key_col = kt_ref[0, :, c : c + 1]
-            query_col = qt_ref[0, :, c : c + 1]
-            state = state * decay_ref[r, c]
-            recalled = jnp.sum(key_col * state, axis=0, keepdims=True)
-            correction = (v_ref[0, c : c + 1, :] - recalled) * beta_ref[r, c]
-            state = state + key_col * correction
-            o_ref[0, c : c + 1, :] = jnp.sum(query_col * state, axis=0, keepdims=True)
-        s_out[0, h] = state
+            ck = t * key_heads + kh
+            key_col = kt_ref[0, :, ck : ck + 1]
+            query_col = qt_ref[0, :, ck : ck + 1]
+            for j, h in enumerate(group):
+                c = t * heads + h
+                state = states[j] * decay_ref[r, c]
+                recalled = jnp.sum(key_col * state, axis=0, keepdims=True)
+                correction = (v_ref[0, c : c + 1, :] - recalled) * beta_ref[r, c]
+                state = state + key_col * correction
+                o_ref[0, c : c + 1, :] = jnp.sum(query_col * state, axis=0, keepdims=True)
+                states[j] = state
+        for j, h in enumerate(group):
+            s_out[0, h] = states[j]
 
 
 def recurrence(decay, beta, qt, kt, values, memory_state):
     rows, heads = memory_state.shape[0], memory_state.shape[1]
     cols = decay.shape[1]
     steps = cols // heads
-    kern = functools.partial(recurrence_kernel, heads=heads, steps=steps)
+    key_cols = kt.shape[2]
+    kern = functools.partial(recurrence_kernel, heads=heads, steps=steps, ratio=cols // key_cols)
     return pl.pallas_call(
         kern,
         grid=(rows,),
         in_specs=[
             pl.BlockSpec(memory_space=pltpu.SMEM),
             pl.BlockSpec(memory_space=pltpu.SMEM),
-            pl.BlockSpec((1, DK, cols), lambda r: (r, 0, 0)),
-            pl.BlockSpec((1, DK, cols), lambda r: (r, 0, 0)),
+            pl.BlockSpec((1, DK, key_cols), lambda r: (r, 0, 0)),
+            pl.BlockSpec((1, DK, key_cols), lambda r: (r, 0, 0)),
             pl.BlockSpec((1, cols, DV), lambda r: (r, 0, 0)),
             pl.BlockSpec((1, heads, DK, DV), lambda r: (r, 0, 0, 0)),
         ],
@@ -211,10 +218,10 @@
     v_conv = conv_steps(conv_state_v, values_now, conv_v).reshape(rows_mem, step_count * heads, DV)
     queries = normalize(qk_conv[:, :, :, 0, :]) * DK ** (-0.5)
     key_vec = normalize(qk_conv[:, :, :, 1, :])
-    queries = jnp.repeat(queries, head_ratio, axis=2)
-    key_vec = jnp.repeat(key_vec, head_ratio, axis=2)
-    qt = queries.transpose(0, 3, 1, 2).reshape(rows_mem, DK, step_count * heads)
-    kt = key_vec.transpose(0, 3, 1, 2).reshape(rows_mem, DK, step_count * heads)
+    key_heads = queries.shape[2]
+    assert key_heads * head_ratio == heads
+    qt = queries.transpose(0, 3, 1, 2).reshape(rows_mem, DK, step_count * key_heads)
+    kt = key_vec.transpose(0, 3, 1, 2).reshape(rows_mem, DK, step_count * key_heads)
 
     split_ba = ba_proj.reshape(rows_mem, step_count, heads, 2).astype(jnp.float32)
     beta_gate = jax.nn.sigmoid(split_ba[..., 0])

time: 71.8 us -> 70.1 us (0.976)
  Pallas kernels: 15.7 us -> 13.6 us
    pallas_call x1, Pallas kernels: 12 us -> 9.9 us  [recurrence(): pl.pallas_call(kern, grid=(rows,), in_specs=[pl.BlockSpec(memory_space=pl...]
    reshape x2 -> x3, local copies, waits for them, and re-layouts: 2.03 us -> 2.14 us  [the longest x1 1.01 us: shards(): key_vec.transpose(0, 3, 1, 2).reshape(rows_mem, DK, step_count * key_heads)]
where the time goes in v6:
time: 70.1 us; the launch traced here: 69.5 us
  waiting for transfers between devices  19.1 us (27%)
  starting transfers between devices  15.3 us (22%)
  Pallas kernels  13.6 us (19%)
  local copies, waits for them, and re-layouts  12.2 us (17%)
  other arithmetic  7.88 us (11%)
  between operations  1.07 us (2%)
    ppermute x1, waiting for transfers between devices, shards(): summed = summed + lax.ppermute(part[s], 'dp', perm)  9.98 us
    pallas_call x1, Pallas kernels, recurrence(): pl.pallas_call(kern, grid=(rows,), in_specs=[pl.BlockSpec(memory_space=pl...  9.9 us
    ppermute x3, starting transfers between devices, gather_pieces(): pieces.append(lax.ppermute(x, axis, [(i, (i + s) % n) for i in range(n)]))  7.01 us
    ppermute x3, waiting for transfers between devices, scatter_sum_rows(): acc = acc + lax.ppermute(send, axis, [(i, (i + s) % n) for i in range(n)])  6.12 us
    pallas_call x1, Pallas kernels, projection(): pl.pallas_call(projection_kernel, out_shape=[jax.ShapeDtypeStruct((rows,...  3.73 us
    ppermute x3, starting transfers between devices, scatter_sum_rows(): acc = acc + lax.ppermute(send, axis, [(i, (i + s) % n) for i in range(n)])  3.11 us
    ppermute x3, starting transfers between devices, gather_rows(): pieces.append(lax.ppermute(x, axis, [(i, (i + s) % n) for i in range(n)]))  3 us
    reshape x2, local copies, waits for them, and re-layouts, shards(): readout = readout.reshape(rows_mem, step_count, heads, DV)  1.89 us
  transfers between devices with their start and end apart: 12, of which 7 were waited for; matrix products, arithmetic and copies ran while one was open for 8% of the time, Pallas kernels for 0%

profile of v6, /device:TPU:0, one launch (start us, length us, event | category | flops | bytes accessed | tf_op | source)
XLA Modules:
  0.0 69.5 jit_solution(4629497278439814453)
XLA Ops:
  0.7 3.1 %collective-permute-start = (bf16[8,4,512]{2,1,0:T(4,128)(2,1)}, bf16[8,4,512]{2,1,0:T(4,128)(2,1)S(1)}, u32[]{:S(2)}, u32[]{:S(2)}) collective-permute-start(bf16[8,4,512]{2,1,0:T(4,128)(2,1)} %param.15), channel_id=1, source_target_pairs={{0,1},{1,2},{2,3},{3,0},{4,5},{5,6},{6,7},{7,4},{8,9},{9,10},{10,1... | collective-permute-start | bytes 98312 | tf_op jit(solution)/shard_map/ppermute | solution.py:73
  3.8 2.6 %collective-permute-start.1 = (bf16[8,4,512]{2,1,0:T(4,128)(2,1)}, bf16[8,4,512]{2,1,0:T(4,128)(2,1)S(1)}, u32[]{:S(2)}, u32[]{:S(2)}) collective-permute-start(bf16[8,4,512]{2,1,0:T(4,128)(2,1)} %param.15), channel_id=1, source_target_pairs={{0,2},{1,3},{2,0},{3,1},{4,6},{5,7},{6,4},{7,5},{8,10},{9,11},{10,... | collective-permute-start | bytes 98312 | tf_op jit(solution)/shard_map/ppermute | solution.py:73
  6.3 1.3 %collective-permute-start.2 = (bf16[8,4,512]{2,1,0:T(4,128)(2,1)}, bf16[8,4,512]{2,1,0:T(4,128)(2,1)S(1)}, u32[]{:S(2)}, u32[]{:S(2)}) collective-permute-start(bf16[8,4,512]{2,1,0:T(4,128)(2,1)} %param.15), channel_id=1, source_target_pairs={{0,3},{1,0},{2,1},{3,2},{4,7},{5,4},{6,5},{7,6},{8,11},{9,8},{10,9... | collective-permute-start | bytes 98312 | tf_op jit(solution)/shard_map/ppermute | solution.py:73
  8.8 0.7 exponential_negate_fusion
  9.5 1.5 %copy.70.wba_ref = bf16[512,16]{1,0:T(8,128)(2,1)} copy(bf16[512,16]{0,1:T(8,128)(2,1)} %param.18) | data formatting | bytes 32768 | tf_op args[3]
  11.1 0.7 add.534
  11.9 0.9 %pad_maximum_fusion.1 = bf16[4,8,4,512]{3,2,1,0:T(4,128)(2,1)S(1)} fusion(bf16[1,8,4,512]{3,2,1,0:T(4,128)(2,1)S(1)} %bitcast.97, bf16[1,8,4,512]{3,2,1,0:T(4,128)(2,1)S(1)} %bitcast.96, bf16[1,8,4,512]{3,2,1,0:T(4,128)(2,1)S(1)} %bitcast.95, bf16[1,8,4,512]{3,2,1,0:T(4,128)(2,1)} %bitcast.94), kind=kLoop, calls=%fused_computation.23 | loop fusion | flops 196608 | bytes 262144 | tf_op jit(solution)/shard_map/stack | solution.py:74
  12.8 0.8 %gather_fusion = bf16[128,512]{1,0:T(8,128)(2,1)S(1)} fusion(bf16[128,512]{1,0:T(8,128)(2,1)S(1)} %reshape.611, s32[1024]{0:T(1024)S(1)} %pad_clamp_fusion.1), kind=kCustom, calls=%fused_computation | custom fusion | bytes 262656 | tf_op jit(solution)/shard_map/jit(_take)/gather | solution.py:198
  13.6 0.7 %broadcast_select_fusion.x_ref = bf16[128,512]{1,0:T(8,128)(2,1)} fusion(bf16[128,512]{1,0:T(8,128)(2,1)S(1)} %gather_fusion, pred[128]{0:T(512)(128)(4,1)S(1)} %compare_and_fusion), kind=kLoop, calls=%fused_computation.35 | loop fusion | flops 65536 | bytes 262272 | tf_op jit(solution)/shard_map/jit(_take)/select_n | solution.py:198
  14.4 3.7 %shard_map.140 = (f32[32,3088]{1,0:T(8,128)}, f32[32,3088]{1,0:T(8,128)}, f32[32,3088]{1,0:T(8,128)}, f32[32,3088]{1,0:T(8,128)}) custom-call(bf16[128,512]{1,0:T(8,128)(2,1)} %broadcast_select_fusion.x_ref, bf16[512,1024]{1,0:T(8,128)(2,1)} %wqk_ref.1, bf16[512,2048]{1,0:T(8,128)(2,1)} %wvz_ref.1, bf16[512,16]{1,0:T(8,128)(2,1)} %copy.70.wba_ref), custom_call_target="tpu_custom_call" | custom-call | flops 404750336 | bytes 4874240 | tf_op jit(solution)/shard_map/pallas_call | solution.py:92
  18.2 0.6 collective-permute-start.3
  18.7 1.3 %collective-permute-done.4 = f32[32,3088]{1,0:T(8,128)S(1)} collective-permute-done((f32[32,3088]{1,0:T(8,128)}, f32[32,3088]{1,0:T(8,128)S(1)}, u32[]{:S(2)}, u32[]{:S(2)}) %collective-permute-start.4) | collective-permute-done | bytes 395296 | tf_op jit(solution)/shard_map/ppermute | solution.py:201
  20.1 1.1 %add.532 = f32[32,3088]{1,0:T(8,128)S(1)} add(f32[32,3088]{1,0:T(8,128)} %get-tuple-element.11, f32[32,3088]{1,0:T(8,128)S(1)} %collective-permute-done.4) | non-fusion elementwise | flops 98816 | bytes 1185792 | tf_op jit(solution)/shard_map/add | solution.py:201
  21.1 1.6 %collective-permute-start.5 = (f32[32,3088]{1,0:T(8,128)S(1)}, f32[32,3088]{1,0:T(8,128)S(1)}, u32[]{:S(2)}, u32[]{:S(2)}) collective-permute-start(f32[32,3088]{1,0:T(8,128)S(1)} %add.532), channel_id=1, source_target_pairs={{0,8},{4,12},{8,0},{12,4},{1,9},{5,13},{9,1},{13,5},{2,10},{6,14},... | collective-permute-start | bytes 1185800 | tf_op jit(solution)/shard_map/ppermute | solution.py:205
  22.7 10.0 %collective-permute-done.5 = f32[32,3088]{1,0:T(8,128)S(1)} collective-permute-done((f32[32,3088]{1,0:T(8,128)S(1)}, f32[32,3088]{1,0:T(8,128)S(1)}, u32[]{:S(2)}, u32[]{:S(2)}) %collective-permute-start.5) | collective-permute-done | bytes 395296 | tf_op jit(solution)/shard_map/ppermute | solution.py:205
  32.7 1.1 %add_convert_fusion = bf16[32,3088]{1,0:T(8,128)(2,1)S(1)} fusion(f32[32,3088]{1,0:T(8,128)S(1)} %collective-permute-done.5, f32[32,3088]{1,0:T(8,128)} %get-tuple-element.9, f32[32,3088]{1,0:T(8,128)S(1)} %collective-permute-done.3), kind=kLoop, calls=%fused_computation.4 | loop fusion | flops 296448 | bytes 1383424 | tf_op jit(solution)/shard_map/convert.5
  34.0 0.1 reshape.613
  34.1 0.1 fusion.41
  34.2 0.1 multiply_reduce_fusion.1
  34.5 1.0 %copy.81.kt_ref = f32[8,128,16]{2,1,0:T(8,128)} copy(f32[8,128,16]{1,0,2:T(8,128)S(1)} %bitcast.87) | data formatting | bytes 131072 | tf_op jit(solution)/shard_map/reshape | solution.py:224
  35.5 0.1 multiply_reduce_fusion.2
  35.7 1.0 %copy.80.qt_ref = f32[8,128,16]{2,1,0:T(8,128)} copy(f32[8,128,16]{1,0,2:T(8,128)S(1)} %bitcast.88) | data formatting | bytes 131072 | tf_op jit(solution)/shard_map/reshape | solution.py:223
  36.8 0.4 fusion.40
  37.5 0.7 %reshape.616.v_ref = f32[8,32,128]{2,1,0:T(8,128)} reshape(f32[8,4,1024]{2,1,0:T(4,128)S(1)} %copy.79) | data formatting | bytes 262144 | tf_op jit(solution)/shard_map/reshape | solution.py:218
  38.4 0.1 copy.93
  38.6 0.7 div.95.beta_ref
  39.3 0.1 copy.72
  39.5 0.6 fusion.19.decay_ref
  40.1 9.9 %shard_map.141 = (f32[8,8,128,128]{3,2,1,0:T(8,128)}, f32[8,32,128]{2,1,0:T(8,128)}) custom-call(f32[8,32]{1,0:T(8,128)} %fusion.19.decay_ref, f32[8,32]{1,0:T(8,128)} %div.95.beta_ref, f32[8,128,16]{2,1,0:T(8,128)} %copy.80.qt_ref, f32[8,128,16]{2,1,0:T(8,128)} %copy.81.kt_ref, f32[8,32,128]{2,1,0:T(8,128)} %reshape.616.v_ref, f32[8,8,128,128]{3,2,1,0:T(8,128)} %s_ref.1), custom_call_target="tpu_custom_call" | custom-call | flops 33554432 | bytes 8388608 | tf_op jit(solution)/shard_map/pallas_call | solution.py:131
  50.0 0.9 %reshape.617 = f32[1,8,4,1024]{3,2,1,0:T(4,128)S(1)} reshape(f32[8,32,128]{2,1,0:T(8,128)} %get-tuple-element.13) | data formatting | bytes 262144 | tf_op jit(solution)/shard_map/reshape | solution.py:233
  51.0 1.0 %multiply_reduce_fusion = f32[8,32]{1,0:T(8,128)S(1)} fusion(f32[8,32,128]{2,1,0:T(8,128)} %get-tuple-element.13), kind=kLoop, calls=%fused_computation.32 | loop fusion | flops 65280 | bytes 132096 | tf_op jit(solution)/shard_map/reduce_sum | solution.py:235
  52.0 0.9 %reshape.618 = f32[8,4,1024]{2,1,0:T(4,128)S(1)} reshape(f32[8,32,128]{2,1,0:T(8,128)} %get-tuple-element.13) | data formatting | bytes 262144 | tf_op jit(solution)/shard_map/reshape | solution.py:233
  53.1 0.2 fusion.11
  53.4 1.6 %collective-permute-start.7 = (bf16[8,4,1024]{2,0,1:T(8,128)(2,1)S(1)}, bf16[8,4,1024]{2,0,1:T(8,128)(2,1)S(1)}, u32[]{:S(2)}, u32[]{:S(2)}) collective-permute-start(bf16[8,4,1024]{2,0,1:T(8,128)(2,1)S(1)} %fusion.11), channel_id=1, source_target_pairs={{0,8},{4,12},{8,0},{12,4},{1,9},{5,13},{9,1},{13,5},{2,10},{6,14},... | collective-permute-start | bytes 196616 | tf_op jit(solution)/shard_map/ppermute | solution.py:34
  55.0 1.4 %collective-permute-start.8 = (bf16[8,4,1024]{2,0,1:T(8,128)(2,1)S(1)}, bf16[8,4,1024]{2,0,1:T(8,128)(2,1)S(1)}, u32[]{:S(2)}, u32[]{:S(2)}) collective-permute-start(bf16[8,4,1024]{2,0,1:T(8,128)(2,1)S(1)} %fusion.11), channel_id=1, source_target_pairs={{0,12},{4,0},{8,4},{12,8},{1,13},{5,1},{9,5},{13,9},{2,14},{6,2},{... | collective-permute-start | bytes 196616 | tf_op jit(solution)/shard_map/ppermute | solution.py:34
  56.3 0.2 fusion.14
  56.5 0.6 collective-permute-done.6
  57.2 0.9 %collective-permute-done.7 = bf16[8,4,1024]{2,0,1:T(8,128)(2,1)S(1)} collective-permute-done((bf16[8,4,1024]{2,0,1:T(8,128)(2,1)S(1)}, bf16[8,4,1024]{2,0,1:T(8,128)(2,1)S(1)}, u32[]{:S(2)}, u32[]{:S(2)}) %collective-permute-start.7) | collective-permute-done | bytes 65568 | tf_op jit(solution)/shard_map/ppermute | solution.py:34
  58.0 0.2 collective-permute-done.8
  58.3 0.6 gather_fusion.1
  58.9 0.2 copy.90
  59.1 0.2 bitcast_select_fusion
  59.3 0.3 fusion
  59.6 0.4 collective-permute-start.10
  60.0 2.7 %collective-permute-start.11 = (f32[32,512]{1,0:T(8,128)S(1)}, f32[32,512]{1,0:T(8,128)S(1)}, u32[]{:S(2)}, u32[]{:S(2)}) collective-permute-start(f32[32,512]{1,0:T(8,128)S(1)} %get-tuple-element.27), channel_id=1, source_target_pairs={{0,3},{1,0},{2,1},{3,2},{4,7},{5,4},{6,5},{7,6},{8,11},{9,8},{10,9... | collective-permute-start | bytes 196616 | tf_op jit(solution)/shard_map/ppermute | solution.py:47
  62.8 4.2 %collective-permute-done.10 = f32[32,512]{1,0:T(8,128)S(1)} collective-permute-done((f32[32,512]{1,0:T(8,128)S(1)}, f32[32,512]{1,0:T(8,128)S(1)}, u32[]{:S(2)}, u32[]{:S(2)}) %collective-permute-start.10) | collective-permute-done | bytes 65568 | tf_op jit(solution)/shard_map/ppermute | solution.py:47
  67.0 1.9 %collective-permute-done.9 = f32[32,512]{1,0:T(8,128)S(1)} collective-permute-done((f32[32,512]{1,0:T(8,128)S(1)}, f32[32,512]{1,0:T(8,128)S(1)}, u32[]{:S(2)}, u32[]{:S(2)}) %collective-permute-start.9) | collective-permute-done | bytes 65568 | tf_op jit(solution)/shard_map/ppermute | solution.py:47
  68.9 0.6 reshape.619
  (80 shorter events, 2.8 us)
Async XLA Ops:
  0.6 58.7 %copy-start = (bf16[1024,512]{1,0:T(8,128)(2,1)S(1)}, bf16[1024,512]{1,0:T(8,128)(2,1)}, u32[]{:S(2)}) copy-start(bf16[1024,512]{1,0:T(8,128)(2,1)} %param.24) | copy-start | bytes 3145732
  0.6 17.5 %copy-start.3 = (bf16[4,1024]{1,0:T(4,128)(2,1)S(1)}, bf16[4,1024]{1,0:T(4,128)(2,1)}, u32[]{:S(2)}) copy-start(bf16[4,1024]{1,0:T(4,128)(2,1)} %param.19) | copy-start | bytes 24580
  0.7 22.0 %copy-start.5 = (f32[128]{0:T(128)S(1)}, f32[128]{0:T(128)}, u32[]{:S(2)}) copy-start(f32[128]{0:T(128)} %param.23) | copy-start | bytes 1540
  0.7 22.0 %copy-start.4 = (bf16[4,1024]{1,0:T(4,128)(2,1)S(1)}, bf16[4,1024]{1,0:T(4,128)(2,1)}, u32[]{:S(2)}) copy-start(bf16[4,1024]{1,0:T(4,128)(2,1)} %param.20) | copy-start | bytes 24580
  0.7 11.2 %collective-permute-start = (bf16[8,4,512]{2,1,0:T(4,128)(2,1)}, bf16[8,4,512]{2,1,0:T(4,128)(2,1)S(1)}, u32[]{:S(2)}, u32[]{:S(2)}) collective-permute-start(bf16[8,4,512]{2,1,0:T(4,128)(2,1)} %param.15), channel_id=1, source_target_pairs={{0,1},{1,2},{2,3},{3,0},{4,5},{5,6},{6,7},{7,4},{8,9},{9,10},{10,1... | collective-permute-start | bytes 98312 | tf_op jit(solution)/shard_map/ppermute | solution.py:73
  3.8 8.1 %collective-permute-start.1 = (bf16[8,4,512]{2,1,0:T(4,128)(2,1)}, bf16[8,4,512]{2,1,0:T(4,128)(2,1)S(1)}, u32[]{:S(2)}, u32[]{:S(2)}) collective-permute-start(bf16[8,4,512]{2,1,0:T(4,128)(2,1)} %param.15), channel_id=1, source_target_pairs={{0,2},{1,3},{2,0},{3,1},{4,6},{5,7},{6,4},{7,5},{8,10},{9,11},{10,... | collective-permute-start | bytes 98312 | tf_op jit(solution)/shard_map/ppermute | solution.py:73
  6.3 5.5 %collective-permute-start.2 = (bf16[8,4,512]{2,1,0:T(4,128)(2,1)}, bf16[8,4,512]{2,1,0:T(4,128)(2,1)S(1)}, u32[]{:S(2)}, u32[]{:S(2)}) collective-permute-start(bf16[8,4,512]{2,1,0:T(4,128)(2,1)} %param.15), channel_id=1, source_target_pairs={{0,3},{1,0},{2,1},{3,2},{4,7},{5,4},{6,5},{7,6},{8,11},{9,8},{10,9... | collective-permute-start | bytes 98312 | tf_op jit(solution)/shard_map/ppermute | solution.py:73
  12.8 21.1 %copy-start.1 = (bf16[8,3,1024]{2,0,1:T(8,128)(2,1)S(1)}, bf16[8,3,1024]{2,0,1:T(8,128)(2,1)}, u32[]{:S(2)}) copy-start(bf16[8,3,1024]{2,0,1:T(8,128)(2,1)} %param.25) | copy-start | bytes 147460
  18.1 19.2 %copy-start.2 = (bf16[8,3,1024]{2,0,1:T(8,128)(2,1)S(1)}, bf16[8,3,1024]{2,0,1:T(8,128)(2,1)}, u32[]{:S(2)}) copy-start(bf16[8,3,1024]{2,0,1:T(8,128)(2,1)} %param.26) | copy-start | bytes 147460
  18.1 2.0 %collective-permute-start.4 = (f32[32,3088]{1,0:T(8,128)}, f32[32,3088]{1,0:T(8,128)S(1)}, u32[]{:S(2)}, u32[]{:S(2)}) collective-permute-start(f32[32,3088]{1,0:T(8,128)} %get-tuple-element.12), channel_id=1, source_target_pairs={{0,4},{4,0},{8,12},{12,8},{1,5},{5,1},{9,13},{13,9},{2,6},{6,2},{1... | collective-permute-start | bytes 1185800 | tf_op jit(solution)/shard_map/ppermute | solution.py:201
  18.2 4.5 %collective-permute-start.3 = (f32[32,3088]{1,0:T(8,128)}, f32[32,3088]{1,0:T(8,128)S(1)}, u32[]{:S(2)}, u32[]{:S(2)}) collective-permute-start(f32[32,3088]{1,0:T(8,128)} %get-tuple-element.10), channel_id=1, source_target_pairs={{0,4},{4,0},{8,12},{12,8},{1,5},{5,1},{9,13},{13,9},{2,6},{6,2},{1... | collective-permute-start | bytes 1185800 | tf_op jit(solution)/shard_map/ppermute | solution.py:201
  21.1 11.6 %collective-permute-start.5 = (f32[32,3088]{1,0:T(8,128)S(1)}, f32[32,3088]{1,0:T(8,128)S(1)}, u32[]{:S(2)}, u32[]{:S(2)}) collective-permute-start(f32[32,3088]{1,0:T(8,128)S(1)} %add.532), channel_id=1, source_target_pairs={{0,8},{4,12},{8,0},{12,4},{1,9},{5,13},{9,1},{13,5},{2,10},{6,14},... | collective-permute-start | bytes 1185800 | tf_op jit(solution)/shard_map/ppermute | solution.py:205
  53.3 3.8 %collective-permute-start.6 = (bf16[8,4,1024]{2,0,1:T(8,128)(2,1)S(1)}, bf16[8,4,1024]{2,0,1:T(8,128)(2,1)S(1)}, u32[]{:S(2)}, u32[]{:S(2)}) collective-permute-start(bf16[8,4,1024]{2,0,1:T(8,128)(2,1)S(1)} %fusion.11), channel_id=1, source_target_pairs={{0,4},{4,8},{8,12},{12,0},{1,5},{5,9},{9,13},{13,1},{2,6},{6,10},{... | collective-permute-start | bytes 196616 | tf_op jit(solution)/shard_map/ppermute | solution.py:34
  53.4 4.6 %collective-permute-start.7 = (bf16[8,4,1024]{2,0,1:T(8,128)(2,1)S(1)}, bf16[8,4,1024]{2,0,1:T(8,128)(2,1)S(1)}, u32[]{:S(2)}, u32[]{:S(2)}) collective-permute-start(bf16[8,4,1024]{2,0,1:T(8,128)(2,1)S(1)} %fusion.11), channel_id=1, source_target_pairs={{0,8},{4,12},{8,0},{12,4},{1,9},{5,13},{9,1},{13,5},{2,10},{6,14},... | collective-permute-start | bytes 196616 | tf_op jit(solution)/shard_map/ppermute | solution.py:34
  55.0 3.3 %collective-permute-start.8 = (bf16[8,4,1024]{2,0,1:T(8,128)(2,1)S(1)}, bf16[8,4,1024]{2,0,1:T(8,128)(2,1)S(1)}, u32[]{:S(2)}, u32[]{:S(2)}) collective-permute-start(bf16[8,4,1024]{2,0,1:T(8,128)(2,1)S(1)} %fusion.11), channel_id=1, source_target_pairs={{0,12},{4,0},{8,4},{12,8},{1,13},{5,1},{9,5},{13,9},{2,14},{6,2},{... | collective-permute-start | bytes 196616 | tf_op jit(solution)/shard_map/ppermute | solution.py:34
  59.6 7.3 %collective-permute-start.10 = (f32[32,512]{1,0:T(8,128)S(1)}, f32[32,512]{1,0:T(8,128)S(1)}, u32[]{:S(2)}, u32[]{:S(2)}) collective-permute-start(f32[32,512]{1,0:T(8,128)S(1)} %get-tuple-element.28), channel_id=1, source_target_pairs={{0,2},{1,3},{2,0},{3,1},{4,6},{5,7},{6,4},{7,5},{8,10},{9,11},{10,... | collective-permute-start | bytes 196616 | tf_op jit(solution)/shard_map/ppermute | solution.py:47
  60.0 6.9 %collective-permute-start.11 = (f32[32,512]{1,0:T(8,128)S(1)}, f32[32,512]{1,0:T(8,128)S(1)}, u32[]{:S(2)}, u32[]{:S(2)}) collective-permute-start(f32[32,512]{1,0:T(8,128)S(1)} %get-tuple-element.27), channel_id=1, source_target_pairs={{0,3},{1,0},{2,1},{3,2},{4,7},{5,4},{6,5},{7,6},{8,11},{9,8},{10,9... | collective-permute-start | bytes 196616 | tf_op jit(solution)/shard_map/ppermute | solution.py:47
  62.8 6.1 %collective-permute-start.9 = (f32[32,512]{1,0:T(8,128)S(1)}, f32[32,512]{1,0:T(8,128)S(1)}, u32[]{:S(2)}, u32[]{:S(2)}) collective-permute-start(f32[32,512]{1,0:T(8,128)S(1)} %get-tuple-element.26), channel_id=1, source_target_pairs={{0,1},{1,2},{2,3},{3,0},{4,5},{5,6},{6,7},{7,4},{8,9},{9,10},{10,1... | collective-permute-start | bytes 196616 | tf_op jit(solution)/shard_map/ppermute | solution.py:47

commit v7 on v6

--- a/solution.py
+++ b/solution.py
@@ -100,9 +100,10 @@
     )(x, w_qk, w_vz, w_ba)
 
 
-def recurrence_kernel(decay_ref, beta_ref, qt_ref, kt_ref, v_ref, s_ref, s_out, o_ref, *, heads, steps, ratio):
+def recurrence_kernel(gates_ref, qt_ref, kt_ref, v_ref, s_ref, s_out, o_ref, *, heads, steps, ratio):
     r = pl.program_id(0)
     key_heads = heads // ratio
+    cols = heads * steps
     for kh in range(key_heads):
         group = [kh * ratio + j for j in range(ratio)]
         states = [s_ref[0, h] for h in group]
@@ -112,47 +113,47 @@
             query_col = qt_ref[0, :, ck : ck + 1]
             for j, h in enumerate(group):
                 c = t * heads + h
-                state = states[j] * decay_ref[r, c]
+                lanes = slice(h * DV, (h + 1) * DV)
+                state = states[j] * gates_ref[r, cols + c]
                 recalled = jnp.sum(key_col * state, axis=0, keepdims=True)
-                correction = (v_ref[0, c : c + 1, :] - recalled) * beta_ref[r, c]
+                correction = (v_ref[0, t : t + 1, lanes] - recalled) * gates_ref[r, c]
                 state = state + key_col * correction
-                o_ref[0, c : c + 1, :] = jnp.sum(query_col * state, axis=0, keepdims=True)
+                o_ref[0, t : t + 1, lanes] = jnp.sum(query_col * state, axis=0, keepdims=True)
                 states[j] = state
         for j, h in enumerate(group):
             s_out[0, h] = states[j]
 
 
-def recurrence(decay, beta, qt, kt, values, memory_state):
+def recurrence(gates, qt, kt, values, memory_state):
     rows, heads = memory_state.shape[0], memory_state.shape[1]
-    cols = decay.shape[1]
-    steps = cols // heads
+    steps = values.shape[1]
     key_cols = kt.shape[2]
-    kern = functools.partial(recurrence_kernel, heads=heads, steps=steps, ratio=cols // key_cols)
+    ratio = heads * steps // key_cols
+    kern = functools.partial(recurrence_kernel, heads=heads, steps=steps, ratio=ratio)
     return pl.pallas_call(
         kern,
         grid=(rows,),
         in_specs=[
             pl.BlockSpec(memory_space=pltpu.SMEM),
-            pl.BlockSpec(memory_space=pltpu.SMEM),
             pl.BlockSpec((1, DK, key_cols), lambda r: (r, 0, 0)),
             pl.BlockSpec((1, DK, key_cols), lambda r: (r, 0, 0)),
-            pl.BlockSpec((1, cols, DV), lambda r: (r, 0, 0)),
+            pl.BlockSpec((1, steps, heads * DV), lambda r: (r, 0, 0)),
             pl.BlockSpec((1, heads, DK, DV), lambda r: (r, 0, 0, 0)),
         ],
         out_specs=[
             pl.BlockSpec((1, heads, DK, DV), lambda r: (r, 0, 0, 0)),
-            pl.BlockSpec((1, cols, DV), lambda r: (r, 0, 0)),
+            pl.BlockSpec((1, steps, heads * DV), lambda r: (r, 0, 0)),
         ],
         out_shape=[
             jax.ShapeDtypeStruct(memory_state.shape, jnp.float32),
-            jax.ShapeDtypeStruct((rows, cols, DV), jnp.float32),
+            jax.ShapeDtypeStruct((rows, steps, heads * DV), jnp.float32),
         ],
         cost_estimate=pl.CostEstimate(
-            flops=8 * rows * cols * DK * DV,
+            flops=8 * rows * heads * steps * DK * DV,
             bytes_accessed=2 * memory_state.size * 4,
             transcendentals=0,
         ),
-    )(decay, beta, qt, kt, values, memory_state)
+    )(gates, qt, kt, values, memory_state)
 
 
 def shards(
@@ -215,7 +216,7 @@
     gate_z = split_vz[:, :, :, 1, :].astype(jnp.float32)
 
     qk_conv = conv_steps(conv_state_qk, qk_proj, conv_qk).reshape(rows_mem, step_count, -1, 2, DK)
-    v_conv = conv_steps(conv_state_v, values_now, conv_v).reshape(rows_mem, step_count * heads, DV)
+    v_conv = conv_steps(conv_state_v, values_now, conv_v)
     queries = normalize(qk_conv[:, :, :, 0, :]) * DK ** (-0.5)
     key_vec = normalize(qk_conv[:, :, :, 1, :])
     key_heads = queries.shape[2]
@@ -226,10 +227,11 @@
     split_ba = ba_proj.reshape(rows_mem, step_count, heads, 2).astype(jnp.float32)
     beta_gate = jax.nn.sigmoid(split_ba[..., 0])
     log_decay = -jnp.exp(a_log)[None, None, :] * jax.nn.softplus(split_ba[..., 1] + dt_bias[None, None, :])
-    decay = jnp.exp(log_decay).reshape(rows_mem, step_count * heads)
-    beta_gate = beta_gate.reshape(rows_mem, step_count * heads)
-
-    new_state, readout = recurrence(decay, beta_gate, qt, kt, v_conv, memory_state)
+    gates = jnp.concatenate(
+        [beta_gate.reshape(rows_mem, -1), jnp.exp(log_decay).reshape(rows_mem, -1)], axis=1
+    )
+
+    new_state, readout = recurrence(gates, qt, kt, v_conv, memory_state)
     readout = readout.reshape(rows_mem, step_count, heads, DV)
 
     scale = lax.rsqrt(jnp.mean(readout * readout, axis=-1, keepdims=True) + 1e-06)

time: 70.1 us -> 71.5 us (1.020)
  waiting for transfers between devices: 19.1 us -> 21.5 us
  other arithmetic: 7.88 us -> 9.65 us
  local copies, waits for them, and re-layouts: 12.2 us -> 10.7 us
  starting transfers between devices: 15.3 us -> 14 us
    reshape x3 -> x0, local copies, waits for them, and re-layouts: 2.61 us -> none  [the longest x2 1.89 us: shards(): readout = readout.reshape(rows_mem, step_count, heads, DV)]
    ppermute x3, waiting for transfers between devices: 1.72 us -> 4.09 us  [gather_rows(): pieces.append(lax.ppermute(x, axis, [(i, (i + s) % n) for i in range(n)]))]
    unnamed x14 -> x12, local copies, waits for them, and re-layouts: 1.64 us -> 3.32 us
    ppermute x3, starting transfers between devices: 3 us -> 1.78 us  [gather_rows(): pieces.append(lax.ppermute(x, axis, [(i, (i + s) % n) for i in range(n)]))]
    mul x0 -> x3, other arithmetic: none -> 1.19 us  [the longest x1 1.02 us: shards(): readout * readout]
    ppermute x3, starting transfers between devices: 7.01 us -> 6.11 us  [gather_pieces(): pieces.append(lax.ppermute(x, axis, [(i, (i + s) % n) for i in range(n)]))]
    ppermute x3, starting transfers between devices: 3.11 us -> 4 us  [scatter_sum_rows(): acc = acc + lax.ppermute(send, axis, [(i, (i + s) % n) for i in range(n)])]
    reduce_sum x1, other arithmetic: 1.01 us -> 0.12 us  [shards(): jnp.mean(readout * readout, axis=-1, keepdims=True) + 1e-06]
  transfers between devices with their start and end apart: 12 -> 12, of which waited for: 7 -> 8; matrix products, arithmetic and copies ran while one was open for 8% -> 10% of each run, Pallas kernels for 0% -> 0%
where the time goes in v7:
time: 71.5 us; the launch traced here: 70.8 us
  waiting for transfers between devices  21.5 us (30%)
  starting transfers between devices  14 us (20%)
  Pallas kernels  13.6 us (19%)
  local copies, waits for them, and re-layouts  10.7 us (15%)
  other arithmetic  9.65 us (13%)
  between operations  1.01 us (1%)
    ppermute x1, waiting for transfers between devices, shards(): summed = summed + lax.ppermute(part[s], 'dp', perm)  9.98 us
    pallas_call x1, Pallas kernels, recurrence(): pl.pallas_call(kern, grid=(rows,), in_specs=[pl.BlockSpec(memory_space=pl...  9.9 us
    ppermute x3, starting transfers between devices, gather_pieces(): pieces.append(lax.ppermute(x, axis, [(i, (i + s) % n) for i in range(n)]))  6.11 us
    ppermute x3, waiting for transfers between devices, scatter_sum_rows(): acc = acc + lax.ppermute(send, axis, [(i, (i + s) % n) for i in range(n)])  6.05 us
    ppermute x3, waiting for transfers between devices, gather_rows(): pieces.append(lax.ppermute(x, axis, [(i, (i + s) % n) for i in range(n)]))  4.09 us
    ppermute x3, starting transfers between devices, scatter_sum_rows(): acc = acc + lax.ppermute(send, axis, [(i, (i + s) % n) for i in range(n)])  4 us
    pallas_call x1, Pallas kernels, projection(): pl.pallas_call(projection_kernel, out_shape=[jax.ShapeDtypeStruct((rows,...  3.73 us
    unnamed x12, local copies, waits for them, and re-layouts  3.32 us
  transfers between devices with their start and end apart: 12, of which 8 were waited for; matrix products, arithmetic and copies ran while one was open for 10% of the time, Pallas kernels for 0%

profile of v7, /device:TPU:0, one launch (start us, length us, event | category | flops | bytes accessed | tf_op | source)
XLA Modules:
  0.0 70.8 jit_solution(6650278689368056833)
XLA Ops:
  0.7 5.1 %collective-permute-start.2 = (bf16[8,4,512]{2,1,0:T(4,128)(2,1)}, bf16[8,4,512]{2,1,0:T(4,128)(2,1)S(1)}, u32[]{:S(2)}, u32[]{:S(2)}) collective-permute-start(bf16[8,4,512]{2,1,0:T(4,128)(2,1)} %param.15), channel_id=1, source_target_pairs={{0,3},{1,0},{2,1},{3,2},{4,7},{5,4},{6,5},{7,6},{8,11},{9,8},{10,9... | collective-permute-start | bytes 98312 | tf_op jit(solution)/shard_map/ppermute | solution.py:73
  5.8 1.0 %collective-permute-start = (bf16[8,4,512]{2,1,0:T(4,128)(2,1)}, bf16[8,4,512]{2,1,0:T(4,128)(2,1)S(1)}, u32[]{:S(2)}, u32[]{:S(2)}) collective-permute-start(bf16[8,4,512]{2,1,0:T(4,128)(2,1)} %param.15), channel_id=1, source_target_pairs={{0,1},{1,2},{2,3},{3,0},{4,5},{5,6},{6,7},{7,4},{8,9},{9,10},{10,1... | collective-permute-start | bytes 98312 | tf_op jit(solution)/shard_map/ppermute | solution.py:73
  7.9 0.7 exponential_negate_fusion
  8.6 1.5 %copy.36.wba_ref = bf16[512,16]{1,0:T(8,128)(2,1)} copy(bf16[512,16]{0,1:T(8,128)(2,1)} %param.18) | data formatting | bytes 32768 | tf_op args[3]
  10.1 0.7 add.525
  10.9 0.8 %copy.41 = bf16[8,3,1024]{2,1,0:T(4,128)(2,1)S(1)} copy(bf16[8,3,1024]{2,0,1:T(8,128)(2,1)} %param.25) | data formatting | bytes 98304 | tf_op args[10]
  11.8 0.8 %copy.45 = bf16[8,3,1024]{2,1,0:T(4,128)(2,1)S(1)} copy(bf16[8,3,1024]{2,0,1:T(8,128)(2,1)} %param.26) | data formatting | bytes 98304 | tf_op args[11]
  12.7 0.9 %pad_maximum_fusion.1 = bf16[4,8,4,512]{3,2,1,0:T(4,128)(2,1)S(1)} fusion(bf16[1,8,4,512]{3,2,1,0:T(4,128)(2,1)S(1)} %bitcast.78, bf16[1,8,4,512]{3,2,1,0:T(4,128)(2,1)S(1)} %bitcast.79, bf16[1,8,4,512]{3,2,1,0:T(4,128)(2,1)S(1)} %bitcast.80, bf16[1,8,4,512]{3,2,1,0:T(4,128)(2,1)} %bitcast.77), kind=kLoop, calls=%fused_computation.27 | loop fusion | flops 196608 | bytes 262144 | tf_op jit(solution)/shard_map/stack | solution.py:74
  13.6 0.8 %gather_fusion = bf16[128,512]{1,0:T(8,128)(2,1)S(1)} fusion(bf16[128,512]{1,0:T(8,128)(2,1)S(1)} %reshape.542, s32[1024]{0:T(1024)S(1)} %pad_clamp_fusion.1), kind=kCustom, calls=%fused_computation | custom fusion | bytes 262656 | tf_op jit(solution)/shard_map/jit(_take)/gather | solution.py:199
  14.4 0.7 %broadcast_select_fusion.x_ref = bf16[128,512]{1,0:T(8,128)(2,1)} fusion(bf16[128,512]{1,0:T(8,128)(2,1)S(1)} %gather_fusion, pred[128]{0:T(512)(128)(4,1)S(1)} %compare_and_fusion), kind=kLoop, calls=%fused_computation.31 | loop fusion | flops 65536 | bytes 262272 | tf_op jit(solution)/shard_map/jit(_take)/select_n | solution.py:199
  15.2 3.7 %shard_map.140 = (f32[32,3088]{1,0:T(8,128)}, f32[32,3088]{1,0:T(8,128)}, f32[32,3088]{1,0:T(8,128)}, f32[32,3088]{1,0:T(8,128)}) custom-call(bf16[128,512]{1,0:T(8,128)(2,1)} %broadcast_select_fusion.x_ref, bf16[512,1024]{1,0:T(8,128)(2,1)} %wqk_ref.1, bf16[512,2048]{1,0:T(8,128)(2,1)} %wvz_ref.1, bf16[512,16]{1,0:T(8,128)(2,1)} %copy.36.wba_ref), custom_call_target="tpu_custom_call" | custom-call | flops 404750336 | bytes 4874240 | tf_op jit(solution)/shard_map/pallas_call | solution.py:92
  19.0 0.6 collective-permute-start.3
  19.5 1.3 %collective-permute-done.4 = f32[32,3088]{1,0:T(8,128)S(1)} collective-permute-done((f32[32,3088]{1,0:T(8,128)}, f32[32,3088]{1,0:T(8,128)S(1)}, u32[]{:S(2)}, u32[]{:S(2)}) %collective-permute-start.4) | collective-permute-done | bytes 395296 | tf_op jit(solution)/shard_map/ppermute | solution.py:202
  20.9 1.1 %add.522 = f32[32,3088]{1,0:T(8,128)S(1)} add(f32[32,3088]{1,0:T(8,128)} %get-tuple-element.11, f32[32,3088]{1,0:T(8,128)S(1)} %collective-permute-done.4) | non-fusion elementwise | flops 98816 | bytes 1185792 | tf_op jit(solution)/shard_map/add | solution.py:202
  21.9 1.6 %collective-permute-start.5 = (f32[32,3088]{1,0:T(8,128)S(1)}, f32[32,3088]{1,0:T(8,128)S(1)}, u32[]{:S(2)}, u32[]{:S(2)}) collective-permute-start(f32[32,3088]{1,0:T(8,128)S(1)} %add.522), channel_id=1, source_target_pairs={{0,8},{4,12},{8,0},{12,4},{1,9},{5,13},{9,1},{13,5},{2,10},{6,14},... | collective-permute-start | bytes 1185800 | tf_op jit(solution)/shard_map/ppermute | solution.py:206
  23.5 10.0 %collective-permute-done.5 = f32[32,3088]{1,0:T(8,128)S(1)} collective-permute-done((f32[32,3088]{1,0:T(8,128)S(1)}, f32[32,3088]{1,0:T(8,128)S(1)}, u32[]{:S(2)}, u32[]{:S(2)}) %collective-permute-start.5) | collective-permute-done | bytes 395296 | tf_op jit(solution)/shard_map/ppermute | solution.py:206
  33.5 1.1 %add_convert_fusion = bf16[32,3088]{1,0:T(8,128)(2,1)S(1)} fusion(f32[32,3088]{1,0:T(8,128)S(1)} %collective-permute-done.5, f32[32,3088]{1,0:T(8,128)} %get-tuple-element.9, f32[32,3088]{1,0:T(8,128)S(1)} %collective-permute-done.3), kind=kLoop, calls=%fused_computation.4 | loop fusion | flops 296448 | bytes 1383424 | tf_op jit(solution)/shard_map/convert.4
  34.7 0.4 slice_reduce_fusion
  35.4 0.1 copy.40
  35.6 0.1 copy.49
  36.0 0.2 divide_multiply_fusion.2
  36.2 0.1 reshape.544
  36.3 0.1 fusion.40
  36.4 0.1 multiply_reduce_fusion.1
  36.6 1.0 %copy.46.qt_ref = f32[8,128,16]{2,1,0:T(8,128)} copy(f32[8,128,16]{1,0,2:T(8,128)S(1)} %bitcast.71) | data formatting | bytes 131072 | tf_op jit(solution)/shard_map/reshape | solution.py:224
  37.6 0.1 multiply_reduce_fusion
  37.8 1.0 %copy.47.kt_ref = f32[8,128,16]{2,1,0:T(8,128)} copy(f32[8,128,16]{1,0,2:T(8,128)S(1)} %bitcast.72) | data formatting | bytes 131072 | tf_op jit(solution)/shard_map/reshape | solution.py:225
  38.9 0.7 pad_maximum_fusion.2.gates_ref
  39.6 0.8 %divide_multiply_fusion.1.v_ref = f32[8,4,1024]{2,1,0:T(4,128)} fusion(f32[8,7,1024]{2,1,0:T(8,128)S(1)} %maximum_convert_fusion.1, f32[1024]{0:T(1024)S(1)} %bitcast.84, f32[1024]{0:T(1024)S(1)} %bitcast.83, f32[1024]{0:T(1024)S(1)} %bitcast.82, f32[1024]{0:T(1024)S(1)} %bitcast.81), kind=kLoop, calls=%fused_computation.9 | loop fusion | flops 360448 | bytes 671744 | tf_op jit(solution)/shard_map/jit(silu)/mul | solution.py:26
  40.5 9.9 %shard_map.141 = (f32[8,8,128,128]{3,2,1,0:T(8,128)}, f32[8,4,1024]{2,1,0:T(4,128)}) custom-call(f32[8,64]{1,0:T(8,128)} %pad_maximum_fusion.2.gates_ref, f32[8,128,16]{2,1,0:T(8,128)} %copy.46.qt_ref, f32[8,128,16]{2,1,0:T(8,128)} %copy.47.kt_ref, f32[8,4,1024]{2,1,0:T(4,128)} %divide_multiply_fusion.1.v_ref, f32[8,8,128,128]{3,2,1,0:T(8,128)} %s_ref.1), custom_call_target="tpu_custom_call" | custom-call | flops 33554432 | bytes 8388608 | tf_op jit(solution)/shard_map/pallas_call | solution.py:133
  50.4 1.0 %mul.299 = f32[8,4,1024]{2,1,0:T(4,128)S(1)} multiply(f32[8,4,1024]{2,1,0:T(4,128)} %get-tuple-element.13, f32[8,4,1024]{2,1,0:T(4,128)} %get-tuple-element.13) | non-fusion elementwise | flops 32768 | bytes 393216 | tf_op jit(solution)/shard_map/mul | solution.py:237
  51.4 0.1 reduce_sum.29
  51.7 1.0 %fusion.12 = bf16[8,4,1024]{2,1,0:T(4,128)(2,1)S(1)} fusion(f32[8,4,1024]{2,1,0:T(4,128)S(1)} %reshape.608, f32[8,4,1024]{2,1,0:T(4,128)} %get-tuple-element.13, f32[8,4,1024]{2,1,0:T(4,128)S(1)} %mul.302, f32[1024]{0:T(1024)S(1)} %broadcast_bitcast_fusion), kind=kLoop, calls=%fused_computation.32 | loop fusion | flops 262144 | bytes 462848 | tf_op jit(solution)/shard_map/convert_element_type | solution.py:239
  52.7 0.5 collective-permute-start.8
  53.2 1.2 %collective-permute-start.7 = (bf16[8,4,1024]{2,1,0:T(4,128)(2,1)S(1)}, bf16[8,4,1024]{2,1,0:T(4,128)(2,1)S(1)}, u32[]{:S(2)}, u32[]{:S(2)}) collective-permute-start(bf16[8,4,1024]{2,1,0:T(4,128)(2,1)S(1)} %fusion.12), channel_id=1, source_target_pairs={{0,8},{4,12},{8,0},{12,4},{1,9},{5,13},{9,1},{13,5},{2,10},{6,14},... | collective-permute-start | bytes 196616 | tf_op jit(solution)/shard_map/ppermute | solution.py:34
  54.4 0.2 collective-permute-start.6
  54.5 0.6 collective-permute-done.8
  55.1 3.3 %collective-permute-done.7 = bf16[8,4,1024]{2,1,0:T(4,128)(2,1)S(1)} collective-permute-done((bf16[8,4,1024]{2,1,0:T(4,128)(2,1)S(1)}, bf16[8,4,1024]{2,1,0:T(4,128)(2,1)S(1)}, u32[]{:S(2)}, u32[]{:S(2)}) %collective-permute-start.7) | collective-permute-done | bytes 65568 | tf_op jit(solution)/shard_map/ppermute | solution.py:34
  58.4 0.2 collective-permute-done.6
  58.6 0.2 pad_maximum_fusion
  58.9 0.8 %gather_fusion.1 = bf16[4,8,4,1024]{3,2,1,0:T(4,128)(2,1)S(1)} fusion(bf16[4,8,4,1024]{3,2,1,0:T(4,128)(2,1)S(1)} %pad_maximum_fusion, s32[1024]{0:T(1024)S(1)} %pad_clamp_fusion), kind=kCustom, calls=%fused_computation.1 | custom fusion | bytes 524304 | tf_op jit(solution)/shard_map/jit(_take)/gather | solution.py:37
  59.7 0.3 fusion
  60.1 2.9 %collective-permute-start.11 = (f32[32,512]{1,0:T(8,128)S(1)}, f32[32,512]{1,0:T(8,128)S(1)}, u32[]{:S(2)}, u32[]{:S(2)}) collective-permute-start(f32[32,512]{1,0:T(8,128)S(1)} %get-tuple-element.27), channel_id=1, source_target_pairs={{0,3},{1,0},{2,1},{3,2},{4,7},{5,4},{6,5},{7,6},{8,11},{9,8},{10,9... | collective-permute-start | bytes 196616 | tf_op jit(solution)/shard_map/ppermute | solution.py:47
  63.0 1.1 %collective-permute-start.10 = (f32[32,512]{1,0:T(8,128)S(1)}, f32[32,512]{1,0:T(8,128)S(1)}, u32[]{:S(2)}, u32[]{:S(2)}) collective-permute-start(f32[32,512]{1,0:T(8,128)S(1)} %get-tuple-element.28), channel_id=1, source_target_pairs={{0,2},{1,3},{2,0},{3,1},{4,6},{5,7},{6,4},{7,5},{8,10},{9,11},{10,... | collective-permute-start | bytes 196616 | tf_op jit(solution)/shard_map/ppermute | solution.py:47
  64.1 0.8 %collective-permute-done.11 = f32[32,512]{1,0:T(8,128)S(1)} collective-permute-done((f32[32,512]{1,0:T(8,128)S(1)}, f32[32,512]{1,0:T(8,128)S(1)}, u32[]{:S(2)}, u32[]{:S(2)}) %collective-permute-start.11) | collective-permute-done | bytes 65568 | tf_op jit(solution)/shard_map/ppermute | solution.py:47
  64.9 3.8 %collective-permute-done.10 = f32[32,512]{1,0:T(8,128)S(1)} collective-permute-done((f32[32,512]{1,0:T(8,128)S(1)}, f32[32,512]{1,0:T(8,128)S(1)}, u32[]{:S(2)}, u32[]{:S(2)}) %collective-permute-start.10) | collective-permute-done | bytes 65568 | tf_op jit(solution)/shard_map/ppermute | solution.py:47
  68.7 1.4 %collective-permute-done.9 = f32[32,512]{1,0:T(8,128)S(1)} collective-permute-done((f32[32,512]{1,0:T(8,128)S(1)}, f32[32,512]{1,0:T(8,128)S(1)}, u32[]{:S(2)}, u32[]{:S(2)}) %collective-permute-start.9) | collective-permute-done | bytes 65568 | tf_op jit(solution)/shard_map/ppermute | solution.py:47
  70.2 0.6 reshape.547
  (71 shorter events, 2.7 us)
Async XLA Ops:
  0.6 59.1 %copy-start = (bf16[1024,512]{1,0:T(8,128)(2,1)S(1)}, bf16[1024,512]{1,0:T(8,128)(2,1)}, u32[]{:S(2)}) copy-start(bf16[1024,512]{1,0:T(8,128)(2,1)} %param.24) | copy-start | bytes 3145732
  0.6 18.3 %copy-start.1 = (bf16[4,1024]{1,0:T(4,128)(2,1)S(1)}, bf16[4,1024]{1,0:T(4,128)(2,1)}, u32[]{:S(2)}) copy-start(bf16[4,1024]{1,0:T(4,128)(2,1)} %param.19) | copy-start | bytes 24580
  0.7 22.8 %copy-start.3 = (f32[128]{0:T(128)S(1)}, f32[128]{0:T(128)}, u32[]{:S(2)}) copy-start(f32[128]{0:T(128)} %param.23) | copy-start | bytes 1540
  0.7 22.8 %copy-start.2 = (bf16[4,1024]{1,0:T(4,128)(2,1)S(1)}, bf16[4,1024]{1,0:T(4,128)(2,1)}, u32[]{:S(2)}) copy-start(bf16[4,1024]{1,0:T(4,128)(2,1)} %param.20) | copy-start | bytes 24580
  0.7 12.0 %collective-permute-start.2 = (bf16[8,4,512]{2,1,0:T(4,128)(2,1)}, bf16[8,4,512]{2,1,0:T(4,128)(2,1)S(1)}, u32[]{:S(2)}, u32[]{:S(2)}) collective-permute-start(bf16[8,4,512]{2,1,0:T(4,128)(2,1)} %param.15), channel_id=1, source_target_pairs={{0,3},{1,0},{2,1},{3,2},{4,7},{5,4},{6,5},{7,6},{8,11},{9,8},{10,9... | collective-permute-start | bytes 98312 | tf_op jit(solution)/shard_map/ppermute | solution.py:73
  5.8 6.9 %collective-permute-start.1 = (bf16[8,4,512]{2,1,0:T(4,128)(2,1)}, bf16[8,4,512]{2,1,0:T(4,128)(2,1)S(1)}, u32[]{:S(2)}, u32[]{:S(2)}) collective-permute-start(bf16[8,4,512]{2,1,0:T(4,128)(2,1)} %param.15), channel_id=1, source_target_pairs={{0,2},{1,3},{2,0},{3,1},{4,6},{5,7},{6,4},{7,5},{8,10},{9,11},{10,... | collective-permute-start | bytes 98312 | tf_op jit(solution)/shard_map/ppermute | solution.py:73
  5.8 6.9 %collective-permute-start = (bf16[8,4,512]{2,1,0:T(4,128)(2,1)}, bf16[8,4,512]{2,1,0:T(4,128)(2,1)S(1)}, u32[]{:S(2)}, u32[]{:S(2)}) collective-permute-start(bf16[8,4,512]{2,1,0:T(4,128)(2,1)} %param.15), channel_id=1, source_target_pairs={{0,1},{1,2},{2,3},{3,0},{4,5},{5,6},{6,7},{7,4},{8,9},{9,10},{10,1... | collective-permute-start | bytes 98312 | tf_op jit(solution)/shard_map/ppermute | solution.py:73
  18.9 2.0 %collective-permute-start.4 = (f32[32,3088]{1,0:T(8,128)}, f32[32,3088]{1,0:T(8,128)S(1)}, u32[]{:S(2)}, u32[]{:S(2)}) collective-permute-start(f32[32,3088]{1,0:T(8,128)} %get-tuple-element.12), channel_id=1, source_target_pairs={{0,4},{4,0},{8,12},{12,8},{1,5},{5,1},{9,13},{13,9},{2,6},{6,2},{1... | collective-permute-start | bytes 1185800 | tf_op jit(solution)/shard_map/ppermute | solution.py:202
  19.0 4.5 %collective-permute-start.3 = (f32[32,3088]{1,0:T(8,128)}, f32[32,3088]{1,0:T(8,128)S(1)}, u32[]{:S(2)}, u32[]{:S(2)}) collective-permute-start(f32[32,3088]{1,0:T(8,128)} %get-tuple-element.10), channel_id=1, source_target_pairs={{0,4},{4,0},{8,12},{12,8},{1,5},{5,1},{9,13},{13,9},{2,6},{6,2},{1... | collective-permute-start | bytes 1185800 | tf_op jit(solution)/shard_map/ppermute | solution.py:202
  21.9 11.6 %collective-permute-start.5 = (f32[32,3088]{1,0:T(8,128)S(1)}, f32[32,3088]{1,0:T(8,128)S(1)}, u32[]{:S(2)}, u32[]{:S(2)}) collective-permute-start(f32[32,3088]{1,0:T(8,128)S(1)} %add.522), channel_id=1, source_target_pairs={{0,8},{4,12},{8,0},{12,4},{1,9},{5,13},{9,1},{13,5},{2,10},{6,14},... | collective-permute-start | bytes 1185800 | tf_op jit(solution)/shard_map/ppermute | solution.py:206
  52.7 2.4 %collective-permute-start.8 = (bf16[8,4,1024]{2,1,0:T(4,128)(2,1)S(1)}, bf16[8,4,1024]{2,1,0:T(4,128)(2,1)S(1)}, u32[]{:S(2)}, u32[]{:S(2)}) collective-permute-start(bf16[8,4,1024]{2,1,0:T(4,128)(2,1)S(1)} %fusion.12), channel_id=1, source_target_pairs={{0,12},{4,0},{8,4},{12,8},{1,13},{5,1},{9,5},{13,9},{2,14},{6,2},{... | collective-permute-start | bytes 196616 | tf_op jit(solution)/shard_map/ppermute | solution.py:34
  53.2 5.3 %collective-permute-start.7 = (bf16[8,4,1024]{2,1,0:T(4,128)(2,1)S(1)}, bf16[8,4,1024]{2,1,0:T(4,128)(2,1)S(1)}, u32[]{:S(2)}, u32[]{:S(2)}) collective-permute-start(bf16[8,4,1024]{2,1,0:T(4,128)(2,1)S(1)} %fusion.12), channel_id=1, source_target_pairs={{0,8},{4,12},{8,0},{12,4},{1,9},{5,13},{9,1},{13,5},{2,10},{6,14},... | collective-permute-start | bytes 196616 | tf_op jit(solution)/shard_map/ppermute | solution.py:34
  54.4 4.3 %collective-permute-start.6 = (bf16[8,4,1024]{2,1,0:T(4,128)(2,1)S(1)}, bf16[8,4,1024]{2,1,0:T(4,128)(2,1)S(1)}, u32[]{:S(2)}, u32[]{:S(2)}) collective-permute-start(bf16[8,4,1024]{2,1,0:T(4,128)(2,1)S(1)} %fusion.12), channel_id=1, source_target_pairs={{0,4},{4,8},{8,12},{12,0},{1,5},{5,9},{9,13},{13,1},{2,6},{6,10},{... | collective-permute-start | bytes 196616 | tf_op jit(solution)/shard_map/ppermute | solution.py:34
  60.1 4.8 %collective-permute-start.11 = (f32[32,512]{1,0:T(8,128)S(1)}, f32[32,512]{1,0:T(8,128)S(1)}, u32[]{:S(2)}, u32[]{:S(2)}) collective-permute-start(f32[32,512]{1,0:T(8,128)S(1)} %get-tuple-element.27), channel_id=1, source_target_pairs={{0,3},{1,0},{2,1},{3,2},{4,7},{5,4},{6,5},{7,6},{8,11},{9,8},{10,9... | collective-permute-start | bytes 196616 | tf_op jit(solution)/shard_map/ppermute | solution.py:47
  63.0 5.7 %collective-permute-start.10 = (f32[32,512]{1,0:T(8,128)S(1)}, f32[32,512]{1,0:T(8,128)S(1)}, u32[]{:S(2)}, u32[]{:S(2)}) collective-permute-start(f32[32,512]{1,0:T(8,128)S(1)} %get-tuple-element.28), channel_id=1, source_target_pairs={{0,2},{1,3},{2,0},{3,1},{4,6},{5,7},{6,4},{7,5},{8,10},{9,11},{10,... | collective-permute-start | bytes 196616 | tf_op jit(solution)/shard_map/ppermute | solution.py:47
  64.1 6.1 %collective-permute-start.9 = (f32[32,512]{1,0:T(8,128)S(1)}, f32[32,512]{1,0:T(8,128)S(1)}, u32[]{:S(2)}, u32[]{:S(2)}) collective-permute-start(f32[32,512]{1,0:T(8,128)S(1)} %get-tuple-element.26), channel_id=1, source_target_pairs={{0,1},{1,2},{2,3},{3,0},{4,5},{5,6},{6,7},{7,4},{8,9},{9,10},{10,1... | collective-permute-start | bytes 196616 | tf_op jit(solution)/shard_map/ppermute | solution.py:47

commit v8 on v7

--- a/solution.py
+++ b/solution.py
@@ -200,13 +200,14 @@
     outs = projection(flat_rows, w_qk, w_vz, w_ba, 2 * chips)
     pair = [(i, i ^ 1) for i in range(n_dp)]
     part = [keep + lax.ppermute(send, "dp", pair) for send, keep in zip(outs[:chips], outs[chips:])]
-    summed = part[0]
+    summed_qk = part[0][:, :width_qk]
+    summed_rest = part[0][:, width_qk:]
     for s in range(1, chips):
         perm = [(i, ((i // 2 + s) % chips) * 2 + i % 2) for i in range(n_dp)]
-        summed = summed + lax.ppermute(part[s], "dp", perm)
-    summed_qk = summed[:, :width_qk]
-    summed_vz = summed[:, width_qk : width_qk + width_vz]
-    summed_ba = summed[:, width_qk + width_vz :]
+        summed_qk = summed_qk + lax.ppermute(part[s][:, :width_qk], "dp", perm)
+        summed_rest = summed_rest + lax.ppermute(part[s][:, width_qk:], "dp", perm)
+    summed_vz = summed_rest[:, :width_vz]
+    summed_ba = summed_rest[:, width_vz:]
     qk_proj = summed_qk.astype(jnp.bfloat16).reshape(rows_mem, step_count, width_qk)
     vz_proj = summed_vz.astype(jnp.bfloat16).reshape(rows_mem, step_count, width_vz)
     ba_proj = summed_ba.astype(jnp.bfloat16).reshape(rows_mem, step_count, -1)

time: 71.5 us -> 66 us (0.923)
  waiting for transfers between devices: 21.5 us -> 17 us
    ppermute x1 -> x2, waiting for transfers between devices: 9.98 us -> 4.94 us  [the longest x1 2.76 us: shards(): summed_qk = summed_qk + lax.ppermute(part[s][:, :width_qk], 'dp', perm)]
    slice x2, local copies, waits for them, and re-layouts: 0.03 us -> 1.72 us  [conv_steps(): taps[k][None, None, :]]
    unnamed x12 -> x16, local copies, waits for them, and re-layouts: 3.32 us -> 1.73 us
    another operation x1, other arithmetic: 1.08 us -> 0.03 us
    add x1 -> x2, other arithmetic: 1.06 us -> 2.1 us  [shards(): keep + lax.ppermute(send, 'dp', pair)]
    ppermute x1 -> x2, starting transfers between devices: 1.55 us -> 2.16 us  [the longest x1 1.55 us: shards(): summed_qk = summed_qk + lax.ppermute(part[s][:, :width_qk], 'dp', perm)]
  transfers between devices with their start and end apart: 12 -> 13, of which waited for: 8 -> 10; matrix products, arithmetic and copies ran while one was open for 10% -> 15% of each run, Pallas kernels for 0% -> 0%
where the time goes in v8:
time: 66 us; the launch traced here: 65.4 us
  waiting for transfers between devices  17 us (26%)
  starting transfers between devices  14 us (21%)
  Pallas kernels  13.6 us (21%)
  local copies, waits for them, and re-layouts  10.2 us (15%)
  other arithmetic  8.99 us (14%)
  between operations  1.09 us (2%)
    pallas_call x1, Pallas kernels, recurrence(): pl.pallas_call(kern, grid=(rows,), in_specs=[pl.BlockSpec(memory_space=pl...  9.9 us
    ppermute x3, starting transfers between devices, gather_pieces(): pieces.append(lax.ppermute(x, axis, [(i, (i + s) % n) for i in range(n)]))  6.11 us
    ppermute x3, waiting for transfers between devices, scatter_sum_rows(): acc = acc + lax.ppermute(send, axis, [(i, (i + s) % n) for i in range(n)])  6.06 us
    ppermute x3, waiting for transfers between devices, gather_rows(): pieces.append(lax.ppermute(x, axis, [(i, (i + s) % n) for i in range(n)]))  4.09 us
    pallas_call x1, Pallas kernels, projection(): pl.pallas_call(projection_kernel, out_shape=[jax.ShapeDtypeStruct((rows,...  3.74 us
    ppermute x3, starting transfers between devices, scatter_sum_rows(): acc = acc + lax.ppermute(send, axis, [(i, (i + s) % n) for i in range(n)])  3.49 us
    ppermute x1, waiting for transfers between devices, shards(): summed_qk = summed_qk + lax.ppermute(part[s][:, :width_qk], 'dp', perm)  2.76 us
    ppermute x1, waiting for transfers between devices, shards(): summed_rest = summed_rest + lax.ppermute(part[s][:, width_qk:], 'dp', perm)  2.17 us
  transfers between devices with their start and end apart: 13, of which 10 were waited for; matrix products, arithmetic and copies ran while one was open for 15% of the time, Pallas kernels for 0%

profile of v8, /device:TPU:0, one launch (start us, length us, event | category | flops | bytes accessed | tf_op | source)
XLA Modules:
  0.0 65.4 jit_solution(9418277802317486636)
XLA Ops:
  0.7 5.1 %collective-permute-start.2 = (bf16[8,4,512]{2,1,0:T(4,128)(2,1)}, bf16[8,4,512]{2,1,0:T(4,128)(2,1)S(1)}, u32[]{:S(2)}, u32[]{:S(2)}) collective-permute-start(bf16[8,4,512]{2,1,0:T(4,128)(2,1)} %param.15), channel_id=1, source_target_pairs={{0,3},{1,0},{2,1},{3,2},{4,7},{5,4},{6,5},{7,6},{8,11},{9,8},{10,9... | collective-permute-start | bytes 98312 | tf_op jit(solution)/shard_map/ppermute | solution.py:73
  5.8 1.0 %collective-permute-start = (bf16[8,4,512]{2,1,0:T(4,128)(2,1)}, bf16[8,4,512]{2,1,0:T(4,128)(2,1)S(1)}, u32[]{:S(2)}, u32[]{:S(2)}) collective-permute-start(bf16[8,4,512]{2,1,0:T(4,128)(2,1)} %param.15), channel_id=1, source_target_pairs={{0,1},{1,2},{2,3},{3,0},{4,5},{5,6},{6,7},{7,4},{8,9},{9,10},{10,1... | collective-permute-start | bytes 98312 | tf_op jit(solution)/shard_map/ppermute | solution.py:73
  7.9 0.9 %fusion.45 = (f32[1,1024]{1,0:T(1,128)S(1)}, f32[1,1024]{1,0:T(1,128)S(1)}, f32[1,1024]{1,0:T(1,128)S(1)}, f32[1,1024]{1,0:T(1,128)S(1)}) fusion(bf16[4,1024]{1,0:T(4,128)(2,1)} %param.19), kind=kLoop, calls=%fused_computation.135 | loop fusion | bytes 32768 | tf_op jit(solution)/shard_map/slice | solution.py:25
  8.8 0.9 %fusion.44 = (f32[1,1024]{1,0:T(1,128)S(1)}, f32[1,1024]{1,0:T(1,128)S(1)}, f32[1,1024]{1,0:T(1,128)S(1)}, f32[1,1024]{1,0:T(1,128)S(1)}) fusion(bf16[4,1024]{1,0:T(4,128)(2,1)} %param.20), kind=kLoop, calls=%fused_computation.134 | loop fusion | bytes 32768 | tf_op jit(solution)/shard_map/slice | solution.py:25
  9.7 1.5 %copy.36.wba_ref = bf16[512,16]{1,0:T(8,128)(2,1)} copy(bf16[512,16]{0,1:T(8,128)(2,1)} %param.18) | data formatting | bytes 32768 | tf_op args[3]
  11.2 0.5 collective-permute-done
  11.7 0.9 %pad_maximum_fusion.1 = bf16[4,8,4,512]{3,2,1,0:T(4,128)(2,1)S(1)} fusion(bf16[1,8,4,512]{3,2,1,0:T(4,128)(2,1)S(1)} %bitcast.78, bf16[1,8,4,512]{3,2,1,0:T(4,128)(2,1)S(1)} %bitcast.79, bf16[1,8,4,512]{3,2,1,0:T(4,128)(2,1)S(1)} %bitcast.80, bf16[1,8,4,512]{3,2,1,0:T(4,128)(2,1)} %bitcast.77), kind=kLoop, calls=%fused_computation.30 | loop fusion | flops 196608 | bytes 262144 | tf_op jit(solution)/shard_map/stack | solution.py:74
  12.6 0.8 %gather_fusion = bf16[128,512]{1,0:T(8,128)(2,1)S(1)} fusion(bf16[128,512]{1,0:T(8,128)(2,1)S(1)} %reshape.542, s32[1024]{0:T(1024)S(1)} %pad_clamp_fusion.1), kind=kCustom, calls=%fused_computation | custom fusion | bytes 262656 | tf_op jit(solution)/shard_map/jit(_take)/gather | solution.py:199
  13.5 0.7 %broadcast_select_fusion.x_ref = bf16[128,512]{1,0:T(8,128)(2,1)} fusion(bf16[128,512]{1,0:T(8,128)(2,1)S(1)} %gather_fusion, pred[128]{0:T(512)(128)(4,1)S(1)} %compare_and_fusion), kind=kLoop, calls=%fused_computation.34 | loop fusion | flops 65536 | bytes 262272 | tf_op jit(solution)/shard_map/jit(_take)/select_n | solution.py:199
  14.2 3.7 %shard_map.140 = (f32[32,3088]{1,0:T(8,128)}, f32[32,3088]{1,0:T(8,128)}, f32[32,3088]{1,0:T(8,128)}, f32[32,3088]{1,0:T(8,128)}) custom-call(bf16[128,512]{1,0:T(8,128)(2,1)} %broadcast_select_fusion.x_ref, bf16[512,1024]{1,0:T(8,128)(2,1)} %wqk_ref.1, bf16[512,2048]{1,0:T(8,128)(2,1)} %wvz_ref.1, bf16[512,16]{1,0:T(8,128)(2,1)} %copy.36.wba_ref), custom_call_target="tpu_custom_call" | custom-call | flops 404750336 | bytes 4874240 | tf_op jit(solution)/shard_map/pallas_call | solution.py:92
  18.0 0.5 collective-permute-start.3
  18.5 1.4 %collective-permute-done.4 = f32[32,3088]{1,0:T(8,128)S(1)} collective-permute-done((f32[32,3088]{1,0:T(8,128)}, f32[32,3088]{1,0:T(8,128)S(1)}, u32[]{:S(2)}, u32[]{:S(2)}) %collective-permute-start.4) | collective-permute-done | bytes 395296 | tf_op jit(solution)/shard_map/ppermute | solution.py:202
  19.9 1.1 %add.525 = f32[32,3088]{1,0:T(8,128)S(1)} add(f32[32,3088]{1,0:T(8,128)} %get-tuple-element.11, f32[32,3088]{1,0:T(8,128)S(1)} %collective-permute-done.4) | non-fusion elementwise | flops 98816 | bytes 1185792 | tf_op jit(solution)/shard_map/add | solution.py:202
  21.0 1.6 %collective-permute-start.6 = (f32[32,1024]{1,0:T(8,128)S(1)}, f32[32,1024]{1,0:T(8,128)S(1)}, u32[]{:S(2)}, u32[]{:S(2)}) collective-permute-start(f32[32,1024]{1,0:T(8,128)S(1)} %slice.133), channel_id=1, source_target_pairs={{0,8},{4,12},{8,0},{12,4},{1,9},{5,13},{9,1},{13,5},{2,10},{6,14},... | collective-permute-start | bytes 393224 | tf_op jit(solution)/shard_map/ppermute | solution.py:207
  23.0 0.6 collective-permute-start.5
  23.6 1.0 %add.524 = f32[32,3088]{1,0:T(8,128)S(1)} add(f32[32,3088]{1,0:T(8,128)} %get-tuple-element.9, f32[32,3088]{1,0:T(8,128)S(1)} %collective-permute-done.3) | non-fusion elementwise | flops 98816 | bytes 1185792 | tf_op jit(solution)/shard_map/add | solution.py:202
  24.6 2.8 %collective-permute-done.6 = f32[32,1024]{1,0:T(8,128)S(1)} collective-permute-done((f32[32,1024]{1,0:T(8,128)S(1)}, f32[32,1024]{1,0:T(8,128)S(1)}, u32[]{:S(2)}, u32[]{:S(2)}) %collective-permute-start.6) | collective-permute-done | bytes 131104 | tf_op jit(solution)/shard_map/ppermute | solution.py:207
  27.5 0.2 divide_multiply_fusion.2
  27.7 0.1 reshape.544
  28.0 0.1 multiply_reduce_fusion.1
  28.2 0.1 multiply_reduce_fusion
  28.3 1.0 %copy.46.qt_ref = f32[8,128,16]{2,1,0:T(8,128)} copy(f32[8,128,16]{1,0,2:T(8,128)S(1)} %bitcast.71) | data formatting | bytes 131072 | tf_op jit(solution)/shard_map/reshape | solution.py:225
  29.4 1.0 %copy.47.kt_ref = f32[8,128,16]{2,1,0:T(8,128)} copy(f32[8,128,16]{1,0,2:T(8,128)S(1)} %bitcast.72) | data formatting | bytes 131072 | tf_op jit(solution)/shard_map/reshape | solution.py:226
  30.4 2.2 %collective-permute-done.5 = f32[32,2064]{1,0:T(8,128)S(1)} collective-permute-done((f32[32,2064]{1,0:T(8,128)S(1)}, f32[32,2064]{1,0:T(8,128)S(1)}, u32[]{:S(2)}, u32[]{:S(2)}) %collective-permute-start.5) | collective-permute-done | bytes 264224 | tf_op jit(solution)/shard_map/ppermute | solution.py:208
  32.7 0.4 slice_reduce_fusion
  33.4 0.1 copy.40
  33.6 0.1 copy.49
  33.9 0.7 %pad_maximum_fusion.2.gates_ref = f32[8,64]{1,0:T(8,128)} fusion(f32[8,32]{1,0:T(8,128)S(1)} %fusion.20, f32[8,32]{1,0:T(8,128)S(1)} %div.86), kind=kLoop, calls=%fused_computation.60 | loop fusion | flops 512 | bytes 4096 | tf_op jit(solution)/shard_map/concatenate | solution.py:231
  34.7 0.8 %divide_multiply_fusion.1.v_ref = f32[8,4,1024]{2,1,0:T(4,128)} fusion(f32[8,7,1024]{2,1,0:T(8,128)S(1)} %maximum_convert_fusion.1, f32[1024]{0:T(1024)S(1)} %bitcast.84, f32[1024]{0:T(1024)S(1)} %bitcast.83, f32[1024]{0:T(1024)S(1)} %bitcast.82, f32[1024]{0:T(1024)S(1)} %bitcast.81), kind=kLoop, calls=%fused_computation.10 | loop fusion | flops 360448 | bytes 671744 | tf_op jit(solution)/shard_map/jit(silu)/mul | solution.py:26
  35.5 9.9 %shard_map.141 = (f32[8,8,128,128]{3,2,1,0:T(8,128)}, f32[8,4,1024]{2,1,0:T(4,128)}) custom-call(f32[8,64]{1,0:T(8,128)} %pad_maximum_fusion.2.gates_ref, f32[8,128,16]{2,1,0:T(8,128)} %copy.46.qt_ref, f32[8,128,16]{2,1,0:T(8,128)} %copy.47.kt_ref, f32[8,4,1024]{2,1,0:T(4,128)} %divide_multiply_fusion.1.v_ref, f32[8,8,128,128]{3,2,1,0:T(8,128)} %s_ref.1), custom_call_target="tpu_custom_call" | custom-call | flops 33554432 | bytes 8388608 | tf_op jit(solution)/shard_map/pallas_call | solution.py:133
  45.4 1.0 %mul.299 = f32[8,4,1024]{2,1,0:T(4,128)S(1)} multiply(f32[8,4,1024]{2,1,0:T(4,128)} %get-tuple-element.13, f32[8,4,1024]{2,1,0:T(4,128)} %get-tuple-element.13) | non-fusion elementwise | flops 32768 | bytes 393216 | tf_op jit(solution)/shard_map/mul | solution.py:238
  46.5 0.1 reduce_sum.29
  46.8 1.0 %fusion.14 = bf16[8,4,1024]{2,1,0:T(4,128)(2,1)S(1)} fusion(f32[8,4,1024]{2,1,0:T(4,128)S(1)} %reshape.608, f32[8,4,1024]{2,1,0:T(4,128)} %get-tuple-element.13, f32[8,4,1024]{2,1,0:T(4,128)S(1)} %mul.302, f32[1024]{0:T(1024)S(1)} %broadcast_bitcast_fusion), kind=kLoop, calls=%fused_computation.35 | loop fusion | flops 262144 | bytes 462848 | tf_op jit(solution)/shard_map/convert_element_type | solution.py:240
  47.8 0.5 collective-permute-start.9
  48.2 1.2 %collective-permute-start.8 = (bf16[8,4,1024]{2,1,0:T(4,128)(2,1)S(1)}, bf16[8,4,1024]{2,1,0:T(4,128)(2,1)S(1)}, u32[]{:S(2)}, u32[]{:S(2)}) collective-permute-start(bf16[8,4,1024]{2,1,0:T(4,128)(2,1)S(1)} %fusion.14), channel_id=1, source_target_pairs={{0,8},{4,12},{8,0},{12,4},{1,9},{5,13},{9,1},{13,5},{2,10},{6,14},... | collective-permute-start | bytes 196616 | tf_op jit(solution)/shard_map/ppermute | solution.py:34
  49.4 0.2 collective-permute-start.7
  49.6 0.6 collective-permute-done.9
  50.1 3.3 %collective-permute-done.8 = bf16[8,4,1024]{2,1,0:T(4,128)(2,1)S(1)} collective-permute-done((bf16[8,4,1024]{2,1,0:T(4,128)(2,1)S(1)}, bf16[8,4,1024]{2,1,0:T(4,128)(2,1)S(1)}, u32[]{:S(2)}, u32[]{:S(2)}) %collective-permute-start.8) | collective-permute-done | bytes 65568 | tf_op jit(solution)/shard_map/ppermute | solution.py:34
  53.5 0.2 collective-permute-done.7
  53.7 0.2 pad_maximum_fusion
  53.9 0.8 %gather_fusion.1 = bf16[4,8,4,1024]{3,2,1,0:T(4,128)(2,1)S(1)} fusion(bf16[4,8,4,1024]{3,2,1,0:T(4,128)(2,1)S(1)} %pad_maximum_fusion, s32[1024]{0:T(1024)S(1)} %pad_clamp_fusion), kind=kCustom, calls=%fused_computation.1 | custom fusion | bytes 524304 | tf_op jit(solution)/shard_map/jit(_take)/gather | solution.py:37
  54.8 0.3 fusion
  55.1 2.4 %collective-permute-start.12 = (f32[32,512]{1,0:T(8,128)S(1)}, f32[32,512]{1,0:T(8,128)S(1)}, u32[]{:S(2)}, u32[]{:S(2)}) collective-permute-start(f32[32,512]{1,0:T(8,128)S(1)} %get-tuple-element.27), channel_id=1, source_target_pairs={{0,3},{1,0},{2,1},{3,2},{4,7},{5,4},{6,5},{7,6},{8,11},{9,8},{10,9... | collective-permute-start | bytes 196616 | tf_op jit(solution)/shard_map/ppermute | solution.py:47
  57.5 1.1 %collective-permute-start.11 = (f32[32,512]{1,0:T(8,128)S(1)}, f32[32,512]{1,0:T(8,128)S(1)}, u32[]{:S(2)}, u32[]{:S(2)}) collective-permute-start(f32[32,512]{1,0:T(8,128)S(1)} %get-tuple-element.28), channel_id=1, source_target_pairs={{0,2},{1,3},{2,0},{3,1},{4,6},{5,7},{6,4},{7,5},{8,10},{9,11},{10,... | collective-permute-start | bytes 196616 | tf_op jit(solution)/shard_map/ppermute | solution.py:47
  58.6 0.8 %collective-permute-done.12 = f32[32,512]{1,0:T(8,128)S(1)} collective-permute-done((f32[32,512]{1,0:T(8,128)S(1)}, f32[32,512]{1,0:T(8,128)S(1)}, u32[]{:S(2)}, u32[]{:S(2)}) %collective-permute-start.12) | collective-permute-done | bytes 65568 | tf_op jit(solution)/shard_map/ppermute | solution.py:47
  59.5 3.8 %collective-permute-done.11 = f32[32,512]{1,0:T(8,128)S(1)} collective-permute-done((f32[32,512]{1,0:T(8,128)S(1)}, f32[32,512]{1,0:T(8,128)S(1)}, u32[]{:S(2)}, u32[]{:S(2)}) %collective-permute-start.11) | collective-permute-done | bytes 65568 | tf_op jit(solution)/shard_map/ppermute | solution.py:47
  63.3 1.4 %collective-permute-done.10 = f32[32,512]{1,0:T(8,128)S(1)} collective-permute-done((f32[32,512]{1,0:T(8,128)S(1)}, f32[32,512]{1,0:T(8,128)S(1)}, u32[]{:S(2)}, u32[]{:S(2)}) %collective-permute-start.10) | collective-permute-done | bytes 65568 | tf_op jit(solution)/shard_map/ppermute | solution.py:47
  64.7 0.6 reshape.547
  (80 shorter events, 2.9 us)
Async XLA Ops:
  0.6 54.1 %copy-start = (bf16[1024,512]{1,0:T(8,128)(2,1)S(1)}, bf16[1024,512]{1,0:T(8,128)(2,1)}, u32[]{:S(2)}) copy-start(bf16[1024,512]{1,0:T(8,128)(2,1)} %param.24) | copy-start | bytes 3145732
  0.6 17.3 %copy-start.3 = (f32[128]{0:T(128)S(1)}, f32[128]{0:T(128)}, u32[]{:S(2)}) copy-start(f32[128]{0:T(128)} %param.23) | copy-start | bytes 1540
  0.7 17.8 %copy-start.5 = (f32[8]{0:T(128)S(1)}, f32[8]{0:T(128)}, u32[]{:S(2)}) copy-start(f32[8]{0:T(128)} %param.21) | copy-start | bytes 100
  0.7 22.0 %copy-start.4 = (f32[8]{0:T(128)S(1)}, f32[8]{0:T(128)}, u32[]{:S(2)}) copy-start(f32[8]{0:T(128)} %param.22) | copy-start | bytes 100
  0.7 22.1 %copy-start.1 = (bf16[8,3,1024]{2,0,1:T(8,128)(2,1)S(1)}, bf16[8,3,1024]{2,0,1:T(8,128)(2,1)}, u32[]{:S(2)}) copy-start(bf16[8,3,1024]{2,0,1:T(8,128)(2,1)} %param.25) | copy-start | bytes 147460
  0.7 22.2 %copy-start.2 = (bf16[8,3,1024]{2,0,1:T(8,128)(2,1)S(1)}, bf16[8,3,1024]{2,0,1:T(8,128)(2,1)}, u32[]{:S(2)}) copy-start(bf16[8,3,1024]{2,0,1:T(8,128)(2,1)} %param.26) | copy-start | bytes 147460
  0.7 10.5 %collective-permute-start.2 = (bf16[8,4,512]{2,1,0:T(4,128)(2,1)}, bf16[8,4,512]{2,1,0:T(4,128)(2,1)S(1)}, u32[]{:S(2)}, u32[]{:S(2)}) collective-permute-start(bf16[8,4,512]{2,1,0:T(4,128)(2,1)} %param.15), channel_id=1, source_target_pairs={{0,3},{1,0},{2,1},{3,2},{4,7},{5,4},{6,5},{7,6},{8,11},{9,8},{10,9... | collective-permute-start | bytes 98312 | tf_op jit(solution)/shard_map/ppermute | solution.py:73
  5.8 5.4 %collective-permute-start.1 = (bf16[8,4,512]{2,1,0:T(4,128)(2,1)}, bf16[8,4,512]{2,1,0:T(4,128)(2,1)S(1)}, u32[]{:S(2)}, u32[]{:S(2)}) collective-permute-start(bf16[8,4,512]{2,1,0:T(4,128)(2,1)} %param.15), channel_id=1, source_target_pairs={{0,2},{1,3},{2,0},{3,1},{4,6},{5,7},{6,4},{7,5},{8,10},{9,11},{10,... | collective-permute-start | bytes 98312 | tf_op jit(solution)/shard_map/ppermute | solution.py:73
  5.8 5.9 %collective-permute-start = (bf16[8,4,512]{2,1,0:T(4,128)(2,1)}, bf16[8,4,512]{2,1,0:T(4,128)(2,1)S(1)}, u32[]{:S(2)}, u32[]{:S(2)}) collective-permute-start(bf16[8,4,512]{2,1,0:T(4,128)(2,1)} %param.15), channel_id=1, source_target_pairs={{0,1},{1,2},{2,3},{3,0},{4,5},{5,6},{6,7},{7,4},{8,9},{9,10},{10,1... | collective-permute-start | bytes 98312 | tf_op jit(solution)/shard_map/ppermute | solution.py:73
  18.0 2.0 %collective-permute-start.4 = (f32[32,3088]{1,0:T(8,128)}, f32[32,3088]{1,0:T(8,128)S(1)}, u32[]{:S(2)}, u32[]{:S(2)}) collective-permute-start(f32[32,3088]{1,0:T(8,128)} %get-tuple-element.12), channel_id=1, source_target_pairs={{0,4},{4,0},{8,12},{12,8},{1,5},{5,1},{9,13},{13,9},{2,6},{6,2},{1... | collective-permute-start | bytes 1185800 | tf_op jit(solution)/shard_map/ppermute | solution.py:202
  18.0 5.6 %collective-permute-start.3 = (f32[32,3088]{1,0:T(8,128)}, f32[32,3088]{1,0:T(8,128)S(1)}, u32[]{:S(2)}, u32[]{:S(2)}) collective-permute-start(f32[32,3088]{1,0:T(8,128)} %get-tuple-element.10), channel_id=1, source_target_pairs={{0,4},{4,0},{8,12},{12,8},{1,5},{5,1},{9,13},{13,9},{2,6},{6,2},{1... | collective-permute-start | bytes 1185800 | tf_op jit(solution)/shard_map/ppermute | solution.py:202
  21.0 6.4 %collective-permute-start.6 = (f32[32,1024]{1,0:T(8,128)S(1)}, f32[32,1024]{1,0:T(8,128)S(1)}, u32[]{:S(2)}, u32[]{:S(2)}) collective-permute-start(f32[32,1024]{1,0:T(8,128)S(1)} %slice.133), channel_id=1, source_target_pairs={{0,8},{4,12},{8,0},{12,4},{1,9},{5,13},{9,1},{13,5},{2,10},{6,14},... | collective-permute-start | bytes 393224 | tf_op jit(solution)/shard_map/ppermute | solution.py:207
  23.0 9.6 %collective-permute-start.5 = (f32[32,2064]{1,0:T(8,128)S(1)}, f32[32,2064]{1,0:T(8,128)S(1)}, u32[]{:S(2)}, u32[]{:S(2)}) collective-permute-start(f32[32,2064]{1,0:T(8,128)S(1)} %slice.128), channel_id=1, source_target_pairs={{0,8},{4,12},{8,0},{12,4},{1,9},{5,13},{9,1},{13,5},{2,10},{6,14},... | collective-permute-start | bytes 792584 | tf_op jit(solution)/shard_map/ppermute | solution.py:208
  47.8 2.4 %collective-permute-start.9 = (bf16[8,4,1024]{2,1,0:T(4,128)(2,1)S(1)}, bf16[8,4,1024]{2,1,0:T(4,128)(2,1)S(1)}, u32[]{:S(2)}, u32[]{:S(2)}) collective-permute-start(bf16[8,4,1024]{2,1,0:T(4,128)(2,1)S(1)} %fusion.14), channel_id=1, source_target_pairs={{0,12},{4,0},{8,4},{12,8},{1,13},{5,1},{9,5},{13,9},{2,14},{6,2},{... | collective-permute-start | bytes 196616 | tf_op jit(solution)/shard_map/ppermute | solution.py:34
  48.2 5.3 %collective-permute-start.8 = (bf16[8,4,1024]{2,1,0:T(4,128)(2,1)S(1)}, bf16[8,4,1024]{2,1,0:T(4,128)(2,1)S(1)}, u32[]{:S(2)}, u32[]{:S(2)}) collective-permute-start(bf16[8,4,1024]{2,1,0:T(4,128)(2,1)S(1)} %fusion.14), channel_id=1, source_target_pairs={{0,8},{4,12},{8,0},{12,4},{1,9},{5,13},{9,1},{13,5},{2,10},{6,14},... | collective-permute-start | bytes 196616 | tf_op jit(solution)/shard_map/ppermute | solution.py:34
  49.4 4.3 %collective-permute-start.7 = (bf16[8,4,1024]{2,1,0:T(4,128)(2,1)S(1)}, bf16[8,4,1024]{2,1,0:T(4,128)(2,1)S(1)}, u32[]{:S(2)}, u32[]{:S(2)}) collective-permute-start(bf16[8,4,1024]{2,1,0:T(4,128)(2,1)S(1)} %fusion.14), channel_id=1, source_target_pairs={{0,4},{4,8},{8,12},{12,0},{1,5},{5,9},{9,13},{13,1},{2,6},{6,10},{... | collective-permute-start | bytes 196616 | tf_op jit(solution)/shard_map/ppermute | solution.py:34
  55.1 4.3 %collective-permute-start.12 = (f32[32,512]{1,0:T(8,128)S(1)}, f32[32,512]{1,0:T(8,128)S(1)}, u32[]{:S(2)}, u32[]{:S(2)}) collective-permute-start(f32[32,512]{1,0:T(8,128)S(1)} %get-tuple-element.27), channel_id=1, source_target_pairs={{0,3},{1,0},{2,1},{3,2},{4,7},{5,4},{6,5},{7,6},{8,11},{9,8},{10,9... | collective-permute-start | bytes 196616 | tf_op jit(solution)/shard_map/ppermute | solution.py:47
  57.5 5.7 %collective-permute-start.11 = (f32[32,512]{1,0:T(8,128)S(1)}, f32[32,512]{1,0:T(8,128)S(1)}, u32[]{:S(2)}, u32[]{:S(2)}) collective-permute-start(f32[32,512]{1,0:T(8,128)S(1)} %get-tuple-element.28), channel_id=1, source_target_pairs={{0,2},{1,3},{2,0},{3,1},{4,6},{5,7},{6,4},{7,5},{8,10},{9,11},{10,... | collective-permute-start | bytes 196616 | tf_op jit(solution)/shard_map/ppermute | solution.py:47
  58.6 6.1 %collective-permute-start.10 = (f32[32,512]{1,0:T(8,128)S(1)}, f32[32,512]{1,0:T(8,128)S(1)}, u32[]{:S(2)}, u32[]{:S(2)}) collective-permute-start(f32[32,512]{1,0:T(8,128)S(1)} %get-tuple-element.26), channel_id=1, source_target_pairs={{0,1},{1,2},{2,3},{3,0},{4,5},{5,6},{6,7},{7,4},{8,9},{9,10},{10,1... | collective-permute-start | bytes 196616 | tf_op jit(solution)/shard_map/ppermute | solution.py:47

commit v9 on v8

--- a/solution.py
+++ b/solution.py
@@ -34,7 +34,7 @@
         pieces.append(lax.ppermute(x, axis, [(i, (i + s) % n) for i in range(n)]))
     stacked = jnp.stack(pieces)
     order = (me - jnp.arange(n)) % n
-    return jnp.take(stacked, order, axis=0).reshape(n * x.shape[0], *x.shape[1:])
+    return jnp.take(stacked, order, axis=0, mode="clip").reshape(n * x.shape[0], *x.shape[1:])
 
 
 def scatter_sum_rows(x, axis):
@@ -74,13 +74,16 @@
     return jnp.stack(pieces)
 
 
-def projection_kernel(x_ref, wqk_ref, wvz_ref, wba_ref, *outs):
+def projection_kernel(x_ref, wqk_ref, wvz_ref, wba_t_ref, *outs):
     x = x_ref[...]
     section = outs[0].shape[0]
     offset = 0
-    for w_ref in (wqk_ref, wvz_ref, wba_ref):
-        width = w_ref.shape[1]
-        y = jnp.dot(x, w_ref[...], preferred_element_type=jnp.float32)
+    for w_ref, transposed in ((wqk_ref, False), (wvz_ref, False), (wba_t_ref, True)):
+        width = w_ref.shape[0 if transposed else 1]
+        contract = 1 if transposed else 0
+        y = lax.dot_general(
+            x, w_ref[...], (((1,), (contract,)), ((), ())), preferred_element_type=jnp.float32
+        )
         for i, o_ref in enumerate(outs):
             o_ref[:, offset : offset + width] = y[i * section : (i + 1) * section]
         offset += width
@@ -97,7 +100,7 @@
             bytes_accessed=2 * x.shape[1] * cols + 2 * x.size + 4 * x.shape[0] * cols,
             transcendentals=0,
         ),
-    )(x, w_qk, w_vz, w_ba)
+    )(x, w_qk, w_vz, w_ba.T)
 
 
 def recurrence_kernel(gates_ref, qt_ref, kt_ref, v_ref, s_ref, s_out, o_ref, *, heads, steps, ratio):
@@ -180,23 +183,25 @@
 
     pieces = gather_pieces(activations, "head")
     n_head, rows_head = pieces.shape[0], pieces.shape[1]
-    flat_pieces = pieces.reshape(-1, pieces.shape[-1])
     me_head = lax.axis_index("head")
     n_dp = lax.axis_size("dp")
     chips = n_dp // 2
     me_dp = lax.axis_index("dp")
     core, chip = me_dp % 2, me_dp // 2
-    local_rows = jnp.arange(rows_mem)
-    steps = jnp.arange(step_count)
-    index_blocks = []
+    assert rows_head % rows_mem == 0
+    sections = []
     for which in (1 - core, core):
         for s in range(chips):
             block = ((chip + s) % chips) * 2 + which
-            rows = block * rows_mem + local_rows
-            source = (me_head - rows // rows_head) % n_head
-            flat = (source * rows_head + rows % rows_head)[:, None] * step_count + steps[None, :]
-            index_blocks.append(flat.reshape(-1))
-    flat_rows = jnp.take(flat_pieces, jnp.concatenate(index_blocks), axis=0)
+            first = block * rows_mem
+            source = (me_head - first // rows_head) % n_head
+            offset = first % rows_head
+            picked = pieces[0]
+            for shift in range(1, n_head):
+                picked = jnp.where(source == shift, pieces[shift], picked)
+            picked = lax.dynamic_slice_in_dim(picked, offset, rows_mem, axis=0)
+            sections.append(picked.reshape(rows_mem * step_count, -1))
+    flat_rows = jnp.concatenate(sections, axis=0)
     outs = projection(flat_rows, w_qk, w_vz, w_ba, 2 * chips)
     pair = [(i, i ^ 1) for i in range(n_dp)]
     part = [keep + lax.ppermute(send, "dp", pair) for send, keep in zip(outs[:chips], outs[chips:])]

time: 66 us -> 62.9 us (0.953)
  local copies, waits for them, and re-layouts: 10.2 us -> 6.41 us
  waiting for transfers between devices: 17 us -> 18.7 us
  other arithmetic: 8.99 us -> 8.23 us
    ppermute x3, waiting for transfers between devices: 0.53 us -> 3.81 us  [gather_pieces(): pieces.append(lax.ppermute(x, axis, [(i, (i + s) % n) for i in range(n)]))]
    ppermute x3, waiting for transfers between devices: 6.06 us -> 4.36 us  [scatter_sum_rows(): acc = acc + lax.ppermute(send, axis, [(i, (i + s) % n) for i in range(n)])]
    unnamed x16 -> x17, local copies, waits for them, and re-layouts: 1.73 us -> 0.25 us
    gather x3 -> x1, local copies, waits for them, and re-layouts: 1.69 us -> 0.77 us  [gather_rows(): jnp.take(stacked, order, axis=0, mode='clip')]
    another operation x2 -> x1, other arithmetic: 0.9 us -> 0.03 us  [the longest x1 0.87 us: gather_pieces(): return jnp.stack(pieces)]
    slice x2, local copies, waits for them, and re-layouts: 1.72 us -> 0.87 us  [conv_steps(): taps[k][None, None, :]]
  transfers between devices with their start and end apart: 13 -> 13, of which waited for: 10 -> 10; matrix products, arithmetic and copies ran while one was open for 15% -> 10% of each run, Pallas kernels for 0% -> 0%
where the time goes in v9:
time: 62.9 us; the launch traced here: 62.4 us
  waiting for transfers between devices  18.7 us (30%)
  starting transfers between devices  13.8 us (22%)
  Pallas kernels  13.6 us (22%)
  other arithmetic  8.23 us (13%)
  local copies, waits for them, and re-layouts  6.41 us (10%)
  between operations  1.28 us (2%)
    pallas_call x1, Pallas kernels, recurrence(): pl.pallas_call(kern, grid=(rows,), in_specs=[pl.BlockSpec(memory_space=pl...  9.9 us
    ppermute x3, starting transfers between devices, gather_pieces(): pieces.append(lax.ppermute(x, axis, [(i, (i + s) % n) for i in range(n)]))  6.11 us
    ppermute x3, waiting for transfers between devices, scatter_sum_rows(): acc = acc + lax.ppermute(send, axis, [(i, (i + s) % n) for i in range(n)])  4.36 us
    ppermute x3, waiting for transfers between devices, gather_rows(): pieces.append(lax.ppermute(x, axis, [(i, (i + s) % n) for i in range(n)]))  4.1 us
    ppermute x3, waiting for transfers between devices, gather_pieces(): pieces.append(lax.ppermute(x, axis, [(i, (i + s) % n) for i in range(n)]))  3.81 us
    pallas_call x1, Pallas kernels, projection(): pl.pallas_call(projection_kernel, out_shape=[jax.ShapeDtypeStruct((rows,...  3.73 us
    ppermute x3, starting transfers between devices, scatter_sum_rows(): acc = acc + lax.ppermute(send, axis, [(i, (i + s) % n) for i in range(n)])  3.21 us
    ppermute x1, waiting for transfers between devices, shards(): summed_qk = summed_qk + lax.ppermute(part[s][:, :width_qk], 'dp', perm)  2.83 us
  transfers between devices with their start and end apart: 13, of which 10 were waited for; matrix products, arithmetic and copies ran while one was open for 10% of the time, Pallas kernels for 0%

profile of v9, /device:TPU:0, one launch (start us, length us, event | category | flops | bytes accessed | tf_op | source)
XLA Modules:
  0.0 62.4 jit_solution(13774792675674894349)
XLA Ops:
  0.7 5.1 %collective-permute-start = (bf16[8,4,512]{2,1,0:T(4,128)(2,1)}, bf16[8,4,512]{2,1,0:T(4,128)(2,1)S(1)}, u32[]{:S(2)}, u32[]{:S(2)}) collective-permute-start(bf16[8,4,512]{2,1,0:T(4,128)(2,1)} %param.15), channel_id=1, source_target_pairs={{0,3},{1,0},{2,1},{3,2},{4,7},{5,4},{6,5},{7,6},{8,11},{9,8},{10,9... | collective-permute-start | bytes 98312 | tf_op jit(solution)/shard_map/ppermute | solution.py:73
  5.8 1.0 %collective-permute-start.2 = (bf16[8,4,512]{2,1,0:T(4,128)(2,1)}, bf16[8,4,512]{2,1,0:T(4,128)(2,1)S(1)}, u32[]{:S(2)}, u32[]{:S(2)}) collective-permute-start(bf16[8,4,512]{2,1,0:T(4,128)(2,1)} %param.15), channel_id=1, source_target_pairs={{0,1},{1,2},{2,3},{3,0},{4,5},{5,6},{6,7},{7,4},{8,9},{9,10},{10,1... | collective-permute-start | bytes 98312 | tf_op jit(solution)/shard_map/ppermute | solution.py:73
  6.8 0.9 %fusion.23 = (f32[1,1024]{1,0:T(1,128)S(1)}, f32[1,1024]{1,0:T(1,128)S(1)}, f32[1,1024]{1,0:T(1,128)S(1)}, f32[1,1024]{1,0:T(1,128)S(1)}) fusion(bf16[4,1024]{1,0:T(4,128)(2,1)} %param.19), kind=kLoop, calls=%fused_computation.69 | loop fusion | bytes 32768 | tf_op jit(solution)/shard_map/slice | solution.py:25
  7.9 2.9 %collective-permute-done.1 = bf16[8,4,512]{2,1,0:T(4,128)(2,1)S(1)} collective-permute-done((bf16[8,4,512]{2,1,0:T(4,128)(2,1)}, bf16[8,4,512]{2,1,0:T(4,128)(2,1)S(1)}, u32[]{:S(2)}, u32[]{:S(2)}) %collective-permute-start.1) | collective-permute-done | bytes 32800 | tf_op jit(solution)/shard_map/ppermute | solution.py:73
  10.8 0.9 %collective-permute-done.2 = bf16[8,4,512]{2,1,0:T(4,128)(2,1)S(1)} collective-permute-done((bf16[8,4,512]{2,1,0:T(4,128)(2,1)}, bf16[8,4,512]{2,1,0:T(4,128)(2,1)S(1)}, u32[]{:S(2)}, u32[]{:S(2)}) %collective-permute-start.2) | collective-permute-done | bytes 32800 | tf_op jit(solution)/shard_map/ppermute | solution.py:73
  11.7 0.8 %select_select_fusion.3 = (bf16[4,8,512]{2,1,0:T(8,128)(2,1)S(1)}, bf16[4,8,512]{2,1,0:T(8,128)(2,1)S(1)}, bf16[4,8,512]{2,1,0:T(8,128)(2,1)S(1)}, bf16[4,8,512]{2,1,0:T(8,128)(2,1)S(1)}) fusion(bf16[4,8,512]{2,1,0:T(8,128)(2,1)S(1)} %bitcast.86, bf16[4,8,512]{2,1,0:T(8,128)(2,1)S(1)} %bitcast.87, bf16[4,8,512]{2,1,0:T(8,128)(2,1)S(1)} %bitcast.88, ...), kind=kLoop, calls=%fused_computation.48 | loop fusion | flops 196608 | bytes 262156 | tf_op jit(solution)/shard_map/jit(_where)/select_n | solution.py:201
  12.6 0.6 %pad_maximum_fusion.1.x_ref = bf16[128,512]{1,0:T(8,128)(2,1)} fusion(bf16[32,512]{1,0:T(8,128)(2,1)S(1)} %reshape.132, bf16[32,512]{1,0:T(8,128)(2,1)S(1)} %reshape.131, bf16[32,512]{1,0:T(8,128)(2,1)S(1)} %reshape.130, bf16[32,512]{1,0:T(8,128)(2,1)S(1)} %reshape.129), kind=kLoop, calls=%fused_computation.27 | loop fusion | flops 524288 | bytes 262144 | tf_op jit(solution)/shard_map/concatenate | solution.py:204
  13.3 3.7 %shard_map.140 = (f32[32,3088]{1,0:T(8,128)}, f32[32,3088]{1,0:T(8,128)}, f32[32,3088]{1,0:T(8,128)}, f32[32,3088]{1,0:T(8,128)}) custom-call(bf16[128,512]{1,0:T(8,128)(2,1)} %pad_maximum_fusion.1.x_ref, bf16[512,1024]{1,0:T(8,128)(2,1)} %wqk_ref.1, bf16[512,2048]{1,0:T(8,128)(2,1)} %wvz_ref.1, bf16[16,512]{1,0:T(8,128)(2,1)} %bitcast.89), custom_call_target="tpu_custom_call" | custom-call | flops 404750336 | bytes 4874240 | tf_op jit(solution)/shard_map/pallas_call | solution.py:95
  17.0 0.6 collective-permute-start.3
  17.6 1.4 %collective-permute-done.4 = f32[32,3088]{1,0:T(8,128)S(1)} collective-permute-done((f32[32,3088]{1,0:T(8,128)}, f32[32,3088]{1,0:T(8,128)S(1)}, u32[]{:S(2)}, u32[]{:S(2)}) %collective-permute-start.4) | collective-permute-done | bytes 395296 | tf_op jit(solution)/shard_map/ppermute | solution.py:207
  18.9 1.1 %add.201 = f32[32,3088]{1,0:T(8,128)S(1)} add(f32[32,3088]{1,0:T(8,128)} %get-tuple-element.11, f32[32,3088]{1,0:T(8,128)S(1)} %collective-permute-done.4) | non-fusion elementwise | flops 98816 | bytes 1185792 | tf_op jit(solution)/shard_map/add | solution.py:207
  20.0 1.6 %collective-permute-start.6 = (f32[32,1024]{1,0:T(8,128)S(1)}, f32[32,1024]{1,0:T(8,128)S(1)}, u32[]{:S(2)}, u32[]{:S(2)}) collective-permute-start(f32[32,1024]{1,0:T(8,128)S(1)} %slice.131), channel_id=1, source_target_pairs={{0,8},{4,12},{8,0},{12,4},{1,9},{5,13},{9,1},{13,5},{2,10},{6,14},... | collective-permute-start | bytes 393224 | tf_op jit(solution)/shard_map/ppermute | solution.py:212
  21.9 0.6 collective-permute-start.5
  22.5 1.0 %add.200 = f32[32,3088]{1,0:T(8,128)S(1)} add(f32[32,3088]{1,0:T(8,128)} %get-tuple-element.9, f32[32,3088]{1,0:T(8,128)S(1)} %collective-permute-done.3) | non-fusion elementwise | flops 98816 | bytes 1185792 | tf_op jit(solution)/shard_map/add | solution.py:207
  23.6 2.8 %collective-permute-done.6 = f32[32,1024]{1,0:T(8,128)S(1)} collective-permute-done((f32[32,1024]{1,0:T(8,128)S(1)}, f32[32,1024]{1,0:T(8,128)S(1)}, u32[]{:S(2)}, u32[]{:S(2)}) %collective-permute-start.6) | collective-permute-done | bytes 131104 | tf_op jit(solution)/shard_map/ppermute | solution.py:212
  26.6 0.2 divide_multiply_fusion.2
  26.7 0.1 reshape.134
  26.9 0.1 fusion.20
  27.0 0.1 multiply_reduce_fusion.1
  27.1 0.1 multiply_reduce_fusion
  27.2 1.0 %copy.43.qt_ref = f32[8,128,16]{2,1,0:T(8,128)} copy(f32[8,128,16]{1,0,2:T(8,128)S(1)} %bitcast.75) | data formatting | bytes 131072 | tf_op jit(solution)/shard_map/reshape | solution.py:230
  28.3 1.0 %copy.44.kt_ref = f32[8,128,16]{2,1,0:T(8,128)} copy(f32[8,128,16]{1,0,2:T(8,128)S(1)} %bitcast.76) | data formatting | bytes 131072 | tf_op jit(solution)/shard_map/reshape | solution.py:231
  29.4 2.2 %collective-permute-done.5 = f32[32,2064]{1,0:T(8,128)S(1)} collective-permute-done((f32[32,2064]{1,0:T(8,128)S(1)}, f32[32,2064]{1,0:T(8,128)S(1)}, u32[]{:S(2)}, u32[]{:S(2)}) %collective-permute-start.5) | collective-permute-done | bytes 264224 | tf_op jit(solution)/shard_map/ppermute | solution.py:213
  31.7 0.4 slice_reduce_fusion
  32.4 0.1 copy.37
  32.6 0.1 copy.46
  32.9 0.7 %pad_maximum_fusion.2.gates_ref = f32[8,64]{1,0:T(8,128)} fusion(f32[8,32]{1,0:T(8,128)S(1)} %fusion.17, f32[8,32]{1,0:T(8,128)S(1)} %div.77), kind=kLoop, calls=%fused_computation.58 | loop fusion | flops 512 | bytes 4096 | tf_op jit(solution)/shard_map/concatenate | solution.py:236
  33.7 0.8 %divide_multiply_fusion.1.v_ref = f32[8,4,1024]{2,1,0:T(4,128)} fusion(f32[8,7,1024]{2,1,0:T(8,128)S(1)} %maximum_convert_fusion.1, f32[1024]{0:T(1024)S(1)} %bitcast.97, f32[1024]{0:T(1024)S(1)} %bitcast.96, f32[1024]{0:T(1024)S(1)} %bitcast.95, f32[1024]{0:T(1024)S(1)} %bitcast.94), kind=kLoop, calls=%fused_computation.7 | loop fusion | flops 360448 | bytes 671744 | tf_op jit(solution)/shard_map/jit(silu)/mul | solution.py:26
  34.5 9.9 %shard_map.141 = (f32[8,8,128,128]{3,2,1,0:T(8,128)}, f32[8,4,1024]{2,1,0:T(4,128)}) custom-call(f32[8,64]{1,0:T(8,128)} %pad_maximum_fusion.2.gates_ref, f32[8,128,16]{2,1,0:T(8,128)} %copy.43.qt_ref, f32[8,128,16]{2,1,0:T(8,128)} %copy.44.kt_ref, f32[8,4,1024]{2,1,0:T(4,128)} %divide_multiply_fusion.1.v_ref, f32[8,8,128,128]{3,2,1,0:T(8,128)} %s_ref.1), custom_call_target="tpu_custom_call" | custom-call | flops 33554432 | bytes 8388608 | tf_op jit(solution)/shard_map/pallas_call | solution.py:136
  44.4 1.0 %mul.231 = f32[8,4,1024]{2,1,0:T(4,128)S(1)} multiply(f32[8,4,1024]{2,1,0:T(4,128)} %get-tuple-element.13, f32[8,4,1024]{2,1,0:T(4,128)} %get-tuple-element.13) | non-fusion elementwise | flops 32768 | bytes 393216 | tf_op jit(solution)/shard_map/mul | solution.py:243
  45.5 0.1 reduce_sum.29
  45.7 0.1 mul.233
  45.8 1.0 %fusion.11 = bf16[8,4,1024]{2,1,0:T(4,128)(2,1)S(1)} fusion(f32[8,4,1024]{2,1,0:T(4,128)S(1)} %reshape.198, f32[8,4,1024]{2,1,0:T(4,128)} %get-tuple-element.13, f32[8,4,1024]{2,1,0:T(4,128)S(1)} %mul.234, f32[1024]{0:T(1024)S(1)} %broadcast_bitcast_fusion), kind=kLoop, calls=%fused_computation.30 | loop fusion | flops 262144 | bytes 462848 | tf_op jit(solution)/shard_map/convert_element_type | solution.py:245
  46.8 0.5 collective-permute-start.9
  47.3 1.2 %collective-permute-start.8 = (bf16[8,4,1024]{2,1,0:T(4,128)(2,1)S(1)}, bf16[8,4,1024]{2,1,0:T(4,128)(2,1)S(1)}, u32[]{:S(2)}, u32[]{:S(2)}) collective-permute-start(bf16[8,4,1024]{2,1,0:T(4,128)(2,1)S(1)} %fusion.11), channel_id=1, source_target_pairs={{0,8},{4,12},{8,0},{12,4},{1,9},{5,13},{9,1},{13,5},{2,10},{6,14},... | collective-permute-start | bytes 196616 | tf_op jit(solution)/shard_map/ppermute | solution.py:34
  48.4 0.2 collective-permute-start.7
  48.6 0.6 collective-permute-done.9
  49.2 3.3 %collective-permute-done.8 = bf16[8,4,1024]{2,1,0:T(4,128)(2,1)S(1)} collective-permute-done((bf16[8,4,1024]{2,1,0:T(4,128)(2,1)S(1)}, bf16[8,4,1024]{2,1,0:T(4,128)(2,1)S(1)}, u32[]{:S(2)}, u32[]{:S(2)}) %collective-permute-start.8) | collective-permute-done | bytes 65568 | tf_op jit(solution)/shard_map/ppermute | solution.py:34
  52.5 0.2 collective-permute-done.7
  52.7 0.2 pad_maximum_fusion
  52.9 0.8 %gather_fusion = bf16[4,8,4,1024]{3,2,1,0:T(4,128)(2,1)S(1)} fusion(bf16[4,8,4,1024]{3,2,1,0:T(4,128)(2,1)S(1)} %pad_maximum_fusion, s32[1024]{0:T(1024)S(1)} %pad_clamp_fusion), kind=kCustom, calls=%fused_computation | custom fusion | bytes 524304 | tf_op jit(solution)/shard_map/jit(_take)/gather | solution.py:37
  53.8 0.3 fusion
  54.1 0.7 %collective-permute-start.12 = (f32[32,512]{1,0:T(8,128)S(1)}, f32[32,512]{1,0:T(8,128)S(1)}, u32[]{:S(2)}, u32[]{:S(2)}) collective-permute-start(f32[32,512]{1,0:T(8,128)S(1)} %get-tuple-element.27), channel_id=1, source_target_pairs={{0,3},{1,0},{2,1},{3,2},{4,7},{5,4},{6,5},{7,6},{8,11},{9,8},{10,9... | collective-permute-start | bytes 196616 | tf_op jit(solution)/shard_map/ppermute | solution.py:47
  54.8 0.6 collective-permute-start.11
  55.4 1.9 %collective-permute-start.10 = (f32[32,512]{1,0:T(8,128)S(1)}, f32[32,512]{1,0:T(8,128)S(1)}, u32[]{:S(2)}, u32[]{:S(2)}) collective-permute-start(f32[32,512]{1,0:T(8,128)S(1)} %get-tuple-element.26), channel_id=1, source_target_pairs={{0,1},{1,2},{2,3},{3,0},{4,5},{5,6},{6,7},{7,4},{8,9},{9,10},{10,1... | collective-permute-start | bytes 196616 | tf_op jit(solution)/shard_map/ppermute | solution.py:47
  57.3 1.1 %collective-permute-done.12 = f32[32,512]{1,0:T(8,128)S(1)} collective-permute-done((f32[32,512]{1,0:T(8,128)S(1)}, f32[32,512]{1,0:T(8,128)S(1)}, u32[]{:S(2)}, u32[]{:S(2)}) %collective-permute-start.12) | collective-permute-done | bytes 65568 | tf_op jit(solution)/shard_map/ppermute | solution.py:47
  58.5 3.2 %collective-permute-done.11 = f32[32,512]{1,0:T(8,128)S(1)} collective-permute-done((f32[32,512]{1,0:T(8,128)S(1)}, f32[32,512]{1,0:T(8,128)S(1)}, u32[]{:S(2)}, u32[]{:S(2)}) %collective-permute-start.11) | collective-permute-done | bytes 65568 | tf_op jit(solution)/shard_map/ppermute | solution.py:47
  61.7 0.6 %reshape.137 = bf16[8,4,512]{2,1,0:T(4,128)(2,1)} reshape(bf16[32,512]{1,0:T(8,128)(2,1)S(1)} %fusion.14) | data formatting | bytes 65536 | tf_op jit(solution)/shard_map/reshape | solution.py:252
  (64 shorter events, 1.5 us)
Async XLA Ops:
  0.6 53.2 %copy-start = (bf16[1024,512]{1,0:T(8,128)(2,1)S(1)}, bf16[1024,512]{1,0:T(8,128)(2,1)}, u32[]{:S(2)}) copy-start(bf16[1024,512]{1,0:T(8,128)(2,1)} %param.24) | copy-start | bytes 3145732
  0.6 16.3 %copy-start.3 = (bf16[4,1024]{1,0:T(4,128)(2,1)S(1)}, bf16[4,1024]{1,0:T(4,128)(2,1)}, u32[]{:S(2)}) copy-start(bf16[4,1024]{1,0:T(4,128)(2,1)} %param.20) | copy-start | bytes 24580
  0.7 16.9 %copy-start.4 = (f32[128]{0:T(128)S(1)}, f32[128]{0:T(128)}, u32[]{:S(2)}) copy-start(f32[128]{0:T(128)} %param.23) | copy-start | bytes 1540
  0.7 20.9 %copy-start.6 = (f32[8]{0:T(128)S(1)}, f32[8]{0:T(128)}, u32[]{:S(2)}) copy-start(f32[8]{0:T(128)} %param.21) | copy-start | bytes 100
  0.7 20.9 %copy-start.5 = (f32[8]{0:T(128)S(1)}, f32[8]{0:T(128)}, u32[]{:S(2)}) copy-start(f32[8]{0:T(128)} %param.22) | copy-start | bytes 100
  0.7 21.1 %copy-start.1 = (bf16[8,3,1024]{2,0,1:T(8,128)(2,1)S(1)}, bf16[8,3,1024]{2,0,1:T(8,128)(2,1)}, u32[]{:S(2)}) copy-start(bf16[8,3,1024]{2,0,1:T(8,128)(2,1)} %param.25) | copy-start | bytes 147460
  0.7 21.1 %copy-start.2 = (bf16[8,3,1024]{2,0,1:T(8,128)(2,1)S(1)}, bf16[8,3,1024]{2,0,1:T(8,128)(2,1)}, u32[]{:S(2)}) copy-start(bf16[8,3,1024]{2,0,1:T(8,128)(2,1)} %param.26) | copy-start | bytes 147460
  0.7 7.2 %collective-permute-start = (bf16[8,4,512]{2,1,0:T(4,128)(2,1)}, bf16[8,4,512]{2,1,0:T(4,128)(2,1)S(1)}, u32[]{:S(2)}, u32[]{:S(2)}) collective-permute-start(bf16[8,4,512]{2,1,0:T(4,128)(2,1)} %param.15), channel_id=1, source_target_pairs={{0,3},{1,0},{2,1},{3,2},{4,7},{5,4},{6,5},{7,6},{8,11},{9,8},{10,9... | collective-permute-start | bytes 98312 | tf_op jit(solution)/shard_map/ppermute | solution.py:73
  5.8 5.0 %collective-permute-start.1 = (bf16[8,4,512]{2,1,0:T(4,128)(2,1)}, bf16[8,4,512]{2,1,0:T(4,128)(2,1)S(1)}, u32[]{:S(2)}, u32[]{:S(2)}) collective-permute-start(bf16[8,4,512]{2,1,0:T(4,128)(2,1)} %param.15), channel_id=1, source_target_pairs={{0,2},{1,3},{2,0},{3,1},{4,6},{5,7},{6,4},{7,5},{8,10},{9,11},{10,... | collective-permute-start | bytes 98312 | tf_op jit(solution)/shard_map/ppermute | solution.py:73
  5.8 5.9 %collective-permute-start.2 = (bf16[8,4,512]{2,1,0:T(4,128)(2,1)}, bf16[8,4,512]{2,1,0:T(4,128)(2,1)S(1)}, u32[]{:S(2)}, u32[]{:S(2)}) collective-permute-start(bf16[8,4,512]{2,1,0:T(4,128)(2,1)} %param.15), channel_id=1, source_target_pairs={{0,1},{1,2},{2,3},{3,0},{4,5},{5,6},{6,7},{7,4},{8,9},{9,10},{10,1... | collective-permute-start | bytes 98312 | tf_op jit(solution)/shard_map/ppermute | solution.py:73
  17.0 2.0 %collective-permute-start.4 = (f32[32,3088]{1,0:T(8,128)}, f32[32,3088]{1,0:T(8,128)S(1)}, u32[]{:S(2)}, u32[]{:S(2)}) collective-permute-start(f32[32,3088]{1,0:T(8,128)} %get-tuple-element.12), channel_id=1, source_target_pairs={{0,4},{4,0},{8,12},{12,8},{1,5},{5,1},{9,13},{13,9},{2,6},{6,2},{1... | collective-permute-start | bytes 1185800 | tf_op jit(solution)/shard_map/ppermute | solution.py:207
  17.0 5.5 %collective-permute-start.3 = (f32[32,3088]{1,0:T(8,128)}, f32[32,3088]{1,0:T(8,128)S(1)}, u32[]{:S(2)}, u32[]{:S(2)}) collective-permute-start(f32[32,3088]{1,0:T(8,128)} %get-tuple-element.10), channel_id=1, source_target_pairs={{0,4},{4,0},{8,12},{12,8},{1,5},{5,1},{9,13},{13,9},{2,6},{6,2},{1... | collective-permute-start | bytes 1185800 | tf_op jit(solution)/shard_map/ppermute | solution.py:207
  20.0 6.4 %collective-permute-start.6 = (f32[32,1024]{1,0:T(8,128)S(1)}, f32[32,1024]{1,0:T(8,128)S(1)}, u32[]{:S(2)}, u32[]{:S(2)}) collective-permute-start(f32[32,1024]{1,0:T(8,128)S(1)} %slice.131), channel_id=1, source_target_pairs={{0,8},{4,12},{8,0},{12,4},{1,9},{5,13},{9,1},{13,5},{2,10},{6,14},... | collective-permute-start | bytes 393224 | tf_op jit(solution)/shard_map/ppermute | solution.py:212
  21.9 9.6 %collective-permute-start.5 = (f32[32,2064]{1,0:T(8,128)S(1)}, f32[32,2064]{1,0:T(8,128)S(1)}, u32[]{:S(2)}, u32[]{:S(2)}) collective-permute-start(f32[32,2064]{1,0:T(8,128)S(1)} %slice.126), channel_id=1, source_target_pairs={{0,8},{4,12},{8,0},{12,4},{1,9},{5,13},{9,1},{13,5},{2,10},{6,14},... | collective-permute-start | bytes 792584 | tf_op jit(solution)/shard_map/ppermute | solution.py:213
  46.8 2.4 %collective-permute-start.9 = (bf16[8,4,1024]{2,1,0:T(4,128)(2,1)S(1)}, bf16[8,4,1024]{2,1,0:T(4,128)(2,1)S(1)}, u32[]{:S(2)}, u32[]{:S(2)}) collective-permute-start(bf16[8,4,1024]{2,1,0:T(4,128)(2,1)S(1)} %fusion.11), channel_id=1, source_target_pairs={{0,12},{4,0},{8,4},{12,8},{1,13},{5,1},{9,5},{13,9},{2,14},{6,2},{... | collective-permute-start | bytes 196616 | tf_op jit(solution)/shard_map/ppermute | solution.py:34
  47.3 5.3 %collective-permute-start.8 = (bf16[8,4,1024]{2,1,0:T(4,128)(2,1)S(1)}, bf16[8,4,1024]{2,1,0:T(4,128)(2,1)S(1)}, u32[]{:S(2)}, u32[]{:S(2)}) collective-permute-start(bf16[8,4,1024]{2,1,0:T(4,128)(2,1)S(1)} %fusion.11), channel_id=1, source_target_pairs={{0,8},{4,12},{8,0},{12,4},{1,9},{5,13},{9,1},{13,5},{2,10},{6,14},... | collective-permute-start | bytes 196616 | tf_op jit(solution)/shard_map/ppermute | solution.py:34
  48.4 4.3 %collective-permute-start.7 = (bf16[8,4,1024]{2,1,0:T(4,128)(2,1)S(1)}, bf16[8,4,1024]{2,1,0:T(4,128)(2,1)S(1)}, u32[]{:S(2)}, u32[]{:S(2)}) collective-permute-start(bf16[8,4,1024]{2,1,0:T(4,128)(2,1)S(1)} %fusion.11), channel_id=1, source_target_pairs={{0,4},{4,8},{8,12},{12,0},{1,5},{5,9},{9,13},{13,1},{2,6},{6,10},{... | collective-permute-start | bytes 196616 | tf_op jit(solution)/shard_map/ppermute | solution.py:34
  54.1 4.3 %collective-permute-start.12 = (f32[32,512]{1,0:T(8,128)S(1)}, f32[32,512]{1,0:T(8,128)S(1)}, u32[]{:S(2)}, u32[]{:S(2)}) collective-permute-start(f32[32,512]{1,0:T(8,128)S(1)} %get-tuple-element.27), channel_id=1, source_target_pairs={{0,3},{1,0},{2,1},{3,2},{4,7},{5,4},{6,5},{7,6},{8,11},{9,8},{10,9... | collective-permute-start | bytes 196616 | tf_op jit(solution)/shard_map/ppermute | solution.py:47
  54.8 6.9 %collective-permute-start.11 = (f32[32,512]{1,0:T(8,128)S(1)}, f32[32,512]{1,0:T(8,128)S(1)}, u32[]{:S(2)}, u32[]{:S(2)}) collective-permute-start(f32[32,512]{1,0:T(8,128)S(1)} %get-tuple-element.28), channel_id=1, source_target_pairs={{0,2},{1,3},{2,0},{3,1},{4,6},{5,7},{6,4},{7,5},{8,10},{9,11},{10,... | collective-permute-start | bytes 196616 | tf_op jit(solution)/shard_map/ppermute | solution.py:47
  55.4 6.3 %collective-permute-start.10 = (f32[32,512]{1,0:T(8,128)S(1)}, f32[32,512]{1,0:T(8,128)S(1)}, u32[]{:S(2)}, u32[]{:S(2)}) collective-permute-start(f32[32,512]{1,0:T(8,128)S(1)} %get-tuple-element.26), channel_id=1, source_target_pairs={{0,1},{1,2},{2,3},{3,0},{4,5},{5,6},{6,7},{7,4},{8,9},{9,10},{10,1... | collective-permute-start | bytes 196616 | tf_op jit(solution)/shard_map/ppermute | solution.py:47

commit v10 on v9

--- a/solution.py
+++ b/solution.py
@@ -74,27 +74,59 @@
     return jnp.stack(pieces)
 
 
-def projection_kernel(x_ref, wqk_ref, wvz_ref, wba_t_ref, *outs):
+def weight_chunks(width):
+    step = 512 if width % 512 == 0 else width
+    return [(c, step) for c in range(0, width, step)]
+
+
+def projection_kernel(x_ref, wqk_hbm, wvz_hbm, wba_t_hbm, *rest):
+    outs = rest[:-4]
+    qk_buf, vz_buf, ba_buf, sems = rest[-4:]
+    section = outs[0].shape[0]
+    width_qk, width_vz = qk_buf.shape[1], vz_buf.shape[1]
+    copies = []
+    for src, buf, offset in ((wqk_hbm, qk_buf, 0), (wvz_hbm, vz_buf, width_qk)):
+        for c, step in weight_chunks(buf.shape[1]):
+            copy = pltpu.make_async_copy(
+                src.at[:, pl.ds(c, step)], buf.at[:, pl.ds(c, step)], sems.at[len(copies)]
+            )
+            copy.start()
+            copies.append((copy, buf, c, step, offset + c))
+    ba_copy = pltpu.make_async_copy(wba_t_hbm, ba_buf, sems.at[len(copies)])
+    ba_copy.start()
     x = x_ref[...]
-    section = outs[0].shape[0]
-    offset = 0
-    for w_ref, transposed in ((wqk_ref, False), (wvz_ref, False), (wba_t_ref, True)):
-        width = w_ref.shape[0 if transposed else 1]
-        contract = 1 if transposed else 0
-        y = lax.dot_general(
-            x, w_ref[...], (((1,), (contract,)), ((), ())), preferred_element_type=jnp.float32
-        )
+    for copy, buf, c, step, column in copies:
+        copy.wait()
+        y = jnp.dot(x, buf[:, c : c + step], preferred_element_type=jnp.float32)
         for i, o_ref in enumerate(outs):
-            o_ref[:, offset : offset + width] = y[i * section : (i + 1) * section]
-        offset += width
+            o_ref[:, column : column + step] = y[i * section : (i + 1) * section]
+    ba_copy.wait()
+    y = lax.dot_general(x, ba_buf[...], (((1,), (1,)), ((), ())), preferred_element_type=jnp.float32)
+    column = width_qk + width_vz
+    for i, o_ref in enumerate(outs):
+        o_ref[:, column : column + ba_buf.shape[0]] = y[i * section : (i + 1) * section]
 
 
 def projection(x, w_qk, w_vz, w_ba, sections):
     rows = x.shape[0] // sections
     cols = w_qk.shape[1] + w_vz.shape[1] + w_ba.shape[1]
+    n_copies = len(weight_chunks(w_qk.shape[1])) + len(weight_chunks(w_vz.shape[1])) + 1
     return pl.pallas_call(
         projection_kernel,
+        in_specs=[
+            pl.BlockSpec(memory_space=pltpu.VMEM),
+            pl.BlockSpec(memory_space=pl.ANY),
+            pl.BlockSpec(memory_space=pl.ANY),
+            pl.BlockSpec(memory_space=pl.ANY),
+        ],
+        out_specs=[pl.BlockSpec(memory_space=pltpu.VMEM)] * sections,
         out_shape=[jax.ShapeDtypeStruct((rows, cols), jnp.float32)] * sections,
+        scratch_shapes=[
+            pltpu.VMEM(w_qk.shape, w_qk.dtype),
+            pltpu.VMEM(w_vz.shape, w_vz.dtype),
+            pltpu.VMEM((w_ba.shape[1], w_ba.shape[0]), w_ba.dtype),
+            pltpu.SemaphoreType.DMA((n_copies,)),
+        ],
         cost_estimate=pl.CostEstimate(
             flops=2 * x.shape[0] * x.shape[1] * cols,
             bytes_accessed=2 * x.shape[1] * cols + 2 * x.size + 4 * x.shape[0] * cols,

time: 62.9 us -> 64.1 us (1.019)
  Pallas kernels: 13.6 us -> 14.7 us
    pallas_call x1, Pallas kernels: 3.73 us -> 4.79 us  [projection(): pl.pallas_call(projection_kernel, in_specs=[pl.BlockSpec(memory_space=plt...]
where the time goes in v10:
time: 64.1 us; the launch traced here: 63.5 us
  waiting for transfers between devices  18.7 us (29%)
  Pallas kernels  14.7 us (23%)
  starting transfers between devices  13.9 us (22%)
  other arithmetic  8.23 us (13%)
  local copies, waits for them, and re-layouts  6.41 us (10%)
  between operations  1.3 us (2%)
    pallas_call x1, Pallas kernels, recurrence(): pl.pallas_call(kern, grid=(rows,), in_specs=[pl.BlockSpec(memory_space=pl...  9.9 us
    ppermute x3, starting transfers between devices, gather_pieces(): pieces.append(lax.ppermute(x, axis, [(i, (i + s) % n) for i in range(n)]))  6.11 us
    pallas_call x1, Pallas kernels, projection(): pl.pallas_call(projection_kernel, in_specs=[pl.BlockSpec(memory_space=plt...  4.79 us
    ppermute x3, waiting for transfers between devices, scatter_sum_rows(): acc = acc + lax.ppermute(send, axis, [(i, (i + s) % n) for i in range(n)])  4.36 us
    ppermute x3, waiting for transfers between devices, gather_rows(): pieces.append(lax.ppermute(x, axis, [(i, (i + s) % n) for i in range(n)]))  4.1 us
    ppermute x3, waiting for transfers between devices, gather_pieces(): pieces.append(lax.ppermute(x, axis, [(i, (i + s) % n) for i in range(n)]))  3.81 us
    ppermute x3, starting transfers between devices, scatter_sum_rows(): acc = acc + lax.ppermute(send, axis, [(i, (i + s) % n) for i in range(n)])  3.21 us
    ppermute x1, waiting for transfers between devices, shards(): summed_qk = summed_qk + lax.ppermute(part[s][:, :width_qk], 'dp', perm)  2.83 us
  transfers between devices with their start and end apart: 13, of which 10 were waited for; matrix products, arithmetic and copies ran while one was open for 10% of the time, Pallas kernels for 0%

profile of v10, /device:TPU:0, one launch (start us, length us, event | category | flops | bytes accessed | tf_op | source)
XLA Modules:
  0.0 63.5 jit_solution(8087063324562536265)
XLA Ops:
  0.7 5.1 %collective-permute-start = (bf16[8,4,512]{2,1,0:T(4,128)(2,1)}, bf16[8,4,512]{2,1,0:T(4,128)(2,1)S(1)}, u32[]{:S(2)}, u32[]{:S(2)}) collective-permute-start(bf16[8,4,512]{2,1,0:T(4,128)(2,1)} %param.15), channel_id=1, source_target_pairs={{0,3},{1,0},{2,1},{3,2},{4,7},{5,4},{6,5},{7,6},{8,11},{9,8},{10,9... | collective-permute-start | bytes 98312 | tf_op jit(solution)/shard_map/ppermute | solution.py:73
  5.8 1.0 %collective-permute-start.2 = (bf16[8,4,512]{2,1,0:T(4,128)(2,1)}, bf16[8,4,512]{2,1,0:T(4,128)(2,1)S(1)}, u32[]{:S(2)}, u32[]{:S(2)}) collective-permute-start(bf16[8,4,512]{2,1,0:T(4,128)(2,1)} %param.15), channel_id=1, source_target_pairs={{0,1},{1,2},{2,3},{3,0},{4,5},{5,6},{6,7},{7,4},{8,9},{9,10},{10,1... | collective-permute-start | bytes 98312 | tf_op jit(solution)/shard_map/ppermute | solution.py:73
  6.8 0.9 %fusion.23 = (f32[1,1024]{1,0:T(1,128)S(1)}, f32[1,1024]{1,0:T(1,128)S(1)}, f32[1,1024]{1,0:T(1,128)S(1)}, f32[1,1024]{1,0:T(1,128)S(1)}) fusion(bf16[4,1024]{1,0:T(4,128)(2,1)} %param.19), kind=kLoop, calls=%fused_computation.69 | loop fusion | bytes 32768 | tf_op jit(solution)/shard_map/slice | solution.py:25
  7.9 2.9 %collective-permute-done.1 = bf16[8,4,512]{2,1,0:T(4,128)(2,1)S(1)} collective-permute-done((bf16[8,4,512]{2,1,0:T(4,128)(2,1)}, bf16[8,4,512]{2,1,0:T(4,128)(2,1)S(1)}, u32[]{:S(2)}, u32[]{:S(2)}) %collective-permute-start.1) | collective-permute-done | bytes 32800 | tf_op jit(solution)/shard_map/ppermute | solution.py:73
  10.8 0.9 %collective-permute-done.2 = bf16[8,4,512]{2,1,0:T(4,128)(2,1)S(1)} collective-permute-done((bf16[8,4,512]{2,1,0:T(4,128)(2,1)}, bf16[8,4,512]{2,1,0:T(4,128)(2,1)S(1)}, u32[]{:S(2)}, u32[]{:S(2)}) %collective-permute-start.2) | collective-permute-done | bytes 32800 | tf_op jit(solution)/shard_map/ppermute | solution.py:73
  11.7 0.8 %select_select_fusion.3 = (bf16[4,8,512]{2,1,0:T(8,128)(2,1)S(1)}, bf16[4,8,512]{2,1,0:T(8,128)(2,1)S(1)}, bf16[4,8,512]{2,1,0:T(8,128)(2,1)S(1)}, bf16[4,8,512]{2,1,0:T(8,128)(2,1)S(1)}) fusion(bf16[4,8,512]{2,1,0:T(8,128)(2,1)S(1)} %bitcast.86, bf16[4,8,512]{2,1,0:T(8,128)(2,1)S(1)} %bitcast.87, bf16[4,8,512]{2,1,0:T(8,128)(2,1)S(1)} %bitcast.88, ...), kind=kLoop, calls=%fused_computation.48 | loop fusion | flops 196608 | bytes 262156 | tf_op jit(solution)/shard_map/jit(_where)/select_n | solution.py:233
  12.6 0.6 %pad_maximum_fusion.1.x_ref = bf16[128,512]{1,0:T(8,128)(2,1)} fusion(bf16[32,512]{1,0:T(8,128)(2,1)S(1)} %reshape.132, bf16[32,512]{1,0:T(8,128)(2,1)S(1)} %reshape.131, bf16[32,512]{1,0:T(8,128)(2,1)S(1)} %reshape.130, bf16[32,512]{1,0:T(8,128)(2,1)S(1)} %reshape.129), kind=kLoop, calls=%fused_computation.27 | loop fusion | flops 524288 | bytes 262144 | tf_op jit(solution)/shard_map/concatenate | solution.py:236
  13.3 4.8 %shard_map.140 = (f32[32,3088]{1,0:T(8,128)}, f32[32,3088]{1,0:T(8,128)}, f32[32,3088]{1,0:T(8,128)}, f32[32,3088]{1,0:T(8,128)}) custom-call(bf16[128,512]{1,0:T(8,128)(2,1)} %pad_maximum_fusion.1.x_ref, bf16[512,1024]{1,0:T(8,128)(2,1)} %wqk_hbm.1, bf16[512,2048]{1,0:T(8,128)(2,1)} %wvz_hbm.1, bf16[16,512]{1,0:T(8,128)(2,1)} %bitcast.89), custom_call_target="tpu_custom_call" | custom-call | flops 404750336 | bytes 4874240 | tf_op jit(solution)/shard_map/pallas_call | solution.py:114
  18.2 0.5 collective-permute-start.3
  18.7 1.4 %collective-permute-done.4 = f32[32,3088]{1,0:T(8,128)S(1)} collective-permute-done((f32[32,3088]{1,0:T(8,128)}, f32[32,3088]{1,0:T(8,128)S(1)}, u32[]{:S(2)}, u32[]{:S(2)}) %collective-permute-start.4) | collective-permute-done | bytes 395296 | tf_op jit(solution)/shard_map/ppermute | solution.py:239
  20.1 1.1 %add.201 = f32[32,3088]{1,0:T(8,128)S(1)} add(f32[32,3088]{1,0:T(8,128)} %get-tuple-element.11, f32[32,3088]{1,0:T(8,128)S(1)} %collective-permute-done.4) | non-fusion elementwise | flops 98816 | bytes 1185792 | tf_op jit(solution)/shard_map/add | solution.py:239
  21.2 1.6 %collective-permute-start.6 = (f32[32,1024]{1,0:T(8,128)S(1)}, f32[32,1024]{1,0:T(8,128)S(1)}, u32[]{:S(2)}, u32[]{:S(2)}) collective-permute-start(f32[32,1024]{1,0:T(8,128)S(1)} %slice.131), channel_id=1, source_target_pairs={{0,8},{4,12},{8,0},{12,4},{1,9},{5,13},{9,1},{13,5},{2,10},{6,14},... | collective-permute-start | bytes 393224 | tf_op jit(solution)/shard_map/ppermute | solution.py:244
  23.1 0.6 collective-permute-start.5
  23.7 1.0 %add.200 = f32[32,3088]{1,0:T(8,128)S(1)} add(f32[32,3088]{1,0:T(8,128)} %get-tuple-element.9, f32[32,3088]{1,0:T(8,128)S(1)} %collective-permute-done.3) | non-fusion elementwise | flops 98816 | bytes 1185792 | tf_op jit(solution)/shard_map/add | solution.py:239
  24.7 2.8 %collective-permute-done.6 = f32[32,1024]{1,0:T(8,128)S(1)} collective-permute-done((f32[32,1024]{1,0:T(8,128)S(1)}, f32[32,1024]{1,0:T(8,128)S(1)}, u32[]{:S(2)}, u32[]{:S(2)}) %collective-permute-start.6) | collective-permute-done | bytes 131104 | tf_op jit(solution)/shard_map/ppermute | solution.py:244
  27.7 0.2 divide_multiply_fusion.2
  27.9 0.1 reshape.134
  28.0 0.1 fusion.20
  28.1 0.1 multiply_reduce_fusion.1
  28.2 0.1 multiply_reduce_fusion
  28.4 1.0 %copy.43.qt_ref = f32[8,128,16]{2,1,0:T(8,128)} copy(f32[8,128,16]{1,0,2:T(8,128)S(1)} %bitcast.75) | data formatting | bytes 131072 | tf_op jit(solution)/shard_map/reshape | solution.py:262
  29.5 1.0 %copy.44.kt_ref = f32[8,128,16]{2,1,0:T(8,128)} copy(f32[8,128,16]{1,0,2:T(8,128)S(1)} %bitcast.76) | data formatting | bytes 131072 | tf_op jit(solution)/shard_map/reshape | solution.py:263
  30.5 2.2 %collective-permute-done.5 = f32[32,2064]{1,0:T(8,128)S(1)} collective-permute-done((f32[32,2064]{1,0:T(8,128)S(1)}, f32[32,2064]{1,0:T(8,128)S(1)}, u32[]{:S(2)}, u32[]{:S(2)}) %collective-permute-start.5) | collective-permute-done | bytes 264224 | tf_op jit(solution)/shard_map/ppermute | solution.py:245
  32.9 0.4 slice_reduce_fusion
  33.6 0.1 copy.37
  33.8 0.1 copy.46
  34.1 0.7 %pad_maximum_fusion.2.gates_ref = f32[8,64]{1,0:T(8,128)} fusion(f32[8,32]{1,0:T(8,128)S(1)} %fusion.17, f32[8,32]{1,0:T(8,128)S(1)} %div.77), kind=kLoop, calls=%fused_computation.58 | loop fusion | flops 512 | bytes 4096 | tf_op jit(solution)/shard_map/concatenate | solution.py:268
  34.8 0.8 %divide_multiply_fusion.1.v_ref = f32[8,4,1024]{2,1,0:T(4,128)} fusion(f32[8,7,1024]{2,1,0:T(8,128)S(1)} %maximum_convert_fusion.1, f32[1024]{0:T(1024)S(1)} %bitcast.97, f32[1024]{0:T(1024)S(1)} %bitcast.96, f32[1024]{0:T(1024)S(1)} %bitcast.95, f32[1024]{0:T(1024)S(1)} %bitcast.94), kind=kLoop, calls=%fused_computation.7 | loop fusion | flops 360448 | bytes 671744 | tf_op jit(solution)/shard_map/jit(silu)/mul | solution.py:26
  35.7 9.9 %shard_map.141 = (f32[8,8,128,128]{3,2,1,0:T(8,128)}, f32[8,4,1024]{2,1,0:T(4,128)}) custom-call(f32[8,64]{1,0:T(8,128)} %pad_maximum_fusion.2.gates_ref, f32[8,128,16]{2,1,0:T(8,128)} %copy.43.qt_ref, f32[8,128,16]{2,1,0:T(8,128)} %copy.44.kt_ref, f32[8,4,1024]{2,1,0:T(4,128)} %divide_multiply_fusion.1.v_ref, f32[8,8,128,128]{3,2,1,0:T(8,128)} %s_ref.1), custom_call_target="tpu_custom_call" | custom-call | flops 33554432 | bytes 8388608 | tf_op jit(solution)/shard_map/pallas_call | solution.py:168
  45.6 1.0 %mul.231 = f32[8,4,1024]{2,1,0:T(4,128)S(1)} multiply(f32[8,4,1024]{2,1,0:T(4,128)} %get-tuple-element.13, f32[8,4,1024]{2,1,0:T(4,128)} %get-tuple-element.13) | non-fusion elementwise | flops 32768 | bytes 393216 | tf_op jit(solution)/shard_map/mul | solution.py:275
  46.6 0.1 reduce_sum.29
  46.8 0.1 mul.233
  46.9 1.0 %fusion.11 = bf16[8,4,1024]{2,1,0:T(4,128)(2,1)S(1)} fusion(f32[8,4,1024]{2,1,0:T(4,128)S(1)} %reshape.198, f32[8,4,1024]{2,1,0:T(4,128)} %get-tuple-element.13, f32[8,4,1024]{2,1,0:T(4,128)S(1)} %mul.234, f32[1024]{0:T(1024)S(1)} %broadcast_bitcast_fusion), kind=kLoop, calls=%fused_computation.30 | loop fusion | flops 262144 | bytes 462848 | tf_op jit(solution)/shard_map/convert_element_type | solution.py:277
  47.9 0.5 collective-permute-start.9
  48.4 1.2 %collective-permute-start.8 = (bf16[8,4,1024]{2,1,0:T(4,128)(2,1)S(1)}, bf16[8,4,1024]{2,1,0:T(4,128)(2,1)S(1)}, u32[]{:S(2)}, u32[]{:S(2)}) collective-permute-start(bf16[8,4,1024]{2,1,0:T(4,128)(2,1)S(1)} %fusion.11), channel_id=1, source_target_pairs={{0,8},{4,12},{8,0},{12,4},{1,9},{5,13},{9,1},{13,5},{2,10},{6,14},... | collective-permute-start | bytes 196616 | tf_op jit(solution)/shard_map/ppermute | solution.py:34
  49.6 0.2 collective-permute-start.7
  49.7 0.6 collective-permute-done.9
  50.3 3.3 %collective-permute-done.8 = bf16[8,4,1024]{2,1,0:T(4,128)(2,1)S(1)} collective-permute-done((bf16[8,4,1024]{2,1,0:T(4,128)(2,1)S(1)}, bf16[8,4,1024]{2,1,0:T(4,128)(2,1)S(1)}, u32[]{:S(2)}, u32[]{:S(2)}) %collective-permute-start.8) | collective-permute-done | bytes 65568 | tf_op jit(solution)/shard_map/ppermute | solution.py:34
  53.6 0.2 collective-permute-done.7
  53.8 0.2 pad_maximum_fusion
  54.1 0.8 %gather_fusion = bf16[4,8,4,1024]{3,2,1,0:T(4,128)(2,1)S(1)} fusion(bf16[4,8,4,1024]{3,2,1,0:T(4,128)(2,1)S(1)} %pad_maximum_fusion, s32[1024]{0:T(1024)S(1)} %pad_clamp_fusion), kind=kCustom, calls=%fused_computation | custom fusion | bytes 524304 | tf_op jit(solution)/shard_map/jit(_take)/gather | solution.py:37
  54.9 0.3 fusion
  55.3 0.7 %collective-permute-start.12 = (f32[32,512]{1,0:T(8,128)S(1)}, f32[32,512]{1,0:T(8,128)S(1)}, u32[]{:S(2)}, u32[]{:S(2)}) collective-permute-start(f32[32,512]{1,0:T(8,128)S(1)} %get-tuple-element.27), channel_id=1, source_target_pairs={{0,3},{1,0},{2,1},{3,2},{4,7},{5,4},{6,5},{7,6},{8,11},{9,8},{10,9... | collective-permute-start | bytes 196616 | tf_op jit(solution)/shard_map/ppermute | solution.py:47
  55.9 0.6 collective-permute-start.11
  56.5 1.9 %collective-permute-start.10 = (f32[32,512]{1,0:T(8,128)S(1)}, f32[32,512]{1,0:T(8,128)S(1)}, u32[]{:S(2)}, u32[]{:S(2)}) collective-permute-start(f32[32,512]{1,0:T(8,128)S(1)} %get-tuple-element.26), channel_id=1, source_target_pairs={{0,1},{1,2},{2,3},{3,0},{4,5},{5,6},{6,7},{7,4},{8,9},{9,10},{10,1... | collective-permute-start | bytes 196616 | tf_op jit(solution)/shard_map/ppermute | solution.py:47
  58.5 1.1 %collective-permute-done.12 = f32[32,512]{1,0:T(8,128)S(1)} collective-permute-done((f32[32,512]{1,0:T(8,128)S(1)}, f32[32,512]{1,0:T(8,128)S(1)}, u32[]{:S(2)}, u32[]{:S(2)}) %collective-permute-start.12) | collective-permute-done | bytes 65568 | tf_op jit(solution)/shard_map/ppermute | solution.py:47
  59.6 3.2 %collective-permute-done.11 = f32[32,512]{1,0:T(8,128)S(1)} collective-permute-done((f32[32,512]{1,0:T(8,128)S(1)}, f32[32,512]{1,0:T(8,128)S(1)}, u32[]{:S(2)}, u32[]{:S(2)}) %collective-permute-start.11) | collective-permute-done | bytes 65568 | tf_op jit(solution)/shard_map/ppermute | solution.py:47
  62.9 0.6 reshape.137
  (64 shorter events, 1.6 us)
Async XLA Ops:
  0.6 54.3 %copy-start = (bf16[1024,512]{1,0:T(8,128)(2,1)S(1)}, bf16[1024,512]{1,0:T(8,128)(2,1)}, u32[]{:S(2)}) copy-start(bf16[1024,512]{1,0:T(8,128)(2,1)} %param.24) | copy-start | bytes 3145732
  0.6 17.5 %copy-start.3 = (bf16[4,1024]{1,0:T(4,128)(2,1)S(1)}, bf16[4,1024]{1,0:T(4,128)(2,1)}, u32[]{:S(2)}) copy-start(bf16[4,1024]{1,0:T(4,128)(2,1)} %param.20) | copy-start | bytes 24580
  0.7 18.1 %copy-start.4 = (f32[128]{0:T(128)S(1)}, f32[128]{0:T(128)}, u32[]{:S(2)}) copy-start(f32[128]{0:T(128)} %param.23) | copy-start | bytes 1540
  0.7 22.0 %copy-start.6 = (f32[8]{0:T(128)S(1)}, f32[8]{0:T(128)}, u32[]{:S(2)}) copy-start(f32[8]{0:T(128)} %param.21) | copy-start | bytes 100
  0.7 22.0 %copy-start.5 = (f32[8]{0:T(128)S(1)}, f32[8]{0:T(128)}, u32[]{:S(2)}) copy-start(f32[8]{0:T(128)} %param.22) | copy-start | bytes 100
  0.7 22.2 %copy-start.1 = (bf16[8,3,1024]{2,0,1:T(8,128)(2,1)S(1)}, bf16[8,3,1024]{2,0,1:T(8,128)(2,1)}, u32[]{:S(2)}) copy-start(bf16[8,3,1024]{2,0,1:T(8,128)(2,1)} %param.25) | copy-start | bytes 147460
  0.7 22.3 %copy-start.2 = (bf16[8,3,1024]{2,0,1:T(8,128)(2,1)S(1)}, bf16[8,3,1024]{2,0,1:T(8,128)(2,1)}, u32[]{:S(2)}) copy-start(bf16[8,3,1024]{2,0,1:T(8,128)(2,1)} %param.26) | copy-start | bytes 147460
  0.7 7.2 %collective-permute-start = (bf16[8,4,512]{2,1,0:T(4,128)(2,1)}, bf16[8,4,512]{2,1,0:T(4,128)(2,1)S(1)}, u32[]{:S(2)}, u32[]{:S(2)}) collective-permute-start(bf16[8,4,512]{2,1,0:T(4,128)(2,1)} %param.15), channel_id=1, source_target_pairs={{0,3},{1,0},{2,1},{3,2},{4,7},{5,4},{6,5},{7,6},{8,11},{9,8},{10,9... | collective-permute-start | bytes 98312 | tf_op jit(solution)/shard_map/ppermute | solution.py:73
  5.8 5.0 %collective-permute-start.1 = (bf16[8,4,512]{2,1,0:T(4,128)(2,1)}, bf16[8,4,512]{2,1,0:T(4,128)(2,1)S(1)}, u32[]{:S(2)}, u32[]{:S(2)}) collective-permute-start(bf16[8,4,512]{2,1,0:T(4,128)(2,1)} %param.15), channel_id=1, source_target_pairs={{0,2},{1,3},{2,0},{3,1},{4,6},{5,7},{6,4},{7,5},{8,10},{9,11},{10,... | collective-permute-start | bytes 98312 | tf_op jit(solution)/shard_map/ppermute | solution.py:73
  5.8 5.9 %collective-permute-start.2 = (bf16[8,4,512]{2,1,0:T(4,128)(2,1)}, bf16[8,4,512]{2,1,0:T(4,128)(2,1)S(1)}, u32[]{:S(2)}, u32[]{:S(2)}) collective-permute-start(bf16[8,4,512]{2,1,0:T(4,128)(2,1)} %param.15), channel_id=1, source_target_pairs={{0,1},{1,2},{2,3},{3,0},{4,5},{5,6},{6,7},{7,4},{8,9},{9,10},{10,1... | collective-permute-start | bytes 98312 | tf_op jit(solution)/shard_map/ppermute | solution.py:73
  18.1 2.0 %collective-permute-start.4 = (f32[32,3088]{1,0:T(8,128)}, f32[32,3088]{1,0:T(8,128)S(1)}, u32[]{:S(2)}, u32[]{:S(2)}) collective-permute-start(f32[32,3088]{1,0:T(8,128)} %get-tuple-element.12), channel_id=1, source_target_pairs={{0,4},{4,0},{8,12},{12,8},{1,5},{5,1},{9,13},{13,9},{2,6},{6,2},{1... | collective-permute-start | bytes 1185800 | tf_op jit(solution)/shard_map/ppermute | solution.py:239
  18.2 5.5 %collective-permute-start.3 = (f32[32,3088]{1,0:T(8,128)}, f32[32,3088]{1,0:T(8,128)S(1)}, u32[]{:S(2)}, u32[]{:S(2)}) collective-permute-start(f32[32,3088]{1,0:T(8,128)} %get-tuple-element.10), channel_id=1, source_target_pairs={{0,4},{4,0},{8,12},{12,8},{1,5},{5,1},{9,13},{13,9},{2,6},{6,2},{1... | collective-permute-start | bytes 1185800 | tf_op jit(solution)/shard_map/ppermute | solution.py:239
  21.2 6.4 %collective-permute-start.6 = (f32[32,1024]{1,0:T(8,128)S(1)}, f32[32,1024]{1,0:T(8,128)S(1)}, u32[]{:S(2)}, u32[]{:S(2)}) collective-permute-start(f32[32,1024]{1,0:T(8,128)S(1)} %slice.131), channel_id=1, source_target_pairs={{0,8},{4,12},{8,0},{12,4},{1,9},{5,13},{9,1},{13,5},{2,10},{6,14},... | collective-permute-start | bytes 393224 | tf_op jit(solution)/shard_map/ppermute | solution.py:244
  23.1 9.7 %collective-permute-start.5 = (f32[32,2064]{1,0:T(8,128)S(1)}, f32[32,2064]{1,0:T(8,128)S(1)}, u32[]{:S(2)}, u32[]{:S(2)}) collective-permute-start(f32[32,2064]{1,0:T(8,128)S(1)} %slice.126), channel_id=1, source_target_pairs={{0,8},{4,12},{8,0},{12,4},{1,9},{5,13},{9,1},{13,5},{2,10},{6,14},... | collective-permute-start | bytes 792584 | tf_op jit(solution)/shard_map/ppermute | solution.py:245
  47.9 2.4 %collective-permute-start.9 = (bf16[8,4,1024]{2,1,0:T(4,128)(2,1)S(1)}, bf16[8,4,1024]{2,1,0:T(4,128)(2,1)S(1)}, u32[]{:S(2)}, u32[]{:S(2)}) collective-permute-start(bf16[8,4,1024]{2,1,0:T(4,128)(2,1)S(1)} %fusion.11), channel_id=1, source_target_pairs={{0,12},{4,0},{8,4},{12,8},{1,13},{5,1},{9,5},{13,9},{2,14},{6,2},{... | collective-permute-start | bytes 196616 | tf_op jit(solution)/shard_map/ppermute | solution.py:34
  48.4 5.3 %collective-permute-start.8 = (bf16[8,4,1024]{2,1,0:T(4,128)(2,1)S(1)}, bf16[8,4,1024]{2,1,0:T(4,128)(2,1)S(1)}, u32[]{:S(2)}, u32[]{:S(2)}) collective-permute-start(bf16[8,4,1024]{2,1,0:T(4,128)(2,1)S(1)} %fusion.11), channel_id=1, source_target_pairs={{0,8},{4,12},{8,0},{12,4},{1,9},{5,13},{9,1},{13,5},{2,10},{6,14},... | collective-permute-start | bytes 196616 | tf_op jit(solution)/shard_map/ppermute | solution.py:34
  49.6 4.3 %collective-permute-start.7 = (bf16[8,4,1024]{2,1,0:T(4,128)(2,1)S(1)}, bf16[8,4,1024]{2,1,0:T(4,128)(2,1)S(1)}, u32[]{:S(2)}, u32[]{:S(2)}) collective-permute-start(bf16[8,4,1024]{2,1,0:T(4,128)(2,1)S(1)} %fusion.11), channel_id=1, source_target_pairs={{0,4},{4,8},{8,12},{12,0},{1,5},{5,9},{9,13},{13,1},{2,6},{6,10},{... | collective-permute-start | bytes 196616 | tf_op jit(solution)/shard_map/ppermute | solution.py:34
  55.3 4.3 %collective-permute-start.12 = (f32[32,512]{1,0:T(8,128)S(1)}, f32[32,512]{1,0:T(8,128)S(1)}, u32[]{:S(2)}, u32[]{:S(2)}) collective-permute-start(f32[32,512]{1,0:T(8,128)S(1)} %get-tuple-element.27), channel_id=1, source_target_pairs={{0,3},{1,0},{2,1},{3,2},{4,7},{5,4},{6,5},{7,6},{8,11},{9,8},{10,9... | collective-permute-start | bytes 196616 | tf_op jit(solution)/shard_map/ppermute | solution.py:47
  55.9 6.9 %collective-permute-start.11 = (f32[32,512]{1,0:T(8,128)S(1)}, f32[32,512]{1,0:T(8,128)S(1)}, u32[]{:S(2)}, u32[]{:S(2)}) collective-permute-start(f32[32,512]{1,0:T(8,128)S(1)} %get-tuple-element.28), channel_id=1, source_target_pairs={{0,2},{1,3},{2,0},{3,1},{4,6},{5,7},{6,4},{7,5},{8,10},{9,11},{10,... | collective-permute-start | bytes 196616 | tf_op jit(solution)/shard_map/ppermute | solution.py:47
  56.5 6.3 %collective-permute-start.10 = (f32[32,512]{1,0:T(8,128)S(1)}, f32[32,512]{1,0:T(8,128)S(1)}, u32[]{:S(2)}, u32[]{:S(2)}) collective-permute-start(f32[32,512]{1,0:T(8,128)S(1)} %get-tuple-element.26), channel_id=1, source_target_pairs={{0,1},{1,2},{2,3},{3,0},{4,5},{5,6},{6,7},{7,4},{8,9},{9,10},{10,1... | collective-permute-start | bytes 196616 | tf_op jit(solution)/shard_map/ppermute | solution.py:47

commit v11 on v9

--- a/solution.py
+++ b/solution.py
@@ -103,7 +103,7 @@
     )(x, w_qk, w_vz, w_ba.T)
 
 
-def recurrence_kernel(gates_ref, qt_ref, kt_ref, v_ref, s_ref, s_out, o_ref, *, heads, steps, ratio):
+def recurrence_kernel(gates_ref, gain_ref, qt_ref, kt_ref, v_ref, z_ref, s_ref, s_out, o_ref, *, heads, steps, ratio):
     r = pl.program_id(0)
     key_heads = heads // ratio
     cols = heads * steps
@@ -121,13 +121,16 @@
                 recalled = jnp.sum(key_col * state, axis=0, keepdims=True)
                 correction = (v_ref[0, t : t + 1, lanes] - recalled) * gates_ref[r, c]
                 state = state + key_col * correction
-                o_ref[0, t : t + 1, lanes] = jnp.sum(query_col * state, axis=0, keepdims=True)
+                readout = jnp.sum(query_col * state, axis=0, keepdims=True)
+                scale = lax.rsqrt(jnp.mean(readout * readout, axis=-1, keepdims=True) + 1e-06)
+                gate = z_ref[0, t : t + 1, lanes]
+                o_ref[0, t : t + 1, lanes] = readout * scale * gain_ref[...] * (gate * jax.nn.sigmoid(gate))
                 states[j] = state
         for j, h in enumerate(group):
             s_out[0, h] = states[j]
 
 
-def recurrence(gates, qt, kt, values, memory_state):
+def recurrence(gates, norm_gain, qt, kt, values, gate_z, memory_state):
     rows, heads = memory_state.shape[0], memory_state.shape[1]
     steps = values.shape[1]
     key_cols = kt.shape[2]
@@ -138,8 +141,10 @@
         grid=(rows,),
         in_specs=[
             pl.BlockSpec(memory_space=pltpu.SMEM),
+            pl.BlockSpec((1, DV), lambda r: (0, 0)),
             pl.BlockSpec((1, DK, key_cols), lambda r: (r, 0, 0)),
             pl.BlockSpec((1, DK, key_cols), lambda r: (r, 0, 0)),
+            pl.BlockSpec((1, steps, heads * DV), lambda r: (r, 0, 0)),
             pl.BlockSpec((1, steps, heads * DV), lambda r: (r, 0, 0)),
             pl.BlockSpec((1, heads, DK, DV), lambda r: (r, 0, 0, 0)),
         ],
@@ -156,7 +161,7 @@
             bytes_accessed=2 * memory_state.size * 4,
             transcendentals=0,
         ),
-    )(gates, qt, kt, values, memory_state)
+    )(gates, norm_gain.reshape(1, DV), qt, kt, values, gate_z, memory_state)
 
 
 def shards(
@@ -237,12 +242,10 @@
         [beta_gate.reshape(rows_mem, -1), jnp.exp(log_decay).reshape(rows_mem, -1)], axis=1
     )
 
-    new_state, readout = recurrence(gates, qt, kt, v_conv, memory_state)
-    readout = readout.reshape(rows_mem, step_count, heads, DV)
-
-    scale = lax.rsqrt(jnp.mean(readout * readout, axis=-1, keepdims=True) + 1e-06)
-    normed = readout * scale * norm_gain[None, None, None, :] * jax.nn.silu(gate_z)
-    normed = normed.reshape(rows_mem, step_count, heads * DV).astype(jnp.bfloat16)
+    new_state, normed = recurrence(
+        gates, norm_gain, qt, kt, v_conv, gate_z.reshape(rows_mem, step_count, heads * DV), memory_state
+    )
+    normed = normed.astype(jnp.bfloat16)
 
     all_normed = gather_rows(normed, "dp")
     partials = jnp.dot(

time: 62.9 us -> 70.9 us (1.13)
  Pallas kernels: 13.6 us -> 22.3 us
  waiting for transfers between devices: 18.7 us -> 15.9 us
  starting transfers between devices: 13.8 us -> 15.9 us
    pallas_call x1, Pallas kernels: 9.9 us -> 18.6 us  [recurrence(): pl.pallas_call(kern, grid=(rows,), in_specs=[pl.BlockSpec(memory_space=pl...]
    ppermute x3, waiting for transfers between devices: 4.1 us -> 0.97 us  [gather_rows(): pieces.append(lax.ppermute(x, axis, [(i, (i + s) % n) for i in range(n)]))]
    ppermute x3, starting transfers between devices: 1.79 us -> 3 us  [gather_rows(): pieces.append(lax.ppermute(x, axis, [(i, (i + s) % n) for i in range(n)]))]
    mul x1 -> x0, other arithmetic: 1.02 us -> none  [shards(): readout * readout]
    another operation x1 -> x2, other arithmetic: 0.24 us -> 1.16 us  [gather_rows(): stacked = jnp.stack(pieces)]
    ppermute x3, starting transfers between devices: 3.21 us -> 4.09 us  [scatter_sum_rows(): acc = acc + lax.ppermute(send, axis, [(i, (i + s) % n) for i in range(n)])]
  transfers between devices with their start and end apart: 13 -> 13, of which waited for: 10 -> 9; matrix products, arithmetic and copies ran while one was open for 10% -> 10% of each run, Pallas kernels for 0% -> 0%
where the time goes in v11:
time: 70.9 us; the launch traced here: 70.5 us
  Pallas kernels  22.3 us (31%)
  starting transfers between devices  15.9 us (22%)
  waiting for transfers between devices  15.9 us (22%)
  other arithmetic  7.93 us (11%)
  local copies, waits for them, and re-layouts  6.83 us (10%)
  between operations  1.24 us (2%)
    pallas_call x1, Pallas kernels, recurrence(): pl.pallas_call(kern, grid=(rows,), in_specs=[pl.BlockSpec(memory_space=pl...  18.6 us
    ppermute x3, starting transfers between devices, gather_pieces(): pieces.append(lax.ppermute(x, axis, [(i, (i + s) % n) for i in range(n)]))  6.11 us
    ppermute x3, waiting for transfers between devices, scatter_sum_rows(): acc = acc + lax.ppermute(send, axis, [(i, (i + s) % n) for i in range(n)])  4.7 us
    ppermute x3, starting transfers between devices, scatter_sum_rows(): acc = acc + lax.ppermute(send, axis, [(i, (i + s) % n) for i in range(n)])  4.09 us
    ppermute x3, waiting for transfers between devices, gather_pieces(): pieces.append(lax.ppermute(x, axis, [(i, (i + s) % n) for i in range(n)]))  3.81 us
    pallas_call x1, Pallas kernels, projection(): pl.pallas_call(projection_kernel, out_shape=[jax.ShapeDtypeStruct((rows,...  3.73 us
    ppermute x3, starting transfers between devices, gather_rows(): pieces.append(lax.ppermute(x, axis, [(i, (i + s) % n) for i in range(n)]))  3 us
    ppermute x1, waiting for transfers between devices, shards(): summed_qk = summed_qk + lax.ppermute(part[s][:, :width_qk], 'dp', perm)  2.85 us
  transfers between devices with their start and end apart: 13, of which 9 were waited for; matrix products, arithmetic and copies ran while one was open for 10% of the time, Pallas kernels for 0%

profile of v11, /device:TPU:0, one launch (start us, length us, event | category | flops | bytes accessed | tf_op | source)
XLA Modules:
  0.0 70.5 jit_solution(4577286159654934900)
XLA Ops:
  0.7 5.1 %collective-permute-start = (bf16[8,4,512]{2,1,0:T(4,128)(2,1)}, bf16[8,4,512]{2,1,0:T(4,128)(2,1)S(1)}, u32[]{:S(2)}, u32[]{:S(2)}) collective-permute-start(bf16[8,4,512]{2,1,0:T(4,128)(2,1)} %param.15), channel_id=1, source_target_pairs={{0,3},{1,0},{2,1},{3,2},{4,7},{5,4},{6,5},{7,6},{8,11},{9,8},{10,9... | collective-permute-start | bytes 98312 | tf_op jit(solution)/shard_map/ppermute | solution.py:73
  5.8 1.0 %collective-permute-start.2 = (bf16[8,4,512]{2,1,0:T(4,128)(2,1)}, bf16[8,4,512]{2,1,0:T(4,128)(2,1)S(1)}, u32[]{:S(2)}, u32[]{:S(2)}) collective-permute-start(bf16[8,4,512]{2,1,0:T(4,128)(2,1)} %param.15), channel_id=1, source_target_pairs={{0,1},{1,2},{2,3},{3,0},{4,5},{5,6},{6,7},{7,4},{8,9},{9,10},{10,1... | collective-permute-start | bytes 98312 | tf_op jit(solution)/shard_map/ppermute | solution.py:73
  6.8 0.9 %fusion.22 = (f32[1,1024]{1,0:T(1,128)S(1)}, f32[1,1024]{1,0:T(1,128)S(1)}, f32[1,1024]{1,0:T(1,128)S(1)}, f32[1,1024]{1,0:T(1,128)S(1)}) fusion(bf16[4,1024]{1,0:T(4,128)(2,1)} %param.19), kind=kLoop, calls=%fused_computation.65 | loop fusion | bytes 32768 | tf_op jit(solution)/shard_map/slice | solution.py:25
  7.9 2.9 %collective-permute-done.1 = bf16[8,4,512]{2,1,0:T(4,128)(2,1)S(1)} collective-permute-done((bf16[8,4,512]{2,1,0:T(4,128)(2,1)}, bf16[8,4,512]{2,1,0:T(4,128)(2,1)S(1)}, u32[]{:S(2)}, u32[]{:S(2)}) %collective-permute-start.1) | collective-permute-done | bytes 32800 | tf_op jit(solution)/shard_map/ppermute | solution.py:73
  10.8 0.9 %collective-permute-done.2 = bf16[8,4,512]{2,1,0:T(4,128)(2,1)S(1)} collective-permute-done((bf16[8,4,512]{2,1,0:T(4,128)(2,1)}, bf16[8,4,512]{2,1,0:T(4,128)(2,1)S(1)}, u32[]{:S(2)}, u32[]{:S(2)}) %collective-permute-start.2) | collective-permute-done | bytes 32800 | tf_op jit(solution)/shard_map/ppermute | solution.py:73
  11.7 0.8 %select_select_fusion.3 = (bf16[4,8,512]{2,1,0:T(8,128)(2,1)S(1)}, bf16[4,8,512]{2,1,0:T(8,128)(2,1)S(1)}, bf16[4,8,512]{2,1,0:T(8,128)(2,1)S(1)}, bf16[4,8,512]{2,1,0:T(8,128)(2,1)S(1)}) fusion(bf16[4,8,512]{2,1,0:T(8,128)(2,1)S(1)} %bitcast.83, bf16[4,8,512]{2,1,0:T(8,128)(2,1)S(1)} %bitcast.84, bf16[4,8,512]{2,1,0:T(8,128)(2,1)S(1)} %bitcast.85, ...), kind=kLoop, calls=%fused_computation.45 | loop fusion | flops 196608 | bytes 262156 | tf_op jit(solution)/shard_map/jit(_where)/select_n | solution.py:206
  12.6 0.7 pad_maximum_fusion.1.x_ref
  13.3 3.7 %shard_map.140 = (f32[32,3088]{1,0:T(8,128)}, f32[32,3088]{1,0:T(8,128)}, f32[32,3088]{1,0:T(8,128)}, f32[32,3088]{1,0:T(8,128)}) custom-call(bf16[128,512]{1,0:T(8,128)(2,1)} %pad_maximum_fusion.1.x_ref, bf16[512,1024]{1,0:T(8,128)(2,1)} %wqk_ref.1, bf16[512,2048]{1,0:T(8,128)(2,1)} %wvz_ref.1, bf16[16,512]{1,0:T(8,128)(2,1)} %bitcast.86), custom_call_target="tpu_custom_call" | custom-call | flops 404750336 | bytes 4874240 | tf_op jit(solution)/shard_map/pallas_call | solution.py:95
  17.0 0.6 collective-permute-start.3
  17.6 1.4 %collective-permute-done.4 = f32[32,3088]{1,0:T(8,128)S(1)} collective-permute-done((f32[32,3088]{1,0:T(8,128)}, f32[32,3088]{1,0:T(8,128)S(1)}, u32[]{:S(2)}, u32[]{:S(2)}) %collective-permute-start.4) | collective-permute-done | bytes 395296 | tf_op jit(solution)/shard_map/ppermute | solution.py:212
  18.9 1.1 %add.185 = f32[32,3088]{1,0:T(8,128)S(1)} add(f32[32,3088]{1,0:T(8,128)} %get-tuple-element.11, f32[32,3088]{1,0:T(8,128)S(1)} %collective-permute-done.4) | non-fusion elementwise | flops 98816 | bytes 1185792 | tf_op jit(solution)/shard_map/add | solution.py:212
  20.0 1.6 %collective-permute-start.6 = (f32[32,1024]{1,0:T(8,128)S(1)}, f32[32,1024]{1,0:T(8,128)S(1)}, u32[]{:S(2)}, u32[]{:S(2)}) collective-permute-start(f32[32,1024]{1,0:T(8,128)S(1)} %slice.131), channel_id=1, source_target_pairs={{0,8},{4,12},{8,0},{12,4},{1,9},{5,13},{9,1},{13,5},{2,10},{6,14},... | collective-permute-start | bytes 393224 | tf_op jit(solution)/shard_map/ppermute | solution.py:217
  21.7 0.1 mul.155
  21.8 0.1 add.189
  21.9 0.6 collective-permute-start.5
  22.5 1.0 %add.184 = f32[32,3088]{1,0:T(8,128)S(1)} add(f32[32,3088]{1,0:T(8,128)} %get-tuple-element.9, f32[32,3088]{1,0:T(8,128)S(1)} %collective-permute-done.3) | non-fusion elementwise | flops 98816 | bytes 1185792 | tf_op jit(solution)/shard_map/add | solution.py:212
  23.6 2.9 %collective-permute-done.6 = f32[32,1024]{1,0:T(8,128)S(1)} collective-permute-done((f32[32,1024]{1,0:T(8,128)S(1)}, f32[32,1024]{1,0:T(8,128)S(1)}, u32[]{:S(2)}, u32[]{:S(2)}) %collective-permute-start.6) | collective-permute-done | bytes 131104 | tf_op jit(solution)/shard_map/ppermute | solution.py:217
  26.6 0.2 divide_multiply_fusion.1
  26.7 0.1 reshape.125
  26.9 0.1 fusion.19
  27.0 0.1 multiply_reduce_fusion.1
  27.1 0.1 multiply_reduce_fusion
  27.2 0.1 fusion.13
  27.3 1.0 %copy.45.kt_ref = f32[8,128,16]{2,1,0:T(8,128)} copy(f32[8,128,16]{1,0,2:T(8,128)S(1)} %bitcast.74) | data formatting | bytes 131072 | tf_op jit(solution)/shard_map/reshape | solution.py:236
  28.3 1.0 %copy.44.qt_ref = f32[8,128,16]{2,1,0:T(8,128)} copy(f32[8,128,16]{1,0,2:T(8,128)S(1)} %bitcast.73) | data formatting | bytes 131072 | tf_op jit(solution)/shard_map/reshape | solution.py:235
  29.3 2.3 %collective-permute-done.5 = f32[32,2064]{1,0:T(8,128)S(1)} collective-permute-done((f32[32,2064]{1,0:T(8,128)S(1)}, f32[32,2064]{1,0:T(8,128)S(1)}, u32[]{:S(2)}, u32[]{:S(2)}) %collective-permute-start.5) | collective-permute-done | bytes 264224 | tf_op jit(solution)/shard_map/ppermute | solution.py:218
  31.7 0.4 fusion.18
  32.2 0.7 reshape.189.z_ref
  33.1 0.1 copy.46
  33.3 0.1 copy.37
  33.5 0.1 squeeze.11
  33.6 0.7 pad_maximum_fusion.2.gates_ref
  34.3 0.8 %divide_multiply_fusion.v_ref = f32[8,4,1024]{2,1,0:T(4,128)} fusion(f32[8,7,1024]{2,1,0:T(8,128)S(1)} %maximum_convert_fusion.1, f32[1024]{0:T(1024)S(1)} %bitcast.94, f32[1024]{0:T(1024)S(1)} %bitcast.93, f32[1024]{0:T(1024)S(1)} %bitcast.92, f32[1024]{0:T(1024)S(1)} %bitcast.91), kind=kLoop, calls=%fused_computation.6 | loop fusion | flops 360448 | bytes 671744 | tf_op jit(solution)/shard_map/jit(silu)/mul | solution.py:26
  35.1 18.6 %shard_map.141 = (f32[8,8,128,128]{3,2,1,0:T(8,128)}, f32[8,4,1024]{2,1,0:T(4,128)}) custom-call(f32[8,64]{1,0:T(8,128)} %pad_maximum_fusion.2.gates_ref, f32[1,128]{1,0:T(1,128)} %bitcast.95, f32[8,128,16]{2,1,0:T(8,128)} %copy.44.qt_ref, f32[8,128,16]{2,1,0:T(8,128)} %copy.45.kt_ref, f32[8,4,1024]{2,1,0:T(4,128)} %divide_multiply_fusion.v_ref, ...), custom_call_target="tpu_custom_call" | custom-call | flops 33554432 | bytes 8388608 | tf_op jit(solution)/shard_map/pallas_call | solution.py:139
  53.7 0.9 %convert_element_type.45 = bf16[8,4,1024]{2,1,0:T(4,128)(2,1)S(1)} convert(f32[8,4,1024]{2,1,0:T(4,128)} %get-tuple-element.13) | non-fusion elementwise | flops 32768 | bytes 196608 | tf_op jit(solution)/shard_map/convert_element_type | solution.py:248
  54.7 1.6 %collective-permute-start.8 = (bf16[8,4,1024]{2,1,0:T(4,128)(2,1)S(1)}, bf16[8,4,1024]{2,1,0:T(4,128)(2,1)S(1)}, u32[]{:S(2)}, u32[]{:S(2)}) collective-permute-start(bf16[8,4,1024]{2,1,0:T(4,128)(2,1)S(1)} %convert_element_type.45), channel_id=1, source_target_pairs={{0,8},{4,12},{8,0},{12,4},{1,9},{5,13},{9,1},{13,5},{2,10},{6,14},... | collective-permute-start | bytes 196616 | tf_op jit(solution)/shard_map/ppermute | solution.py:34
  56.3 1.4 %collective-permute-start.9 = (bf16[8,4,1024]{2,1,0:T(4,128)(2,1)S(1)}, bf16[8,4,1024]{2,1,0:T(4,128)(2,1)S(1)}, u32[]{:S(2)}, u32[]{:S(2)}) collective-permute-start(bf16[8,4,1024]{2,1,0:T(4,128)(2,1)S(1)} %convert_element_type.45), channel_id=1, source_target_pairs={{0,12},{4,0},{8,4},{12,8},{1,13},{5,1},{9,5},{13,9},{2,14},{6,2},{... | collective-permute-start | bytes 196616 | tf_op jit(solution)/shard_map/ppermute | solution.py:34
  57.7 0.9 %convert_bitcast_fusion = bf16[1,8,4,1024]{3,2,1,0:T(4,128)(2,1)S(1)} fusion(f32[8,4,1024]{2,1,0:T(4,128)} %get-tuple-element.13), kind=kLoop, calls=%fused_computation.66 | loop fusion | flops 32768 | bytes 196608 | tf_op jit(solution)/shard_map/stack | solution.py:35
  58.6 0.7 %collective-permute-done.8 = bf16[8,4,1024]{2,1,0:T(4,128)(2,1)S(1)} collective-permute-done((bf16[8,4,1024]{2,1,0:T(4,128)(2,1)S(1)}, bf16[8,4,1024]{2,1,0:T(4,128)(2,1)S(1)}, u32[]{:S(2)}, u32[]{:S(2)}) %collective-permute-start.8) | collective-permute-done | bytes 65568 | tf_op jit(solution)/shard_map/ppermute | solution.py:34
  59.4 0.2 collective-permute-done.9
  59.6 0.2 pad_maximum_fusion
  59.8 0.8 %gather_fusion = bf16[4,8,4,1024]{3,2,1,0:T(4,128)(2,1)S(1)} fusion(bf16[4,8,4,1024]{3,2,1,0:T(4,128)(2,1)S(1)} %pad_maximum_fusion, s32[1024]{0:T(1024)S(1)} %pad_clamp_fusion), kind=kCustom, calls=%fused_computation | custom fusion | bytes 524304 | tf_op jit(solution)/shard_map/jit(_take)/gather | solution.py:37
  60.7 0.3 fusion
  61.1 1.2 %collective-permute-start.11 = (f32[32,512]{1,0:T(8,128)S(1)}, f32[32,512]{1,0:T(8,128)S(1)}, u32[]{:S(2)}, u32[]{:S(2)}) collective-permute-start(f32[32,512]{1,0:T(8,128)S(1)} %get-tuple-element.28), channel_id=1, source_target_pairs={{0,2},{1,3},{2,0},{3,1},{4,6},{5,7},{6,4},{7,5},{8,10},{9,11},{10,... | collective-permute-start | bytes 196616 | tf_op jit(solution)/shard_map/ppermute | solution.py:47
  62.3 2.8 %collective-permute-start.12 = (f32[32,512]{1,0:T(8,128)S(1)}, f32[32,512]{1,0:T(8,128)S(1)}, u32[]{:S(2)}, u32[]{:S(2)}) collective-permute-start(f32[32,512]{1,0:T(8,128)S(1)} %get-tuple-element.27), channel_id=1, source_target_pairs={{0,3},{1,0},{2,1},{3,2},{4,7},{5,4},{6,5},{7,6},{8,11},{9,8},{10,9... | collective-permute-start | bytes 196616 | tf_op jit(solution)/shard_map/ppermute | solution.py:47
  65.1 2.8 %collective-permute-done.10 = f32[32,512]{1,0:T(8,128)S(1)} collective-permute-done((f32[32,512]{1,0:T(8,128)S(1)}, f32[32,512]{1,0:T(8,128)S(1)}, u32[]{:S(2)}, u32[]{:S(2)}) %collective-permute-start.10) | collective-permute-done | bytes 65568 | tf_op jit(solution)/shard_map/ppermute | solution.py:47
  68.0 1.9 %collective-permute-done.11 = f32[32,512]{1,0:T(8,128)S(1)} collective-permute-done((f32[32,512]{1,0:T(8,128)S(1)}, f32[32,512]{1,0:T(8,128)S(1)}, u32[]{:S(2)}, u32[]{:S(2)}) %collective-permute-start.11) | collective-permute-done | bytes 65568 | tf_op jit(solution)/shard_map/ppermute | solution.py:47
  69.9 0.6 reshape.128
  (56 shorter events, 1.1 us)
Async XLA Ops:
  0.6 60.1 %copy-start = (bf16[1024,512]{1,0:T(8,128)(2,1)S(1)}, bf16[1024,512]{1,0:T(8,128)(2,1)}, u32[]{:S(2)}) copy-start(bf16[1024,512]{1,0:T(8,128)(2,1)} %param.24) | copy-start | bytes 3145732
  0.6 16.3 %copy-start.3 = (bf16[4,1024]{1,0:T(4,128)(2,1)S(1)}, bf16[4,1024]{1,0:T(4,128)(2,1)}, u32[]{:S(2)}) copy-start(bf16[4,1024]{1,0:T(4,128)(2,1)} %param.20) | copy-start | bytes 24580
  0.7 16.9 %copy-start.5 = (f32[8]{0:T(128)S(1)}, f32[8]{0:T(128)}, u32[]{:S(2)}) copy-start(f32[8]{0:T(128)} %param.21) | copy-start | bytes 100
  0.7 20.9 %copy-start.1 = (bf16[8,3,1024]{2,0,1:T(8,128)(2,1)S(1)}, bf16[8,3,1024]{2,0,1:T(8,128)(2,1)}, u32[]{:S(2)}) copy-start(bf16[8,3,1024]{2,0,1:T(8,128)(2,1)} %param.25) | copy-start | bytes 147460
  0.7 21.0 %copy-start.2 = (bf16[8,3,1024]{2,0,1:T(8,128)(2,1)S(1)}, bf16[8,3,1024]{2,0,1:T(8,128)(2,1)}, u32[]{:S(2)}) copy-start(bf16[8,3,1024]{2,0,1:T(8,128)(2,1)} %param.26) | copy-start | bytes 147460
  0.7 21.1 %copy-start.4 = (f32[8]{0:T(128)S(1)}, f32[8]{0:T(128)}, u32[]{:S(2)}) copy-start(f32[8]{0:T(128)} %param.22) | copy-start | bytes 100
  0.7 7.2 %collective-permute-start = (bf16[8,4,512]{2,1,0:T(4,128)(2,1)}, bf16[8,4,512]{2,1,0:T(4,128)(2,1)S(1)}, u32[]{:S(2)}, u32[]{:S(2)}) collective-permute-start(bf16[8,4,512]{2,1,0:T(4,128)(2,1)} %param.15), channel_id=1, source_target_pairs={{0,3},{1,0},{2,1},{3,2},{4,7},{5,4},{6,5},{7,6},{8,11},{9,8},{10,9... | collective-permute-start | bytes 98312 | tf_op jit(solution)/shard_map/ppermute | solution.py:73
  5.8 5.0 %collective-permute-start.1 = (bf16[8,4,512]{2,1,0:T(4,128)(2,1)}, bf16[8,4,512]{2,1,0:T(4,128)(2,1)S(1)}, u32[]{:S(2)}, u32[]{:S(2)}) collective-permute-start(bf16[8,4,512]{2,1,0:T(4,128)(2,1)} %param.15), channel_id=1, source_target_pairs={{0,2},{1,3},{2,0},{3,1},{4,6},{5,7},{6,4},{7,5},{8,10},{9,11},{10,... | collective-permute-start | bytes 98312 | tf_op jit(solution)/shard_map/ppermute | solution.py:73
  5.8 5.9 %collective-permute-start.2 = (bf16[8,4,512]{2,1,0:T(4,128)(2,1)}, bf16[8,4,512]{2,1,0:T(4,128)(2,1)S(1)}, u32[]{:S(2)}, u32[]{:S(2)}) collective-permute-start(bf16[8,4,512]{2,1,0:T(4,128)(2,1)} %param.15), channel_id=1, source_target_pairs={{0,1},{1,2},{2,3},{3,0},{4,5},{5,6},{6,7},{7,4},{8,9},{9,10},{10,1... | collective-permute-start | bytes 98312 | tf_op jit(solution)/shard_map/ppermute | solution.py:73
  17.0 2.0 %collective-permute-start.4 = (f32[32,3088]{1,0:T(8,128)}, f32[32,3088]{1,0:T(8,128)S(1)}, u32[]{:S(2)}, u32[]{:S(2)}) collective-permute-start(f32[32,3088]{1,0:T(8,128)} %get-tuple-element.12), channel_id=1, source_target_pairs={{0,4},{4,0},{8,12},{12,8},{1,5},{5,1},{9,13},{13,9},{2,6},{6,2},{1... | collective-permute-start | bytes 1185800 | tf_op jit(solution)/shard_map/ppermute | solution.py:212
  17.0 5.5 %collective-permute-start.3 = (f32[32,3088]{1,0:T(8,128)}, f32[32,3088]{1,0:T(8,128)S(1)}, u32[]{:S(2)}, u32[]{:S(2)}) collective-permute-start(f32[32,3088]{1,0:T(8,128)} %get-tuple-element.10), channel_id=1, source_target_pairs={{0,4},{4,0},{8,12},{12,8},{1,5},{5,1},{9,13},{13,9},{2,6},{6,2},{1... | collective-permute-start | bytes 1185800 | tf_op jit(solution)/shard_map/ppermute | solution.py:212
  20.0 6.4 %collective-permute-start.6 = (f32[32,1024]{1,0:T(8,128)S(1)}, f32[32,1024]{1,0:T(8,128)S(1)}, u32[]{:S(2)}, u32[]{:S(2)}) collective-permute-start(f32[32,1024]{1,0:T(8,128)S(1)} %slice.131), channel_id=1, source_target_pairs={{0,8},{4,12},{8,0},{12,4},{1,9},{5,13},{9,1},{13,5},{2,10},{6,14},... | collective-permute-start | bytes 393224 | tf_op jit(solution)/shard_map/ppermute | solution.py:217
  21.9 9.7 %collective-permute-start.5 = (f32[32,2064]{1,0:T(8,128)S(1)}, f32[32,2064]{1,0:T(8,128)S(1)}, u32[]{:S(2)}, u32[]{:S(2)}) collective-permute-start(f32[32,2064]{1,0:T(8,128)S(1)} %slice.126), channel_id=1, source_target_pairs={{0,8},{4,12},{8,0},{12,4},{1,9},{5,13},{9,1},{13,5},{2,10},{6,14},... | collective-permute-start | bytes 792584 | tf_op jit(solution)/shard_map/ppermute | solution.py:218
  54.7 3.9 %collective-permute-start.7 = (bf16[8,4,1024]{2,1,0:T(4,128)(2,1)S(1)}, bf16[8,4,1024]{2,1,0:T(4,128)(2,1)S(1)}, u32[]{:S(2)}, u32[]{:S(2)}) collective-permute-start(bf16[8,4,1024]{2,1,0:T(4,128)(2,1)S(1)} %convert_element_type.45), channel_id=1, source_target_pairs={{0,4},{4,8},{8,12},{12,0},{1,5},{5,9},{9,13},{13,1},{2,6},{6,10},{... | collective-permute-start | bytes 196616 | tf_op jit(solution)/shard_map/ppermute | solution.py:34
  54.7 4.6 %collective-permute-start.8 = (bf16[8,4,1024]{2,1,0:T(4,128)(2,1)S(1)}, bf16[8,4,1024]{2,1,0:T(4,128)(2,1)S(1)}, u32[]{:S(2)}, u32[]{:S(2)}) collective-permute-start(bf16[8,4,1024]{2,1,0:T(4,128)(2,1)S(1)} %convert_element_type.45), channel_id=1, source_target_pairs={{0,8},{4,12},{8,0},{12,4},{1,9},{5,13},{9,1},{13,5},{2,10},{6,14},... | collective-permute-start | bytes 196616 | tf_op jit(solution)/shard_map/ppermute | solution.py:34
  56.3 3.3 %collective-permute-start.9 = (bf16[8,4,1024]{2,1,0:T(4,128)(2,1)S(1)}, bf16[8,4,1024]{2,1,0:T(4,128)(2,1)S(1)}, u32[]{:S(2)}, u32[]{:S(2)}) collective-permute-start(bf16[8,4,1024]{2,1,0:T(4,128)(2,1)S(1)} %convert_element_type.45), channel_id=1, source_target_pairs={{0,12},{4,0},{8,4},{12,8},{1,13},{5,1},{9,5},{13,9},{2,14},{6,2},{... | collective-permute-start | bytes 196616 | tf_op jit(solution)/shard_map/ppermute | solution.py:34
  61.0 6.9 %collective-permute-start.10 = (f32[32,512]{1,0:T(8,128)S(1)}, f32[32,512]{1,0:T(8,128)S(1)}, u32[]{:S(2)}, u32[]{:S(2)}) collective-permute-start(f32[32,512]{1,0:T(8,128)S(1)} %get-tuple-element.26), channel_id=1, source_target_pairs={{0,1},{1,2},{2,3},{3,0},{4,5},{5,6},{6,7},{7,4},{8,9},{9,10},{10,1... | collective-permute-start | bytes 196616 | tf_op jit(solution)/shard_map/ppermute | solution.py:47
  61.1 8.7 %collective-permute-start.11 = (f32[32,512]{1,0:T(8,128)S(1)}, f32[32,512]{1,0:T(8,128)S(1)}, u32[]{:S(2)}, u32[]{:S(2)}) collective-permute-start(f32[32,512]{1,0:T(8,128)S(1)} %get-tuple-element.28), channel_id=1, source_target_pairs={{0,2},{1,3},{2,0},{3,1},{4,6},{5,7},{6,4},{7,5},{8,10},{9,11},{10,... | collective-permute-start | bytes 196616 | tf_op jit(solution)/shard_map/ppermute | solution.py:47
  62.3 7.6 %collective-permute-start.12 = (f32[32,512]{1,0:T(8,128)S(1)}, f32[32,512]{1,0:T(8,128)S(1)}, u32[]{:S(2)}, u32[]{:S(2)}) collective-permute-start(f32[32,512]{1,0:T(8,128)S(1)} %get-tuple-element.27), channel_id=1, source_target_pairs={{0,3},{1,0},{2,1},{3,2},{4,7},{5,4},{6,5},{7,6},{8,11},{9,8},{10,9... | collective-permute-start | bytes 196616 | tf_op jit(solution)/shard_map/ppermute | solution.py:47

commit v12 on v9

--- a/solution.py
+++ b/solution.py
@@ -121,7 +121,7 @@
                 recalled = jnp.sum(key_col * state, axis=0, keepdims=True)
                 correction = (v_ref[0, t : t + 1, lanes] - recalled) * gates_ref[r, c]
                 state = state + key_col * correction
-                o_ref[0, t : t + 1, lanes] = jnp.sum(query_col * state, axis=0, keepdims=True)
+                o_ref[0, t, h : h + 1, :] = jnp.sum(query_col * state, axis=0, keepdims=True)
                 states[j] = state
         for j, h in enumerate(group):
             s_out[0, h] = states[j]
@@ -145,11 +145,11 @@
         ],
         out_specs=[
             pl.BlockSpec((1, heads, DK, DV), lambda r: (r, 0, 0, 0)),
-            pl.BlockSpec((1, steps, heads * DV), lambda r: (r, 0, 0)),
+            pl.BlockSpec((1, steps, heads, DV), lambda r: (r, 0, 0, 0)),
         ],
         out_shape=[
             jax.ShapeDtypeStruct(memory_state.shape, jnp.float32),
-            jax.ShapeDtypeStruct((rows, steps, heads * DV), jnp.float32),
+            jax.ShapeDtypeStruct((rows, steps, heads, DV), jnp.float32),
         ],
         cost_estimate=pl.CostEstimate(
             flops=8 * rows * heads * steps * DK * DV,
@@ -238,16 +238,18 @@
     )
 
     new_state, readout = recurrence(gates, qt, kt, v_conv, memory_state)
-    readout = readout.reshape(rows_mem, step_count, heads, DV)
 
     scale = lax.rsqrt(jnp.mean(readout * readout, axis=-1, keepdims=True) + 1e-06)
     normed = readout * scale * norm_gain[None, None, None, :] * jax.nn.silu(gate_z)
-    normed = normed.reshape(rows_mem, step_count, heads * DV).astype(jnp.bfloat16)
+    normed = normed.astype(jnp.bfloat16)
 
     all_normed = gather_rows(normed, "dp")
-    partials = jnp.dot(
-        all_normed.reshape(-1, all_normed.shape[-1]), w_out, preferred_element_type=jnp.float32
-    )
+    partials = jnp.einsum(
+        "rthd,hde->rte",
+        all_normed,
+        w_out.reshape(heads, DV, -1),
+        preferred_element_type=jnp.float32,
+    ).reshape(-1, w_out.shape[1])
     layer_out = scatter_sum_rows(partials, "head")
     layer_out = layer_out.astype(jnp.bfloat16).reshape(-1, step_count, w_out.shape[1])
     return (layer_out, new_state)

time: 62.9 us -> 62.3 us (level)
  starting transfers between devices: 13.8 us -> 15.9 us
  local copies, waits for them, and re-layouts: 6.41 us -> 5.07 us
  waiting for transfers between devices: 18.7 us -> 18 us
    ppermute x3, waiting for transfers between devices: 4.1 us -> 1.9 us  [gather_rows(): pieces.append(lax.ppermute(x, axis, [(i, (i + s) % n) for i in range(n)]))]
    ppermute x3, starting transfers between devices: 1.79 us -> 3.01 us  [gather_rows(): pieces.append(lax.ppermute(x, axis, [(i, (i + s) % n) for i in range(n)]))]
    ppermute x3, waiting for transfers between devices: 3.81 us -> 4.91 us  [gather_pieces(): pieces.append(lax.ppermute(x, axis, [(i, (i + s) % n) for i in range(n)]))]
    mul x1 -> x0, other arithmetic: 1.02 us -> none  [shards(): readout * readout]
    reduce_sum x1, other arithmetic: 0.12 us -> 1.01 us  [shards(): jnp.mean(readout * readout, axis=-1, keepdims=True) + 1e-06]
    ppermute x3, starting transfers between devices: 3.21 us -> 4.09 us  [scatter_sum_rows(): acc = acc + lax.ppermute(send, axis, [(i, (i + s) % n) for i in range(n)])]
    slice x2, local copies, waits for them, and re-layouts: 0.87 us -> 0.03 us  [conv_steps(): taps[k][None, None, :]]
  transfers between devices with their start and end apart: 13 -> 13, of which waited for: 10 -> 11; matrix products, arithmetic and copies ran while one was open for 10% -> 9% of each run, Pallas kernels for 0% -> 0%
where the time goes in v12:
time: 62.3 us; the launch traced here: 61.8 us
  waiting for transfers between devices  18 us (29%)
  starting transfers between devices  15.9 us (26%)
  Pallas kernels  13.6 us (22%)
  other arithmetic  7.9 us (13%)
  local copies, waits for them, and re-layouts  5.07 us (8%)
  between operations  1.02 us (2%)
    pallas_call x1, Pallas kernels, recurrence(): pl.pallas_call(kern, grid=(rows,), in_specs=[pl.BlockSpec(memory_space=pl...  9.9 us
    ppermute x3, starting transfers between devices, gather_pieces(): pieces.append(lax.ppermute(x, axis, [(i, (i + s) % n) for i in range(n)]))  6.11 us
    ppermute x3, waiting for transfers between devices, gather_pieces(): pieces.append(lax.ppermute(x, axis, [(i, (i + s) % n) for i in range(n)]))  4.91 us
    ppermute x3, waiting for transfers between devices, scatter_sum_rows(): acc = acc + lax.ppermute(send, axis, [(i, (i + s) % n) for i in range(n)])  4.71 us
    ppermute x3, starting transfers between devices, scatter_sum_rows(): acc = acc + lax.ppermute(send, axis, [(i, (i + s) % n) for i in range(n)])  4.09 us
    pallas_call x1, Pallas kernels, projection(): pl.pallas_call(projection_kernel, out_shape=[jax.ShapeDtypeStruct((rows,...  3.72 us
    ppermute x3, starting transfers between devices, gather_rows(): pieces.append(lax.ppermute(x, axis, [(i, (i + s) % n) for i in range(n)]))  3.01 us
    ppermute x1, waiting for transfers between devices, shards(): summed_qk = summed_qk + lax.ppermute(part[s][:, :width_qk], 'dp', perm)  2.85 us
  transfers between devices with their start and end apart: 13, of which 11 were waited for; matrix products, arithmetic and copies ran while one was open for 9% of the time, Pallas kernels for 0%

profile of v12, /device:TPU:0, one launch (start us, length us, event | category | flops | bytes accessed | tf_op | source)
XLA Modules:
  0.0 61.8 jit_solution(15775277369488591071)
XLA Ops:
  0.7 5.1 %collective-permute-start = (bf16[8,4,512]{2,1,0:T(4,128)(2,1)}, bf16[8,4,512]{2,1,0:T(4,128)(2,1)S(1)}, u32[]{:S(2)}, u32[]{:S(2)}) collective-permute-start(bf16[8,4,512]{2,1,0:T(4,128)(2,1)} %param.15), channel_id=1, source_target_pairs={{0,3},{1,0},{2,1},{3,2},{4,7},{5,4},{6,5},{7,6},{8,11},{9,8},{10,9... | collective-permute-start | bytes 98312 | tf_op jit(solution)/shard_map/ppermute | solution.py:73
  5.8 1.0 %collective-permute-start.2 = (bf16[8,4,512]{2,1,0:T(4,128)(2,1)}, bf16[8,4,512]{2,1,0:T(4,128)(2,1)S(1)}, u32[]{:S(2)}, u32[]{:S(2)}) collective-permute-start(bf16[8,4,512]{2,1,0:T(4,128)(2,1)} %param.15), channel_id=1, source_target_pairs={{0,1},{1,2},{2,3},{3,0},{4,5},{5,6},{6,7},{7,4},{8,9},{9,10},{10,1... | collective-permute-start | bytes 98312 | tf_op jit(solution)/shard_map/ppermute | solution.py:73
  6.8 0.9 %collective-permute-done = bf16[8,4,512]{2,1,0:T(4,128)(2,1)S(1)} collective-permute-done((bf16[8,4,512]{2,1,0:T(4,128)(2,1)}, bf16[8,4,512]{2,1,0:T(4,128)(2,1)S(1)}, u32[]{:S(2)}, u32[]{:S(2)}) %collective-permute-start) | collective-permute-done | bytes 32800 | tf_op jit(solution)/shard_map/ppermute | solution.py:73
  7.7 3.1 %collective-permute-done.1 = bf16[8,4,512]{2,1,0:T(4,128)(2,1)S(1)} collective-permute-done((bf16[8,4,512]{2,1,0:T(4,128)(2,1)}, bf16[8,4,512]{2,1,0:T(4,128)(2,1)S(1)}, u32[]{:S(2)}, u32[]{:S(2)}) %collective-permute-start.1) | collective-permute-done | bytes 32800 | tf_op jit(solution)/shard_map/ppermute | solution.py:73
  10.8 0.9 %collective-permute-done.2 = bf16[8,4,512]{2,1,0:T(4,128)(2,1)S(1)} collective-permute-done((bf16[8,4,512]{2,1,0:T(4,128)(2,1)}, bf16[8,4,512]{2,1,0:T(4,128)(2,1)S(1)}, u32[]{:S(2)}, u32[]{:S(2)}) %collective-permute-start.2) | collective-permute-done | bytes 32800 | tf_op jit(solution)/shard_map/ppermute | solution.py:73
  11.7 0.8 %select_select_fusion.3 = (bf16[4,8,512]{2,1,0:T(8,128)(2,1)S(1)}, bf16[4,8,512]{2,1,0:T(8,128)(2,1)S(1)}, bf16[4,8,512]{2,1,0:T(8,128)(2,1)S(1)}, bf16[4,8,512]{2,1,0:T(8,128)(2,1)S(1)}) fusion(bf16[4,8,512]{2,1,0:T(8,128)(2,1)S(1)} %bitcast.93, bf16[4,8,512]{2,1,0:T(8,128)(2,1)S(1)} %bitcast.94, bf16[4,8,512]{2,1,0:T(8,128)(2,1)S(1)} %bitcast.95, ...), kind=kLoop, calls=%fused_computation.53 | loop fusion | flops 196608 | bytes 262156 | tf_op jit(solution)/shard_map/jit(_where)/select_n | solution.py:201
  12.6 0.7 %pad_maximum_fusion.1.x_ref = bf16[128,512]{1,0:T(8,128)(2,1)} fusion(bf16[32,512]{1,0:T(8,128)(2,1)S(1)} %reshape.130, bf16[32,512]{1,0:T(8,128)(2,1)S(1)} %reshape.129, bf16[32,512]{1,0:T(8,128)(2,1)S(1)} %reshape.128, bf16[32,512]{1,0:T(8,128)(2,1)S(1)} %reshape.127), kind=kLoop, calls=%fused_computation.31 | loop fusion | flops 524288 | bytes 262144 | tf_op jit(solution)/shard_map/concatenate | solution.py:204
  13.3 3.7 %shard_map.140 = (f32[32,3088]{1,0:T(8,128)}, f32[32,3088]{1,0:T(8,128)}, f32[32,3088]{1,0:T(8,128)}, f32[32,3088]{1,0:T(8,128)}) custom-call(bf16[128,512]{1,0:T(8,128)(2,1)} %pad_maximum_fusion.1.x_ref, bf16[512,1024]{1,0:T(8,128)(2,1)} %wqk_ref.1, bf16[512,2048]{1,0:T(8,128)(2,1)} %wvz_ref.1, bf16[16,512]{1,0:T(8,128)(2,1)} %bitcast.96), custom_call_target="tpu_custom_call" | custom-call | flops 404750336 | bytes 4874240 | tf_op jit(solution)/shard_map/pallas_call | solution.py:95
  17.0 0.6 collective-permute-start.3
  17.6 1.3 %collective-permute-done.4 = f32[32,3088]{1,0:T(8,128)S(1)} collective-permute-done((f32[32,3088]{1,0:T(8,128)}, f32[32,3088]{1,0:T(8,128)S(1)}, u32[]{:S(2)}, u32[]{:S(2)}) %collective-permute-start.4) | collective-permute-done | bytes 395296 | tf_op jit(solution)/shard_map/ppermute | solution.py:207
  18.9 1.1 %add.200 = f32[32,3088]{1,0:T(8,128)S(1)} add(f32[32,3088]{1,0:T(8,128)} %get-tuple-element.11, f32[32,3088]{1,0:T(8,128)S(1)} %collective-permute-done.4) | non-fusion elementwise | flops 98816 | bytes 1185792 | tf_op jit(solution)/shard_map/add | solution.py:207
  20.0 1.6 %collective-permute-start.6 = (f32[32,1024]{1,0:T(8,128)S(1)}, f32[32,1024]{1,0:T(8,128)S(1)}, u32[]{:S(2)}, u32[]{:S(2)}) collective-permute-start(f32[32,1024]{1,0:T(8,128)S(1)} %slice.131), channel_id=1, source_target_pairs={{0,8},{4,12},{8,0},{12,4},{1,9},{5,13},{9,1},{13,5},{2,10},{6,14},... | collective-permute-start | bytes 393224 | tf_op jit(solution)/shard_map/ppermute | solution.py:212
  21.7 0.1 mul.181
  21.8 0.1 add.204
  21.9 0.6 collective-permute-start.5
  22.5 1.0 %add.199 = f32[32,3088]{1,0:T(8,128)S(1)} add(f32[32,3088]{1,0:T(8,128)} %get-tuple-element.9, f32[32,3088]{1,0:T(8,128)S(1)} %collective-permute-done.3) | non-fusion elementwise | flops 98816 | bytes 1185792 | tf_op jit(solution)/shard_map/add | solution.py:207
  23.6 2.8 %collective-permute-done.6 = f32[32,1024]{1,0:T(8,128)S(1)} collective-permute-done((f32[32,1024]{1,0:T(8,128)S(1)}, f32[32,1024]{1,0:T(8,128)S(1)}, u32[]{:S(2)}, u32[]{:S(2)}) %collective-permute-start.6) | collective-permute-done | bytes 131104 | tf_op jit(solution)/shard_map/ppermute | solution.py:212
  26.6 0.2 divide_multiply_fusion.1
  26.7 0.1 reshape.132
  26.9 0.1 fusion.23
  27.0 0.1 multiply_reduce_fusion.2
  27.1 0.1 multiply_reduce_fusion.1
  27.2 0.1 fusion.17
  27.3 1.0 %copy.56.kt_ref = f32[8,128,16]{2,1,0:T(8,128)} copy(f32[8,128,16]{1,0,2:T(8,128)S(1)} %bitcast.83) | data formatting | bytes 131072 | tf_op jit(solution)/shard_map/reshape | solution.py:231
  28.3 1.0 %copy.55.qt_ref = f32[8,128,16]{2,1,0:T(8,128)} copy(f32[8,128,16]{1,0,2:T(8,128)S(1)} %bitcast.82) | data formatting | bytes 131072 | tf_op jit(solution)/shard_map/reshape | solution.py:230
  29.4 2.2 %collective-permute-done.5 = f32[32,2064]{1,0:T(8,128)S(1)} collective-permute-done((f32[32,2064]{1,0:T(8,128)S(1)}, f32[32,2064]{1,0:T(8,128)S(1)}, u32[]{:S(2)}, u32[]{:S(2)}) %collective-permute-start.5) | collective-permute-done | bytes 264224 | tf_op jit(solution)/shard_map/ppermute | solution.py:213
  31.8 0.4 fusion.22
  32.3 0.1 reshape.197
  32.4 0.1 copy.61
  32.6 0.1 copy.48
  32.8 0.1 squeeze.11
  33.0 0.7 %pad_maximum_fusion.2.gates_ref = f32[8,64]{1,0:T(8,128)} fusion(f32[8,32]{1,0:T(8,128)S(1)} %fusion.19, f32[8,32]{1,0:T(8,128)S(1)} %div.76), kind=kLoop, calls=%fused_computation.63 | loop fusion | flops 512 | bytes 4096 | tf_op jit(solution)/shard_map/concatenate | solution.py:236
  33.6 0.8 %divide_multiply_fusion.v_ref = f32[8,4,1024]{2,1,0:T(4,128)} fusion(f32[8,7,1024]{2,1,0:T(8,128)S(1)} %maximum_convert_fusion.1, f32[1024]{0:T(1024)S(1)} %bitcast.100, f32[1024]{0:T(1024)S(1)} %bitcast.99, f32[1024]{0:T(1024)S(1)} %bitcast.98, f32[1024]{0:T(1024)S(1)} %bitcast.97), kind=kLoop, calls=%fused_computation.8 | loop fusion | flops 360448 | bytes 671744 | tf_op jit(solution)/shard_map/jit(silu)/mul | solution.py:26
  34.5 9.9 %shard_map.141 = (f32[8,8,128,128]{3,2,1,0:T(8,128)}, f32[8,4,8,128]{3,2,1,0:T(8,128)}) custom-call(f32[8,64]{1,0:T(8,128)} %pad_maximum_fusion.2.gates_ref, f32[8,128,16]{2,1,0:T(8,128)} %copy.55.qt_ref, f32[8,128,16]{2,1,0:T(8,128)} %copy.56.kt_ref, f32[8,4,1024]{2,1,0:T(4,128)} %divide_multiply_fusion.v_ref, f32[8,8,128,128]{3,2,1,0:T(8,128)} %s_ref.1), custom_call_target="tpu_custom_call" | custom-call | flops 33554432 | bytes 8388608 | tf_op jit(solution)/shard_map/pallas_call | solution.py:136
  44.4 1.0 %multiply_reduce_fusion = f32[8,4,8]{2,1,0:T(4,128)S(1)} fusion(f32[8,4,8,128]{3,2,1,0:T(8,128)} %get-tuple-element.13), kind=kLoop, calls=%fused_computation.34 | loop fusion | flops 65280 | bytes 132096 | tf_op jit(solution)/shard_map/reduce_sum | solution.py:242
  45.4 1.0 %fusion.13 = bf16[8,4,8,128]{3,2,1,0:T(8,128)(2,1)S(1)} fusion(f32[8,4,8,128]{3,2,1,0:T(8,128)} %get-tuple-element.13, bf16[8,4,8,1,128]{4,3,2,1,0:T(2,128)(2,1)S(1)} %get-tuple-element.29, f32[128]{0:T(128)S(1)} %copy-done.5, f32[8,4,8]{2,1,0:T(4,128)S(1)} %add_rsqrt_fusion), kind=kLoop, calls=%fused_computation.35 | loop fusion | flops 294912 | bytes 263680 | tf_op jit(solution)/shard_map/convert_element_type | solution.py:244
  46.5 1.6 %collective-permute-start.8 = (bf16[8,4,8,128]{3,2,1,0:T(8,128)(2,1)S(1)}, bf16[8,4,8,128]{3,2,1,0:T(8,128)(2,1)S(1)}, u32[]{:S(2)}, u32[]{:S(2)}) collective-permute-start(bf16[8,4,8,128]{3,2,1,0:T(8,128)(2,1)S(1)} %fusion.13), channel_id=1, source_target_pairs={{0,8},{4,12},{8,0},{12,4},{1,9},{5,13},{9,1},{13,5},{2,10},{6,14},... | collective-permute-start | bytes 196616 | tf_op jit(solution)/shard_map/ppermute | solution.py:34
  48.1 1.4 %collective-permute-start.9 = (bf16[8,4,8,128]{3,2,1,0:T(8,128)(2,1)S(1)}, bf16[8,4,8,128]{3,2,1,0:T(8,128)(2,1)S(1)}, u32[]{:S(2)}, u32[]{:S(2)}) collective-permute-start(bf16[8,4,8,128]{3,2,1,0:T(8,128)(2,1)S(1)} %fusion.13), channel_id=1, source_target_pairs={{0,12},{4,0},{8,4},{12,8},{1,13},{5,1},{9,5},{13,9},{2,14},{6,2},{... | collective-permute-start | bytes 196616 | tf_op jit(solution)/shard_map/ppermute | solution.py:34
  49.4 0.8 %collective-permute-done.7 = bf16[8,4,8,128]{3,2,1,0:T(8,128)(2,1)S(1)} collective-permute-done((bf16[8,4,8,128]{3,2,1,0:T(8,128)(2,1)S(1)}, bf16[8,4,8,128]{3,2,1,0:T(8,128)(2,1)S(1)}, u32[]{:S(2)}, u32[]{:S(2)}) %collective-permute-start.7) | collective-permute-done | bytes 65568 | tf_op jit(solution)/shard_map/ppermute | solution.py:34
  50.3 0.9 %collective-permute-done.8 = bf16[8,4,8,128]{3,2,1,0:T(8,128)(2,1)S(1)} collective-permute-done((bf16[8,4,8,128]{3,2,1,0:T(8,128)(2,1)S(1)}, bf16[8,4,8,128]{3,2,1,0:T(8,128)(2,1)S(1)}, u32[]{:S(2)}, u32[]{:S(2)}) %collective-permute-start.8) | collective-permute-done | bytes 65568 | tf_op jit(solution)/shard_map/ppermute | solution.py:34
  51.1 0.2 collective-permute-done.9
  51.4 0.6 gather_fusion
  52.0 0.3 convolution_bitcast_fusion
  52.4 1.2 %collective-permute-start.11 = (f32[32,512]{1,0:T(8,128)S(1)}, f32[32,512]{1,0:T(8,128)S(1)}, u32[]{:S(2)}, u32[]{:S(2)}) collective-permute-start(f32[32,512]{1,0:T(8,128)S(1)} %get-tuple-element.28), channel_id=1, source_target_pairs={{0,2},{1,3},{2,0},{3,1},{4,6},{5,7},{6,4},{7,5},{8,10},{9,11},{10,... | collective-permute-start | bytes 196616 | tf_op jit(solution)/shard_map/ppermute | solution.py:47
  53.6 2.8 %collective-permute-start.12 = (f32[32,512]{1,0:T(8,128)S(1)}, f32[32,512]{1,0:T(8,128)S(1)}, u32[]{:S(2)}, u32[]{:S(2)}) collective-permute-start(f32[32,512]{1,0:T(8,128)S(1)} %get-tuple-element.27), channel_id=1, source_target_pairs={{0,3},{1,0},{2,1},{3,2},{4,7},{5,4},{6,5},{7,6},{8,11},{9,8},{10,9... | collective-permute-start | bytes 196616 | tf_op jit(solution)/shard_map/ppermute | solution.py:47
  56.4 2.8 %collective-permute-done.10 = f32[32,512]{1,0:T(8,128)S(1)} collective-permute-done((f32[32,512]{1,0:T(8,128)S(1)}, f32[32,512]{1,0:T(8,128)S(1)}, u32[]{:S(2)}, u32[]{:S(2)}) %collective-permute-start.10) | collective-permute-done | bytes 65568 | tf_op jit(solution)/shard_map/ppermute | solution.py:47
  59.3 1.9 %collective-permute-done.11 = f32[32,512]{1,0:T(8,128)S(1)} collective-permute-done((f32[32,512]{1,0:T(8,128)S(1)}, f32[32,512]{1,0:T(8,128)S(1)}, u32[]{:S(2)}, u32[]{:S(2)}) %collective-permute-start.11) | collective-permute-done | bytes 65568 | tf_op jit(solution)/shard_map/ppermute | solution.py:47
  61.2 0.6 %reshape.137 = bf16[8,4,512]{2,1,0:T(4,128)(2,1)} reshape(bf16[32,512]{1,0:T(8,128)(2,1)S(1)} %fusion.16) | data formatting | bytes 65536 | tf_op jit(solution)/shard_map/reshape | solution.py:254
  (58 shorter events, 1.0 us)
Async XLA Ops:
  0.6 51.4 %copy-start = (bf16[1024,512]{1,0:T(8,128)(2,1)S(1)}, bf16[1024,512]{1,0:T(8,128)(2,1)}, u32[]{:S(2)}) copy-start(bf16[1024,512]{1,0:T(8,128)(2,1)} %param.24) | copy-start | bytes 3145732
  0.6 16.3 %copy-start.3 = (bf16[4,1024]{1,0:T(4,128)(2,1)S(1)}, bf16[4,1024]{1,0:T(4,128)(2,1)}, u32[]{:S(2)}) copy-start(bf16[4,1024]{1,0:T(4,128)(2,1)} %param.19) | copy-start | bytes 24580
  0.7 16.9 %copy-start.4 = (bf16[4,1024]{1,0:T(4,128)(2,1)S(1)}, bf16[4,1024]{1,0:T(4,128)(2,1)}, u32[]{:S(2)}) copy-start(bf16[4,1024]{1,0:T(4,128)(2,1)} %param.20) | copy-start | bytes 24580
  0.7 20.9 %copy-start.7 = (f32[8]{0:T(128)S(1)}, f32[8]{0:T(128)}, u32[]{:S(2)}) copy-start(f32[8]{0:T(128)} %param.21) | copy-start | bytes 100
  0.7 20.9 %copy-start.1 = (bf16[8,3,1024]{2,0,1:T(8,128)(2,1)S(1)}, bf16[8,3,1024]{2,0,1:T(8,128)(2,1)}, u32[]{:S(2)}) copy-start(bf16[8,3,1024]{2,0,1:T(8,128)(2,1)} %param.25) | copy-start | bytes 147460
  0.7 21.0 %copy-start.2 = (bf16[8,3,1024]{2,0,1:T(8,128)(2,1)S(1)}, bf16[8,3,1024]{2,0,1:T(8,128)(2,1)}, u32[]{:S(2)}) copy-start(bf16[8,3,1024]{2,0,1:T(8,128)(2,1)} %param.26) | copy-start | bytes 147460
  0.7 21.1 %copy-start.6 = (f32[8]{0:T(128)S(1)}, f32[8]{0:T(128)}, u32[]{:S(2)}) copy-start(f32[8]{0:T(128)} %param.22) | copy-start | bytes 100
  0.7 7.0 %collective-permute-start = (bf16[8,4,512]{2,1,0:T(4,128)(2,1)}, bf16[8,4,512]{2,1,0:T(4,128)(2,1)S(1)}, u32[]{:S(2)}, u32[]{:S(2)}) collective-permute-start(bf16[8,4,512]{2,1,0:T(4,128)(2,1)} %param.15), channel_id=1, source_target_pairs={{0,3},{1,0},{2,1},{3,2},{4,7},{5,4},{6,5},{7,6},{8,11},{9,8},{10,9... | collective-permute-start | bytes 98312 | tf_op jit(solution)/shard_map/ppermute | solution.py:73
  5.8 5.0 %collective-permute-start.1 = (bf16[8,4,512]{2,1,0:T(4,128)(2,1)}, bf16[8,4,512]{2,1,0:T(4,128)(2,1)S(1)}, u32[]{:S(2)}, u32[]{:S(2)}) collective-permute-start(bf16[8,4,512]{2,1,0:T(4,128)(2,1)} %param.15), channel_id=1, source_target_pairs={{0,2},{1,3},{2,0},{3,1},{4,6},{5,7},{6,4},{7,5},{8,10},{9,11},{10,... | collective-permute-start | bytes 98312 | tf_op jit(solution)/shard_map/ppermute | solution.py:73
  5.8 5.9 %collective-permute-start.2 = (bf16[8,4,512]{2,1,0:T(4,128)(2,1)}, bf16[8,4,512]{2,1,0:T(4,128)(2,1)S(1)}, u32[]{:S(2)}, u32[]{:S(2)}) collective-permute-start(bf16[8,4,512]{2,1,0:T(4,128)(2,1)} %param.15), channel_id=1, source_target_pairs={{0,1},{1,2},{2,3},{3,0},{4,5},{5,6},{6,7},{7,4},{8,9},{9,10},{10,1... | collective-permute-start | bytes 98312 | tf_op jit(solution)/shard_map/ppermute | solution.py:73
  17.0 2.0 %collective-permute-start.4 = (f32[32,3088]{1,0:T(8,128)}, f32[32,3088]{1,0:T(8,128)S(1)}, u32[]{:S(2)}, u32[]{:S(2)}) collective-permute-start(f32[32,3088]{1,0:T(8,128)} %get-tuple-element.12), channel_id=1, source_target_pairs={{0,4},{4,0},{8,12},{12,8},{1,5},{5,1},{9,13},{13,9},{2,6},{6,2},{1... | collective-permute-start | bytes 1185800 | tf_op jit(solution)/shard_map/ppermute | solution.py:207
  17.0 5.5 %collective-permute-start.3 = (f32[32,3088]{1,0:T(8,128)}, f32[32,3088]{1,0:T(8,128)S(1)}, u32[]{:S(2)}, u32[]{:S(2)}) collective-permute-start(f32[32,3088]{1,0:T(8,128)} %get-tuple-element.10), channel_id=1, source_target_pairs={{0,4},{4,0},{8,12},{12,8},{1,5},{5,1},{9,13},{13,9},{2,6},{6,2},{1... | collective-permute-start | bytes 1185800 | tf_op jit(solution)/shard_map/ppermute | solution.py:207
  20.0 6.4 %collective-permute-start.6 = (f32[32,1024]{1,0:T(8,128)S(1)}, f32[32,1024]{1,0:T(8,128)S(1)}, u32[]{:S(2)}, u32[]{:S(2)}) collective-permute-start(f32[32,1024]{1,0:T(8,128)S(1)} %slice.131), channel_id=1, source_target_pairs={{0,8},{4,12},{8,0},{12,4},{1,9},{5,13},{9,1},{13,5},{2,10},{6,14},... | collective-permute-start | bytes 393224 | tf_op jit(solution)/shard_map/ppermute | solution.py:212
  21.9 9.7 %collective-permute-start.5 = (f32[32,2064]{1,0:T(8,128)S(1)}, f32[32,2064]{1,0:T(8,128)S(1)}, u32[]{:S(2)}, u32[]{:S(2)}) collective-permute-start(f32[32,2064]{1,0:T(8,128)S(1)} %slice.126), channel_id=1, source_target_pairs={{0,8},{4,12},{8,0},{12,4},{1,9},{5,13},{9,1},{13,5},{2,10},{6,14},... | collective-permute-start | bytes 792584 | tf_op jit(solution)/shard_map/ppermute | solution.py:213
  31.6 13.8 %copy-start.5 = (f32[128]{0:T(128)S(1)}, f32[128]{0:T(128)}, u32[]{:S(2)}) copy-start(f32[128]{0:T(128)} %param.23) | copy-start | bytes 1540
  46.4 3.8 %collective-permute-start.7 = (bf16[8,4,8,128]{3,2,1,0:T(8,128)(2,1)S(1)}, bf16[8,4,8,128]{3,2,1,0:T(8,128)(2,1)S(1)}, u32[]{:S(2)}, u32[]{:S(2)}) collective-permute-start(bf16[8,4,8,128]{3,2,1,0:T(8,128)(2,1)S(1)} %fusion.13), channel_id=1, source_target_pairs={{0,4},{4,8},{8,12},{12,0},{1,5},{5,9},{9,13},{13,1},{2,6},{6,10},{... | collective-permute-start | bytes 196616 | tf_op jit(solution)/shard_map/ppermute | solution.py:34
  46.5 4.6 %collective-permute-start.8 = (bf16[8,4,8,128]{3,2,1,0:T(8,128)(2,1)S(1)}, bf16[8,4,8,128]{3,2,1,0:T(8,128)(2,1)S(1)}, u32[]{:S(2)}, u32[]{:S(2)}) collective-permute-start(bf16[8,4,8,128]{3,2,1,0:T(8,128)(2,1)S(1)} %fusion.13), channel_id=1, source_target_pairs={{0,8},{4,12},{8,0},{12,4},{1,9},{5,13},{9,1},{13,5},{2,10},{6,14},... | collective-permute-start | bytes 196616 | tf_op jit(solution)/shard_map/ppermute | solution.py:34
  48.1 3.3 %collective-permute-start.9 = (bf16[8,4,8,128]{3,2,1,0:T(8,128)(2,1)S(1)}, bf16[8,4,8,128]{3,2,1,0:T(8,128)(2,1)S(1)}, u32[]{:S(2)}, u32[]{:S(2)}) collective-permute-start(bf16[8,4,8,128]{3,2,1,0:T(8,128)(2,1)S(1)} %fusion.13), channel_id=1, source_target_pairs={{0,12},{4,0},{8,4},{12,8},{1,13},{5,1},{9,5},{13,9},{2,14},{6,2},{... | collective-permute-start | bytes 196616 | tf_op jit(solution)/shard_map/ppermute | solution.py:34
  52.3 6.9 %collective-permute-start.10 = (f32[32,512]{1,0:T(8,128)S(1)}, f32[32,512]{1,0:T(8,128)S(1)}, u32[]{:S(2)}, u32[]{:S(2)}) collective-permute-start(f32[32,512]{1,0:T(8,128)S(1)} %get-tuple-element.26), channel_id=1, source_target_pairs={{0,1},{1,2},{2,3},{3,0},{4,5},{5,6},{6,7},{7,4},{8,9},{9,10},{10,1... | collective-permute-start | bytes 196616 | tf_op jit(solution)/shard_map/ppermute | solution.py:47
  52.4 8.7 %collective-permute-start.11 = (f32[32,512]{1,0:T(8,128)S(1)}, f32[32,512]{1,0:T(8,128)S(1)}, u32[]{:S(2)}, u32[]{:S(2)}) collective-permute-start(f32[32,512]{1,0:T(8,128)S(1)} %get-tuple-element.28), channel_id=1, source_target_pairs={{0,2},{1,3},{2,0},{3,1},{4,6},{5,7},{6,4},{7,5},{8,10},{9,11},{10,... | collective-permute-start | bytes 196616 | tf_op jit(solution)/shard_map/ppermute | solution.py:47
  53.6 7.6 %collective-permute-start.12 = (f32[32,512]{1,0:T(8,128)S(1)}, f32[32,512]{1,0:T(8,128)S(1)}, u32[]{:S(2)}, u32[]{:S(2)}) collective-permute-start(f32[32,512]{1,0:T(8,128)S(1)} %get-tuple-element.27), channel_id=1, source_target_pairs={{0,3},{1,0},{2,1},{3,2},{4,7},{5,4},{6,5},{7,6},{8,11},{9,8},{10,9... | collective-permute-start | bytes 196616 | tf_op jit(solution)/shard_map/ppermute | solution.py:47

commit v13 on v12

--- a/solution.py
+++ b/solution.py
@@ -75,6 +75,7 @@
 
 
 def projection_kernel(x_ref, wqk_ref, wvz_ref, wba_t_ref, *outs):
+    k = pl.program_id(0)
     x = x_ref[...]
     section = outs[0].shape[0]
     offset = 0
@@ -85,15 +86,34 @@
             x, w_ref[...], (((1,), (contract,)), ((), ())), preferred_element_type=jnp.float32
         )
         for i, o_ref in enumerate(outs):
-            o_ref[:, offset : offset + width] = y[i * section : (i + 1) * section]
+            part = y[i * section : (i + 1) * section]
+
+            @pl.when(k == 0)
+            def _():
+                o_ref[:, offset : offset + width] = part
+
+            @pl.when(k > 0)
+            def _():
+                o_ref[:, offset : offset + width] += part
+
         offset += width
 
 
 def projection(x, w_qk, w_vz, w_ba, sections):
     rows = x.shape[0] // sections
     cols = w_qk.shape[1] + w_vz.shape[1] + w_ba.shape[1]
+    features = x.shape[1]
+    block = 256 if features % 256 == 0 else features
     return pl.pallas_call(
         projection_kernel,
+        grid=(features // block,),
+        in_specs=[
+            pl.BlockSpec((x.shape[0], block), lambda k: (0, k)),
+            pl.BlockSpec((block, w_qk.shape[1]), lambda k: (k, 0)),
+            pl.BlockSpec((block, w_vz.shape[1]), lambda k: (k, 0)),
+            pl.BlockSpec((w_ba.shape[1], block), lambda k: (0, k)),
+        ],
+        out_specs=[pl.BlockSpec((rows, cols), lambda k: (0, 0))] * sections,
         out_shape=[jax.ShapeDtypeStruct((rows, cols), jnp.float32)] * sections,
         cost_estimate=pl.CostEstimate(
             flops=2 * x.shape[0] * x.shape[1] * cols,

time: 62.3 us -> 62.9 us (level)
  no operation moved by 1% of the time
where the time goes in v13:
time: 62.9 us; the launch traced here: 62.4 us
  waiting for transfers between devices  17.9 us (28%)
  starting transfers between devices  15.9 us (25%)
  Pallas kernels  14.2 us (23%)
  other arithmetic  7.9 us (13%)
  local copies, waits for them, and re-layouts  5.07 us (8%)
  between operations  1.02 us (2%)
    pallas_call x1, Pallas kernels, recurrence(): pl.pallas_call(kern, grid=(rows,), in_specs=[pl.BlockSpec(memory_space=pl...  9.9 us
    ppermute x3, starting transfers between devices, gather_pieces(): pieces.append(lax.ppermute(x, axis, [(i, (i + s) % n) for i in range(n)]))  6.11 us
    ppermute x3, waiting for transfers between devices, gather_pieces(): pieces.append(lax.ppermute(x, axis, [(i, (i + s) % n) for i in range(n)]))  4.91 us
    ppermute x3, waiting for transfers between devices, scatter_sum_rows(): acc = acc + lax.ppermute(send, axis, [(i, (i + s) % n) for i in range(n)])  4.69 us
    pallas_call x1, Pallas kernels, projection(): pl.pallas_call(projection_kernel, grid=(features // block,), in_specs=[pl...  4.3 us
    ppermute x3, starting transfers between devices, scatter_sum_rows(): acc = acc + lax.ppermute(send, axis, [(i, (i + s) % n) for i in range(n)])  4.11 us
    ppermute x3, starting transfers between devices, gather_rows(): pieces.append(lax.ppermute(x, axis, [(i, (i + s) % n) for i in range(n)]))  2.99 us
    ppermute x1, waiting for transfers between devices, shards(): summed_qk = summed_qk + lax.ppermute(part[s][:, :width_qk], 'dp', perm)  2.85 us
  transfers between devices with their start and end apart: 13, of which 11 were waited for; matrix products, arithmetic and copies ran while one was open for 9% of the time, Pallas kernels for 0%

profile of v13, /device:TPU:0, one launch (start us, length us, event | category | flops | bytes accessed | tf_op | source)
XLA Modules:
  0.0 62.4 jit_solution(6293647613529566344)
XLA Ops:
  0.7 5.1 %collective-permute-start = (bf16[8,4,512]{2,1,0:T(4,128)(2,1)}, bf16[8,4,512]{2,1,0:T(4,128)(2,1)S(1)}, u32[]{:S(2)}, u32[]{:S(2)}) collective-permute-start(bf16[8,4,512]{2,1,0:T(4,128)(2,1)} %param.15), channel_id=1, source_target_pairs={{0,3},{1,0},{2,1},{3,2},{4,7},{5,4},{6,5},{7,6},{8,11},{9,8},{10,9... | collective-permute-start | bytes 98312 | tf_op jit(solution)/shard_map/ppermute | solution.py:73
  5.8 1.0 %collective-permute-start.2 = (bf16[8,4,512]{2,1,0:T(4,128)(2,1)}, bf16[8,4,512]{2,1,0:T(4,128)(2,1)S(1)}, u32[]{:S(2)}, u32[]{:S(2)}) collective-permute-start(bf16[8,4,512]{2,1,0:T(4,128)(2,1)} %param.15), channel_id=1, source_target_pairs={{0,1},{1,2},{2,3},{3,0},{4,5},{5,6},{6,7},{7,4},{8,9},{9,10},{10,1... | collective-permute-start | bytes 98312 | tf_op jit(solution)/shard_map/ppermute | solution.py:73
  6.8 0.9 %collective-permute-done = bf16[8,4,512]{2,1,0:T(4,128)(2,1)S(1)} collective-permute-done((bf16[8,4,512]{2,1,0:T(4,128)(2,1)}, bf16[8,4,512]{2,1,0:T(4,128)(2,1)S(1)}, u32[]{:S(2)}, u32[]{:S(2)}) %collective-permute-start) | collective-permute-done | bytes 32800 | tf_op jit(solution)/shard_map/ppermute | solution.py:73
  7.7 3.1 %collective-permute-done.1 = bf16[8,4,512]{2,1,0:T(4,128)(2,1)S(1)} collective-permute-done((bf16[8,4,512]{2,1,0:T(4,128)(2,1)}, bf16[8,4,512]{2,1,0:T(4,128)(2,1)S(1)}, u32[]{:S(2)}, u32[]{:S(2)}) %collective-permute-start.1) | collective-permute-done | bytes 32800 | tf_op jit(solution)/shard_map/ppermute | solution.py:73
  10.8 0.9 %collective-permute-done.2 = bf16[8,4,512]{2,1,0:T(4,128)(2,1)S(1)} collective-permute-done((bf16[8,4,512]{2,1,0:T(4,128)(2,1)}, bf16[8,4,512]{2,1,0:T(4,128)(2,1)S(1)}, u32[]{:S(2)}, u32[]{:S(2)}) %collective-permute-start.2) | collective-permute-done | bytes 32800 | tf_op jit(solution)/shard_map/ppermute | solution.py:73
  11.7 0.8 %select_select_fusion.3 = (bf16[4,8,512]{2,1,0:T(8,128)(2,1)S(1)}, bf16[4,8,512]{2,1,0:T(8,128)(2,1)S(1)}, bf16[4,8,512]{2,1,0:T(8,128)(2,1)S(1)}, bf16[4,8,512]{2,1,0:T(8,128)(2,1)S(1)}) fusion(bf16[4,8,512]{2,1,0:T(8,128)(2,1)S(1)} %bitcast.93, bf16[4,8,512]{2,1,0:T(8,128)(2,1)S(1)} %bitcast.94, bf16[4,8,512]{2,1,0:T(8,128)(2,1)S(1)} %bitcast.95, ...), kind=kLoop, calls=%fused_computation.53 | loop fusion | flops 196608 | bytes 262156 | tf_op jit(solution)/shard_map/jit(_where)/select_n | solution.py:221
  12.6 0.7 %pad_maximum_fusion.1.x_ref = bf16[128,512]{1,0:T(8,128)(2,1)} fusion(bf16[32,512]{1,0:T(8,128)(2,1)S(1)} %reshape.130, bf16[32,512]{1,0:T(8,128)(2,1)S(1)} %reshape.129, bf16[32,512]{1,0:T(8,128)(2,1)S(1)} %reshape.128, bf16[32,512]{1,0:T(8,128)(2,1)S(1)} %reshape.127), kind=kLoop, calls=%fused_computation.31 | loop fusion | flops 524288 | bytes 262144 | tf_op jit(solution)/shard_map/concatenate | solution.py:224
  13.3 4.3 %shard_map.140 = (f32[32,3088]{1,0:T(8,128)}, f32[32,3088]{1,0:T(8,128)}, f32[32,3088]{1,0:T(8,128)}, f32[32,3088]{1,0:T(8,128)}) custom-call(bf16[128,512]{1,0:T(8,128)(2,1)} %pad_maximum_fusion.1.x_ref, bf16[512,1024]{1,0:T(8,128)(2,1)} %wqk_ref.1, bf16[512,2048]{1,0:T(8,128)(2,1)} %wvz_ref.1, bf16[16,512]{1,0:T(8,128)(2,1)} %bitcast.96), custom_call_target="tpu_custom_call" | custom-call | flops 404750336 | bytes 4874240 | tf_op jit(solution)/shard_map/pallas_call | solution.py:107
  17.6 0.6 collective-permute-start.3
  18.2 1.3 %collective-permute-done.4 = f32[32,3088]{1,0:T(8,128)S(1)} collective-permute-done((f32[32,3088]{1,0:T(8,128)}, f32[32,3088]{1,0:T(8,128)S(1)}, u32[]{:S(2)}, u32[]{:S(2)}) %collective-permute-start.4) | collective-permute-done | bytes 395296 | tf_op jit(solution)/shard_map/ppermute | solution.py:227
  19.5 1.1 %add.200 = f32[32,3088]{1,0:T(8,128)S(1)} add(f32[32,3088]{1,0:T(8,128)} %get-tuple-element.11, f32[32,3088]{1,0:T(8,128)S(1)} %collective-permute-done.4) | non-fusion elementwise | flops 98816 | bytes 1185792 | tf_op jit(solution)/shard_map/add | solution.py:227
  20.6 1.5 %collective-permute-start.6 = (f32[32,1024]{1,0:T(8,128)S(1)}, f32[32,1024]{1,0:T(8,128)S(1)}, u32[]{:S(2)}, u32[]{:S(2)}) collective-permute-start(f32[32,1024]{1,0:T(8,128)S(1)} %slice.131), channel_id=1, source_target_pairs={{0,8},{4,12},{8,0},{12,4},{1,9},{5,13},{9,1},{13,5},{2,10},{6,14},... | collective-permute-start | bytes 393224 | tf_op jit(solution)/shard_map/ppermute | solution.py:232
  22.3 0.1 mul.181
  22.4 0.1 add.204
  22.5 0.6 collective-permute-start.5
  23.1 1.0 %add.199 = f32[32,3088]{1,0:T(8,128)S(1)} add(f32[32,3088]{1,0:T(8,128)} %get-tuple-element.9, f32[32,3088]{1,0:T(8,128)S(1)} %collective-permute-done.3) | non-fusion elementwise | flops 98816 | bytes 1185792 | tf_op jit(solution)/shard_map/add | solution.py:227
  24.2 2.8 %collective-permute-done.6 = f32[32,1024]{1,0:T(8,128)S(1)} collective-permute-done((f32[32,1024]{1,0:T(8,128)S(1)}, f32[32,1024]{1,0:T(8,128)S(1)}, u32[]{:S(2)}, u32[]{:S(2)}) %collective-permute-start.6) | collective-permute-done | bytes 131104 | tf_op jit(solution)/shard_map/ppermute | solution.py:232
  27.1 0.2 divide_multiply_fusion.1
  27.3 0.1 reshape.132
  27.4 0.1 fusion.23
  27.6 0.1 multiply_reduce_fusion.2
  27.7 0.1 multiply_reduce_fusion.1
  27.8 0.1 fusion.17
  27.9 1.0 %copy.56.kt_ref = f32[8,128,16]{2,1,0:T(8,128)} copy(f32[8,128,16]{1,0,2:T(8,128)S(1)} %bitcast.83) | data formatting | bytes 131072 | tf_op jit(solution)/shard_map/reshape | solution.py:251
  28.9 1.0 %copy.55.qt_ref = f32[8,128,16]{2,1,0:T(8,128)} copy(f32[8,128,16]{1,0,2:T(8,128)S(1)} %bitcast.82) | data formatting | bytes 131072 | tf_op jit(solution)/shard_map/reshape | solution.py:250
  29.9 2.2 %collective-permute-done.5 = f32[32,2064]{1,0:T(8,128)S(1)} collective-permute-done((f32[32,2064]{1,0:T(8,128)S(1)}, f32[32,2064]{1,0:T(8,128)S(1)}, u32[]{:S(2)}, u32[]{:S(2)}) %collective-permute-start.5) | collective-permute-done | bytes 264224 | tf_op jit(solution)/shard_map/ppermute | solution.py:233
  32.3 0.4 fusion.22
  32.9 0.1 reshape.197
  33.0 0.1 copy.61
  33.2 0.1 copy.48
  33.4 0.1 squeeze.11
  33.5 0.7 %pad_maximum_fusion.2.gates_ref = f32[8,64]{1,0:T(8,128)} fusion(f32[8,32]{1,0:T(8,128)S(1)} %fusion.19, f32[8,32]{1,0:T(8,128)S(1)} %div.76), kind=kLoop, calls=%fused_computation.63 | loop fusion | flops 512 | bytes 4096 | tf_op jit(solution)/shard_map/concatenate | solution.py:256
  34.2 0.8 %divide_multiply_fusion.v_ref = f32[8,4,1024]{2,1,0:T(4,128)} fusion(f32[8,7,1024]{2,1,0:T(8,128)S(1)} %maximum_convert_fusion.1, f32[1024]{0:T(1024)S(1)} %bitcast.100, f32[1024]{0:T(1024)S(1)} %bitcast.99, f32[1024]{0:T(1024)S(1)} %bitcast.98, f32[1024]{0:T(1024)S(1)} %bitcast.97), kind=kLoop, calls=%fused_computation.8 | loop fusion | flops 360448 | bytes 671744 | tf_op jit(solution)/shard_map/jit(silu)/mul | solution.py:26
  35.0 9.9 %shard_map.141 = (f32[8,8,128,128]{3,2,1,0:T(8,128)}, f32[8,4,8,128]{3,2,1,0:T(8,128)}) custom-call(f32[8,64]{1,0:T(8,128)} %pad_maximum_fusion.2.gates_ref, f32[8,128,16]{2,1,0:T(8,128)} %copy.55.qt_ref, f32[8,128,16]{2,1,0:T(8,128)} %copy.56.kt_ref, f32[8,4,1024]{2,1,0:T(4,128)} %divide_multiply_fusion.v_ref, f32[8,8,128,128]{3,2,1,0:T(8,128)} %s_ref.1), custom_call_target="tpu_custom_call" | custom-call | flops 33554432 | bytes 8388608 | tf_op jit(solution)/shard_map/pallas_call | solution.py:156
  44.9 1.0 %multiply_reduce_fusion = f32[8,4,8]{2,1,0:T(4,128)S(1)} fusion(f32[8,4,8,128]{3,2,1,0:T(8,128)} %get-tuple-element.13), kind=kLoop, calls=%fused_computation.34 | loop fusion | flops 65280 | bytes 132096 | tf_op jit(solution)/shard_map/reduce_sum | solution.py:262
  46.0 1.0 %fusion.13 = bf16[8,4,8,128]{3,2,1,0:T(8,128)(2,1)S(1)} fusion(f32[8,4,8,128]{3,2,1,0:T(8,128)} %get-tuple-element.13, bf16[8,4,8,1,128]{4,3,2,1,0:T(2,128)(2,1)S(1)} %get-tuple-element.29, f32[128]{0:T(128)S(1)} %copy-done.5, f32[8,4,8]{2,1,0:T(4,128)S(1)} %add_rsqrt_fusion), kind=kLoop, calls=%fused_computation.35 | loop fusion | flops 294912 | bytes 263680 | tf_op jit(solution)/shard_map/convert_element_type | solution.py:264
  47.1 1.5 %collective-permute-start.8 = (bf16[8,4,8,128]{3,2,1,0:T(8,128)(2,1)S(1)}, bf16[8,4,8,128]{3,2,1,0:T(8,128)(2,1)S(1)}, u32[]{:S(2)}, u32[]{:S(2)}) collective-permute-start(bf16[8,4,8,128]{3,2,1,0:T(8,128)(2,1)S(1)} %fusion.13), channel_id=1, source_target_pairs={{0,8},{4,12},{8,0},{12,4},{1,9},{5,13},{9,1},{13,5},{2,10},{6,14},... | collective-permute-start | bytes 196616 | tf_op jit(solution)/shard_map/ppermute | solution.py:34
  48.6 1.4 %collective-permute-start.9 = (bf16[8,4,8,128]{3,2,1,0:T(8,128)(2,1)S(1)}, bf16[8,4,8,128]{3,2,1,0:T(8,128)(2,1)S(1)}, u32[]{:S(2)}, u32[]{:S(2)}) collective-permute-start(bf16[8,4,8,128]{3,2,1,0:T(8,128)(2,1)S(1)} %fusion.13), channel_id=1, source_target_pairs={{0,12},{4,0},{8,4},{12,8},{1,13},{5,1},{9,5},{13,9},{2,14},{6,2},{... | collective-permute-start | bytes 196616 | tf_op jit(solution)/shard_map/ppermute | solution.py:34
  50.0 0.8 %collective-permute-done.7 = bf16[8,4,8,128]{3,2,1,0:T(8,128)(2,1)S(1)} collective-permute-done((bf16[8,4,8,128]{3,2,1,0:T(8,128)(2,1)S(1)}, bf16[8,4,8,128]{3,2,1,0:T(8,128)(2,1)S(1)}, u32[]{:S(2)}, u32[]{:S(2)}) %collective-permute-start.7) | collective-permute-done | bytes 65568 | tf_op jit(solution)/shard_map/ppermute | solution.py:34
  50.8 0.9 %collective-permute-done.8 = bf16[8,4,8,128]{3,2,1,0:T(8,128)(2,1)S(1)} collective-permute-done((bf16[8,4,8,128]{3,2,1,0:T(8,128)(2,1)S(1)}, bf16[8,4,8,128]{3,2,1,0:T(8,128)(2,1)S(1)}, u32[]{:S(2)}, u32[]{:S(2)}) %collective-permute-start.8) | collective-permute-done | bytes 65568 | tf_op jit(solution)/shard_map/ppermute | solution.py:34
  51.7 0.2 collective-permute-done.9
  51.9 0.6 gather_fusion
  52.6 0.3 convolution_bitcast_fusion
  53.0 1.2 %collective-permute-start.11 = (f32[32,512]{1,0:T(8,128)S(1)}, f32[32,512]{1,0:T(8,128)S(1)}, u32[]{:S(2)}, u32[]{:S(2)}) collective-permute-start(f32[32,512]{1,0:T(8,128)S(1)} %get-tuple-element.28), channel_id=1, source_target_pairs={{0,2},{1,3},{2,0},{3,1},{4,6},{5,7},{6,4},{7,5},{8,10},{9,11},{10,... | collective-permute-start | bytes 196616 | tf_op jit(solution)/shard_map/ppermute | solution.py:47
  54.2 2.8 %collective-permute-start.12 = (f32[32,512]{1,0:T(8,128)S(1)}, f32[32,512]{1,0:T(8,128)S(1)}, u32[]{:S(2)}, u32[]{:S(2)}) collective-permute-start(f32[32,512]{1,0:T(8,128)S(1)} %get-tuple-element.27), channel_id=1, source_target_pairs={{0,3},{1,0},{2,1},{3,2},{4,7},{5,4},{6,5},{7,6},{8,11},{9,8},{10,9... | collective-permute-start | bytes 196616 | tf_op jit(solution)/shard_map/ppermute | solution.py:47
  57.0 2.8 %collective-permute-done.10 = f32[32,512]{1,0:T(8,128)S(1)} collective-permute-done((f32[32,512]{1,0:T(8,128)S(1)}, f32[32,512]{1,0:T(8,128)S(1)}, u32[]{:S(2)}, u32[]{:S(2)}) %collective-permute-start.10) | collective-permute-done | bytes 65568 | tf_op jit(solution)/shard_map/ppermute | solution.py:47
  59.8 1.9 %collective-permute-done.11 = f32[32,512]{1,0:T(8,128)S(1)} collective-permute-done((f32[32,512]{1,0:T(8,128)S(1)}, f32[32,512]{1,0:T(8,128)S(1)}, u32[]{:S(2)}, u32[]{:S(2)}) %collective-permute-start.11) | collective-permute-done | bytes 65568 | tf_op jit(solution)/shard_map/ppermute | solution.py:47
  61.7 0.6 %reshape.137 = bf16[8,4,512]{2,1,0:T(4,128)(2,1)} reshape(bf16[32,512]{1,0:T(8,128)(2,1)S(1)} %fusion.16) | data formatting | bytes 65536 | tf_op jit(solution)/shard_map/reshape | solution.py:274
  (58 shorter events, 1.0 us)
Async XLA Ops:
  0.6 51.9 %copy-start = (bf16[1024,512]{1,0:T(8,128)(2,1)S(1)}, bf16[1024,512]{1,0:T(8,128)(2,1)}, u32[]{:S(2)}) copy-start(bf16[1024,512]{1,0:T(8,128)(2,1)} %param.24) | copy-start | bytes 3145732
  0.6 16.9 %copy-start.3 = (bf16[4,1024]{1,0:T(4,128)(2,1)S(1)}, bf16[4,1024]{1,0:T(4,128)(2,1)}, u32[]{:S(2)}) copy-start(bf16[4,1024]{1,0:T(4,128)(2,1)} %param.19) | copy-start | bytes 24580
  0.7 17.5 %copy-start.4 = (bf16[4,1024]{1,0:T(4,128)(2,1)S(1)}, bf16[4,1024]{1,0:T(4,128)(2,1)}, u32[]{:S(2)}) copy-start(bf16[4,1024]{1,0:T(4,128)(2,1)} %param.20) | copy-start | bytes 24580
  0.7 21.5 %copy-start.7 = (f32[8]{0:T(128)S(1)}, f32[8]{0:T(128)}, u32[]{:S(2)}) copy-start(f32[8]{0:T(128)} %param.21) | copy-start | bytes 100
  0.7 21.5 %copy-start.1 = (bf16[8,3,1024]{2,0,1:T(8,128)(2,1)S(1)}, bf16[8,3,1024]{2,0,1:T(8,128)(2,1)}, u32[]{:S(2)}) copy-start(bf16[8,3,1024]{2,0,1:T(8,128)(2,1)} %param.25) | copy-start | bytes 147460
  0.7 21.5 %copy-start.2 = (bf16[8,3,1024]{2,0,1:T(8,128)(2,1)S(1)}, bf16[8,3,1024]{2,0,1:T(8,128)(2,1)}, u32[]{:S(2)}) copy-start(bf16[8,3,1024]{2,0,1:T(8,128)(2,1)} %param.26) | copy-start | bytes 147460
  0.7 21.7 %copy-start.6 = (f32[8]{0:T(128)S(1)}, f32[8]{0:T(128)}, u32[]{:S(2)}) copy-start(f32[8]{0:T(128)} %param.22) | copy-start | bytes 100
  0.7 7.0 %collective-permute-start = (bf16[8,4,512]{2,1,0:T(4,128)(2,1)}, bf16[8,4,512]{2,1,0:T(4,128)(2,1)S(1)}, u32[]{:S(2)}, u32[]{:S(2)}) collective-permute-start(bf16[8,4,512]{2,1,0:T(4,128)(2,1)} %param.15), channel_id=1, source_target_pairs={{0,3},{1,0},{2,1},{3,2},{4,7},{5,4},{6,5},{7,6},{8,11},{9,8},{10,9... | collective-permute-start | bytes 98312 | tf_op jit(solution)/shard_map/ppermute | solution.py:73
  5.8 5.0 %collective-permute-start.1 = (bf16[8,4,512]{2,1,0:T(4,128)(2,1)}, bf16[8,4,512]{2,1,0:T(4,128)(2,1)S(1)}, u32[]{:S(2)}, u32[]{:S(2)}) collective-permute-start(bf16[8,4,512]{2,1,0:T(4,128)(2,1)} %param.15), channel_id=1, source_target_pairs={{0,2},{1,3},{2,0},{3,1},{4,6},{5,7},{6,4},{7,5},{8,10},{9,11},{10,... | collective-permute-start | bytes 98312 | tf_op jit(solution)/shard_map/ppermute | solution.py:73
  5.8 5.9 %collective-permute-start.2 = (bf16[8,4,512]{2,1,0:T(4,128)(2,1)}, bf16[8,4,512]{2,1,0:T(4,128)(2,1)S(1)}, u32[]{:S(2)}, u32[]{:S(2)}) collective-permute-start(bf16[8,4,512]{2,1,0:T(4,128)(2,1)} %param.15), channel_id=1, source_target_pairs={{0,1},{1,2},{2,3},{3,0},{4,5},{5,6},{6,7},{7,4},{8,9},{9,10},{10,1... | collective-permute-start | bytes 98312 | tf_op jit(solution)/shard_map/ppermute | solution.py:73
  17.6 2.0 %collective-permute-start.4 = (f32[32,3088]{1,0:T(8,128)}, f32[32,3088]{1,0:T(8,128)S(1)}, u32[]{:S(2)}, u32[]{:S(2)}) collective-permute-start(f32[32,3088]{1,0:T(8,128)} %get-tuple-element.12), channel_id=1, source_target_pairs={{0,4},{4,0},{8,12},{12,8},{1,5},{5,1},{9,13},{13,9},{2,6},{6,2},{1... | collective-permute-start | bytes 1185800 | tf_op jit(solution)/shard_map/ppermute | solution.py:227
  17.6 5.5 %collective-permute-start.3 = (f32[32,3088]{1,0:T(8,128)}, f32[32,3088]{1,0:T(8,128)S(1)}, u32[]{:S(2)}, u32[]{:S(2)}) collective-permute-start(f32[32,3088]{1,0:T(8,128)} %get-tuple-element.10), channel_id=1, source_target_pairs={{0,4},{4,0},{8,12},{12,8},{1,5},{5,1},{9,13},{13,9},{2,6},{6,2},{1... | collective-permute-start | bytes 1185800 | tf_op jit(solution)/shard_map/ppermute | solution.py:227
  20.6 6.4 %collective-permute-start.6 = (f32[32,1024]{1,0:T(8,128)S(1)}, f32[32,1024]{1,0:T(8,128)S(1)}, u32[]{:S(2)}, u32[]{:S(2)}) collective-permute-start(f32[32,1024]{1,0:T(8,128)S(1)} %slice.131), channel_id=1, source_target_pairs={{0,8},{4,12},{8,0},{12,4},{1,9},{5,13},{9,1},{13,5},{2,10},{6,14},... | collective-permute-start | bytes 393224 | tf_op jit(solution)/shard_map/ppermute | solution.py:232
  22.5 9.7 %collective-permute-start.5 = (f32[32,2064]{1,0:T(8,128)S(1)}, f32[32,2064]{1,0:T(8,128)S(1)}, u32[]{:S(2)}, u32[]{:S(2)}) collective-permute-start(f32[32,2064]{1,0:T(8,128)S(1)} %slice.126), channel_id=1, source_target_pairs={{0,8},{4,12},{8,0},{12,4},{1,9},{5,13},{9,1},{13,5},{2,10},{6,14},... | collective-permute-start | bytes 792584 | tf_op jit(solution)/shard_map/ppermute | solution.py:233
  32.2 13.8 %copy-start.5 = (f32[128]{0:T(128)S(1)}, f32[128]{0:T(128)}, u32[]{:S(2)}) copy-start(f32[128]{0:T(128)} %param.23) | copy-start | bytes 1540
  47.0 3.8 %collective-permute-start.7 = (bf16[8,4,8,128]{3,2,1,0:T(8,128)(2,1)S(1)}, bf16[8,4,8,128]{3,2,1,0:T(8,128)(2,1)S(1)}, u32[]{:S(2)}, u32[]{:S(2)}) collective-permute-start(bf16[8,4,8,128]{3,2,1,0:T(8,128)(2,1)S(1)} %fusion.13), channel_id=1, source_target_pairs={{0,4},{4,8},{8,12},{12,0},{1,5},{5,9},{9,13},{13,1},{2,6},{6,10},{... | collective-permute-start | bytes 196616 | tf_op jit(solution)/shard_map/ppermute | solution.py:34
  47.1 4.6 %collective-permute-start.8 = (bf16[8,4,8,128]{3,2,1,0:T(8,128)(2,1)S(1)}, bf16[8,4,8,128]{3,2,1,0:T(8,128)(2,1)S(1)}, u32[]{:S(2)}, u32[]{:S(2)}) collective-permute-start(bf16[8,4,8,128]{3,2,1,0:T(8,128)(2,1)S(1)} %fusion.13), channel_id=1, source_target_pairs={{0,8},{4,12},{8,0},{12,4},{1,9},{5,13},{9,1},{13,5},{2,10},{6,14},... | collective-permute-start | bytes 196616 | tf_op jit(solution)/shard_map/ppermute | solution.py:34
  48.6 3.3 %collective-permute-start.9 = (bf16[8,4,8,128]{3,2,1,0:T(8,128)(2,1)S(1)}, bf16[8,4,8,128]{3,2,1,0:T(8,128)(2,1)S(1)}, u32[]{:S(2)}, u32[]{:S(2)}) collective-permute-start(bf16[8,4,8,128]{3,2,1,0:T(8,128)(2,1)S(1)} %fusion.13), channel_id=1, source_target_pairs={{0,12},{4,0},{8,4},{12,8},{1,13},{5,1},{9,5},{13,9},{2,14},{6,2},{... | collective-permute-start | bytes 196616 | tf_op jit(solution)/shard_map/ppermute | solution.py:34
  52.9 6.9 %collective-permute-start.10 = (f32[32,512]{1,0:T(8,128)S(1)}, f32[32,512]{1,0:T(8,128)S(1)}, u32[]{:S(2)}, u32[]{:S(2)}) collective-permute-start(f32[32,512]{1,0:T(8,128)S(1)} %get-tuple-element.26), channel_id=1, source_target_pairs={{0,1},{1,2},{2,3},{3,0},{4,5},{5,6},{6,7},{7,4},{8,9},{9,10},{10,1... | collective-permute-start | bytes 196616 | tf_op jit(solution)/shard_map/ppermute | solution.py:47
  53.0 8.7 %collective-permute-start.11 = (f32[32,512]{1,0:T(8,128)S(1)}, f32[32,512]{1,0:T(8,128)S(1)}, u32[]{:S(2)}, u32[]{:S(2)}) collective-permute-start(f32[32,512]{1,0:T(8,128)S(1)} %get-tuple-element.28), channel_id=1, source_target_pairs={{0,2},{1,3},{2,0},{3,1},{4,6},{5,7},{6,4},{7,5},{8,10},{9,11},{10,... | collective-permute-start | bytes 196616 | tf_op jit(solution)/shard_map/ppermute | solution.py:47
  54.2 7.5 %collective-permute-start.12 = (f32[32,512]{1,0:T(8,128)S(1)}, f32[32,512]{1,0:T(8,128)S(1)}, u32[]{:S(2)}, u32[]{:S(2)}) collective-permute-start(f32[32,512]{1,0:T(8,128)S(1)} %get-tuple-element.27), channel_id=1, source_target_pairs={{0,3},{1,0},{2,1},{3,2},{4,7},{5,4},{6,5},{7,6},{8,11},{9,8},{10,9... | collective-permute-start | bytes 196616 | tf_op jit(solution)/shard_map/ppermute | solution.py:47

commit v14 on v12

--- a/solution.py
+++ b/solution.py
@@ -77,8 +77,10 @@
 def projection_kernel(x_ref, wqk_ref, wvz_ref, wba_t_ref, *outs):
     x = x_ref[...]
     section = outs[0].shape[0]
-    offset = 0
-    for w_ref, transposed in ((wqk_ref, False), (wvz_ref, False), (wba_t_ref, True)):
+    width_qk, width_ba = wqk_ref.shape[1], wba_t_ref.shape[0]
+    padded_ba = -(-width_ba // 128) * 128
+    placed = ((wqk_ref, False, 0), (wba_t_ref, True, width_qk), (wvz_ref, False, width_qk + padded_ba))
+    for w_ref, transposed, offset in placed:
         width = w_ref.shape[0 if transposed else 1]
         contract = 1 if transposed else 0
         y = lax.dot_general(
@@ -86,12 +88,16 @@
         )
         for i, o_ref in enumerate(outs):
             o_ref[:, offset : offset + width] = y[i * section : (i + 1) * section]
-        offset += width
+    for o_ref in outs:
+        o_ref[:, width_qk + width_ba : width_qk + padded_ba] = jnp.zeros(
+            (section, padded_ba - width_ba), jnp.float32
+        )
 
 
 def projection(x, w_qk, w_vz, w_ba, sections):
     rows = x.shape[0] // sections
-    cols = w_qk.shape[1] + w_vz.shape[1] + w_ba.shape[1]
+    padded_ba = -(-w_ba.shape[1] // 128) * 128
+    cols = w_qk.shape[1] + padded_ba + w_vz.shape[1]
     return pl.pallas_call(
         projection_kernel,
         out_shape=[jax.ShapeDtypeStruct((rows, cols), jnp.float32)] * sections,
@@ -205,14 +211,16 @@
     outs = projection(flat_rows, w_qk, w_vz, w_ba, 2 * chips)
     pair = [(i, i ^ 1) for i in range(n_dp)]
     part = [keep + lax.ppermute(send, "dp", pair) for send, keep in zip(outs[:chips], outs[chips:])]
-    summed_qk = part[0][:, :width_qk]
-    summed_rest = part[0][:, width_qk:]
+    width_ba = w_ba.shape[1]
+    split = width_qk + (-(-width_ba // 128) * 128)
+    summed_first = part[0][:, :split]
+    summed_vz = part[0][:, split:]
     for s in range(1, chips):
         perm = [(i, ((i // 2 + s) % chips) * 2 + i % 2) for i in range(n_dp)]
-        summed_qk = summed_qk + lax.ppermute(part[s][:, :width_qk], "dp", perm)
-        summed_rest = summed_rest + lax.ppermute(part[s][:, width_qk:], "dp", perm)
-    summed_vz = summed_rest[:, :width_vz]
-    summed_ba = summed_rest[:, width_vz:]
+        summed_first = summed_first + lax.ppermute(part[s][:, :split], "dp", perm)
+        summed_vz = summed_vz + lax.ppermute(part[s][:, split:], "dp", perm)
+    summed_qk = summed_first[:, :width_qk]
+    summed_ba = summed_first[:, width_qk : width_qk + width_ba]
     qk_proj = summed_qk.astype(jnp.bfloat16).reshape(rows_mem, step_count, width_qk)
     vz_proj = summed_vz.astype(jnp.bfloat16).reshape(rows_mem, step_count, width_vz)
     ba_proj = summed_ba.astype(jnp.bfloat16).reshape(rows_mem, step_count, -1)

time: 62.3 us -> 60.9 us (0.978)
  waiting for transfers between devices: 18 us -> 16.6 us
    ppermute x2, waiting for transfers between devices: 5.09 us -> 3.71 us  [the longest x1 3.2 us: shards(): summed_first = summed_first + lax.ppermute(part[s][:, :split], 'dp', perm)]
  transfers between devices with their start and end apart: 13 -> 13, of which waited for: 11 -> 11; matrix products, arithmetic and copies ran while one was open for 9% -> 11% of each run, Pallas kernels for 0% -> 0%
where the time goes in v14:
time: 60.9 us; the launch traced here: 60.4 us
  waiting for transfers between devices  16.6 us (27%)
  starting transfers between devices  15.9 us (26%)
  Pallas kernels  13.6 us (22%)
  other arithmetic  7.91 us (13%)
  local copies, waits for them, and re-layouts  5.07 us (8%)
  between operations  1.02 us (2%)
    pallas_call x1, Pallas kernels, recurrence(): pl.pallas_call(kern, grid=(rows,), in_specs=[pl.BlockSpec(memory_space=pl...  9.9 us
    ppermute x3, starting transfers between devices, gather_pieces(): pieces.append(lax.ppermute(x, axis, [(i, (i + s) % n) for i in range(n)]))  6.11 us
    ppermute x3, waiting for transfers between devices, gather_pieces(): pieces.append(lax.ppermute(x, axis, [(i, (i + s) % n) for i in range(n)]))  4.91 us
    ppermute x3, waiting for transfers between devices, scatter_sum_rows(): acc = acc + lax.ppermute(send, axis, [(i, (i + s) % n) for i in range(n)])  4.7 us
    ppermute x3, starting transfers between devices, scatter_sum_rows(): acc = acc + lax.ppermute(send, axis, [(i, (i + s) % n) for i in range(n)])  4.09 us
    pallas_call x1, Pallas kernels, projection(): pl.pallas_call(projection_kernel, out_shape=[jax.ShapeDtypeStruct((rows,...  3.72 us
    ppermute x1, waiting for transfers between devices, shards(): summed_first = summed_first + lax.ppermute(part[s][:, :split], 'dp', perm)  3.2 us
    ppermute x3, starting transfers between devices, gather_rows(): pieces.append(lax.ppermute(x, axis, [(i, (i + s) % n) for i in range(n)]))  3.01 us
  transfers between devices with their start and end apart: 13, of which 11 were waited for; matrix products, arithmetic and copies ran while one was open for 11% of the time, Pallas kernels for 0%

profile of v14, /device:TPU:0, one launch (start us, length us, event | category | flops | bytes accessed | tf_op | source)
XLA Modules:
  0.0 60.4 jit_solution(626972248558378123)
XLA Ops:
  0.7 5.1 %collective-permute-start = (bf16[8,4,512]{2,1,0:T(4,128)(2,1)}, bf16[8,4,512]{2,1,0:T(4,128)(2,1)S(1)}, u32[]{:S(2)}, u32[]{:S(2)}) collective-permute-start(bf16[8,4,512]{2,1,0:T(4,128)(2,1)} %param.15), channel_id=1, source_target_pairs={{0,3},{1,0},{2,1},{3,2},{4,7},{5,4},{6,5},{7,6},{8,11},{9,8},{10,9... | collective-permute-start | bytes 98312 | tf_op jit(solution)/shard_map/ppermute | solution.py:73
  5.8 1.0 %collective-permute-start.2 = (bf16[8,4,512]{2,1,0:T(4,128)(2,1)}, bf16[8,4,512]{2,1,0:T(4,128)(2,1)S(1)}, u32[]{:S(2)}, u32[]{:S(2)}) collective-permute-start(bf16[8,4,512]{2,1,0:T(4,128)(2,1)} %param.15), channel_id=1, source_target_pairs={{0,1},{1,2},{2,3},{3,0},{4,5},{5,6},{6,7},{7,4},{8,9},{9,10},{10,1... | collective-permute-start | bytes 98312 | tf_op jit(solution)/shard_map/ppermute | solution.py:73
  6.8 0.9 %collective-permute-done = bf16[8,4,512]{2,1,0:T(4,128)(2,1)S(1)} collective-permute-done((bf16[8,4,512]{2,1,0:T(4,128)(2,1)}, bf16[8,4,512]{2,1,0:T(4,128)(2,1)S(1)}, u32[]{:S(2)}, u32[]{:S(2)}) %collective-permute-start) | collective-permute-done | bytes 32800 | tf_op jit(solution)/shard_map/ppermute | solution.py:73
  7.7 3.1 %collective-permute-done.1 = bf16[8,4,512]{2,1,0:T(4,128)(2,1)S(1)} collective-permute-done((bf16[8,4,512]{2,1,0:T(4,128)(2,1)}, bf16[8,4,512]{2,1,0:T(4,128)(2,1)S(1)}, u32[]{:S(2)}, u32[]{:S(2)}) %collective-permute-start.1) | collective-permute-done | bytes 32800 | tf_op jit(solution)/shard_map/ppermute | solution.py:73
  10.8 0.9 %collective-permute-done.2 = bf16[8,4,512]{2,1,0:T(4,128)(2,1)S(1)} collective-permute-done((bf16[8,4,512]{2,1,0:T(4,128)(2,1)}, bf16[8,4,512]{2,1,0:T(4,128)(2,1)S(1)}, u32[]{:S(2)}, u32[]{:S(2)}) %collective-permute-start.2) | collective-permute-done | bytes 32800 | tf_op jit(solution)/shard_map/ppermute | solution.py:73
  11.7 0.8 %select_select_fusion.3 = (bf16[4,8,512]{2,1,0:T(8,128)(2,1)S(1)}, bf16[4,8,512]{2,1,0:T(8,128)(2,1)S(1)}, bf16[4,8,512]{2,1,0:T(8,128)(2,1)S(1)}, bf16[4,8,512]{2,1,0:T(8,128)(2,1)S(1)}) fusion(bf16[4,8,512]{2,1,0:T(8,128)(2,1)S(1)} %bitcast.93, bf16[4,8,512]{2,1,0:T(8,128)(2,1)S(1)} %bitcast.94, bf16[4,8,512]{2,1,0:T(8,128)(2,1)S(1)} %bitcast.95, ...), kind=kLoop, calls=%fused_computation.53 | loop fusion | flops 196608 | bytes 262156 | tf_op jit(solution)/shard_map/jit(_where)/select_n | solution.py:207
  12.6 0.7 %pad_maximum_fusion.1.x_ref = bf16[128,512]{1,0:T(8,128)(2,1)} fusion(bf16[32,512]{1,0:T(8,128)(2,1)S(1)} %reshape.130, bf16[32,512]{1,0:T(8,128)(2,1)S(1)} %reshape.129, bf16[32,512]{1,0:T(8,128)(2,1)S(1)} %reshape.128, bf16[32,512]{1,0:T(8,128)(2,1)S(1)} %reshape.127), kind=kLoop, calls=%fused_computation.31 | loop fusion | flops 524288 | bytes 262144 | tf_op jit(solution)/shard_map/concatenate | solution.py:210
  13.3 3.7 %shard_map.140 = (f32[32,3200]{1,0:T(8,128)}, f32[32,3200]{1,0:T(8,128)}, f32[32,3200]{1,0:T(8,128)}, f32[32,3200]{1,0:T(8,128)}) custom-call(bf16[128,512]{1,0:T(8,128)(2,1)} %pad_maximum_fusion.1.x_ref, bf16[512,1024]{1,0:T(8,128)(2,1)} %wqk_ref.1, bf16[512,2048]{1,0:T(8,128)(2,1)} %wvz_ref.1, bf16[16,512]{1,0:T(8,128)(2,1)} %bitcast.96), custom_call_target="tpu_custom_call" | custom-call | flops 419430400 | bytes 5046272 | tf_op jit(solution)/shard_map/pallas_call | solution.py:101
  17.0 0.6 collective-permute-start.3
  17.6 1.3 %collective-permute-done.4 = f32[32,3200]{1,0:T(8,128)S(1)} collective-permute-done((f32[32,3200]{1,0:T(8,128)}, f32[32,3200]{1,0:T(8,128)S(1)}, u32[]{:S(2)}, u32[]{:S(2)}) %collective-permute-start.4) | collective-permute-done | bytes 409632 | tf_op jit(solution)/shard_map/ppermute | solution.py:213
  18.9 1.1 %add.200 = f32[32,3200]{1,0:T(8,128)S(1)} add(f32[32,3200]{1,0:T(8,128)} %get-tuple-element.11, f32[32,3200]{1,0:T(8,128)S(1)} %collective-permute-done.4) | non-fusion elementwise | flops 102400 | bytes 1228800 | tf_op jit(solution)/shard_map/add | solution.py:213
  20.0 1.6 %collective-permute-start.5 = (f32[32,1152]{1,0:T(8,128)S(1)}, f32[32,1152]{1,0:T(8,128)S(1)}, u32[]{:S(2)}, u32[]{:S(2)}) collective-permute-start(f32[32,1152]{1,0:T(8,128)S(1)} %slice.126), channel_id=1, source_target_pairs={{0,8},{4,12},{8,0},{12,4},{1,9},{5,13},{9,1},{13,5},{2,10},{6,14},... | collective-permute-start | bytes 442376 | tf_op jit(solution)/shard_map/ppermute | solution.py:220
  21.7 0.1 mul.181
  21.8 0.1 add.204
  21.9 0.6 collective-permute-start.6
  22.5 1.0 %add.199 = f32[32,3200]{1,0:T(8,128)S(1)} add(f32[32,3200]{1,0:T(8,128)} %get-tuple-element.9, f32[32,3200]{1,0:T(8,128)S(1)} %collective-permute-done.3) | non-fusion elementwise | flops 102400 | bytes 1228800 | tf_op jit(solution)/shard_map/add | solution.py:213
  23.6 3.2 %collective-permute-done.5 = f32[32,1152]{1,0:T(8,128)S(1)} collective-permute-done((f32[32,1152]{1,0:T(8,128)S(1)}, f32[32,1152]{1,0:T(8,128)S(1)}, u32[]{:S(2)}, u32[]{:S(2)}) %collective-permute-start.5) | collective-permute-done | bytes 147488 | tf_op jit(solution)/shard_map/ppermute | solution.py:220
  26.9 0.2 divide_multiply_fusion.1
  27.1 0.1 reshape.132
  27.2 0.1 fusion.23
  27.4 0.1 multiply_reduce_fusion.2
  27.5 0.1 multiply_reduce_fusion.1
  27.6 0.1 fusion.17
  27.7 1.0 %copy.56.kt_ref = f32[8,128,16]{2,1,0:T(8,128)} copy(f32[8,128,16]{1,0,2:T(8,128)S(1)} %bitcast.83) | data formatting | bytes 131072 | tf_op jit(solution)/shard_map/reshape | solution.py:239
  28.7 1.0 %copy.55.qt_ref = f32[8,128,16]{2,1,0:T(8,128)} copy(f32[8,128,16]{1,0,2:T(8,128)S(1)} %bitcast.82) | data formatting | bytes 131072 | tf_op jit(solution)/shard_map/reshape | solution.py:238
  29.8 0.1 reshape.197
  29.9 0.1 copy.61
  30.2 0.1 copy.48
  30.3 0.1 squeeze.11
  30.4 0.7 %pad_maximum_fusion.2.gates_ref = f32[8,64]{1,0:T(8,128)} fusion(f32[8,32]{1,0:T(8,128)S(1)} %fusion.19, f32[8,32]{1,0:T(8,128)S(1)} %div.76), kind=kLoop, calls=%fused_computation.63 | loop fusion | flops 512 | bytes 4096 | tf_op jit(solution)/shard_map/concatenate | solution.py:244
  31.1 0.5 collective-permute-done.6
  31.7 0.4 fusion.22
  32.3 0.8 %divide_multiply_fusion.v_ref = f32[8,4,1024]{2,1,0:T(4,128)} fusion(f32[8,7,1024]{2,1,0:T(8,128)S(1)} %maximum_convert_fusion.1, f32[1024]{0:T(1024)S(1)} %bitcast.100, f32[1024]{0:T(1024)S(1)} %bitcast.99, f32[1024]{0:T(1024)S(1)} %bitcast.98, f32[1024]{0:T(1024)S(1)} %bitcast.97), kind=kLoop, calls=%fused_computation.10 | loop fusion | flops 360448 | bytes 671744 | tf_op jit(solution)/shard_map/jit(silu)/mul | solution.py:26
  33.1 9.9 %shard_map.141 = (f32[8,8,128,128]{3,2,1,0:T(8,128)}, f32[8,4,8,128]{3,2,1,0:T(8,128)}) custom-call(f32[8,64]{1,0:T(8,128)} %pad_maximum_fusion.2.gates_ref, f32[8,128,16]{2,1,0:T(8,128)} %copy.55.qt_ref, f32[8,128,16]{2,1,0:T(8,128)} %copy.56.kt_ref, f32[8,4,1024]{2,1,0:T(4,128)} %divide_multiply_fusion.v_ref, f32[8,8,128,128]{3,2,1,0:T(8,128)} %s_ref.1), custom_call_target="tpu_custom_call" | custom-call | flops 33554432 | bytes 8388608 | tf_op jit(solution)/shard_map/pallas_call | solution.py:142
  43.0 1.0 %multiply_reduce_fusion = f32[8,4,8]{2,1,0:T(4,128)S(1)} fusion(f32[8,4,8,128]{3,2,1,0:T(8,128)} %get-tuple-element.13), kind=kLoop, calls=%fused_computation.34 | loop fusion | flops 65280 | bytes 132096 | tf_op jit(solution)/shard_map/reduce_sum | solution.py:250
  44.0 1.0 %fusion.13 = bf16[8,4,8,128]{3,2,1,0:T(8,128)(2,1)S(1)} fusion(f32[8,4,8,128]{3,2,1,0:T(8,128)} %get-tuple-element.13, bf16[8,4,8,1,128]{4,3,2,1,0:T(2,128)(2,1)S(1)} %get-tuple-element.29, f32[128]{0:T(128)S(1)} %copy-done.5, f32[8,4,8]{2,1,0:T(4,128)S(1)} %add_rsqrt_fusion), kind=kLoop, calls=%fused_computation.35 | loop fusion | flops 294912 | bytes 263680 | tf_op jit(solution)/shard_map/convert_element_type | solution.py:252
  45.1 1.6 %collective-permute-start.8 = (bf16[8,4,8,128]{3,2,1,0:T(8,128)(2,1)S(1)}, bf16[8,4,8,128]{3,2,1,0:T(8,128)(2,1)S(1)}, u32[]{:S(2)}, u32[]{:S(2)}) collective-permute-start(bf16[8,4,8,128]{3,2,1,0:T(8,128)(2,1)S(1)} %fusion.13), channel_id=1, source_target_pairs={{0,8},{4,12},{8,0},{12,4},{1,9},{5,13},{9,1},{13,5},{2,10},{6,14},... | collective-permute-start | bytes 196616 | tf_op jit(solution)/shard_map/ppermute | solution.py:34
  46.7 1.4 %collective-permute-start.9 = (bf16[8,4,8,128]{3,2,1,0:T(8,128)(2,1)S(1)}, bf16[8,4,8,128]{3,2,1,0:T(8,128)(2,1)S(1)}, u32[]{:S(2)}, u32[]{:S(2)}) collective-permute-start(bf16[8,4,8,128]{3,2,1,0:T(8,128)(2,1)S(1)} %fusion.13), channel_id=1, source_target_pairs={{0,12},{4,0},{8,4},{12,8},{1,13},{5,1},{9,5},{13,9},{2,14},{6,2},{... | collective-permute-start | bytes 196616 | tf_op jit(solution)/shard_map/ppermute | solution.py:34
  48.1 0.8 %collective-permute-done.7 = bf16[8,4,8,128]{3,2,1,0:T(8,128)(2,1)S(1)} collective-permute-done((bf16[8,4,8,128]{3,2,1,0:T(8,128)(2,1)S(1)}, bf16[8,4,8,128]{3,2,1,0:T(8,128)(2,1)S(1)}, u32[]{:S(2)}, u32[]{:S(2)}) %collective-permute-start.7) | collective-permute-done | bytes 65568 | tf_op jit(solution)/shard_map/ppermute | solution.py:34
  48.9 0.8 %collective-permute-done.8 = bf16[8,4,8,128]{3,2,1,0:T(8,128)(2,1)S(1)} collective-permute-done((bf16[8,4,8,128]{3,2,1,0:T(8,128)(2,1)S(1)}, bf16[8,4,8,128]{3,2,1,0:T(8,128)(2,1)S(1)}, u32[]{:S(2)}, u32[]{:S(2)}) %collective-permute-start.8) | collective-permute-done | bytes 65568 | tf_op jit(solution)/shard_map/ppermute | solution.py:34
  49.7 0.2 collective-permute-done.9
  50.0 0.6 gather_fusion
  50.6 0.3 convolution_bitcast_fusion
  51.0 1.2 %collective-permute-start.11 = (f32[32,512]{1,0:T(8,128)S(1)}, f32[32,512]{1,0:T(8,128)S(1)}, u32[]{:S(2)}, u32[]{:S(2)}) collective-permute-start(f32[32,512]{1,0:T(8,128)S(1)} %get-tuple-element.28), channel_id=1, source_target_pairs={{0,2},{1,3},{2,0},{3,1},{4,6},{5,7},{6,4},{7,5},{8,10},{9,11},{10,... | collective-permute-start | bytes 196616 | tf_op jit(solution)/shard_map/ppermute | solution.py:47
  52.2 2.8 %collective-permute-start.12 = (f32[32,512]{1,0:T(8,128)S(1)}, f32[32,512]{1,0:T(8,128)S(1)}, u32[]{:S(2)}, u32[]{:S(2)}) collective-permute-start(f32[32,512]{1,0:T(8,128)S(1)} %get-tuple-element.27), channel_id=1, source_target_pairs={{0,3},{1,0},{2,1},{3,2},{4,7},{5,4},{6,5},{7,6},{8,11},{9,8},{10,9... | collective-permute-start | bytes 196616 | tf_op jit(solution)/shard_map/ppermute | solution.py:47
  55.1 2.8 %collective-permute-done.10 = f32[32,512]{1,0:T(8,128)S(1)} collective-permute-done((f32[32,512]{1,0:T(8,128)S(1)}, f32[32,512]{1,0:T(8,128)S(1)}, u32[]{:S(2)}, u32[]{:S(2)}) %collective-permute-start.10) | collective-permute-done | bytes 65568 | tf_op jit(solution)/shard_map/ppermute | solution.py:47
  57.9 1.9 %collective-permute-done.11 = f32[32,512]{1,0:T(8,128)S(1)} collective-permute-done((f32[32,512]{1,0:T(8,128)S(1)}, f32[32,512]{1,0:T(8,128)S(1)}, u32[]{:S(2)}, u32[]{:S(2)}) %collective-permute-start.11) | collective-permute-done | bytes 65568 | tf_op jit(solution)/shard_map/ppermute | solution.py:47
  59.8 0.6 %reshape.137 = bf16[8,4,512]{2,1,0:T(4,128)(2,1)} reshape(bf16[32,512]{1,0:T(8,128)(2,1)S(1)} %fusion.16) | data formatting | bytes 65536 | tf_op jit(solution)/shard_map/reshape | solution.py:262
  (58 shorter events, 1.0 us)
Async XLA Ops:
  0.6 50.0 %copy-start = (bf16[1024,512]{1,0:T(8,128)(2,1)S(1)}, bf16[1024,512]{1,0:T(8,128)(2,1)}, u32[]{:S(2)}) copy-start(bf16[1024,512]{1,0:T(8,128)(2,1)} %param.24) | copy-start | bytes 3145732
  0.6 16.3 %copy-start.3 = (bf16[4,1024]{1,0:T(4,128)(2,1)S(1)}, bf16[4,1024]{1,0:T(4,128)(2,1)}, u32[]{:S(2)}) copy-start(bf16[4,1024]{1,0:T(4,128)(2,1)} %param.20) | copy-start | bytes 24580
  0.7 16.9 %copy-start.4 = (bf16[4,1024]{1,0:T(4,128)(2,1)S(1)}, bf16[4,1024]{1,0:T(4,128)(2,1)}, u32[]{:S(2)}) copy-start(bf16[4,1024]{1,0:T(4,128)(2,1)} %param.19) | copy-start | bytes 24580
  0.7 20.9 %copy-start.7 = (f32[8]{0:T(128)S(1)}, f32[8]{0:T(128)}, u32[]{:S(2)}) copy-start(f32[8]{0:T(128)} %param.21) | copy-start | bytes 100
  0.7 20.9 %copy-start.1 = (bf16[8,3,1024]{2,0,1:T(8,128)(2,1)S(1)}, bf16[8,3,1024]{2,0,1:T(8,128)(2,1)}, u32[]{:S(2)}) copy-start(bf16[8,3,1024]{2,0,1:T(8,128)(2,1)} %param.26) | copy-start | bytes 147460
  0.7 21.0 %copy-start.2 = (bf16[8,3,1024]{2,0,1:T(8,128)(2,1)S(1)}, bf16[8,3,1024]{2,0,1:T(8,128)(2,1)}, u32[]{:S(2)}) copy-start(bf16[8,3,1024]{2,0,1:T(8,128)(2,1)} %param.25) | copy-start | bytes 147460
  0.7 21.1 %copy-start.6 = (f32[8]{0:T(128)S(1)}, f32[8]{0:T(128)}, u32[]{:S(2)}) copy-start(f32[8]{0:T(128)} %param.22) | copy-start | bytes 100
  0.7 7.0 %collective-permute-start = (bf16[8,4,512]{2,1,0:T(4,128)(2,1)}, bf16[8,4,512]{2,1,0:T(4,128)(2,1)S(1)}, u32[]{:S(2)}, u32[]{:S(2)}) collective-permute-start(bf16[8,4,512]{2,1,0:T(4,128)(2,1)} %param.15), channel_id=1, source_target_pairs={{0,3},{1,0},{2,1},{3,2},{4,7},{5,4},{6,5},{7,6},{8,11},{9,8},{10,9... | collective-permute-start | bytes 98312 | tf_op jit(solution)/shard_map/ppermute | solution.py:73
  5.8 5.0 %collective-permute-start.1 = (bf16[8,4,512]{2,1,0:T(4,128)(2,1)}, bf16[8,4,512]{2,1,0:T(4,128)(2,1)S(1)}, u32[]{:S(2)}, u32[]{:S(2)}) collective-permute-start(bf16[8,4,512]{2,1,0:T(4,128)(2,1)} %param.15), channel_id=1, source_target_pairs={{0,2},{1,3},{2,0},{3,1},{4,6},{5,7},{6,4},{7,5},{8,10},{9,11},{10,... | collective-permute-start | bytes 98312 | tf_op jit(solution)/shard_map/ppermute | solution.py:73
  5.8 5.9 %collective-permute-start.2 = (bf16[8,4,512]{2,1,0:T(4,128)(2,1)}, bf16[8,4,512]{2,1,0:T(4,128)(2,1)S(1)}, u32[]{:S(2)}, u32[]{:S(2)}) collective-permute-start(bf16[8,4,512]{2,1,0:T(4,128)(2,1)} %param.15), channel_id=1, source_target_pairs={{0,1},{1,2},{2,3},{3,0},{4,5},{5,6},{6,7},{7,4},{8,9},{9,10},{10,1... | collective-permute-start | bytes 98312 | tf_op jit(solution)/shard_map/ppermute | solution.py:73
  17.0 2.0 %collective-permute-start.4 = (f32[32,3200]{1,0:T(8,128)}, f32[32,3200]{1,0:T(8,128)S(1)}, u32[]{:S(2)}, u32[]{:S(2)}) collective-permute-start(f32[32,3200]{1,0:T(8,128)} %get-tuple-element.12), channel_id=1, source_target_pairs={{0,4},{4,0},{8,12},{12,8},{1,5},{5,1},{9,13},{13,9},{2,6},{6,2},{1... | collective-permute-start | bytes 1228808 | tf_op jit(solution)/shard_map/ppermute | solution.py:213
  17.0 5.5 %collective-permute-start.3 = (f32[32,3200]{1,0:T(8,128)}, f32[32,3200]{1,0:T(8,128)S(1)}, u32[]{:S(2)}, u32[]{:S(2)}) collective-permute-start(f32[32,3200]{1,0:T(8,128)} %get-tuple-element.10), channel_id=1, source_target_pairs={{0,4},{4,0},{8,12},{12,8},{1,5},{5,1},{9,13},{13,9},{2,6},{6,2},{1... | collective-permute-start | bytes 1228808 | tf_op jit(solution)/shard_map/ppermute | solution.py:213
  20.0 6.8 %collective-permute-start.5 = (f32[32,1152]{1,0:T(8,128)S(1)}, f32[32,1152]{1,0:T(8,128)S(1)}, u32[]{:S(2)}, u32[]{:S(2)}) collective-permute-start(f32[32,1152]{1,0:T(8,128)S(1)} %slice.126), channel_id=1, source_target_pairs={{0,8},{4,12},{8,0},{12,4},{1,9},{5,13},{9,1},{13,5},{2,10},{6,14},... | collective-permute-start | bytes 442376 | tf_op jit(solution)/shard_map/ppermute | solution.py:220
  21.9 9.7 %collective-permute-start.6 = (f32[32,2048]{1,0:T(8,128)S(1)}, f32[32,2048]{1,0:T(8,128)S(1)}, u32[]{:S(2)}, u32[]{:S(2)}) collective-permute-start(f32[32,2048]{1,0:T(8,128)S(1)} %slice.142), channel_id=1, source_target_pairs={{0,8},{4,12},{8,0},{12,4},{1,9},{5,13},{9,1},{13,5},{2,10},{6,14},... | collective-permute-start | bytes 786440 | tf_op jit(solution)/shard_map/ppermute | solution.py:221
  29.9 14.1 %copy-start.5 = (f32[128]{0:T(128)S(1)}, f32[128]{0:T(128)}, u32[]{:S(2)}) copy-start(f32[128]{0:T(128)} %param.23) | copy-start | bytes 1540
  45.1 3.8 %collective-permute-start.7 = (bf16[8,4,8,128]{3,2,1,0:T(8,128)(2,1)S(1)}, bf16[8,4,8,128]{3,2,1,0:T(8,128)(2,1)S(1)}, u32[]{:S(2)}, u32[]{:S(2)}) collective-permute-start(bf16[8,4,8,128]{3,2,1,0:T(8,128)(2,1)S(1)} %fusion.13), channel_id=1, source_target_pairs={{0,4},{4,8},{8,12},{12,0},{1,5},{5,9},{9,13},{13,1},{2,6},{6,10},{... | collective-permute-start | bytes 196616 | tf_op jit(solution)/shard_map/ppermute | solution.py:34
  45.1 4.6 %collective-permute-start.8 = (bf16[8,4,8,128]{3,2,1,0:T(8,128)(2,1)S(1)}, bf16[8,4,8,128]{3,2,1,0:T(8,128)(2,1)S(1)}, u32[]{:S(2)}, u32[]{:S(2)}) collective-permute-start(bf16[8,4,8,128]{3,2,1,0:T(8,128)(2,1)S(1)} %fusion.13), channel_id=1, source_target_pairs={{0,8},{4,12},{8,0},{12,4},{1,9},{5,13},{9,1},{13,5},{2,10},{6,14},... | collective-permute-start | bytes 196616 | tf_op jit(solution)/shard_map/ppermute | solution.py:34
  46.7 3.3 %collective-permute-start.9 = (bf16[8,4,8,128]{3,2,1,0:T(8,128)(2,1)S(1)}, bf16[8,4,8,128]{3,2,1,0:T(8,128)(2,1)S(1)}, u32[]{:S(2)}, u32[]{:S(2)}) collective-permute-start(bf16[8,4,8,128]{3,2,1,0:T(8,128)(2,1)S(1)} %fusion.13), channel_id=1, source_target_pairs={{0,12},{4,0},{8,4},{12,8},{1,13},{5,1},{9,5},{13,9},{2,14},{6,2},{... | collective-permute-start | bytes 196616 | tf_op jit(solution)/shard_map/ppermute | solution.py:34
  51.0 6.9 %collective-permute-start.10 = (f32[32,512]{1,0:T(8,128)S(1)}, f32[32,512]{1,0:T(8,128)S(1)}, u32[]{:S(2)}, u32[]{:S(2)}) collective-permute-start(f32[32,512]{1,0:T(8,128)S(1)} %get-tuple-element.26), channel_id=1, source_target_pairs={{0,1},{1,2},{2,3},{3,0},{4,5},{5,6},{6,7},{7,4},{8,9},{9,10},{10,1... | collective-permute-start | bytes 196616 | tf_op jit(solution)/shard_map/ppermute | solution.py:47
  51.0 8.7 %collective-permute-start.11 = (f32[32,512]{1,0:T(8,128)S(1)}, f32[32,512]{1,0:T(8,128)S(1)}, u32[]{:S(2)}, u32[]{:S(2)}) collective-permute-start(f32[32,512]{1,0:T(8,128)S(1)} %get-tuple-element.28), channel_id=1, source_target_pairs={{0,2},{1,3},{2,0},{3,1},{4,6},{5,7},{6,4},{7,5},{8,10},{9,11},{10,... | collective-permute-start | bytes 196616 | tf_op jit(solution)/shard_map/ppermute | solution.py:47
  52.2 7.6 %collective-permute-start.12 = (f32[32,512]{1,0:T(8,128)S(1)}, f32[32,512]{1,0:T(8,128)S(1)}, u32[]{:S(2)}, u32[]{:S(2)}) collective-permute-start(f32[32,512]{1,0:T(8,128)S(1)} %get-tuple-element.27), channel_id=1, source_target_pairs={{0,3},{1,0},{2,1},{3,2},{4,7},{5,4},{6,5},{7,6},{8,11},{9,8},{10,9... | collective-permute-start | bytes 196616 | tf_op jit(solution)/shard_map/ppermute | solution.py:47

commit v15 on v14

--- a/solution.py
+++ b/solution.py
@@ -86,6 +86,16 @@
         y = lax.dot_general(
             x, w_ref[...], (((1,), (contract,)), ((), ())), preferred_element_type=jnp.float32
         )
+        if w_ref is wvz_ref:
+            half = width // 2
+            for h in range(width // (2 * DV)):
+                for i, o_ref in enumerate(outs):
+                    rows = y[i * section : (i + 1) * section]
+                    o_ref[:, offset + h * DV : offset + (h + 1) * DV] = rows[:, 2 * h * DV : (2 * h + 1) * DV]
+                    o_ref[:, offset + half + h * DV : offset + half + (h + 1) * DV] = rows[
+                        :, (2 * h + 1) * DV : (2 * h + 2) * DV
+                    ]
+            continue
         for i, o_ref in enumerate(outs):
             o_ref[:, offset : offset + width] = y[i * section : (i + 1) * section]
     for o_ref in outs:
@@ -213,21 +223,20 @@
     part = [keep + lax.ppermute(send, "dp", pair) for send, keep in zip(outs[:chips], outs[chips:])]
     width_ba = w_ba.shape[1]
     split = width_qk + (-(-width_ba // 128) * 128)
-    summed_first = part[0][:, :split]
-    summed_vz = part[0][:, split:]
+    bounds = [(0, split), (split, split + width_vz)]
+    summed = [part[0][:, lo:hi] for lo, hi in bounds]
     for s in range(1, chips):
         perm = [(i, ((i // 2 + s) % chips) * 2 + i % 2) for i in range(n_dp)]
-        summed_first = summed_first + lax.ppermute(part[s][:, :split], "dp", perm)
-        summed_vz = summed_vz + lax.ppermute(part[s][:, split:], "dp", perm)
+        summed = [acc + lax.ppermute(part[s][:, lo:hi], "dp", perm) for acc, (lo, hi) in zip(summed, bounds)]
+    summed_first, summed_vz = summed
+    summed_v = summed_vz[:, : width_vz // 2]
+    summed_z = summed_vz[:, width_vz // 2 :]
     summed_qk = summed_first[:, :width_qk]
     summed_ba = summed_first[:, width_qk : width_qk + width_ba]
     qk_proj = summed_qk.astype(jnp.bfloat16).reshape(rows_mem, step_count, width_qk)
-    vz_proj = summed_vz.astype(jnp.bfloat16).reshape(rows_mem, step_count, width_vz)
     ba_proj = summed_ba.astype(jnp.bfloat16).reshape(rows_mem, step_count, -1)
-
-    split_vz = vz_proj.reshape(rows_mem, step_count, heads, 2, DV)
-    values_now = split_vz[:, :, :, 0, :].reshape(rows_mem, step_count, heads * DV)
-    gate_z = split_vz[:, :, :, 1, :].astype(jnp.float32)
+    values_now = summed_v.astype(jnp.bfloat16).reshape(rows_mem, step_count, heads * DV)
+    gate_z = summed_z.astype(jnp.bfloat16).astype(jnp.float32).reshape(rows_mem, step_count, heads, DV)
 
     qk_conv = conv_steps(conv_state_qk, qk_proj, conv_qk).reshape(rows_mem, step_count, -1, 2, DK)
     v_conv = conv_steps(conv_state_v, values_now, conv_v)

time: 60.9 us -> 60.2 us (0.989)
  starting transfers between devices: 15.9 us -> 13.8 us
  waiting for transfers between devices: 16.6 us -> 18.4 us
    ppermute x3, waiting for transfers between devices: 1.9 us -> 4.1 us  [gather_rows(): pieces.append(lax.ppermute(x, axis, [(i, (i + s) % n) for i in range(n)]))]
    ppermute x3, starting transfers between devices: 3.01 us -> 1.78 us  [gather_rows(): pieces.append(lax.ppermute(x, axis, [(i, (i + s) % n) for i in range(n)]))]
    ppermute x3, starting transfers between devices: 4.09 us -> 3.2 us  [scatter_sum_rows(): acc = acc + lax.ppermute(send, axis, [(i, (i + s) % n) for i in range(n)])]
where the time goes in v15:
time: 60.2 us; the launch traced here: 59.7 us
  waiting for transfers between devices  18.4 us (31%)
  starting transfers between devices  13.8 us (23%)
  Pallas kernels  13.6 us (23%)
  other arithmetic  7.93 us (13%)
  local copies, waits for them, and re-layouts  4.59 us (8%)
  between operations  1.02 us (2%)
    pallas_call x1, Pallas kernels, recurrence(): pl.pallas_call(kern, grid=(rows,), in_specs=[pl.BlockSpec(memory_space=pl...  9.9 us
    ppermute x3, starting transfers between devices, gather_pieces(): pieces.append(lax.ppermute(x, axis, [(i, (i + s) % n) for i in range(n)]))  6.11 us
    ppermute x3, waiting for transfers between devices, gather_pieces(): pieces.append(lax.ppermute(x, axis, [(i, (i + s) % n) for i in range(n)]))  4.91 us
    ppermute x3, waiting for transfers between devices, scatter_sum_rows(): acc = acc + lax.ppermute(send, axis, [(i, (i + s) % n) for i in range(n)])  4.36 us
    ppermute x3, waiting for transfers between devices, gather_rows(): pieces.append(lax.ppermute(x, axis, [(i, (i + s) % n) for i in range(n)]))  4.1 us
    pallas_call x1, Pallas kernels, projection(): pl.pallas_call(projection_kernel, out_shape=[jax.ShapeDtypeStruct((rows,...  3.72 us
    ppermute x2, waiting for transfers between devices, shards(): lax.ppermute(part[s][:, lo:hi], 'dp', perm)  3.69 us
    ppermute x3, starting transfers between devices, scatter_sum_rows(): acc = acc + lax.ppermute(send, axis, [(i, (i + s) % n) for i in range(n)])  3.2 us
  transfers between devices with their start and end apart: 13, of which 11 were waited for; matrix products, arithmetic and copies ran while one was open for 11% of the time, Pallas kernels for 0%

profile of v15, /device:TPU:0, one launch (start us, length us, event | category | flops | bytes accessed | tf_op | source)
XLA Modules:
  0.0 59.7 jit_solution(7123858343898091195)
XLA Ops:
  0.7 5.1 %collective-permute-start = (bf16[8,4,512]{2,1,0:T(4,128)(2,1)}, bf16[8,4,512]{2,1,0:T(4,128)(2,1)S(1)}, u32[]{:S(2)}, u32[]{:S(2)}) collective-permute-start(bf16[8,4,512]{2,1,0:T(4,128)(2,1)} %param.15), channel_id=1, source_target_pairs={{0,3},{1,0},{2,1},{3,2},{4,7},{5,4},{6,5},{7,6},{8,11},{9,8},{10,9... | collective-permute-start | bytes 98312 | tf_op jit(solution)/shard_map/ppermute | solution.py:73
  5.8 1.0 %collective-permute-start.2 = (bf16[8,4,512]{2,1,0:T(4,128)(2,1)}, bf16[8,4,512]{2,1,0:T(4,128)(2,1)S(1)}, u32[]{:S(2)}, u32[]{:S(2)}) collective-permute-start(bf16[8,4,512]{2,1,0:T(4,128)(2,1)} %param.15), channel_id=1, source_target_pairs={{0,1},{1,2},{2,3},{3,0},{4,5},{5,6},{6,7},{7,4},{8,9},{9,10},{10,1... | collective-permute-start | bytes 98312 | tf_op jit(solution)/shard_map/ppermute | solution.py:73
  6.8 0.9 %collective-permute-done = bf16[8,4,512]{2,1,0:T(4,128)(2,1)S(1)} collective-permute-done((bf16[8,4,512]{2,1,0:T(4,128)(2,1)}, bf16[8,4,512]{2,1,0:T(4,128)(2,1)S(1)}, u32[]{:S(2)}, u32[]{:S(2)}) %collective-permute-start) | collective-permute-done | bytes 32800 | tf_op jit(solution)/shard_map/ppermute | solution.py:73
  7.7 3.1 %collective-permute-done.1 = bf16[8,4,512]{2,1,0:T(4,128)(2,1)S(1)} collective-permute-done((bf16[8,4,512]{2,1,0:T(4,128)(2,1)}, bf16[8,4,512]{2,1,0:T(4,128)(2,1)S(1)}, u32[]{:S(2)}, u32[]{:S(2)}) %collective-permute-start.1) | collective-permute-done | bytes 32800 | tf_op jit(solution)/shard_map/ppermute | solution.py:73
  10.8 0.9 %collective-permute-done.2 = bf16[8,4,512]{2,1,0:T(4,128)(2,1)S(1)} collective-permute-done((bf16[8,4,512]{2,1,0:T(4,128)(2,1)}, bf16[8,4,512]{2,1,0:T(4,128)(2,1)S(1)}, u32[]{:S(2)}, u32[]{:S(2)}) %collective-permute-start.2) | collective-permute-done | bytes 32800 | tf_op jit(solution)/shard_map/ppermute | solution.py:73
  11.7 0.8 %select_select_fusion.3 = (bf16[4,8,512]{2,1,0:T(8,128)(2,1)S(1)}, bf16[4,8,512]{2,1,0:T(8,128)(2,1)S(1)}, bf16[4,8,512]{2,1,0:T(8,128)(2,1)S(1)}, bf16[4,8,512]{2,1,0:T(8,128)(2,1)S(1)}) fusion(bf16[4,8,512]{2,1,0:T(8,128)(2,1)S(1)} %bitcast.91, bf16[4,8,512]{2,1,0:T(8,128)(2,1)S(1)} %bitcast.92, bf16[4,8,512]{2,1,0:T(8,128)(2,1)S(1)} %bitcast.93, ...), kind=kLoop, calls=%fused_computation.46 | loop fusion | flops 196608 | bytes 262156 | tf_op jit(solution)/shard_map/jit(_where)/select_n | solution.py:217
  12.6 0.7 %pad_maximum_fusion.1.x_ref = bf16[128,512]{1,0:T(8,128)(2,1)} fusion(bf16[32,512]{1,0:T(8,128)(2,1)S(1)} %reshape.137, bf16[32,512]{1,0:T(8,128)(2,1)S(1)} %reshape.136, bf16[32,512]{1,0:T(8,128)(2,1)S(1)} %reshape.135, bf16[32,512]{1,0:T(8,128)(2,1)S(1)} %reshape.134), kind=kLoop, calls=%fused_computation.24 | loop fusion | flops 524288 | bytes 262144 | tf_op jit(solution)/shard_map/concatenate | solution.py:220
  13.3 3.7 %shard_map.140 = (f32[32,3200]{1,0:T(8,128)}, f32[32,3200]{1,0:T(8,128)}, f32[32,3200]{1,0:T(8,128)}, f32[32,3200]{1,0:T(8,128)}) custom-call(bf16[128,512]{1,0:T(8,128)(2,1)} %pad_maximum_fusion.1.x_ref, bf16[512,1024]{1,0:T(8,128)(2,1)} %wqk_ref.1, bf16[512,2048]{1,0:T(8,128)(2,1)} %wvz_ref.1, bf16[16,512]{1,0:T(8,128)(2,1)} %bitcast.94), custom_call_target="tpu_custom_call" | custom-call | flops 419430400 | bytes 5046272 | tf_op jit(solution)/shard_map/pallas_call | solution.py:111
  17.0 0.6 collective-permute-start.3
  17.6 1.3 %collective-permute-done.4 = f32[32,3200]{1,0:T(8,128)S(1)} collective-permute-done((f32[32,3200]{1,0:T(8,128)}, f32[32,3200]{1,0:T(8,128)S(1)}, u32[]{:S(2)}, u32[]{:S(2)}) %collective-permute-start.4) | collective-permute-done | bytes 409632 | tf_op jit(solution)/shard_map/ppermute | solution.py:223
  18.9 1.1 %add.200 = f32[32,3200]{1,0:T(8,128)S(1)} add(f32[32,3200]{1,0:T(8,128)} %get-tuple-element.11, f32[32,3200]{1,0:T(8,128)S(1)} %collective-permute-done.4) | non-fusion elementwise | flops 102400 | bytes 1228800 | tf_op jit(solution)/shard_map/add | solution.py:223
  20.0 1.6 %collective-permute-start.5 = (f32[32,1152]{1,0:T(8,128)S(1)}, f32[32,1152]{1,0:T(8,128)S(1)}, u32[]{:S(2)}, u32[]{:S(2)}) collective-permute-start(f32[32,1152]{1,0:T(8,128)S(1)} %slice.128), channel_id=1, source_target_pairs={{0,8},{4,12},{8,0},{12,4},{1,9},{5,13},{9,1},{13,5},{2,10},{6,14},... | collective-permute-start | bytes 442376 | tf_op jit(solution)/shard_map/ppermute | solution.py:230
  21.6 0.1 add.204
  21.7 0.1 mul.181
  21.9 0.6 %collective-permute-start.6 = (f32[32,2048]{1,0:T(8,128)S(1)}, f32[32,2048]{1,0:T(8,128)S(1)}, u32[]{:S(2)}, u32[]{:S(2)}) collective-permute-start(f32[32,2048]{1,0:T(8,128)S(1)} %slice.144), channel_id=1, source_target_pairs={{0,8},{4,12},{8,0},{12,4},{1,9},{5,13},{9,1},{13,5},{2,10},{6,14},... | collective-permute-start | bytes 786440 | tf_op jit(solution)/shard_map/ppermute | solution.py:230
  22.6 1.0 %add.199 = f32[32,3200]{1,0:T(8,128)S(1)} add(f32[32,3200]{1,0:T(8,128)} %get-tuple-element.9, f32[32,3200]{1,0:T(8,128)S(1)} %collective-permute-done.3) | non-fusion elementwise | flops 102400 | bytes 1228800 | tf_op jit(solution)/shard_map/add | solution.py:223
  23.6 3.2 %collective-permute-done.5 = f32[32,1152]{1,0:T(8,128)S(1)} collective-permute-done((f32[32,1152]{1,0:T(8,128)S(1)}, f32[32,1152]{1,0:T(8,128)S(1)}, u32[]{:S(2)}, u32[]{:S(2)}) %collective-permute-start.5) | collective-permute-done | bytes 147488 | tf_op jit(solution)/shard_map/ppermute | solution.py:230
  26.9 0.1 reshape.207
  27.0 0.1 copy.34
  27.2 0.1 copy.43
  27.6 0.2 divide_multiply_fusion.1
  27.8 0.1 reshape.139
  27.9 0.1 fusion.18
  28.0 0.1 multiply_reduce_fusion.2
  28.1 0.1 multiply_reduce_fusion.1
  28.2 1.0 %copy.39.qt_ref = f32[8,128,16]{2,1,0:T(8,128)} copy(f32[8,128,16]{1,0,2:T(8,128)S(1)} %bitcast.80) | data formatting | bytes 131072 | tf_op jit(solution)/shard_map/reshape | solution.py:247
  29.3 0.1 fusion.12
  29.4 1.0 %copy.40.kt_ref = f32[8,128,16]{2,1,0:T(8,128)} copy(f32[8,128,16]{1,0,2:T(8,128)S(1)} %bitcast.81) | data formatting | bytes 131072 | tf_op jit(solution)/shard_map/reshape | solution.py:248
  30.4 0.7 %pad_maximum_fusion.2.gates_ref = f32[8,64]{1,0:T(8,128)} fusion(f32[8,32]{1,0:T(8,128)S(1)} %fusion.14, f32[8,32]{1,0:T(8,128)S(1)} %div.76), kind=kLoop, calls=%fused_computation.56 | loop fusion | flops 512 | bytes 4096 | tf_op jit(solution)/shard_map/concatenate | solution.py:253
  31.1 0.5 collective-permute-done.6
  31.8 0.8 %divide_multiply_fusion.v_ref = f32[8,4,1024]{2,1,0:T(4,128)} fusion(f32[8,7,1024]{2,1,0:T(8,128)S(1)} %maximum_convert_fusion.1, f32[1024]{0:T(1024)S(1)} %bitcast.98, f32[1024]{0:T(1024)S(1)} %bitcast.97, f32[1024]{0:T(1024)S(1)} %bitcast.96, f32[1024]{0:T(1024)S(1)} %bitcast.95), kind=kLoop, calls=%fused_computation.8 | loop fusion | flops 360448 | bytes 671744 | tf_op jit(solution)/shard_map/jit(silu)/mul | solution.py:26
  32.6 9.9 %shard_map.141 = (f32[8,8,128,128]{3,2,1,0:T(8,128)}, f32[8,4,8,128]{3,2,1,0:T(8,128)}) custom-call(f32[8,64]{1,0:T(8,128)} %pad_maximum_fusion.2.gates_ref, f32[8,128,16]{2,1,0:T(8,128)} %copy.39.qt_ref, f32[8,128,16]{2,1,0:T(8,128)} %copy.40.kt_ref, f32[8,4,1024]{2,1,0:T(4,128)} %divide_multiply_fusion.v_ref, f32[8,8,128,128]{3,2,1,0:T(8,128)} %s_ref.1), custom_call_target="tpu_custom_call" | custom-call | flops 33554432 | bytes 8388608 | tf_op jit(solution)/shard_map/pallas_call | solution.py:152
  42.5 1.0 %multiply_reduce_fusion = f32[8,4,8]{2,1,0:T(4,128)S(1)} fusion(f32[8,4,8,128]{3,2,1,0:T(8,128)} %get-tuple-element.13), kind=kLoop, calls=%fused_computation.29 | loop fusion | flops 65280 | bytes 132096 | tf_op jit(solution)/shard_map/reduce_sum | solution.py:259
  43.6 1.0 %multiply_convert_fusion = bf16[8,4,8,128]{3,2,1,0:T(8,128)(2,1)S(1)} fusion(f32[8,4,8,128]{3,2,1,0:T(8,128)S(1)} %bitcast.79, f32[8,4,8,128]{3,2,1,0:T(8,128)} %get-tuple-element.13, f32[128]{0:T(128)S(1)} %copy-done.5, f32[8,4,8]{2,1,0:T(4,128)S(1)} %add_rsqrt_fusion), kind=kLoop, calls=%fused_computation.28 | loop fusion | flops 262144 | bytes 329216 | tf_op jit(solution)/shard_map/convert_element_type | solution.py:261
  44.6 0.5 collective-permute-start.9
  45.0 1.2 %collective-permute-start.8 = (bf16[8,4,8,128]{3,2,1,0:T(8,128)(2,1)S(1)}, bf16[8,4,8,128]{3,2,1,0:T(8,128)(2,1)S(1)}, u32[]{:S(2)}, u32[]{:S(2)}) collective-permute-start(bf16[8,4,8,128]{3,2,1,0:T(8,128)(2,1)S(1)} %multiply_convert_fusion), channel_id=1, source_target_pairs={{0,8},{4,12},{8,0},{12,4},{1,9},{5,13},{9,1},{13,5},{2,10},{6,14},... | collective-permute-start | bytes 196616 | tf_op jit(solution)/shard_map/ppermute | solution.py:34
  46.2 0.2 collective-permute-start.7
  46.4 0.6 collective-permute-done.9
  47.0 3.3 %collective-permute-done.8 = bf16[8,4,8,128]{3,2,1,0:T(8,128)(2,1)S(1)} collective-permute-done((bf16[8,4,8,128]{3,2,1,0:T(8,128)(2,1)S(1)}, bf16[8,4,8,128]{3,2,1,0:T(8,128)(2,1)S(1)}, u32[]{:S(2)}, u32[]{:S(2)}) %collective-permute-start.8) | collective-permute-done | bytes 65568 | tf_op jit(solution)/shard_map/ppermute | solution.py:34
  50.3 0.2 collective-permute-done.7
  50.5 0.6 %gather_fusion = bf16[4,8,4,8,128]{4,3,2,1,0:T(8,128)(2,1)S(1)} fusion(bf16[4,8,4,8,128]{4,3,2,1,0:T(8,128)(2,1)S(1)} %pad_maximum_fusion, s32[1024]{0:T(1024)S(1)} %pad_clamp_fusion), kind=kCustom, calls=%fused_computation | custom fusion | bytes 524304 | tf_op jit(solution)/shard_map/jit(_take)/gather | solution.py:37
  51.1 0.3 convolution_bitcast_fusion
  51.5 0.7 %collective-permute-start.12 = (f32[32,512]{1,0:T(8,128)S(1)}, f32[32,512]{1,0:T(8,128)S(1)}, u32[]{:S(2)}, u32[]{:S(2)}) collective-permute-start(f32[32,512]{1,0:T(8,128)S(1)} %get-tuple-element.27), channel_id=1, source_target_pairs={{0,3},{1,0},{2,1},{3,2},{4,7},{5,4},{6,5},{7,6},{8,11},{9,8},{10,9... | collective-permute-start | bytes 196616 | tf_op jit(solution)/shard_map/ppermute | solution.py:47
  52.1 0.6 %collective-permute-start.11 = (f32[32,512]{1,0:T(8,128)S(1)}, f32[32,512]{1,0:T(8,128)S(1)}, u32[]{:S(2)}, u32[]{:S(2)}) collective-permute-start(f32[32,512]{1,0:T(8,128)S(1)} %get-tuple-element.28), channel_id=1, source_target_pairs={{0,2},{1,3},{2,0},{3,1},{4,6},{5,7},{6,4},{7,5},{8,10},{9,11},{10,... | collective-permute-start | bytes 196616 | tf_op jit(solution)/shard_map/ppermute | solution.py:47
  52.7 1.9 %collective-permute-start.10 = (f32[32,512]{1,0:T(8,128)S(1)}, f32[32,512]{1,0:T(8,128)S(1)}, u32[]{:S(2)}, u32[]{:S(2)}) collective-permute-start(f32[32,512]{1,0:T(8,128)S(1)} %get-tuple-element.26), channel_id=1, source_target_pairs={{0,1},{1,2},{2,3},{3,0},{4,5},{5,6},{6,7},{7,4},{8,9},{9,10},{10,1... | collective-permute-start | bytes 196616 | tf_op jit(solution)/shard_map/ppermute | solution.py:47
  54.7 1.1 %collective-permute-done.12 = f32[32,512]{1,0:T(8,128)S(1)} collective-permute-done((f32[32,512]{1,0:T(8,128)S(1)}, f32[32,512]{1,0:T(8,128)S(1)}, u32[]{:S(2)}, u32[]{:S(2)}) %collective-permute-start.12) | collective-permute-done | bytes 65568 | tf_op jit(solution)/shard_map/ppermute | solution.py:47
  55.8 3.2 %collective-permute-done.11 = f32[32,512]{1,0:T(8,128)S(1)} collective-permute-done((f32[32,512]{1,0:T(8,128)S(1)}, f32[32,512]{1,0:T(8,128)S(1)}, u32[]{:S(2)}, u32[]{:S(2)}) %collective-permute-start.11) | collective-permute-done | bytes 65568 | tf_op jit(solution)/shard_map/ppermute | solution.py:47
  59.1 0.6 %reshape.147 = bf16[8,4,512]{2,1,0:T(4,128)(2,1)} reshape(bf16[32,512]{1,0:T(8,128)(2,1)S(1)} %fusion.11) | data formatting | bytes 65536 | tf_op jit(solution)/shard_map/reshape | solution.py:271
  (58 shorter events, 1.0 us)
Async XLA Ops:
  0.6 50.5 %copy-start = (bf16[1024,512]{1,0:T(8,128)(2,1)S(1)}, bf16[1024,512]{1,0:T(8,128)(2,1)}, u32[]{:S(2)}) copy-start(bf16[1024,512]{1,0:T(8,128)(2,1)} %param.24) | copy-start | bytes 3145732
  0.6 16.3 %copy-start.3 = (bf16[4,1024]{1,0:T(4,128)(2,1)S(1)}, bf16[4,1024]{1,0:T(4,128)(2,1)}, u32[]{:S(2)}) copy-start(bf16[4,1024]{1,0:T(4,128)(2,1)} %param.19) | copy-start | bytes 24580
  0.7 16.9 %copy-start.4 = (bf16[4,1024]{1,0:T(4,128)(2,1)S(1)}, bf16[4,1024]{1,0:T(4,128)(2,1)}, u32[]{:S(2)}) copy-start(bf16[4,1024]{1,0:T(4,128)(2,1)} %param.20) | copy-start | bytes 24580
  0.7 20.9 %copy-start.7 = (f32[8]{0:T(128)S(1)}, f32[8]{0:T(128)}, u32[]{:S(2)}) copy-start(f32[8]{0:T(128)} %param.21) | copy-start | bytes 100
  0.7 20.9 %copy-start.6 = (f32[8]{0:T(128)S(1)}, f32[8]{0:T(128)}, u32[]{:S(2)}) copy-start(f32[8]{0:T(128)} %param.22) | copy-start | bytes 100
  0.7 21.1 %copy-start.1 = (bf16[8,3,1024]{2,0,1:T(8,128)(2,1)S(1)}, bf16[8,3,1024]{2,0,1:T(8,128)(2,1)}, u32[]{:S(2)}) copy-start(bf16[8,3,1024]{2,0,1:T(8,128)(2,1)} %param.25) | copy-start | bytes 147460
  0.7 21.1 %copy-start.2 = (bf16[8,3,1024]{2,0,1:T(8,128)(2,1)S(1)}, bf16[8,3,1024]{2,0,1:T(8,128)(2,1)}, u32[]{:S(2)}) copy-start(bf16[8,3,1024]{2,0,1:T(8,128)(2,1)} %param.26) | copy-start | bytes 147460
  0.7 7.0 %collective-permute-start = (bf16[8,4,512]{2,1,0:T(4,128)(2,1)}, bf16[8,4,512]{2,1,0:T(4,128)(2,1)S(1)}, u32[]{:S(2)}, u32[]{:S(2)}) collective-permute-start(bf16[8,4,512]{2,1,0:T(4,128)(2,1)} %param.15), channel_id=1, source_target_pairs={{0,3},{1,0},{2,1},{3,2},{4,7},{5,4},{6,5},{7,6},{8,11},{9,8},{10,9... | collective-permute-start | bytes 98312 | tf_op jit(solution)/shard_map/ppermute | solution.py:73
  5.8 5.0 %collective-permute-start.1 = (bf16[8,4,512]{2,1,0:T(4,128)(2,1)}, bf16[8,4,512]{2,1,0:T(4,128)(2,1)S(1)}, u32[]{:S(2)}, u32[]{:S(2)}) collective-permute-start(bf16[8,4,512]{2,1,0:T(4,128)(2,1)} %param.15), channel_id=1, source_target_pairs={{0,2},{1,3},{2,0},{3,1},{4,6},{5,7},{6,4},{7,5},{8,10},{9,11},{10,... | collective-permute-start | bytes 98312 | tf_op jit(solution)/shard_map/ppermute | solution.py:73
  5.8 5.9 %collective-permute-start.2 = (bf16[8,4,512]{2,1,0:T(4,128)(2,1)}, bf16[8,4,512]{2,1,0:T(4,128)(2,1)S(1)}, u32[]{:S(2)}, u32[]{:S(2)}) collective-permute-start(bf16[8,4,512]{2,1,0:T(4,128)(2,1)} %param.15), channel_id=1, source_target_pairs={{0,1},{1,2},{2,3},{3,0},{4,5},{5,6},{6,7},{7,4},{8,9},{9,10},{10,1... | collective-permute-start | bytes 98312 | tf_op jit(solution)/shard_map/ppermute | solution.py:73
  17.0 2.0 %collective-permute-start.4 = (f32[32,3200]{1,0:T(8,128)}, f32[32,3200]{1,0:T(8,128)S(1)}, u32[]{:S(2)}, u32[]{:S(2)}) collective-permute-start(f32[32,3200]{1,0:T(8,128)} %get-tuple-element.12), channel_id=1, source_target_pairs={{0,4},{4,0},{8,12},{12,8},{1,5},{5,1},{9,13},{13,9},{2,6},{6,2},{1... | collective-permute-start | bytes 1228808 | tf_op jit(solution)/shard_map/ppermute | solution.py:223
  17.0 5.5 %collective-permute-start.3 = (f32[32,3200]{1,0:T(8,128)}, f32[32,3200]{1,0:T(8,128)S(1)}, u32[]{:S(2)}, u32[]{:S(2)}) collective-permute-start(f32[32,3200]{1,0:T(8,128)} %get-tuple-element.10), channel_id=1, source_target_pairs={{0,4},{4,0},{8,12},{12,8},{1,5},{5,1},{9,13},{13,9},{2,6},{6,2},{1... | collective-permute-start | bytes 1228808 | tf_op jit(solution)/shard_map/ppermute | solution.py:223
  20.0 6.8 %collective-permute-start.5 = (f32[32,1152]{1,0:T(8,128)S(1)}, f32[32,1152]{1,0:T(8,128)S(1)}, u32[]{:S(2)}, u32[]{:S(2)}) collective-permute-start(f32[32,1152]{1,0:T(8,128)S(1)} %slice.128), channel_id=1, source_target_pairs={{0,8},{4,12},{8,0},{12,4},{1,9},{5,13},{9,1},{13,5},{2,10},{6,14},... | collective-permute-start | bytes 442376 | tf_op jit(solution)/shard_map/ppermute | solution.py:230
  21.9 9.7 %collective-permute-start.6 = (f32[32,2048]{1,0:T(8,128)S(1)}, f32[32,2048]{1,0:T(8,128)S(1)}, u32[]{:S(2)}, u32[]{:S(2)}) collective-permute-start(f32[32,2048]{1,0:T(8,128)S(1)} %slice.144), channel_id=1, source_target_pairs={{0,8},{4,12},{8,0},{12,4},{1,9},{5,13},{9,1},{13,5},{2,10},{6,14},... | collective-permute-start | bytes 786440 | tf_op jit(solution)/shard_map/ppermute | solution.py:230
  29.4 14.2 %copy-start.5 = (f32[128]{0:T(128)S(1)}, f32[128]{0:T(128)}, u32[]{:S(2)}) copy-start(f32[128]{0:T(128)} %param.23) | copy-start | bytes 1540
  44.6 2.4 %collective-permute-start.9 = (bf16[8,4,8,128]{3,2,1,0:T(8,128)(2,1)S(1)}, bf16[8,4,8,128]{3,2,1,0:T(8,128)(2,1)S(1)}, u32[]{:S(2)}, u32[]{:S(2)}) collective-permute-start(bf16[8,4,8,128]{3,2,1,0:T(8,128)(2,1)S(1)} %multiply_convert_fusion), channel_id=1, source_target_pairs={{0,12},{4,0},{8,4},{12,8},{1,13},{5,1},{9,5},{13,9},{2,14},{6,2},{... | collective-permute-start | bytes 196616 | tf_op jit(solution)/shard_map/ppermute | solution.py:34
  45.0 5.3 %collective-permute-start.8 = (bf16[8,4,8,128]{3,2,1,0:T(8,128)(2,1)S(1)}, bf16[8,4,8,128]{3,2,1,0:T(8,128)(2,1)S(1)}, u32[]{:S(2)}, u32[]{:S(2)}) collective-permute-start(bf16[8,4,8,128]{3,2,1,0:T(8,128)(2,1)S(1)} %multiply_convert_fusion), channel_id=1, source_target_pairs={{0,8},{4,12},{8,0},{12,4},{1,9},{5,13},{9,1},{13,5},{2,10},{6,14},... | collective-permute-start | bytes 196616 | tf_op jit(solution)/shard_map/ppermute | solution.py:34
  46.2 4.3 %collective-permute-start.7 = (bf16[8,4,8,128]{3,2,1,0:T(8,128)(2,1)S(1)}, bf16[8,4,8,128]{3,2,1,0:T(8,128)(2,1)S(1)}, u32[]{:S(2)}, u32[]{:S(2)}) collective-permute-start(bf16[8,4,8,128]{3,2,1,0:T(8,128)(2,1)S(1)} %multiply_convert_fusion), channel_id=1, source_target_pairs={{0,4},{4,8},{8,12},{12,0},{1,5},{5,9},{9,13},{13,1},{2,6},{6,10},{... | collective-permute-start | bytes 196616 | tf_op jit(solution)/shard_map/ppermute | solution.py:34
  51.5 4.3 %collective-permute-start.12 = (f32[32,512]{1,0:T(8,128)S(1)}, f32[32,512]{1,0:T(8,128)S(1)}, u32[]{:S(2)}, u32[]{:S(2)}) collective-permute-start(f32[32,512]{1,0:T(8,128)S(1)} %get-tuple-element.27), channel_id=1, source_target_pairs={{0,3},{1,0},{2,1},{3,2},{4,7},{5,4},{6,5},{7,6},{8,11},{9,8},{10,9... | collective-permute-start | bytes 196616 | tf_op jit(solution)/shard_map/ppermute | solution.py:47
  52.1 6.9 %collective-permute-start.11 = (f32[32,512]{1,0:T(8,128)S(1)}, f32[32,512]{1,0:T(8,128)S(1)}, u32[]{:S(2)}, u32[]{:S(2)}) collective-permute-start(f32[32,512]{1,0:T(8,128)S(1)} %get-tuple-element.28), channel_id=1, source_target_pairs={{0,2},{1,3},{2,0},{3,1},{4,6},{5,7},{6,4},{7,5},{8,10},{9,11},{10,... | collective-permute-start | bytes 196616 | tf_op jit(solution)/shard_map/ppermute | solution.py:47
  52.7 6.3 %collective-permute-start.10 = (f32[32,512]{1,0:T(8,128)S(1)}, f32[32,512]{1,0:T(8,128)S(1)}, u32[]{:S(2)}, u32[]{:S(2)}) collective-permute-start(f32[32,512]{1,0:T(8,128)S(1)} %get-tuple-element.26), channel_id=1, source_target_pairs={{0,1},{1,2},{2,3},{3,0},{4,5},{5,6},{6,7},{7,4},{8,9},{9,10},{10,1... | collective-permute-start | bytes 196616 | tf_op jit(solution)/shard_map/ppermute | solution.py:47

commit v16 on v15

--- a/solution.py
+++ b/solution.py
@@ -219,15 +219,18 @@
             sections.append(picked.reshape(rows_mem * step_count, -1))
     flat_rows = jnp.concatenate(sections, axis=0)
     outs = projection(flat_rows, w_qk, w_vz, w_ba, 2 * chips)
-    pair = [(i, i ^ 1) for i in range(n_dp)]
-    part = [keep + lax.ppermute(send, "dp", pair) for send, keep in zip(outs[:chips], outs[chips:])]
     width_ba = w_ba.shape[1]
     split = width_qk + (-(-width_ba // 128) * 128)
     bounds = [(0, split), (split, split + width_vz)]
-    summed = [part[0][:, lo:hi] for lo, hi in bounds]
+    pair = [(i, i ^ 1) for i in range(n_dp)]
+    part = [
+        [keep[:, lo:hi] + lax.ppermute(send[:, lo:hi], "dp", pair) for lo, hi in bounds]
+        for send, keep in zip(outs[:chips], outs[chips:])
+    ]
+    summed = list(part[0])
     for s in range(1, chips):
         perm = [(i, ((i // 2 + s) % chips) * 2 + i % 2) for i in range(n_dp)]
-        summed = [acc + lax.ppermute(part[s][:, lo:hi], "dp", perm) for acc, (lo, hi) in zip(summed, bounds)]
+        summed = [acc + lax.ppermute(piece, "dp", perm) for acc, piece in zip(summed, part[s])]
     summed_first, summed_vz = summed
     summed_v = summed_vz[:, : width_vz // 2]
     summed_z = summed_vz[:, width_vz // 2 :]

time: 60.2 us -> 64 us (1.063)
  local copies, waits for them, and re-layouts: 4.59 us -> 10.1 us
  waiting for transfers between devices: 18.4 us -> 15 us
  other arithmetic: 7.93 us -> 8.69 us
    slice x2 -> x4, local copies, waits for them, and re-layouts: 0.03 us -> 3.84 us  [shards(): send[:, lo:hi]]
    ppermute x3, waiting for transfers between devices: 4.91 us -> 2.95 us  [gather_pieces(): pieces.append(lax.ppermute(x, axis, [(i, (i + s) % n) for i in range(n)]))]
    slice x2, local copies, waits for them, and re-layouts: 0.03 us -> 1.72 us  [conv_steps(): taps[k][None, None, :]]
    ppermute x4 -> x6, waiting for transfers between devices: 5.04 us -> 3.64 us  [the longest x2 3.63 us: shards(): lax.ppermute(piece, 'dp', perm)]
    another operation x2, other arithmetic: 0.04 us -> 0.98 us
    ppermute x4 -> x6, starting transfers between devices: 2.72 us -> 3.22 us  [the longest x2 2.16 us: shards(): lax.ppermute(piece, 'dp', perm)]
  transfers between devices with their start and end apart: 13 -> 15, of which waited for: 11 -> 8; matrix products, arithmetic and copies ran while one was open for 11% -> 19% of each run, Pallas kernels for 0% -> 0%
where the time goes in v16:
time: 64 us; the launch traced here: 63.3 us
  waiting for transfers between devices  15 us (23%)
  starting transfers between devices  14.3 us (22%)
  Pallas kernels  13.6 us (21%)
  local copies, waits for them, and re-layouts  10.1 us (16%)
  other arithmetic  8.69 us (14%)
  between operations  1.32 us (2%)
    pallas_call x1, Pallas kernels, recurrence(): pl.pallas_call(kern, grid=(rows,), in_specs=[pl.BlockSpec(memory_space=pl...  9.9 us
    ppermute x3, starting transfers between devices, gather_pieces(): pieces.append(lax.ppermute(x, axis, [(i, (i + s) % n) for i in range(n)]))  6.11 us
    ppermute x3, waiting for transfers between devices, scatter_sum_rows(): acc = acc + lax.ppermute(send, axis, [(i, (i + s) % n) for i in range(n)])  4.36 us
    ppermute x3, waiting for transfers between devices, gather_rows(): pieces.append(lax.ppermute(x, axis, [(i, (i + s) % n) for i in range(n)]))  4.1 us
    slice x4, local copies, waits for them, and re-layouts, shards(): send[:, lo:hi]  3.84 us
    pallas_call x1, Pallas kernels, projection(): pl.pallas_call(projection_kernel, out_shape=[jax.ShapeDtypeStruct((rows,...  3.7 us
    ppermute x2, waiting for transfers between devices, shards(): lax.ppermute(piece, 'dp', perm)  3.63 us
    ppermute x3, starting transfers between devices, scatter_sum_rows(): acc = acc + lax.ppermute(send, axis, [(i, (i + s) % n) for i in range(n)])  3.21 us
  transfers between devices with their start and end apart: 15, of which 8 were waited for; matrix products, arithmetic and copies ran while one was open for 19% of the time, Pallas kernels for 0%

profile of v16, /device:TPU:0, one launch (start us, length us, event | category | flops | bytes accessed | tf_op | source)
XLA Modules:
  0.0 63.3 jit_solution(10263415286809808845)
XLA Ops:
  0.7 5.1 %collective-permute-start = (bf16[8,4,512]{2,1,0:T(4,128)(2,1)}, bf16[8,4,512]{2,1,0:T(4,128)(2,1)S(1)}, u32[]{:S(2)}, u32[]{:S(2)}) collective-permute-start(bf16[8,4,512]{2,1,0:T(4,128)(2,1)} %param.15), channel_id=1, source_target_pairs={{0,3},{1,0},{2,1},{3,2},{4,7},{5,4},{6,5},{7,6},{8,11},{9,8},{10,9... | collective-permute-start | bytes 98312 | tf_op jit(solution)/shard_map/ppermute | solution.py:73
  5.8 1.0 %collective-permute-start.2 = (bf16[8,4,512]{2,1,0:T(4,128)(2,1)}, bf16[8,4,512]{2,1,0:T(4,128)(2,1)S(1)}, u32[]{:S(2)}, u32[]{:S(2)}) collective-permute-start(bf16[8,4,512]{2,1,0:T(4,128)(2,1)} %param.15), channel_id=1, source_target_pairs={{0,1},{1,2},{2,3},{3,0},{4,5},{5,6},{6,7},{7,4},{8,9},{9,10},{10,1... | collective-permute-start | bytes 98312 | tf_op jit(solution)/shard_map/ppermute | solution.py:73
  6.8 0.9 %fusion.19 = (f32[1,1024]{1,0:T(1,128)S(1)}, f32[1,1024]{1,0:T(1,128)S(1)}, f32[1,1024]{1,0:T(1,128)S(1)}, f32[1,1024]{1,0:T(1,128)S(1)}) fusion(bf16[4,1024]{1,0:T(4,128)(2,1)} %param.19), kind=kLoop, calls=%fused_computation.67 | loop fusion | bytes 32768 | tf_op jit(solution)/shard_map/slice | solution.py:25
  7.7 0.9 %fusion.18 = (f32[1,1024]{1,0:T(1,128)S(1)}, f32[1,1024]{1,0:T(1,128)S(1)}, f32[1,1024]{1,0:T(1,128)S(1)}, f32[1,1024]{1,0:T(1,128)S(1)}) fusion(bf16[4,1024]{1,0:T(4,128)(2,1)} %param.20), kind=kLoop, calls=%fused_computation.66 | loop fusion | bytes 32768 | tf_op jit(solution)/shard_map/slice | solution.py:25
  8.8 2.0 %collective-permute-done.1 = bf16[8,4,512]{2,1,0:T(4,128)(2,1)S(1)} collective-permute-done((bf16[8,4,512]{2,1,0:T(4,128)(2,1)}, bf16[8,4,512]{2,1,0:T(4,128)(2,1)S(1)}, u32[]{:S(2)}, u32[]{:S(2)}) %collective-permute-start.1) | collective-permute-done | bytes 32800 | tf_op jit(solution)/shard_map/ppermute | solution.py:73
  10.8 0.9 %collective-permute-done.2 = bf16[8,4,512]{2,1,0:T(4,128)(2,1)S(1)} collective-permute-done((bf16[8,4,512]{2,1,0:T(4,128)(2,1)}, bf16[8,4,512]{2,1,0:T(4,128)(2,1)S(1)}, u32[]{:S(2)}, u32[]{:S(2)}) %collective-permute-start.2) | collective-permute-done | bytes 32800 | tf_op jit(solution)/shard_map/ppermute | solution.py:73
  11.7 0.8 %select_select_fusion.3 = (bf16[4,8,512]{2,1,0:T(8,128)(2,1)S(1)}, bf16[4,8,512]{2,1,0:T(8,128)(2,1)S(1)}, bf16[4,8,512]{2,1,0:T(8,128)(2,1)S(1)}, bf16[4,8,512]{2,1,0:T(8,128)(2,1)S(1)}) fusion(bf16[4,8,512]{2,1,0:T(8,128)(2,1)S(1)} %bitcast.91, bf16[4,8,512]{2,1,0:T(8,128)(2,1)S(1)} %bitcast.92, bf16[4,8,512]{2,1,0:T(8,128)(2,1)S(1)} %bitcast.93, ...), kind=kLoop, calls=%fused_computation.46 | loop fusion | flops 196608 | bytes 262156 | tf_op jit(solution)/shard_map/jit(_where)/select_n | solution.py:217
  12.6 0.7 %pad_maximum_fusion.1.x_ref = bf16[128,512]{1,0:T(8,128)(2,1)} fusion(bf16[32,512]{1,0:T(8,128)(2,1)S(1)} %reshape.137, bf16[32,512]{1,0:T(8,128)(2,1)S(1)} %reshape.136, bf16[32,512]{1,0:T(8,128)(2,1)S(1)} %reshape.135, bf16[32,512]{1,0:T(8,128)(2,1)S(1)} %reshape.134), kind=kLoop, calls=%fused_computation.24 | loop fusion | flops 524288 | bytes 262144 | tf_op jit(solution)/shard_map/concatenate | solution.py:220
  13.3 3.7 %shard_map.140 = (f32[32,3200]{1,0:T(8,128)}, f32[32,3200]{1,0:T(8,128)}, f32[32,3200]{1,0:T(8,128)}, f32[32,3200]{1,0:T(8,128)}) custom-call(bf16[128,512]{1,0:T(8,128)(2,1)} %pad_maximum_fusion.1.x_ref, bf16[512,1024]{1,0:T(8,128)(2,1)} %wqk_ref.1, bf16[512,2048]{1,0:T(8,128)(2,1)} %wvz_ref.1, bf16[16,512]{1,0:T(8,128)(2,1)} %bitcast.94), custom_call_target="tpu_custom_call" | custom-call | flops 419430400 | bytes 5046272 | tf_op jit(solution)/shard_map/pallas_call | solution.py:111
  17.0 1.0 %slice.103 = f32[32,1152]{1,0:T(8,128)S(1)} slice(f32[32,3200]{1,0:T(8,128)} %get-tuple-element.12), slice={[0:32], [0:1152]} | slice | bytes 294912 | tf_op jit(solution)/shard_map/slice | solution.py:227
  18.4 1.0 %slice.121 = f32[32,2048]{1,0:T(8,128)S(1)} slice(f32[32,3200]{1,0:T(8,128)} %get-tuple-element.12), slice={[0:32], [1152:3200]} | slice | bytes 524288 | tf_op jit(solution)/shard_map/slice | solution.py:227
  19.4 1.0 %slice.119 = f32[32,2048]{1,0:T(8,128)S(1)} slice(f32[32,3200]{1,0:T(8,128)} %get-tuple-element.10), slice={[0:32], [1152:3200]} | slice | bytes 524288 | tf_op jit(solution)/shard_map/slice | solution.py:227
  20.4 0.9 %slice.101 = f32[32,1152]{1,0:T(8,128)S(1)} slice(f32[32,3200]{1,0:T(8,128)} %get-tuple-element.10), slice={[0:32], [0:1152]} | slice | bytes 294912 | tf_op jit(solution)/shard_map/slice | solution.py:227
  21.3 0.5 collective-permute-start.7
  21.9 0.4 collective-permute-start.3
  22.3 0.9 %slice_add_fusion.1 = f32[32,1152]{1,0:T(8,128)S(1)} fusion(f32[32,1152]{1,0:T(8,128)S(1)} %collective-permute-done.4, f32[32,3200]{1,0:T(8,128)} %get-tuple-element.11), kind=kLoop, calls=%fused_computation.7 | loop fusion | flops 36864 | bytes 442368 | tf_op jit(solution)/shard_map/add | solution.py:227
  23.2 1.6 %collective-permute-start.5 = (f32[32,1152]{1,0:T(8,128)S(1)}, f32[32,1152]{1,0:T(8,128)S(1)}, u32[]{:S(2)}, u32[]{:S(2)}) collective-permute-start(f32[32,1152]{1,0:T(8,128)S(1)} %slice_add_fusion.1), channel_id=1, source_target_pairs={{0,8},{4,12},{8,0},{12,4},{1,9},{5,13},{9,1},{13,5},{2,10},{6,14},... | collective-permute-start | bytes 442376 | tf_op jit(solution)/shard_map/ppermute | solution.py:233
  24.8 1.0 %slice_add_fusion = f32[32,2048]{1,0:T(8,128)S(1)} fusion(f32[32,2048]{1,0:T(8,128)S(1)} %collective-permute-done.7, f32[32,3200]{1,0:T(8,128)} %get-tuple-element.11), kind=kLoop, calls=%fused_computation.5 | loop fusion | flops 65536 | bytes 786432 | tf_op jit(solution)/shard_map/add | solution.py:227
  25.8 0.6 collective-permute-start.8
  26.4 3.6 %collective-permute-done.5 = f32[32,1152]{1,0:T(8,128)S(1)} collective-permute-done((f32[32,1152]{1,0:T(8,128)S(1)}, f32[32,1152]{1,0:T(8,128)S(1)}, u32[]{:S(2)}, u32[]{:S(2)}) %collective-permute-start.5) | collective-permute-done | bytes 147488 | tf_op jit(solution)/shard_map/ppermute | solution.py:233
  30.0 0.9 %add_convert_fusion.1 = bf16[32,1152]{1,0:T(8,128)(2,1)S(1)} fusion(f32[32,1152]{1,0:T(8,128)S(1)} %collective-permute-done.5, f32[32,1152]{1,0:T(8,128)S(1)} %collective-permute-done.3, f32[32,3200]{1,0:T(8,128)} %get-tuple-element.9), kind=kLoop, calls=%fused_computation.6 | loop fusion | flops 110592 | bytes 516096 | tf_op jit(solution)/shard_map/convert.5
  31.1 0.1 copy.34
  31.4 0.1 copy.43
  31.7 0.2 divide_multiply_fusion.1
  31.9 0.1 reshape.139
  32.0 0.1 fusion.16
  32.1 0.1 multiply_reduce_fusion.2
  32.3 0.1 multiply_reduce_fusion.1
  32.4 1.0 %copy.39.qt_ref = f32[8,128,16]{2,1,0:T(8,128)} copy(f32[8,128,16]{1,0,2:T(8,128)S(1)} %bitcast.80) | data formatting | bytes 131072 | tf_op jit(solution)/shard_map/reshape | solution.py:250
  33.5 1.0 %copy.40.kt_ref = f32[8,128,16]{2,1,0:T(8,128)} copy(f32[8,128,16]{1,0,2:T(8,128)S(1)} %bitcast.81) | data formatting | bytes 131072 | tf_op jit(solution)/shard_map/reshape | solution.py:251
  34.5 0.7 %pad_maximum_fusion.2.gates_ref = f32[8,64]{1,0:T(8,128)} fusion(f32[8,32]{1,0:T(8,128)S(1)} %fusion.12, f32[8,32]{1,0:T(8,128)S(1)} %div.76), kind=kLoop, calls=%fused_computation.56 | loop fusion | flops 512 | bytes 4096 | tf_op jit(solution)/shard_map/concatenate | solution.py:256
  35.4 0.8 %divide_multiply_fusion.v_ref = f32[8,4,1024]{2,1,0:T(4,128)} fusion(f32[8,7,1024]{2,1,0:T(8,128)S(1)} %maximum_convert_fusion.1, f32[1024]{0:T(1024)S(1)} %bitcast.98, f32[1024]{0:T(1024)S(1)} %bitcast.97, f32[1024]{0:T(1024)S(1)} %bitcast.96, f32[1024]{0:T(1024)S(1)} %bitcast.95), kind=kLoop, calls=%fused_computation.8 | loop fusion | flops 360448 | bytes 671744 | tf_op jit(solution)/shard_map/jit(silu)/mul | solution.py:26
  36.3 9.9 %shard_map.141 = (f32[8,8,128,128]{3,2,1,0:T(8,128)}, f32[8,4,8,128]{3,2,1,0:T(8,128)}) custom-call(f32[8,64]{1,0:T(8,128)} %pad_maximum_fusion.2.gates_ref, f32[8,128,16]{2,1,0:T(8,128)} %copy.39.qt_ref, f32[8,128,16]{2,1,0:T(8,128)} %copy.40.kt_ref, f32[8,4,1024]{2,1,0:T(4,128)} %divide_multiply_fusion.v_ref, f32[8,8,128,128]{3,2,1,0:T(8,128)} %s_ref.1), custom_call_target="tpu_custom_call" | custom-call | flops 33554432 | bytes 8388608 | tf_op jit(solution)/shard_map/pallas_call | solution.py:152
  46.2 1.0 %multiply_reduce_fusion = f32[8,4,8]{2,1,0:T(4,128)S(1)} fusion(f32[8,4,8,128]{3,2,1,0:T(8,128)} %get-tuple-element.13), kind=kLoop, calls=%fused_computation.29 | loop fusion | flops 65280 | bytes 132096 | tf_op jit(solution)/shard_map/reduce_sum | solution.py:262
  47.2 1.0 %multiply_convert_fusion = bf16[8,4,8,128]{3,2,1,0:T(8,128)(2,1)S(1)} fusion(f32[8,4,8,128]{3,2,1,0:T(8,128)S(1)} %bitcast.79, f32[8,4,8,128]{3,2,1,0:T(8,128)} %get-tuple-element.13, f32[128]{0:T(128)S(1)} %copy-done.4, f32[8,4,8]{2,1,0:T(4,128)S(1)} %add_rsqrt_fusion), kind=kLoop, calls=%fused_computation.28 | loop fusion | flops 262144 | bytes 329216 | tf_op jit(solution)/shard_map/convert_element_type | solution.py:264
  48.3 1.6 %collective-permute-start.10 = (bf16[8,4,8,128]{3,2,1,0:T(8,128)(2,1)S(1)}, bf16[8,4,8,128]{3,2,1,0:T(8,128)(2,1)S(1)}, u32[]{:S(2)}, u32[]{:S(2)}) collective-permute-start(bf16[8,4,8,128]{3,2,1,0:T(8,128)(2,1)S(1)} %multiply_convert_fusion), channel_id=1, source_target_pairs={{0,8},{4,12},{8,0},{12,4},{1,9},{5,13},{9,1},{13,5},{2,10},{6,14},... | collective-permute-start | bytes 196616 | tf_op jit(solution)/shard_map/ppermute | solution.py:34
  49.9 0.2 collective-permute-start.9
  50.0 0.2 collective-permute-done.11
  50.2 3.7 %collective-permute-done.10 = bf16[8,4,8,128]{3,2,1,0:T(8,128)(2,1)S(1)} collective-permute-done((bf16[8,4,8,128]{3,2,1,0:T(8,128)(2,1)S(1)}, bf16[8,4,8,128]{3,2,1,0:T(8,128)(2,1)S(1)}, u32[]{:S(2)}, u32[]{:S(2)}) %collective-permute-start.10) | collective-permute-done | bytes 65568 | tf_op jit(solution)/shard_map/ppermute | solution.py:34
  53.9 0.2 collective-permute-done.9
  54.2 0.6 gather_fusion
  54.8 0.3 convolution_bitcast_fusion
  55.1 0.7 %collective-permute-start.14 = (f32[32,512]{1,0:T(8,128)S(1)}, f32[32,512]{1,0:T(8,128)S(1)}, u32[]{:S(2)}, u32[]{:S(2)}) collective-permute-start(f32[32,512]{1,0:T(8,128)S(1)} %get-tuple-element.27), channel_id=1, source_target_pairs={{0,3},{1,0},{2,1},{3,2},{4,7},{5,4},{6,5},{7,6},{8,11},{9,8},{10,9... | collective-permute-start | bytes 196616 | tf_op jit(solution)/shard_map/ppermute | solution.py:47
  55.8 0.6 collective-permute-start.13
  56.4 1.9 %collective-permute-start.12 = (f32[32,512]{1,0:T(8,128)S(1)}, f32[32,512]{1,0:T(8,128)S(1)}, u32[]{:S(2)}, u32[]{:S(2)}) collective-permute-start(f32[32,512]{1,0:T(8,128)S(1)} %get-tuple-element.26), channel_id=1, source_target_pairs={{0,1},{1,2},{2,3},{3,0},{4,5},{5,6},{6,7},{7,4},{8,9},{9,10},{10,1... | collective-permute-start | bytes 196616 | tf_op jit(solution)/shard_map/ppermute | solution.py:47
  58.3 1.1 %collective-permute-done.14 = f32[32,512]{1,0:T(8,128)S(1)} collective-permute-done((f32[32,512]{1,0:T(8,128)S(1)}, f32[32,512]{1,0:T(8,128)S(1)}, u32[]{:S(2)}, u32[]{:S(2)}) %collective-permute-start.14) | collective-permute-done | bytes 65568 | tf_op jit(solution)/shard_map/ppermute | solution.py:47
  59.5 3.2 %collective-permute-done.13 = f32[32,512]{1,0:T(8,128)S(1)} collective-permute-done((f32[32,512]{1,0:T(8,128)S(1)}, f32[32,512]{1,0:T(8,128)S(1)}, u32[]{:S(2)}, u32[]{:S(2)}) %collective-permute-start.13) | collective-permute-done | bytes 65568 | tf_op jit(solution)/shard_map/ppermute | solution.py:47
  62.7 0.6 reshape.147
  (62 shorter events, 1.5 us)
Async XLA Ops:
  0.6 54.1 %copy-start = (bf16[1024,512]{1,0:T(8,128)(2,1)S(1)}, bf16[1024,512]{1,0:T(8,128)(2,1)}, u32[]{:S(2)}) copy-start(bf16[1024,512]{1,0:T(8,128)(2,1)} %param.24) | copy-start | bytes 3145732
  0.6 17.4 %copy-start.6 = (f32[8]{0:T(128)S(1)}, f32[8]{0:T(128)}, u32[]{:S(2)}) copy-start(f32[8]{0:T(128)} %param.21) | copy-start | bytes 100
  0.7 17.4 %copy-start.5 = (f32[8]{0:T(128)S(1)}, f32[8]{0:T(128)}, u32[]{:S(2)}) copy-start(f32[8]{0:T(128)} %param.22) | copy-start | bytes 100
  0.7 17.6 %copy-start.2 = (bf16[8,3,1024]{2,0,1:T(8,128)(2,1)S(1)}, bf16[8,3,1024]{2,0,1:T(8,128)(2,1)}, u32[]{:S(2)}) copy-start(bf16[8,3,1024]{2,0,1:T(8,128)(2,1)} %param.25) | copy-start | bytes 147460
  0.7 17.7 %copy-start.3 = (bf16[8,3,1024]{2,0,1:T(8,128)(2,1)S(1)}, bf16[8,3,1024]{2,0,1:T(8,128)(2,1)}, u32[]{:S(2)}) copy-start(bf16[8,3,1024]{2,0,1:T(8,128)(2,1)} %param.26) | copy-start | bytes 147460
  0.7 8.1 %collective-permute-start = (bf16[8,4,512]{2,1,0:T(4,128)(2,1)}, bf16[8,4,512]{2,1,0:T(4,128)(2,1)S(1)}, u32[]{:S(2)}, u32[]{:S(2)}) collective-permute-start(bf16[8,4,512]{2,1,0:T(4,128)(2,1)} %param.15), channel_id=1, source_target_pairs={{0,3},{1,0},{2,1},{3,2},{4,7},{5,4},{6,5},{7,6},{8,11},{9,8},{10,9... | collective-permute-start | bytes 98312 | tf_op jit(solution)/shard_map/ppermute | solution.py:73
  5.8 5.0 %collective-permute-start.1 = (bf16[8,4,512]{2,1,0:T(4,128)(2,1)}, bf16[8,4,512]{2,1,0:T(4,128)(2,1)S(1)}, u32[]{:S(2)}, u32[]{:S(2)}) collective-permute-start(bf16[8,4,512]{2,1,0:T(4,128)(2,1)} %param.15), channel_id=1, source_target_pairs={{0,2},{1,3},{2,0},{3,1},{4,6},{5,7},{6,4},{7,5},{8,10},{9,11},{10,... | collective-permute-start | bytes 98312 | tf_op jit(solution)/shard_map/ppermute | solution.py:73
  5.8 5.9 %collective-permute-start.2 = (bf16[8,4,512]{2,1,0:T(4,128)(2,1)}, bf16[8,4,512]{2,1,0:T(4,128)(2,1)S(1)}, u32[]{:S(2)}, u32[]{:S(2)}) collective-permute-start(bf16[8,4,512]{2,1,0:T(4,128)(2,1)} %param.15), channel_id=1, source_target_pairs={{0,1},{1,2},{2,3},{3,0},{4,5},{5,6},{6,7},{7,4},{8,9},{9,10},{10,1... | collective-permute-start | bytes 98312 | tf_op jit(solution)/shard_map/ppermute | solution.py:73
  17.0 18.3 %copy-start.1 = (f32[32,3200]{1,0:T(8,128)S(1)}, f32[32,3200]{1,0:T(8,128)}, u32[]{:S(2)}) copy-start(f32[32,3200]{1,0:T(8,128)} %get-tuple-element.9) | copy-start | bytes 1228804
  17.9 4.4 %collective-permute-start.4 = (f32[32,1152]{1,0:T(8,128)S(1)}, f32[32,1152]{1,0:T(8,128)S(1)}, u32[]{:S(2)}, u32[]{:S(2)}) collective-permute-start(f32[32,1152]{1,0:T(8,128)S(1)} %slice.103), channel_id=1, source_target_pairs={{0,4},{4,0},{8,12},{12,8},{1,5},{5,1},{9,13},{13,9},{2,6},{6,2},{1... | collective-permute-start | bytes 442376 | tf_op jit(solution)/shard_map/ppermute | solution.py:227
  21.3 3.5 %collective-permute-start.7 = (f32[32,2048]{1,0:T(8,128)S(1)}, f32[32,2048]{1,0:T(8,128)S(1)}, u32[]{:S(2)}, u32[]{:S(2)}) collective-permute-start(f32[32,2048]{1,0:T(8,128)S(1)} %slice.121), channel_id=1, source_target_pairs={{0,4},{4,0},{8,12},{12,8},{1,5},{5,1},{9,13},{13,9},{2,6},{6,2},{1... | collective-permute-start | bytes 786440 | tf_op jit(solution)/shard_map/ppermute | solution.py:227
  21.8 13.4 %collective-permute-start.6 = (f32[32,2048]{1,0:T(8,128)S(1)}, f32[32,2048]{1,0:T(8,128)S(1)}, u32[]{:S(2)}, u32[]{:S(2)}) collective-permute-start(f32[32,2048]{1,0:T(8,128)S(1)} %slice.119), channel_id=1, source_target_pairs={{0,4},{4,0},{8,12},{12,8},{1,5},{5,1},{9,13},{13,9},{2,6},{6,2},{1... | collective-permute-start | bytes 786440 | tf_op jit(solution)/shard_map/ppermute | solution.py:227
  21.9 4.5 %collective-permute-start.3 = (f32[32,1152]{1,0:T(8,128)S(1)}, f32[32,1152]{1,0:T(8,128)S(1)}, u32[]{:S(2)}, u32[]{:S(2)}) collective-permute-start(f32[32,1152]{1,0:T(8,128)S(1)} %slice.101), channel_id=1, source_target_pairs={{0,4},{4,0},{8,12},{12,8},{1,5},{5,1},{9,13},{13,9},{2,6},{6,2},{1... | collective-permute-start | bytes 442376 | tf_op jit(solution)/shard_map/ppermute | solution.py:227
  23.2 6.8 %collective-permute-start.5 = (f32[32,1152]{1,0:T(8,128)S(1)}, f32[32,1152]{1,0:T(8,128)S(1)}, u32[]{:S(2)}, u32[]{:S(2)}) collective-permute-start(f32[32,1152]{1,0:T(8,128)S(1)} %slice_add_fusion.1), channel_id=1, source_target_pairs={{0,8},{4,12},{8,0},{12,4},{1,9},{5,13},{9,1},{13,5},{2,10},{6,14},... | collective-permute-start | bytes 442376 | tf_op jit(solution)/shard_map/ppermute | solution.py:233
  25.8 9.4 %collective-permute-start.8 = (f32[32,2048]{1,0:T(8,128)S(1)}, f32[32,2048]{1,0:T(8,128)S(1)}, u32[]{:S(2)}, u32[]{:S(2)}) collective-permute-start(f32[32,2048]{1,0:T(8,128)S(1)} %slice_add_fusion), channel_id=1, source_target_pairs={{0,8},{4,12},{8,0},{12,4},{1,9},{5,13},{9,1},{13,5},{2,10},{6,14},... | collective-permute-start | bytes 786440 | tf_op jit(solution)/shard_map/ppermute | solution.py:233
  34.5 12.7 %copy-start.4 = (f32[128]{0:T(128)S(1)}, f32[128]{0:T(128)}, u32[]{:S(2)}) copy-start(f32[128]{0:T(128)} %param.23) | copy-start | bytes 1540
  48.2 2.0 %collective-permute-start.11 = (bf16[8,4,8,128]{3,2,1,0:T(8,128)(2,1)S(1)}, bf16[8,4,8,128]{3,2,1,0:T(8,128)(2,1)S(1)}, u32[]{:S(2)}, u32[]{:S(2)}) collective-permute-start(bf16[8,4,8,128]{3,2,1,0:T(8,128)(2,1)S(1)} %multiply_convert_fusion), channel_id=1, source_target_pairs={{0,12},{4,0},{8,4},{12,8},{1,13},{5,1},{9,5},{13,9},{2,14},{6,2},{... | collective-permute-start | bytes 196616 | tf_op jit(solution)/shard_map/ppermute | solution.py:34
  48.3 5.6 %collective-permute-start.10 = (bf16[8,4,8,128]{3,2,1,0:T(8,128)(2,1)S(1)}, bf16[8,4,8,128]{3,2,1,0:T(8,128)(2,1)S(1)}, u32[]{:S(2)}, u32[]{:S(2)}) collective-permute-start(bf16[8,4,8,128]{3,2,1,0:T(8,128)(2,1)S(1)} %multiply_convert_fusion), channel_id=1, source_target_pairs={{0,8},{4,12},{8,0},{12,4},{1,9},{5,13},{9,1},{13,5},{2,10},{6,14},... | collective-permute-start | bytes 196616 | tf_op jit(solution)/shard_map/ppermute | solution.py:34
  49.9 4.3 %collective-permute-start.9 = (bf16[8,4,8,128]{3,2,1,0:T(8,128)(2,1)S(1)}, bf16[8,4,8,128]{3,2,1,0:T(8,128)(2,1)S(1)}, u32[]{:S(2)}, u32[]{:S(2)}) collective-permute-start(bf16[8,4,8,128]{3,2,1,0:T(8,128)(2,1)S(1)} %multiply_convert_fusion), channel_id=1, source_target_pairs={{0,4},{4,8},{8,12},{12,0},{1,5},{5,9},{9,13},{13,1},{2,6},{6,10},{... | collective-permute-start | bytes 196616 | tf_op jit(solution)/shard_map/ppermute | solution.py:34
  55.1 4.3 %collective-permute-start.14 = (f32[32,512]{1,0:T(8,128)S(1)}, f32[32,512]{1,0:T(8,128)S(1)}, u32[]{:S(2)}, u32[]{:S(2)}) collective-permute-start(f32[32,512]{1,0:T(8,128)S(1)} %get-tuple-element.27), channel_id=1, source_target_pairs={{0,3},{1,0},{2,1},{3,2},{4,7},{5,4},{6,5},{7,6},{8,11},{9,8},{10,9... | collective-permute-start | bytes 196616 | tf_op jit(solution)/shard_map/ppermute | solution.py:47
  55.8 6.9 %collective-permute-start.13 = (f32[32,512]{1,0:T(8,128)S(1)}, f32[32,512]{1,0:T(8,128)S(1)}, u32[]{:S(2)}, u32[]{:S(2)}) collective-permute-start(f32[32,512]{1,0:T(8,128)S(1)} %get-tuple-element.28), channel_id=1, source_target_pairs={{0,2},{1,3},{2,0},{3,1},{4,6},{5,7},{6,4},{7,5},{8,10},{9,11},{10,... | collective-permute-start | bytes 196616 | tf_op jit(solution)/shard_map/ppermute | solution.py:47
  56.4 6.3 %collective-permute-start.12 = (f32[32,512]{1,0:T(8,128)S(1)}, f32[32,512]{1,0:T(8,128)S(1)}, u32[]{:S(2)}, u32[]{:S(2)}) collective-permute-start(f32[32,512]{1,0:T(8,128)S(1)} %get-tuple-element.26), channel_id=1, source_target_pairs={{0,1},{1,2},{2,3},{3,0},{4,5},{5,6},{6,7},{7,4},{8,9},{9,10},{10,1... | collective-permute-start | bytes 196616 | tf_op jit(solution)/shard_map/ppermute | solution.py:47

commit v17 on v15

--- a/solution.py
+++ b/solution.py
@@ -119,28 +119,35 @@
     )(x, w_qk, w_vz, w_ba.T)
 
 
-def recurrence_kernel(gates_ref, qt_ref, kt_ref, v_ref, s_ref, s_out, o_ref, *, heads, steps, ratio):
-    r = pl.program_id(0)
+def recurrence_kernel(gates_ref, qt_ref, kt_ref, v_ref, s_ref, s_out, o_ref, *, heads, steps, ratio, block):
+    key_heads = heads // ratio
+    cols = heads * steps
+    for b in range(block):
+        recurrence_row(gates_ref, qt_ref, kt_ref, v_ref, s_ref, s_out, o_ref, b, heads, steps, ratio)
+
+
+def recurrence_row(gates_ref, qt_ref, kt_ref, v_ref, s_ref, s_out, o_ref, b, heads, steps, ratio):
+    r = pl.program_id(0) * s_ref.shape[0] + b
     key_heads = heads // ratio
     cols = heads * steps
     for kh in range(key_heads):
         group = [kh * ratio + j for j in range(ratio)]
-        states = [s_ref[0, h] for h in group]
+        states = [s_ref[b, h] for h in group]
         for t in range(steps):
             ck = t * key_heads + kh
-            key_col = kt_ref[0, :, ck : ck + 1]
-            query_col = qt_ref[0, :, ck : ck + 1]
+            key_col = kt_ref[b, :, ck : ck + 1]
+            query_col = qt_ref[b, :, ck : ck + 1]
             for j, h in enumerate(group):
                 c = t * heads + h
                 lanes = slice(h * DV, (h + 1) * DV)
                 state = states[j] * gates_ref[r, cols + c]
                 recalled = jnp.sum(key_col * state, axis=0, keepdims=True)
-                correction = (v_ref[0, t : t + 1, lanes] - recalled) * gates_ref[r, c]
+                correction = (v_ref[b, t : t + 1, lanes] - recalled) * gates_ref[r, c]
                 state = state + key_col * correction
-                o_ref[0, t, h : h + 1, :] = jnp.sum(query_col * state, axis=0, keepdims=True)
+                o_ref[b, t, h : h + 1, :] = jnp.sum(query_col * state, axis=0, keepdims=True)
                 states[j] = state
         for j, h in enumerate(group):
-            s_out[0, h] = states[j]
+            s_out[b, h] = states[j]
 
 
 def recurrence(gates, qt, kt, values, memory_state):
@@ -148,20 +155,21 @@
     steps = values.shape[1]
     key_cols = kt.shape[2]
     ratio = heads * steps // key_cols
-    kern = functools.partial(recurrence_kernel, heads=heads, steps=steps, ratio=ratio)
+    block = 2 if rows % 2 == 0 else 1
+    kern = functools.partial(recurrence_kernel, heads=heads, steps=steps, ratio=ratio, block=block)
     return pl.pallas_call(
         kern,
-        grid=(rows,),
+        grid=(rows // block,),
         in_specs=[
             pl.BlockSpec(memory_space=pltpu.SMEM),
-            pl.BlockSpec((1, DK, key_cols), lambda r: (r, 0, 0)),
-            pl.BlockSpec((1, DK, key_cols), lambda r: (r, 0, 0)),
-            pl.BlockSpec((1, steps, heads * DV), lambda r: (r, 0, 0)),
-            pl.BlockSpec((1, heads, DK, DV), lambda r: (r, 0, 0, 0)),
+            pl.BlockSpec((block, DK, key_cols), lambda r: (r, 0, 0)),
+            pl.BlockSpec((block, DK, key_cols), lambda r: (r, 0, 0)),
+            pl.BlockSpec((block, steps, heads * DV), lambda r: (r, 0, 0)),
+            pl.BlockSpec((block, heads, DK, DV), lambda r: (r, 0, 0, 0)),
         ],
         out_specs=[
-            pl.BlockSpec((1, heads, DK, DV), lambda r: (r, 0, 0, 0)),
-            pl.BlockSpec((1, steps, heads, DV), lambda r: (r, 0, 0, 0)),
+            pl.BlockSpec((block, heads, DK, DV), lambda r: (r, 0, 0, 0)),
+            pl.BlockSpec((block, steps, heads, DV), lambda r: (r, 0, 0, 0)),
         ],
         out_shape=[
             jax.ShapeDtypeStruct(memory_state.shape, jnp.float32),

time: 60.2 us -> 59 us (0.980)
  Pallas kernels: 13.6 us -> 12.5 us
    pallas_call x1, Pallas kernels: 9.9 us -> 8.75 us  [recurrence(): pl.pallas_call(kern, grid=(rows // block,), in_specs=[pl.BlockSpec(memory...]
where the time goes in v17:
time: 59 us; the launch traced here: 58.6 us
  waiting for transfers between devices  18.4 us (31%)
  starting transfers between devices  13.8 us (23%)
  Pallas kernels  12.5 us (21%)
  other arithmetic  7.93 us (13%)
  local copies, waits for them, and re-layouts  4.59 us (8%)
  between operations  1.02 us (2%)
    pallas_call x1, Pallas kernels, recurrence(): pl.pallas_call(kern, grid=(rows // block,), in_specs=[pl.BlockSpec(memory...  8.75 us
    ppermute x3, starting transfers between devices, gather_pieces(): pieces.append(lax.ppermute(x, axis, [(i, (i + s) % n) for i in range(n)]))  6.11 us
    ppermute x3, waiting for transfers between devices, gather_pieces(): pieces.append(lax.ppermute(x, axis, [(i, (i + s) % n) for i in range(n)]))  4.91 us
    ppermute x3, waiting for transfers between devices, scatter_sum_rows(): acc = acc + lax.ppermute(send, axis, [(i, (i + s) % n) for i in range(n)])  4.36 us
    ppermute x3, waiting for transfers between devices, gather_rows(): pieces.append(lax.ppermute(x, axis, [(i, (i + s) % n) for i in range(n)]))  4.1 us
    pallas_call x1, Pallas kernels, projection(): pl.pallas_call(projection_kernel, out_shape=[jax.ShapeDtypeStruct((rows,...  3.72 us
    ppermute x2, waiting for transfers between devices, shards(): lax.ppermute(part[s][:, lo:hi], 'dp', perm)  3.69 us
    ppermute x3, starting transfers between devices, scatter_sum_rows(): acc = acc + lax.ppermute(send, axis, [(i, (i + s) % n) for i in range(n)])  3.2 us
  transfers between devices with their start and end apart: 13, of which 11 were waited for; matrix products, arithmetic and copies ran while one was open for 11% of the time, Pallas kernels for 0%

profile of v17, /device:TPU:0, one launch (start us, length us, event | category | flops | bytes accessed | tf_op | source)
XLA Modules:
  0.0 58.6 jit_solution(4705038545529632270)
XLA Ops:
  0.7 5.1 %collective-permute-start = (bf16[8,4,512]{2,1,0:T(4,128)(2,1)}, bf16[8,4,512]{2,1,0:T(4,128)(2,1)S(1)}, u32[]{:S(2)}, u32[]{:S(2)}) collective-permute-start(bf16[8,4,512]{2,1,0:T(4,128)(2,1)} %param.15), channel_id=1, source_target_pairs={{0,3},{1,0},{2,1},{3,2},{4,7},{5,4},{6,5},{7,6},{8,11},{9,8},{10,9... | collective-permute-start | bytes 98312 | tf_op jit(solution)/shard_map/ppermute | solution.py:73
  5.8 1.0 %collective-permute-start.2 = (bf16[8,4,512]{2,1,0:T(4,128)(2,1)}, bf16[8,4,512]{2,1,0:T(4,128)(2,1)S(1)}, u32[]{:S(2)}, u32[]{:S(2)}) collective-permute-start(bf16[8,4,512]{2,1,0:T(4,128)(2,1)} %param.15), channel_id=1, source_target_pairs={{0,1},{1,2},{2,3},{3,0},{4,5},{5,6},{6,7},{7,4},{8,9},{9,10},{10,1... | collective-permute-start | bytes 98312 | tf_op jit(solution)/shard_map/ppermute | solution.py:73
  6.8 0.9 %collective-permute-done = bf16[8,4,512]{2,1,0:T(4,128)(2,1)S(1)} collective-permute-done((bf16[8,4,512]{2,1,0:T(4,128)(2,1)}, bf16[8,4,512]{2,1,0:T(4,128)(2,1)S(1)}, u32[]{:S(2)}, u32[]{:S(2)}) %collective-permute-start) | collective-permute-done | bytes 32800 | tf_op jit(solution)/shard_map/ppermute | solution.py:73
  7.7 3.1 %collective-permute-done.1 = bf16[8,4,512]{2,1,0:T(4,128)(2,1)S(1)} collective-permute-done((bf16[8,4,512]{2,1,0:T(4,128)(2,1)}, bf16[8,4,512]{2,1,0:T(4,128)(2,1)S(1)}, u32[]{:S(2)}, u32[]{:S(2)}) %collective-permute-start.1) | collective-permute-done | bytes 32800 | tf_op jit(solution)/shard_map/ppermute | solution.py:73
  10.8 0.9 %collective-permute-done.2 = bf16[8,4,512]{2,1,0:T(4,128)(2,1)S(1)} collective-permute-done((bf16[8,4,512]{2,1,0:T(4,128)(2,1)}, bf16[8,4,512]{2,1,0:T(4,128)(2,1)S(1)}, u32[]{:S(2)}, u32[]{:S(2)}) %collective-permute-start.2) | collective-permute-done | bytes 32800 | tf_op jit(solution)/shard_map/ppermute | solution.py:73
  11.7 0.8 %select_select_fusion.3 = (bf16[4,8,512]{2,1,0:T(8,128)(2,1)S(1)}, bf16[4,8,512]{2,1,0:T(8,128)(2,1)S(1)}, bf16[4,8,512]{2,1,0:T(8,128)(2,1)S(1)}, bf16[4,8,512]{2,1,0:T(8,128)(2,1)S(1)}) fusion(bf16[4,8,512]{2,1,0:T(8,128)(2,1)S(1)} %bitcast.91, bf16[4,8,512]{2,1,0:T(8,128)(2,1)S(1)} %bitcast.92, bf16[4,8,512]{2,1,0:T(8,128)(2,1)S(1)} %bitcast.93, ...), kind=kLoop, calls=%fused_computation.46 | loop fusion | flops 196608 | bytes 262156 | tf_op jit(solution)/shard_map/jit(_where)/select_n | solution.py:225
  12.6 0.7 %pad_maximum_fusion.1.x_ref = bf16[128,512]{1,0:T(8,128)(2,1)} fusion(bf16[32,512]{1,0:T(8,128)(2,1)S(1)} %reshape.137, bf16[32,512]{1,0:T(8,128)(2,1)S(1)} %reshape.136, bf16[32,512]{1,0:T(8,128)(2,1)S(1)} %reshape.135, bf16[32,512]{1,0:T(8,128)(2,1)S(1)} %reshape.134), kind=kLoop, calls=%fused_computation.24 | loop fusion | flops 524288 | bytes 262144 | tf_op jit(solution)/shard_map/concatenate | solution.py:228
  13.3 3.7 %shard_map.140 = (f32[32,3200]{1,0:T(8,128)}, f32[32,3200]{1,0:T(8,128)}, f32[32,3200]{1,0:T(8,128)}, f32[32,3200]{1,0:T(8,128)}) custom-call(bf16[128,512]{1,0:T(8,128)(2,1)} %pad_maximum_fusion.1.x_ref, bf16[512,1024]{1,0:T(8,128)(2,1)} %wqk_ref.1, bf16[512,2048]{1,0:T(8,128)(2,1)} %wvz_ref.1, bf16[16,512]{1,0:T(8,128)(2,1)} %bitcast.94), custom_call_target="tpu_custom_call" | custom-call | flops 419430400 | bytes 5046272 | tf_op jit(solution)/shard_map/pallas_call | solution.py:111
  17.0 0.6 collective-permute-start.3
  17.6 1.3 %collective-permute-done.4 = f32[32,3200]{1,0:T(8,128)S(1)} collective-permute-done((f32[32,3200]{1,0:T(8,128)}, f32[32,3200]{1,0:T(8,128)S(1)}, u32[]{:S(2)}, u32[]{:S(2)}) %collective-permute-start.4) | collective-permute-done | bytes 409632 | tf_op jit(solution)/shard_map/ppermute | solution.py:231
  18.9 1.1 %add.200 = f32[32,3200]{1,0:T(8,128)S(1)} add(f32[32,3200]{1,0:T(8,128)} %get-tuple-element.11, f32[32,3200]{1,0:T(8,128)S(1)} %collective-permute-done.4) | non-fusion elementwise | flops 102400 | bytes 1228800 | tf_op jit(solution)/shard_map/add | solution.py:231
  20.0 1.6 %collective-permute-start.5 = (f32[32,1152]{1,0:T(8,128)S(1)}, f32[32,1152]{1,0:T(8,128)S(1)}, u32[]{:S(2)}, u32[]{:S(2)}) collective-permute-start(f32[32,1152]{1,0:T(8,128)S(1)} %slice.128), channel_id=1, source_target_pairs={{0,8},{4,12},{8,0},{12,4},{1,9},{5,13},{9,1},{13,5},{2,10},{6,14},... | collective-permute-start | bytes 442376 | tf_op jit(solution)/shard_map/ppermute | solution.py:238
  21.6 0.1 add.204
  21.7 0.1 mul.181
  21.9 0.6 %collective-permute-start.6 = (f32[32,2048]{1,0:T(8,128)S(1)}, f32[32,2048]{1,0:T(8,128)S(1)}, u32[]{:S(2)}, u32[]{:S(2)}) collective-permute-start(f32[32,2048]{1,0:T(8,128)S(1)} %slice.144), channel_id=1, source_target_pairs={{0,8},{4,12},{8,0},{12,4},{1,9},{5,13},{9,1},{13,5},{2,10},{6,14},... | collective-permute-start | bytes 786440 | tf_op jit(solution)/shard_map/ppermute | solution.py:238
  22.6 1.0 %add.199 = f32[32,3200]{1,0:T(8,128)S(1)} add(f32[32,3200]{1,0:T(8,128)} %get-tuple-element.9, f32[32,3200]{1,0:T(8,128)S(1)} %collective-permute-done.3) | non-fusion elementwise | flops 102400 | bytes 1228800 | tf_op jit(solution)/shard_map/add | solution.py:231
  23.6 3.2 %collective-permute-done.5 = f32[32,1152]{1,0:T(8,128)S(1)} collective-permute-done((f32[32,1152]{1,0:T(8,128)S(1)}, f32[32,1152]{1,0:T(8,128)S(1)}, u32[]{:S(2)}, u32[]{:S(2)}) %collective-permute-start.5) | collective-permute-done | bytes 147488 | tf_op jit(solution)/shard_map/ppermute | solution.py:238
  26.9 0.1 reshape.207
  27.0 0.1 copy.34
  27.2 0.1 copy.43
  27.6 0.2 divide_multiply_fusion.1
  27.8 0.1 reshape.139
  27.9 0.1 fusion.18
  28.0 0.1 multiply_reduce_fusion.2
  28.1 0.1 multiply_reduce_fusion.1
  28.2 1.0 %copy.39.qt_ref = f32[8,128,16]{2,1,0:T(8,128)} copy(f32[8,128,16]{1,0,2:T(8,128)S(1)} %bitcast.80) | data formatting | bytes 131072 | tf_op jit(solution)/shard_map/reshape | solution.py:255
  29.3 0.1 fusion.12
  29.4 1.0 %copy.40.kt_ref = f32[8,128,16]{2,1,0:T(8,128)} copy(f32[8,128,16]{1,0,2:T(8,128)S(1)} %bitcast.81) | data formatting | bytes 131072 | tf_op jit(solution)/shard_map/reshape | solution.py:256
  30.4 0.7 %pad_maximum_fusion.2.gates_ref = f32[8,64]{1,0:T(8,128)} fusion(f32[8,32]{1,0:T(8,128)S(1)} %fusion.14, f32[8,32]{1,0:T(8,128)S(1)} %div.76), kind=kLoop, calls=%fused_computation.56 | loop fusion | flops 512 | bytes 4096 | tf_op jit(solution)/shard_map/concatenate | solution.py:261
  31.1 0.5 collective-permute-done.6
  31.8 0.8 %divide_multiply_fusion.v_ref = f32[8,4,1024]{2,1,0:T(4,128)} fusion(f32[8,7,1024]{2,1,0:T(8,128)S(1)} %maximum_convert_fusion.1, f32[1024]{0:T(1024)S(1)} %bitcast.98, f32[1024]{0:T(1024)S(1)} %bitcast.97, f32[1024]{0:T(1024)S(1)} %bitcast.96, f32[1024]{0:T(1024)S(1)} %bitcast.95), kind=kLoop, calls=%fused_computation.8 | loop fusion | flops 360448 | bytes 671744 | tf_op jit(solution)/shard_map/jit(silu)/mul | solution.py:26
  32.6 8.7 %shard_map.141 = (f32[8,8,128,128]{3,2,1,0:T(8,128)}, f32[8,4,8,128]{3,2,1,0:T(8,128)}) custom-call(f32[8,64]{1,0:T(8,128)} %pad_maximum_fusion.2.gates_ref, f32[8,128,16]{2,1,0:T(8,128)} %copy.39.qt_ref, f32[8,128,16]{2,1,0:T(8,128)} %copy.40.kt_ref, f32[8,4,1024]{2,1,0:T(4,128)} %divide_multiply_fusion.v_ref, f32[8,8,128,128]{3,2,1,0:T(8,128)} %s_ref.1), custom_call_target="tpu_custom_call" | custom-call | flops 33554432 | bytes 8388608 | tf_op jit(solution)/shard_map/pallas_call | solution.py:160
  41.4 1.0 %multiply_reduce_fusion = f32[8,4,8]{2,1,0:T(4,128)S(1)} fusion(f32[8,4,8,128]{3,2,1,0:T(8,128)} %get-tuple-element.13), kind=kLoop, calls=%fused_computation.29 | loop fusion | flops 65280 | bytes 132096 | tf_op jit(solution)/shard_map/reduce_sum | solution.py:267
  42.4 1.0 %multiply_convert_fusion = bf16[8,4,8,128]{3,2,1,0:T(8,128)(2,1)S(1)} fusion(f32[8,4,8,128]{3,2,1,0:T(8,128)S(1)} %bitcast.79, f32[8,4,8,128]{3,2,1,0:T(8,128)} %get-tuple-element.13, f32[128]{0:T(128)S(1)} %copy-done.5, f32[8,4,8]{2,1,0:T(4,128)S(1)} %add_rsqrt_fusion), kind=kLoop, calls=%fused_computation.28 | loop fusion | flops 262144 | bytes 329216 | tf_op jit(solution)/shard_map/convert_element_type | solution.py:269
  43.4 0.5 collective-permute-start.9
  43.9 1.2 %collective-permute-start.8 = (bf16[8,4,8,128]{3,2,1,0:T(8,128)(2,1)S(1)}, bf16[8,4,8,128]{3,2,1,0:T(8,128)(2,1)S(1)}, u32[]{:S(2)}, u32[]{:S(2)}) collective-permute-start(bf16[8,4,8,128]{3,2,1,0:T(8,128)(2,1)S(1)} %multiply_convert_fusion), channel_id=1, source_target_pairs={{0,8},{4,12},{8,0},{12,4},{1,9},{5,13},{9,1},{13,5},{2,10},{6,14},... | collective-permute-start | bytes 196616 | tf_op jit(solution)/shard_map/ppermute | solution.py:34
  45.1 0.2 collective-permute-start.7
  45.2 0.6 collective-permute-done.9
  45.8 3.3 %collective-permute-done.8 = bf16[8,4,8,128]{3,2,1,0:T(8,128)(2,1)S(1)} collective-permute-done((bf16[8,4,8,128]{3,2,1,0:T(8,128)(2,1)S(1)}, bf16[8,4,8,128]{3,2,1,0:T(8,128)(2,1)S(1)}, u32[]{:S(2)}, u32[]{:S(2)}) %collective-permute-start.8) | collective-permute-done | bytes 65568 | tf_op jit(solution)/shard_map/ppermute | solution.py:34
  49.1 0.2 collective-permute-done.7
  49.4 0.6 %gather_fusion = bf16[4,8,4,8,128]{4,3,2,1,0:T(8,128)(2,1)S(1)} fusion(bf16[4,8,4,8,128]{4,3,2,1,0:T(8,128)(2,1)S(1)} %pad_maximum_fusion, s32[1024]{0:T(1024)S(1)} %pad_clamp_fusion), kind=kCustom, calls=%fused_computation | custom fusion | bytes 524304 | tf_op jit(solution)/shard_map/jit(_take)/gather | solution.py:37
  50.0 0.3 convolution_bitcast_fusion
  50.3 0.7 %collective-permute-start.12 = (f32[32,512]{1,0:T(8,128)S(1)}, f32[32,512]{1,0:T(8,128)S(1)}, u32[]{:S(2)}, u32[]{:S(2)}) collective-permute-start(f32[32,512]{1,0:T(8,128)S(1)} %get-tuple-element.27), channel_id=1, source_target_pairs={{0,3},{1,0},{2,1},{3,2},{4,7},{5,4},{6,5},{7,6},{8,11},{9,8},{10,9... | collective-permute-start | bytes 196616 | tf_op jit(solution)/shard_map/ppermute | solution.py:47
  51.0 0.6 %collective-permute-start.11 = (f32[32,512]{1,0:T(8,128)S(1)}, f32[32,512]{1,0:T(8,128)S(1)}, u32[]{:S(2)}, u32[]{:S(2)}) collective-permute-start(f32[32,512]{1,0:T(8,128)S(1)} %get-tuple-element.28), channel_id=1, source_target_pairs={{0,2},{1,3},{2,0},{3,1},{4,6},{5,7},{6,4},{7,5},{8,10},{9,11},{10,... | collective-permute-start | bytes 196616 | tf_op jit(solution)/shard_map/ppermute | solution.py:47
  51.6 1.9 %collective-permute-start.10 = (f32[32,512]{1,0:T(8,128)S(1)}, f32[32,512]{1,0:T(8,128)S(1)}, u32[]{:S(2)}, u32[]{:S(2)}) collective-permute-start(f32[32,512]{1,0:T(8,128)S(1)} %get-tuple-element.26), channel_id=1, source_target_pairs={{0,1},{1,2},{2,3},{3,0},{4,5},{5,6},{6,7},{7,4},{8,9},{9,10},{10,1... | collective-permute-start | bytes 196616 | tf_op jit(solution)/shard_map/ppermute | solution.py:47
  53.5 1.1 %collective-permute-done.12 = f32[32,512]{1,0:T(8,128)S(1)} collective-permute-done((f32[32,512]{1,0:T(8,128)S(1)}, f32[32,512]{1,0:T(8,128)S(1)}, u32[]{:S(2)}, u32[]{:S(2)}) %collective-permute-start.12) | collective-permute-done | bytes 65568 | tf_op jit(solution)/shard_map/ppermute | solution.py:47
  54.7 3.2 %collective-permute-done.11 = f32[32,512]{1,0:T(8,128)S(1)} collective-permute-done((f32[32,512]{1,0:T(8,128)S(1)}, f32[32,512]{1,0:T(8,128)S(1)}, u32[]{:S(2)}, u32[]{:S(2)}) %collective-permute-start.11) | collective-permute-done | bytes 65568 | tf_op jit(solution)/shard_map/ppermute | solution.py:47
  57.9 0.6 %reshape.147 = bf16[8,4,512]{2,1,0:T(4,128)(2,1)} reshape(bf16[32,512]{1,0:T(8,128)(2,1)S(1)} %fusion.11) | data formatting | bytes 65536 | tf_op jit(solution)/shard_map/reshape | solution.py:279
  (58 shorter events, 1.0 us)
Async XLA Ops:
  0.6 49.3 %copy-start = (bf16[1024,512]{1,0:T(8,128)(2,1)S(1)}, bf16[1024,512]{1,0:T(8,128)(2,1)}, u32[]{:S(2)}) copy-start(bf16[1024,512]{1,0:T(8,128)(2,1)} %param.24) | copy-start | bytes 3145732
  0.6 16.3 %copy-start.3 = (bf16[4,1024]{1,0:T(4,128)(2,1)S(1)}, bf16[4,1024]{1,0:T(4,128)(2,1)}, u32[]{:S(2)}) copy-start(bf16[4,1024]{1,0:T(4,128)(2,1)} %param.19) | copy-start | bytes 24580
  0.7 16.9 %copy-start.4 = (bf16[4,1024]{1,0:T(4,128)(2,1)S(1)}, bf16[4,1024]{1,0:T(4,128)(2,1)}, u32[]{:S(2)}) copy-start(bf16[4,1024]{1,0:T(4,128)(2,1)} %param.20) | copy-start | bytes 24580
  0.7 20.9 %copy-start.7 = (f32[8]{0:T(128)S(1)}, f32[8]{0:T(128)}, u32[]{:S(2)}) copy-start(f32[8]{0:T(128)} %param.21) | copy-start | bytes 100
  0.7 20.9 %copy-start.6 = (f32[8]{0:T(128)S(1)}, f32[8]{0:T(128)}, u32[]{:S(2)}) copy-start(f32[8]{0:T(128)} %param.22) | copy-start | bytes 100
  0.7 21.1 %copy-start.1 = (bf16[8,3,1024]{2,0,1:T(8,128)(2,1)S(1)}, bf16[8,3,1024]{2,0,1:T(8,128)(2,1)}, u32[]{:S(2)}) copy-start(bf16[8,3,1024]{2,0,1:T(8,128)(2,1)} %param.25) | copy-start | bytes 147460
  0.7 21.1 %copy-start.2 = (bf16[8,3,1024]{2,0,1:T(8,128)(2,1)S(1)}, bf16[8,3,1024]{2,0,1:T(8,128)(2,1)}, u32[]{:S(2)}) copy-start(bf16[8,3,1024]{2,0,1:T(8,128)(2,1)} %param.26) | copy-start | bytes 147460
  0.7 7.0 %collective-permute-start = (bf16[8,4,512]{2,1,0:T(4,128)(2,1)}, bf16[8,4,512]{2,1,0:T(4,128)(2,1)S(1)}, u32[]{:S(2)}, u32[]{:S(2)}) collective-permute-start(bf16[8,4,512]{2,1,0:T(4,128)(2,1)} %param.15), channel_id=1, source_target_pairs={{0,3},{1,0},{2,1},{3,2},{4,7},{5,4},{6,5},{7,6},{8,11},{9,8},{10,9... | collective-permute-start | bytes 98312 | tf_op jit(solution)/shard_map/ppermute | solution.py:73
  5.8 5.0 %collective-permute-start.1 = (bf16[8,4,512]{2,1,0:T(4,128)(2,1)}, bf16[8,4,512]{2,1,0:T(4,128)(2,1)S(1)}, u32[]{:S(2)}, u32[]{:S(2)}) collective-permute-start(bf16[8,4,512]{2,1,0:T(4,128)(2,1)} %param.15), channel_id=1, source_target_pairs={{0,2},{1,3},{2,0},{3,1},{4,6},{5,7},{6,4},{7,5},{8,10},{9,11},{10,... | collective-permute-start | bytes 98312 | tf_op jit(solution)/shard_map/ppermute | solution.py:73
  5.8 5.9 %collective-permute-start.2 = (bf16[8,4,512]{2,1,0:T(4,128)(2,1)}, bf16[8,4,512]{2,1,0:T(4,128)(2,1)S(1)}, u32[]{:S(2)}, u32[]{:S(2)}) collective-permute-start(bf16[8,4,512]{2,1,0:T(4,128)(2,1)} %param.15), channel_id=1, source_target_pairs={{0,1},{1,2},{2,3},{3,0},{4,5},{5,6},{6,7},{7,4},{8,9},{9,10},{10,1... | collective-permute-start | bytes 98312 | tf_op jit(solution)/shard_map/ppermute | solution.py:73
  17.0 2.0 %collective-permute-start.4 = (f32[32,3200]{1,0:T(8,128)}, f32[32,3200]{1,0:T(8,128)S(1)}, u32[]{:S(2)}, u32[]{:S(2)}) collective-permute-start(f32[32,3200]{1,0:T(8,128)} %get-tuple-element.12), channel_id=1, source_target_pairs={{0,4},{4,0},{8,12},{12,8},{1,5},{5,1},{9,13},{13,9},{2,6},{6,2},{1... | collective-permute-start | bytes 1228808 | tf_op jit(solution)/shard_map/ppermute | solution.py:231
  17.0 5.5 %collective-permute-start.3 = (f32[32,3200]{1,0:T(8,128)}, f32[32,3200]{1,0:T(8,128)S(1)}, u32[]{:S(2)}, u32[]{:S(2)}) collective-permute-start(f32[32,3200]{1,0:T(8,128)} %get-tuple-element.10), channel_id=1, source_target_pairs={{0,4},{4,0},{8,12},{12,8},{1,5},{5,1},{9,13},{13,9},{2,6},{6,2},{1... | collective-permute-start | bytes 1228808 | tf_op jit(solution)/shard_map/ppermute | solution.py:231
  20.0 6.8 %collective-permute-start.5 = (f32[32,1152]{1,0:T(8,128)S(1)}, f32[32,1152]{1,0:T(8,128)S(1)}, u32[]{:S(2)}, u32[]{:S(2)}) collective-permute-start(f32[32,1152]{1,0:T(8,128)S(1)} %slice.128), channel_id=1, source_target_pairs={{0,8},{4,12},{8,0},{12,4},{1,9},{5,13},{9,1},{13,5},{2,10},{6,14},... | collective-permute-start | bytes 442376 | tf_op jit(solution)/shard_map/ppermute | solution.py:238
  21.9 9.7 %collective-permute-start.6 = (f32[32,2048]{1,0:T(8,128)S(1)}, f32[32,2048]{1,0:T(8,128)S(1)}, u32[]{:S(2)}, u32[]{:S(2)}) collective-permute-start(f32[32,2048]{1,0:T(8,128)S(1)} %slice.144), channel_id=1, source_target_pairs={{0,8},{4,12},{8,0},{12,4},{1,9},{5,13},{9,1},{13,5},{2,10},{6,14},... | collective-permute-start | bytes 786440 | tf_op jit(solution)/shard_map/ppermute | solution.py:238
  29.4 13.1 %copy-start.5 = (f32[128]{0:T(128)S(1)}, f32[128]{0:T(128)}, u32[]{:S(2)}) copy-start(f32[128]{0:T(128)} %param.23) | copy-start | bytes 1540
  43.4 2.4 %collective-permute-start.9 = (bf16[8,4,8,128]{3,2,1,0:T(8,128)(2,1)S(1)}, bf16[8,4,8,128]{3,2,1,0:T(8,128)(2,1)S(1)}, u32[]{:S(2)}, u32[]{:S(2)}) collective-permute-start(bf16[8,4,8,128]{3,2,1,0:T(8,128)(2,1)S(1)} %multiply_convert_fusion), channel_id=1, source_target_pairs={{0,12},{4,0},{8,4},{12,8},{1,13},{5,1},{9,5},{13,9},{2,14},{6,2},{... | collective-permute-start | bytes 196616 | tf_op jit(solution)/shard_map/ppermute | solution.py:34
  43.9 5.3 %collective-permute-start.8 = (bf16[8,4,8,128]{3,2,1,0:T(8,128)(2,1)S(1)}, bf16[8,4,8,128]{3,2,1,0:T(8,128)(2,1)S(1)}, u32[]{:S(2)}, u32[]{:S(2)}) collective-permute-start(bf16[8,4,8,128]{3,2,1,0:T(8,128)(2,1)S(1)} %multiply_convert_fusion), channel_id=1, source_target_pairs={{0,8},{4,12},{8,0},{12,4},{1,9},{5,13},{9,1},{13,5},{2,10},{6,14},... | collective-permute-start | bytes 196616 | tf_op jit(solution)/shard_map/ppermute | solution.py:34
  45.1 4.3 %collective-permute-start.7 = (bf16[8,4,8,128]{3,2,1,0:T(8,128)(2,1)S(1)}, bf16[8,4,8,128]{3,2,1,0:T(8,128)(2,1)S(1)}, u32[]{:S(2)}, u32[]{:S(2)}) collective-permute-start(bf16[8,4,8,128]{3,2,1,0:T(8,128)(2,1)S(1)} %multiply_convert_fusion), channel_id=1, source_target_pairs={{0,4},{4,8},{8,12},{12,0},{1,5},{5,9},{9,13},{13,1},{2,6},{6,10},{... | collective-permute-start | bytes 196616 | tf_op jit(solution)/shard_map/ppermute | solution.py:34
  50.3 4.3 %collective-permute-start.12 = (f32[32,512]{1,0:T(8,128)S(1)}, f32[32,512]{1,0:T(8,128)S(1)}, u32[]{:S(2)}, u32[]{:S(2)}) collective-permute-start(f32[32,512]{1,0:T(8,128)S(1)} %get-tuple-element.27), channel_id=1, source_target_pairs={{0,3},{1,0},{2,1},{3,2},{4,7},{5,4},{6,5},{7,6},{8,11},{9,8},{10,9... | collective-permute-start | bytes 196616 | tf_op jit(solution)/shard_map/ppermute | solution.py:47
  51.0 6.9 %collective-permute-start.11 = (f32[32,512]{1,0:T(8,128)S(1)}, f32[32,512]{1,0:T(8,128)S(1)}, u32[]{:S(2)}, u32[]{:S(2)}) collective-permute-start(f32[32,512]{1,0:T(8,128)S(1)} %get-tuple-element.28), channel_id=1, source_target_pairs={{0,2},{1,3},{2,0},{3,1},{4,6},{5,7},{6,4},{7,5},{8,10},{9,11},{10,... | collective-permute-start | bytes 196616 | tf_op jit(solution)/shard_map/ppermute | solution.py:47
  51.6 6.3 %collective-permute-start.10 = (f32[32,512]{1,0:T(8,128)S(1)}, f32[32,512]{1,0:T(8,128)S(1)}, u32[]{:S(2)}, u32[]{:S(2)}) collective-permute-start(f32[32,512]{1,0:T(8,128)S(1)} %get-tuple-element.26), channel_id=1, source_target_pairs={{0,1},{1,2},{2,3},{3,0},{4,5},{5,6},{6,7},{7,4},{8,9},{9,10},{10,1... | collective-permute-start | bytes 196616 | tf_op jit(solution)/shard_map/ppermute | solution.py:47

commit v18 on v17

--- a/solution.py
+++ b/solution.py
@@ -155,7 +155,7 @@
     steps = values.shape[1]
     key_cols = kt.shape[2]
     ratio = heads * steps // key_cols
-    block = 2 if rows % 2 == 0 else 1
+    block = 4 if rows % 4 == 0 else 1
     kern = functools.partial(recurrence_kernel, heads=heads, steps=steps, ratio=ratio, block=block)
     return pl.pallas_call(
         kern,

time: 59 us -> 59.3 us (level)
  no operation moved by 1% of the time
where the time goes in v18:
time: 59.3 us; the launch traced here: 59 us
  waiting for transfers between devices  18.4 us (31%)
  starting transfers between devices  13.8 us (23%)
  Pallas kernels  12.9 us (22%)
  other arithmetic  7.93 us (13%)
  local copies, waits for them, and re-layouts  4.59 us (8%)
  between operations  1.02 us (2%)
    pallas_call x1, Pallas kernels, recurrence(): pl.pallas_call(kern, grid=(rows // block,), in_specs=[pl.BlockSpec(memory...  9.17 us
    ppermute x3, starting transfers between devices, gather_pieces(): pieces.append(lax.ppermute(x, axis, [(i, (i + s) % n) for i in range(n)]))  6.11 us
    ppermute x3, waiting for transfers between devices, gather_pieces(): pieces.append(lax.ppermute(x, axis, [(i, (i + s) % n) for i in range(n)]))  4.91 us
    ppermute x3, waiting for transfers between devices, scatter_sum_rows(): acc = acc + lax.ppermute(send, axis, [(i, (i + s) % n) for i in range(n)])  4.36 us
    ppermute x3, waiting for transfers between devices, gather_rows(): pieces.append(lax.ppermute(x, axis, [(i, (i + s) % n) for i in range(n)]))  4.1 us
    pallas_call x1, Pallas kernels, projection(): pl.pallas_call(projection_kernel, out_shape=[jax.ShapeDtypeStruct((rows,...  3.72 us
    ppermute x2, waiting for transfers between devices, shards(): lax.ppermute(part[s][:, lo:hi], 'dp', perm)  3.69 us
    ppermute x3, starting transfers between devices, scatter_sum_rows(): acc = acc + lax.ppermute(send, axis, [(i, (i + s) % n) for i in range(n)])  3.21 us
  transfers between devices with their start and end apart: 13, of which 11 were waited for; matrix products, arithmetic and copies ran while one was open for 11% of the time, Pallas kernels for 0%

profile of v18, /device:TPU:0, one launch (start us, length us, event | category | flops | bytes accessed | tf_op | source)
XLA Modules:
  0.0 59.0 jit_solution(4139186520978397625)
XLA Ops:
  0.7 5.1 %collective-permute-start = (bf16[8,4,512]{2,1,0:T(4,128)(2,1)}, bf16[8,4,512]{2,1,0:T(4,128)(2,1)S(1)}, u32[]{:S(2)}, u32[]{:S(2)}) collective-permute-start(bf16[8,4,512]{2,1,0:T(4,128)(2,1)} %param.15), channel_id=1, source_target_pairs={{0,3},{1,0},{2,1},{3,2},{4,7},{5,4},{6,5},{7,6},{8,11},{9,8},{10,9... | collective-permute-start | bytes 98312 | tf_op jit(solution)/shard_map/ppermute | solution.py:73
  5.8 1.0 %collective-permute-start.2 = (bf16[8,4,512]{2,1,0:T(4,128)(2,1)}, bf16[8,4,512]{2,1,0:T(4,128)(2,1)S(1)}, u32[]{:S(2)}, u32[]{:S(2)}) collective-permute-start(bf16[8,4,512]{2,1,0:T(4,128)(2,1)} %param.15), channel_id=1, source_target_pairs={{0,1},{1,2},{2,3},{3,0},{4,5},{5,6},{6,7},{7,4},{8,9},{9,10},{10,1... | collective-permute-start | bytes 98312 | tf_op jit(solution)/shard_map/ppermute | solution.py:73
  6.8 0.9 %collective-permute-done = bf16[8,4,512]{2,1,0:T(4,128)(2,1)S(1)} collective-permute-done((bf16[8,4,512]{2,1,0:T(4,128)(2,1)}, bf16[8,4,512]{2,1,0:T(4,128)(2,1)S(1)}, u32[]{:S(2)}, u32[]{:S(2)}) %collective-permute-start) | collective-permute-done | bytes 32800 | tf_op jit(solution)/shard_map/ppermute | solution.py:73
  7.7 3.1 %collective-permute-done.1 = bf16[8,4,512]{2,1,0:T(4,128)(2,1)S(1)} collective-permute-done((bf16[8,4,512]{2,1,0:T(4,128)(2,1)}, bf16[8,4,512]{2,1,0:T(4,128)(2,1)S(1)}, u32[]{:S(2)}, u32[]{:S(2)}) %collective-permute-start.1) | collective-permute-done | bytes 32800 | tf_op jit(solution)/shard_map/ppermute | solution.py:73
  10.8 0.9 %collective-permute-done.2 = bf16[8,4,512]{2,1,0:T(4,128)(2,1)S(1)} collective-permute-done((bf16[8,4,512]{2,1,0:T(4,128)(2,1)}, bf16[8,4,512]{2,1,0:T(4,128)(2,1)S(1)}, u32[]{:S(2)}, u32[]{:S(2)}) %collective-permute-start.2) | collective-permute-done | bytes 32800 | tf_op jit(solution)/shard_map/ppermute | solution.py:73
  11.7 0.8 %select_select_fusion.3 = (bf16[4,8,512]{2,1,0:T(8,128)(2,1)S(1)}, bf16[4,8,512]{2,1,0:T(8,128)(2,1)S(1)}, bf16[4,8,512]{2,1,0:T(8,128)(2,1)S(1)}, bf16[4,8,512]{2,1,0:T(8,128)(2,1)S(1)}) fusion(bf16[4,8,512]{2,1,0:T(8,128)(2,1)S(1)} %bitcast.91, bf16[4,8,512]{2,1,0:T(8,128)(2,1)S(1)} %bitcast.92, bf16[4,8,512]{2,1,0:T(8,128)(2,1)S(1)} %bitcast.93, ...), kind=kLoop, calls=%fused_computation.46 | loop fusion | flops 196608 | bytes 262156 | tf_op jit(solution)/shard_map/jit(_where)/select_n | solution.py:225
  12.6 0.7 %pad_maximum_fusion.1.x_ref = bf16[128,512]{1,0:T(8,128)(2,1)} fusion(bf16[32,512]{1,0:T(8,128)(2,1)S(1)} %reshape.137, bf16[32,512]{1,0:T(8,128)(2,1)S(1)} %reshape.136, bf16[32,512]{1,0:T(8,128)(2,1)S(1)} %reshape.135, bf16[32,512]{1,0:T(8,128)(2,1)S(1)} %reshape.134), kind=kLoop, calls=%fused_computation.24 | loop fusion | flops 524288 | bytes 262144 | tf_op jit(solution)/shard_map/concatenate | solution.py:228
  13.3 3.7 %shard_map.140 = (f32[32,3200]{1,0:T(8,128)}, f32[32,3200]{1,0:T(8,128)}, f32[32,3200]{1,0:T(8,128)}, f32[32,3200]{1,0:T(8,128)}) custom-call(bf16[128,512]{1,0:T(8,128)(2,1)} %pad_maximum_fusion.1.x_ref, bf16[512,1024]{1,0:T(8,128)(2,1)} %wqk_ref.1, bf16[512,2048]{1,0:T(8,128)(2,1)} %wvz_ref.1, bf16[16,512]{1,0:T(8,128)(2,1)} %bitcast.94), custom_call_target="tpu_custom_call" | custom-call | flops 419430400 | bytes 5046272 | tf_op jit(solution)/shard_map/pallas_call | solution.py:111
  17.0 0.6 collective-permute-start.3
  17.6 1.3 %collective-permute-done.4 = f32[32,3200]{1,0:T(8,128)S(1)} collective-permute-done((f32[32,3200]{1,0:T(8,128)}, f32[32,3200]{1,0:T(8,128)S(1)}, u32[]{:S(2)}, u32[]{:S(2)}) %collective-permute-start.4) | collective-permute-done | bytes 409632 | tf_op jit(solution)/shard_map/ppermute | solution.py:231
  18.9 1.1 %add.200 = f32[32,3200]{1,0:T(8,128)S(1)} add(f32[32,3200]{1,0:T(8,128)} %get-tuple-element.11, f32[32,3200]{1,0:T(8,128)S(1)} %collective-permute-done.4) | non-fusion elementwise | flops 102400 | bytes 1228800 | tf_op jit(solution)/shard_map/add | solution.py:231
  20.0 1.6 %collective-permute-start.5 = (f32[32,1152]{1,0:T(8,128)S(1)}, f32[32,1152]{1,0:T(8,128)S(1)}, u32[]{:S(2)}, u32[]{:S(2)}) collective-permute-start(f32[32,1152]{1,0:T(8,128)S(1)} %slice.128), channel_id=1, source_target_pairs={{0,8},{4,12},{8,0},{12,4},{1,9},{5,13},{9,1},{13,5},{2,10},{6,14},... | collective-permute-start | bytes 442376 | tf_op jit(solution)/shard_map/ppermute | solution.py:238
  21.6 0.1 add.204
  21.7 0.1 mul.181
  21.9 0.6 %collective-permute-start.6 = (f32[32,2048]{1,0:T(8,128)S(1)}, f32[32,2048]{1,0:T(8,128)S(1)}, u32[]{:S(2)}, u32[]{:S(2)}) collective-permute-start(f32[32,2048]{1,0:T(8,128)S(1)} %slice.144), channel_id=1, source_target_pairs={{0,8},{4,12},{8,0},{12,4},{1,9},{5,13},{9,1},{13,5},{2,10},{6,14},... | collective-permute-start | bytes 786440 | tf_op jit(solution)/shard_map/ppermute | solution.py:238
  22.6 1.0 %add.199 = f32[32,3200]{1,0:T(8,128)S(1)} add(f32[32,3200]{1,0:T(8,128)} %get-tuple-element.9, f32[32,3200]{1,0:T(8,128)S(1)} %collective-permute-done.3) | non-fusion elementwise | flops 102400 | bytes 1228800 | tf_op jit(solution)/shard_map/add | solution.py:231
  23.6 3.2 %collective-permute-done.5 = f32[32,1152]{1,0:T(8,128)S(1)} collective-permute-done((f32[32,1152]{1,0:T(8,128)S(1)}, f32[32,1152]{1,0:T(8,128)S(1)}, u32[]{:S(2)}, u32[]{:S(2)}) %collective-permute-start.5) | collective-permute-done | bytes 147488 | tf_op jit(solution)/shard_map/ppermute | solution.py:238
  26.9 0.1 reshape.207
  27.0 0.1 copy.34
  27.2 0.1 copy.43
  27.6 0.2 divide_multiply_fusion.1
  27.8 0.1 reshape.139
  27.9 0.1 fusion.18
  28.0 0.1 multiply_reduce_fusion.2
  28.1 0.1 multiply_reduce_fusion.1
  28.2 1.0 %copy.39.qt_ref = f32[8,128,16]{2,1,0:T(8,128)} copy(f32[8,128,16]{1,0,2:T(8,128)S(1)} %bitcast.80) | data formatting | bytes 131072 | tf_op jit(solution)/shard_map/reshape | solution.py:255
  29.3 0.1 fusion.12
  29.4 1.0 %copy.40.kt_ref = f32[8,128,16]{2,1,0:T(8,128)} copy(f32[8,128,16]{1,0,2:T(8,128)S(1)} %bitcast.81) | data formatting | bytes 131072 | tf_op jit(solution)/shard_map/reshape | solution.py:256
  30.4 0.7 %pad_maximum_fusion.2.gates_ref = f32[8,64]{1,0:T(8,128)} fusion(f32[8,32]{1,0:T(8,128)S(1)} %fusion.14, f32[8,32]{1,0:T(8,128)S(1)} %div.76), kind=kLoop, calls=%fused_computation.56 | loop fusion | flops 512 | bytes 4096 | tf_op jit(solution)/shard_map/concatenate | solution.py:261
  31.1 0.5 collective-permute-done.6
  31.8 0.8 %divide_multiply_fusion.v_ref = f32[8,4,1024]{2,1,0:T(4,128)} fusion(f32[8,7,1024]{2,1,0:T(8,128)S(1)} %maximum_convert_fusion.1, f32[1024]{0:T(1024)S(1)} %bitcast.98, f32[1024]{0:T(1024)S(1)} %bitcast.97, f32[1024]{0:T(1024)S(1)} %bitcast.96, f32[1024]{0:T(1024)S(1)} %bitcast.95), kind=kLoop, calls=%fused_computation.8 | loop fusion | flops 360448 | bytes 671744 | tf_op jit(solution)/shard_map/jit(silu)/mul | solution.py:26
  32.6 9.2 %shard_map.141 = (f32[8,8,128,128]{3,2,1,0:T(8,128)}, f32[8,4,8,128]{3,2,1,0:T(8,128)}) custom-call(f32[8,64]{1,0:T(8,128)} %pad_maximum_fusion.2.gates_ref, f32[8,128,16]{2,1,0:T(8,128)} %copy.39.qt_ref, f32[8,128,16]{2,1,0:T(8,128)} %copy.40.kt_ref, f32[8,4,1024]{2,1,0:T(4,128)} %divide_multiply_fusion.v_ref, f32[8,8,128,128]{3,2,1,0:T(8,128)} %s_ref.1), custom_call_target="tpu_custom_call" | custom-call | flops 33554432 | bytes 8388608 | tf_op jit(solution)/shard_map/pallas_call | solution.py:160
  41.8 1.0 %multiply_reduce_fusion = f32[8,4,8]{2,1,0:T(4,128)S(1)} fusion(f32[8,4,8,128]{3,2,1,0:T(8,128)} %get-tuple-element.13), kind=kLoop, calls=%fused_computation.29 | loop fusion | flops 65280 | bytes 132096 | tf_op jit(solution)/shard_map/reduce_sum | solution.py:267
  42.9 1.0 %multiply_convert_fusion = bf16[8,4,8,128]{3,2,1,0:T(8,128)(2,1)S(1)} fusion(f32[8,4,8,128]{3,2,1,0:T(8,128)S(1)} %bitcast.79, f32[8,4,8,128]{3,2,1,0:T(8,128)} %get-tuple-element.13, f32[128]{0:T(128)S(1)} %copy-done.5, f32[8,4,8]{2,1,0:T(4,128)S(1)} %add_rsqrt_fusion), kind=kLoop, calls=%fused_computation.28 | loop fusion | flops 262144 | bytes 329216 | tf_op jit(solution)/shard_map/convert_element_type | solution.py:269
  43.9 0.5 collective-permute-start.9
  44.3 1.2 %collective-permute-start.8 = (bf16[8,4,8,128]{3,2,1,0:T(8,128)(2,1)S(1)}, bf16[8,4,8,128]{3,2,1,0:T(8,128)(2,1)S(1)}, u32[]{:S(2)}, u32[]{:S(2)}) collective-permute-start(bf16[8,4,8,128]{3,2,1,0:T(8,128)(2,1)S(1)} %multiply_convert_fusion), channel_id=1, source_target_pairs={{0,8},{4,12},{8,0},{12,4},{1,9},{5,13},{9,1},{13,5},{2,10},{6,14},... | collective-permute-start | bytes 196616 | tf_op jit(solution)/shard_map/ppermute | solution.py:34
  45.5 0.2 collective-permute-start.7
  45.7 0.6 collective-permute-done.9
  46.2 3.3 %collective-permute-done.8 = bf16[8,4,8,128]{3,2,1,0:T(8,128)(2,1)S(1)} collective-permute-done((bf16[8,4,8,128]{3,2,1,0:T(8,128)(2,1)S(1)}, bf16[8,4,8,128]{3,2,1,0:T(8,128)(2,1)S(1)}, u32[]{:S(2)}, u32[]{:S(2)}) %collective-permute-start.8) | collective-permute-done | bytes 65568 | tf_op jit(solution)/shard_map/ppermute | solution.py:34
  49.6 0.2 collective-permute-done.7
  49.8 0.6 %gather_fusion = bf16[4,8,4,8,128]{4,3,2,1,0:T(8,128)(2,1)S(1)} fusion(bf16[4,8,4,8,128]{4,3,2,1,0:T(8,128)(2,1)S(1)} %pad_maximum_fusion, s32[1024]{0:T(1024)S(1)} %pad_clamp_fusion), kind=kCustom, calls=%fused_computation | custom fusion | bytes 524304 | tf_op jit(solution)/shard_map/jit(_take)/gather | solution.py:37
  50.4 0.3 convolution_bitcast_fusion
  50.8 0.7 %collective-permute-start.12 = (f32[32,512]{1,0:T(8,128)S(1)}, f32[32,512]{1,0:T(8,128)S(1)}, u32[]{:S(2)}, u32[]{:S(2)}) collective-permute-start(f32[32,512]{1,0:T(8,128)S(1)} %get-tuple-element.27), channel_id=1, source_target_pairs={{0,3},{1,0},{2,1},{3,2},{4,7},{5,4},{6,5},{7,6},{8,11},{9,8},{10,9... | collective-permute-start | bytes 196616 | tf_op jit(solution)/shard_map/ppermute | solution.py:47
  51.4 0.6 %collective-permute-start.11 = (f32[32,512]{1,0:T(8,128)S(1)}, f32[32,512]{1,0:T(8,128)S(1)}, u32[]{:S(2)}, u32[]{:S(2)}) collective-permute-start(f32[32,512]{1,0:T(8,128)S(1)} %get-tuple-element.28), channel_id=1, source_target_pairs={{0,2},{1,3},{2,0},{3,1},{4,6},{5,7},{6,4},{7,5},{8,10},{9,11},{10,... | collective-permute-start | bytes 196616 | tf_op jit(solution)/shard_map/ppermute | solution.py:47
  52.0 1.9 %collective-permute-start.10 = (f32[32,512]{1,0:T(8,128)S(1)}, f32[32,512]{1,0:T(8,128)S(1)}, u32[]{:S(2)}, u32[]{:S(2)}) collective-permute-start(f32[32,512]{1,0:T(8,128)S(1)} %get-tuple-element.26), channel_id=1, source_target_pairs={{0,1},{1,2},{2,3},{3,0},{4,5},{5,6},{6,7},{7,4},{8,9},{9,10},{10,1... | collective-permute-start | bytes 196616 | tf_op jit(solution)/shard_map/ppermute | solution.py:47
  54.0 1.1 %collective-permute-done.12 = f32[32,512]{1,0:T(8,128)S(1)} collective-permute-done((f32[32,512]{1,0:T(8,128)S(1)}, f32[32,512]{1,0:T(8,128)S(1)}, u32[]{:S(2)}, u32[]{:S(2)}) %collective-permute-start.12) | collective-permute-done | bytes 65568 | tf_op jit(solution)/shard_map/ppermute | solution.py:47
  55.1 3.2 %collective-permute-done.11 = f32[32,512]{1,0:T(8,128)S(1)} collective-permute-done((f32[32,512]{1,0:T(8,128)S(1)}, f32[32,512]{1,0:T(8,128)S(1)}, u32[]{:S(2)}, u32[]{:S(2)}) %collective-permute-start.11) | collective-permute-done | bytes 65568 | tf_op jit(solution)/shard_map/ppermute | solution.py:47
  58.3 0.6 %reshape.147 = bf16[8,4,512]{2,1,0:T(4,128)(2,1)} reshape(bf16[32,512]{1,0:T(8,128)(2,1)S(1)} %fusion.11) | data formatting | bytes 65536 | tf_op jit(solution)/shard_map/reshape | solution.py:279
  (58 shorter events, 1.0 us)
Async XLA Ops:
  0.6 49.8 %copy-start = (bf16[1024,512]{1,0:T(8,128)(2,1)S(1)}, bf16[1024,512]{1,0:T(8,128)(2,1)}, u32[]{:S(2)}) copy-start(bf16[1024,512]{1,0:T(8,128)(2,1)} %param.24) | copy-start | bytes 3145732
  0.6 16.3 %copy-start.3 = (bf16[4,1024]{1,0:T(4,128)(2,1)S(1)}, bf16[4,1024]{1,0:T(4,128)(2,1)}, u32[]{:S(2)}) copy-start(bf16[4,1024]{1,0:T(4,128)(2,1)} %param.19) | copy-start | bytes 24580
  0.7 16.9 %copy-start.4 = (bf16[4,1024]{1,0:T(4,128)(2,1)S(1)}, bf16[4,1024]{1,0:T(4,128)(2,1)}, u32[]{:S(2)}) copy-start(bf16[4,1024]{1,0:T(4,128)(2,1)} %param.20) | copy-start | bytes 24580
  0.7 20.9 %copy-start.7 = (f32[8]{0:T(128)S(1)}, f32[8]{0:T(128)}, u32[]{:S(2)}) copy-start(f32[8]{0:T(128)} %param.21) | copy-start | bytes 100
  0.7 20.9 %copy-start.6 = (f32[8]{0:T(128)S(1)}, f32[8]{0:T(128)}, u32[]{:S(2)}) copy-start(f32[8]{0:T(128)} %param.22) | copy-start | bytes 100
  0.7 21.1 %copy-start.1 = (bf16[8,3,1024]{2,0,1:T(8,128)(2,1)S(1)}, bf16[8,3,1024]{2,0,1:T(8,128)(2,1)}, u32[]{:S(2)}) copy-start(bf16[8,3,1024]{2,0,1:T(8,128)(2,1)} %param.25) | copy-start | bytes 147460
  0.7 21.1 %copy-start.2 = (bf16[8,3,1024]{2,0,1:T(8,128)(2,1)S(1)}, bf16[8,3,1024]{2,0,1:T(8,128)(2,1)}, u32[]{:S(2)}) copy-start(bf16[8,3,1024]{2,0,1:T(8,128)(2,1)} %param.26) | copy-start | bytes 147460
  0.7 7.0 %collective-permute-start = (bf16[8,4,512]{2,1,0:T(4,128)(2,1)}, bf16[8,4,512]{2,1,0:T(4,128)(2,1)S(1)}, u32[]{:S(2)}, u32[]{:S(2)}) collective-permute-start(bf16[8,4,512]{2,1,0:T(4,128)(2,1)} %param.15), channel_id=1, source_target_pairs={{0,3},{1,0},{2,1},{3,2},{4,7},{5,4},{6,5},{7,6},{8,11},{9,8},{10,9... | collective-permute-start | bytes 98312 | tf_op jit(solution)/shard_map/ppermute | solution.py:73
  5.8 5.0 %collective-permute-start.1 = (bf16[8,4,512]{2,1,0:T(4,128)(2,1)}, bf16[8,4,512]{2,1,0:T(4,128)(2,1)S(1)}, u32[]{:S(2)}, u32[]{:S(2)}) collective-permute-start(bf16[8,4,512]{2,1,0:T(4,128)(2,1)} %param.15), channel_id=1, source_target_pairs={{0,2},{1,3},{2,0},{3,1},{4,6},{5,7},{6,4},{7,5},{8,10},{9,11},{10,... | collective-permute-start | bytes 98312 | tf_op jit(solution)/shard_map/ppermute | solution.py:73
  5.8 5.9 %collective-permute-start.2 = (bf16[8,4,512]{2,1,0:T(4,128)(2,1)}, bf16[8,4,512]{2,1,0:T(4,128)(2,1)S(1)}, u32[]{:S(2)}, u32[]{:S(2)}) collective-permute-start(bf16[8,4,512]{2,1,0:T(4,128)(2,1)} %param.15), channel_id=1, source_target_pairs={{0,1},{1,2},{2,3},{3,0},{4,5},{5,6},{6,7},{7,4},{8,9},{9,10},{10,1... | collective-permute-start | bytes 98312 | tf_op jit(solution)/shard_map/ppermute | solution.py:73
  17.0 2.0 %collective-permute-start.4 = (f32[32,3200]{1,0:T(8,128)}, f32[32,3200]{1,0:T(8,128)S(1)}, u32[]{:S(2)}, u32[]{:S(2)}) collective-permute-start(f32[32,3200]{1,0:T(8,128)} %get-tuple-element.12), channel_id=1, source_target_pairs={{0,4},{4,0},{8,12},{12,8},{1,5},{5,1},{9,13},{13,9},{2,6},{6,2},{1... | collective-permute-start | bytes 1228808 | tf_op jit(solution)/shard_map/ppermute | solution.py:231
  17.0 5.5 %collective-permute-start.3 = (f32[32,3200]{1,0:T(8,128)}, f32[32,3200]{1,0:T(8,128)S(1)}, u32[]{:S(2)}, u32[]{:S(2)}) collective-permute-start(f32[32,3200]{1,0:T(8,128)} %get-tuple-element.10), channel_id=1, source_target_pairs={{0,4},{4,0},{8,12},{12,8},{1,5},{5,1},{9,13},{13,9},{2,6},{6,2},{1... | collective-permute-start | bytes 1228808 | tf_op jit(solution)/shard_map/ppermute | solution.py:231
  20.0 6.8 %collective-permute-start.5 = (f32[32,1152]{1,0:T(8,128)S(1)}, f32[32,1152]{1,0:T(8,128)S(1)}, u32[]{:S(2)}, u32[]{:S(2)}) collective-permute-start(f32[32,1152]{1,0:T(8,128)S(1)} %slice.128), channel_id=1, source_target_pairs={{0,8},{4,12},{8,0},{12,4},{1,9},{5,13},{9,1},{13,5},{2,10},{6,14},... | collective-permute-start | bytes 442376 | tf_op jit(solution)/shard_map/ppermute | solution.py:238
  21.9 9.7 %collective-permute-start.6 = (f32[32,2048]{1,0:T(8,128)S(1)}, f32[32,2048]{1,0:T(8,128)S(1)}, u32[]{:S(2)}, u32[]{:S(2)}) collective-permute-start(f32[32,2048]{1,0:T(8,128)S(1)} %slice.144), channel_id=1, source_target_pairs={{0,8},{4,12},{8,0},{12,4},{1,9},{5,13},{9,1},{13,5},{2,10},{6,14},... | collective-permute-start | bytes 786440 | tf_op jit(solution)/shard_map/ppermute | solution.py:238
  29.4 13.5 %copy-start.5 = (f32[128]{0:T(128)S(1)}, f32[128]{0:T(128)}, u32[]{:S(2)}) copy-start(f32[128]{0:T(128)} %param.23) | copy-start | bytes 1540
  43.9 2.4 %collective-permute-start.9 = (bf16[8,4,8,128]{3,2,1,0:T(8,128)(2,1)S(1)}, bf16[8,4,8,128]{3,2,1,0:T(8,128)(2,1)S(1)}, u32[]{:S(2)}, u32[]{:S(2)}) collective-permute-start(bf16[8,4,8,128]{3,2,1,0:T(8,128)(2,1)S(1)} %multiply_convert_fusion), channel_id=1, source_target_pairs={{0,12},{4,0},{8,4},{12,8},{1,13},{5,1},{9,5},{13,9},{2,14},{6,2},{... | collective-permute-start | bytes 196616 | tf_op jit(solution)/shard_map/ppermute | solution.py:34
  44.3 5.3 %collective-permute-start.8 = (bf16[8,4,8,128]{3,2,1,0:T(8,128)(2,1)S(1)}, bf16[8,4,8,128]{3,2,1,0:T(8,128)(2,1)S(1)}, u32[]{:S(2)}, u32[]{:S(2)}) collective-permute-start(bf16[8,4,8,128]{3,2,1,0:T(8,128)(2,1)S(1)} %multiply_convert_fusion), channel_id=1, source_target_pairs={{0,8},{4,12},{8,0},{12,4},{1,9},{5,13},{9,1},{13,5},{2,10},{6,14},... | collective-permute-start | bytes 196616 | tf_op jit(solution)/shard_map/ppermute | solution.py:34
  45.5 4.3 %collective-permute-start.7 = (bf16[8,4,8,128]{3,2,1,0:T(8,128)(2,1)S(1)}, bf16[8,4,8,128]{3,2,1,0:T(8,128)(2,1)S(1)}, u32[]{:S(2)}, u32[]{:S(2)}) collective-permute-start(bf16[8,4,8,128]{3,2,1,0:T(8,128)(2,1)S(1)} %multiply_convert_fusion), channel_id=1, source_target_pairs={{0,4},{4,8},{8,12},{12,0},{1,5},{5,9},{9,13},{13,1},{2,6},{6,10},{... | collective-permute-start | bytes 196616 | tf_op jit(solution)/shard_map/ppermute | solution.py:34
  50.8 4.3 %collective-permute-start.12 = (f32[32,512]{1,0:T(8,128)S(1)}, f32[32,512]{1,0:T(8,128)S(1)}, u32[]{:S(2)}, u32[]{:S(2)}) collective-permute-start(f32[32,512]{1,0:T(8,128)S(1)} %get-tuple-element.27), channel_id=1, source_target_pairs={{0,3},{1,0},{2,1},{3,2},{4,7},{5,4},{6,5},{7,6},{8,11},{9,8},{10,9... | collective-permute-start | bytes 196616 | tf_op jit(solution)/shard_map/ppermute | solution.py:47
  51.4 6.9 %collective-permute-start.11 = (f32[32,512]{1,0:T(8,128)S(1)}, f32[32,512]{1,0:T(8,128)S(1)}, u32[]{:S(2)}, u32[]{:S(2)}) collective-permute-start(f32[32,512]{1,0:T(8,128)S(1)} %get-tuple-element.28), channel_id=1, source_target_pairs={{0,2},{1,3},{2,0},{3,1},{4,6},{5,7},{6,4},{7,5},{8,10},{9,11},{10,... | collective-permute-start | bytes 196616 | tf_op jit(solution)/shard_map/ppermute | solution.py:47
  52.0 6.3 %collective-permute-start.10 = (f32[32,512]{1,0:T(8,128)S(1)}, f32[32,512]{1,0:T(8,128)S(1)}, u32[]{:S(2)}, u32[]{:S(2)}) collective-permute-start(f32[32,512]{1,0:T(8,128)S(1)} %get-tuple-element.26), channel_id=1, source_target_pairs={{0,1},{1,2},{2,3},{3,0},{4,5},{5,6},{6,7},{7,4},{8,9},{9,10},{10,1... | collective-permute-start | bytes 196616 | tf_op jit(solution)/shard_map/ppermute | solution.py:47
